TPU v7x, 32 devices: a whole 2x2x4 slice. The times are simulated.
32 devices in a mesh: clip: 2 (over y), strip: 4 (over z), tm: 4 (over x, core).
Axes of the slice: x: 2, y: 2, z: 4, core: 2. Of those that a mesh axis runs over, the one named last changes fastest.
Arguments:
- frames: bfloat16 [8, 12, 160, 384], P(('clip', 'tm'), 'strip'), parts along dimension 0, may hold values from -6 to 6
- cache_frames: bfloat16 [4, 12, 160, 384], P('clip', 'strip'), parts along dimension 0, may hold values from -6 to 6
- attn_gain: float32 [384], replicated, may hold values from 0.1 to 1.9
- query_weight: bfloat16 [384, 384], replicated, may hold values from -4 to 4
- key_weight: bfloat16 [384, 384], replicated, may hold values from -2 to 2
- value_weight: bfloat16 [384, 384], replicated, may hold values from -0.3125 to 0.3125
- out_weight: bfloat16 [384, 384], replicated, may hold values from -0.3125 to 0.3125
- conv_gain: float32 [384], replicated, may hold values from 0.1 to 1.9
- conv_weight: bfloat16 [3, 3, 3, 384, 384], replicated, may hold values from -0.0625 to 0.0625
Outputs:
- decoded: bfloat16 [8, 12, 160, 384], P(('clip', 'tm'), 'strip'), parts along dimension 0
There are 2 independent parts, one for each index of `clip`. A program takes and returns all parts, laid end to end along the dimension named above; an argument that names none is the same for every part. Nothing has to cross between parts.
All inputs are finite; a program needn't handle non-finite values.
Results may differ from a plain program's by a relative error of at most 0.009.
Values may be sent and summed in bfloat16 or wider, within the bound.
No kernel may reach another device: no remote copies, remote signals or barrier semaphores. Data moves between devices by JAX's collectives and lax.ppermute only.
A program may use at most 128 MiB of HBM per device.

v0:
```python
import jax
import jax.numpy as jnp
from jax import lax
from jax.sharding import PartitionSpec as P


def passed_along(x, axis, by):
    size = lax.axis_size(axis)
    pairs = [(i, i + by) for i in range(size) if 0 <= i + by < size]
    return lax.ppermute(x, axis, pairs)


def with_halo(x, sides, width):
    for axis, dim in sides:
        size, length = (lax.axis_size(axis), x.shape[dim])
        up = [(i, (i + 1) % size) for i in range(size - 1)]
        down = [(j, i) for i, j in up]
        last = lax.slice_in_dim(x, length - width, length, axis=dim)
        leading = lax.slice_in_dim(x, 0, width, axis=dim)
        before = lax.ppermute(last, axis, up)
        after = lax.ppermute(leading, axis, down)
        x = jnp.concatenate([before, x, after], axis=dim)
    return x


def rms_scale(values, gain):
    wide = values.astype(jnp.float32)
    return wide * lax.rsqrt(jnp.mean(wide * wide, axis=-1, keepdims=True) + 1e-06) * gain


def attend(carry, query, keys, values, scale):
    peak, total, summed = carry
    scores = (
        lax.dot_general(query, keys, (((1,), (1,)), ((), ())), preferred_element_type=jnp.float32)
        * scale
    )
    fresh = jnp.maximum(peak, jnp.max(scores, axis=1))
    weights = jnp.exp(scores - fresh[:, None])
    total = jnp.sum(weights, axis=1)
    summed = jnp.dot(weights.astype(jnp.bfloat16), values, preferred_element_type=jnp.float32)
    return (fresh, total, summed)


def shards(
    frames,
    cache_frames,
    attn_gain,
    query_weight,
    key_weight,
    value_weight,
    out_weight,
    conv_gain,
    conv_weight,
):
    rows = frames.shape[1]
    cols = frames.shape[2]
    width = frames.shape[3]
    flat = frames.reshape(-1, width)
    count = flat.shape[0]
    scale = 1.0 / jnp.sqrt(jnp.float32(width))
    normed = rms_scale(flat, attn_gain).astype(jnp.bfloat16)
    query = jnp.dot(normed, query_weight, preferred_element_type=jnp.float32).astype(jnp.bfloat16)
    start_carry = (
        jnp.full((count,), -1e30, jnp.float32),
        jnp.zeros((count,), jnp.float32),
        jnp.zeros((count, width), jnp.float32),
    )
    keys = jnp.dot(normed, key_weight, preferred_element_type=jnp.float32).astype(jnp.bfloat16)
    values = jnp.dot(normed, value_weight, preferred_element_type=jnp.float32).astype(jnp.bfloat16)
    peak, total, summed = attend(
        start_carry,
        query,
        lax.all_gather(keys, "strip", axis=0, tiled=True),
        lax.all_gather(values, "strip", axis=0, tiled=True),
        scale,
    )
    attended = (summed / total[:, None]).astype(jnp.bfloat16)
    resid = (
        flat.astype(jnp.float32) + jnp.dot(attended, out_weight, preferred_element_type=jnp.float32)
    ).astype(jnp.bfloat16)
    act = jax.nn.silu(rms_scale(resid, conv_gain)).astype(jnp.bfloat16).reshape(rows, cols, width)
    frame_index = lax.axis_index("tm")
    prior = passed_along(act, "tm", 1)
    prior = jnp.where(frame_index == 0, cache_frames[1], prior)
    older = passed_along(prior, "tm", 1)
    older = jnp.where(frame_index == 0, cache_frames[0], older)
    stacked = jnp.stack([older, prior, act])
    padded = with_halo(stacked, (("strip", 1),), 1)
    padded = jnp.pad(padded, ((0, 0), (0, 0), (1, 1), (0, 0)))
    widened = jnp.concatenate(
        [padded[:, :, 0:cols], padded[:, :, 1 : cols + 1], padded[:, :, 2 : cols + 2]], axis=-1
    )
    kernel = conv_weight.reshape(3, 3, 3 * width, width)
    result = resid.astype(jnp.float32)
    for step_t in range(3):
        for step_r in range(3):
            window = widened[step_t, step_r : step_r + rows].reshape(-1, 3 * width)
            result = result + jnp.dot(
                window, kernel[step_t, step_r], preferred_element_type=jnp.float32
            )
    return result.astype(jnp.bfloat16).reshape(1, rows, cols, width)


def solution(mesh):
    return jax.shard_map(
        shards,
        mesh=mesh,
        in_specs=(
            P(("clip", "tm"), "strip", None, None),
            P("clip", "strip", None, None),
            P(),
            P(),
            P(),
            P(),
            P(),
            P(),
            P(),
        ),
        out_specs=P(("clip", "tm"), "strip", None, None),
        check_vma=False,
    )
```

profile of v0, /device:TPU:10, one launch (start us, length us, event | category | flops | bytes accessed | tf_op | source)
XLA Modules:
  0.0 138.5 jit_solution(2790233576153170872)
XLA Ops:
  6.5 0.0 copy-start
  6.5 0.0 all-gather.3.cloned.1.call-start
  6.5 1.2 multiply_reduce_fusion.2
  7.8 0.1 rsqrt.20
  7.9 1.1 fusion.41
  9.0 2.1 %convolution_convert_fusion.1 = bf16[480,384]{1,0:T(8,128)(2,1)} fusion(bf16[480,384]{1,0:T(8,128)(2,1)S(1)} %fusion.41, bf16[384,384]{1,0:T(8,128)(2,1)} %param.13), kind=kOutput, calls=%fused_computation.32 | convolution fusion | flops 141742080 | bytes 1032192 | tf_op jit(solution)/shard_map/dot_general | solution.py:68
  11.1 0.0 all-gather.3.cloned.1.call-update
  11.1 0.0 all-gather.5.cloned.1.call-start
  11.2 0.0 copy-done.3
  11.2 1.1 convolution_convert_fusion
  12.3 0.0 all-gather.5.cloned.1.call-update
  12.3 34.7 %all-gather.3.cloned.1.call-done = bf16[1920,384]{1,0:T(8,128)(2,1)} async-done(((bf16[480,384]{1,0:T(8,128)(2,1)}), bf16[1920,384]{1,0:T(8,128)(2,1)}) %all-gather.3.cloned.1.call-update) | async-done | bytes 1474576 | tf_op jit(solution)/shard_map/all_gather | solution.py:73
  47.0 0.0 copy-done
  47.0 4.6 %multiply_reduce_fusion = (f32[480]{0:T(512)S(1)}, f32[480,1920]{1,0:T(8,128)}) fusion(bf16[1920,384]{1,0:T(8,128)(2,1)} %all-gather.3.cloned.1.call-done, bf16[480,384]{1,0:T(8,128)(2,1)S(1)} %fusion.41, bf16[384,384]{1,0:T(8,128)(2,1)S(1)} %copy-done), kind=kOutput, calls=%fused_computation.5 | convolution fusion | flops 851373568 | bytes 5826432 | tf_op jit(solution)/shard_map/dot_general | solution.py:34
  51.6 2.9 %fusion.1 = f32[480]{0:T(512)S(1)} fusion(f32[480,1920]{1,0:T(8,128)} %get-tuple-element.19, f32[480]{0:T(512)S(1)} %broadcast_maximum_fusion), kind=kLoop, calls=%fused_computation.6 | loop fusion | flops 2764320 | bytes 3690240 | tf_op jit(solution)/shard_map/reduce_sum | solution.py:39
  54.5 28.4 %all-gather.5.cloned.1.call-done = bf16[1920,384]{1,0:T(8,128)(2,1)} async-done(((bf16[480,384]{1,0:T(8,128)(2,1)}), bf16[1920,384]{1,0:T(8,128)(2,1)}) %all-gather.5.cloned.1.call-update) | async-done | bytes 1474576 | tf_op jit(solution)/shard_map/all_gather | solution.py:74
  82.9 0.0 copy-done.1
  82.9 0.0 copy-done.5
  82.9 4.1 %multiply_reduce_fusion.1 = (f32[480]{0:T(512)S(1)}, f32[480,384]{1,0:T(8,128)S(1)}) fusion(bf16[384,384]{1,0:T(8,128)(2,1)S(1)} %copy-done.5, bf16[1920,384]{1,0:T(8,128)(2,1)} %all-gather.5.cloned.1.call-done, f32[480,1920]{1,0:T(8,128)} %get-tuple-element.19, f32[480]{0:T(512)S(1)} %broadcast_maximum_fusion, f32[480]{0:T(512)S(1)} %fusion.1, ...), kind=kOutput, calls=%fused_computation.58 | convolution fusion | flops 853585408 | bytes 6567552 | tf_op jit(solution)/shard_map/dot_general | solution.py:79
  87.1 0.0 copy-done.4
  87.1 0.3 multiply_convert_fusion
  87.4 1.9 %collective-permute-start = (bf16[3,160,384]{2,1,0:T(8,128)(2,1)S(1)}, bf16[3,160,384]{2,1,0:T(8,128)(2,1)S(1)}, u32[]{:S(2)}, u32[]{:S(2)}) collective-permute-start(bf16[3,160,384]{2,1,0:T(8,128)(2,1)S(1)} %bitcast.74), channel_id=1, source_target_pairs={{0,1},{1,2},{2,3},{4,5},{5,6},{6,7},{8,9},{9,10},{10,11},{12,13},{... | collective-permute-start | bytes 1105928 | tf_op jit(solution)/shard_map/ppermute | solution.py:10
  89.3 6.9 %collective-permute-done = bf16[3,160,384]{2,1,0:T(8,128)(2,1)S(1)} collective-permute-done((bf16[3,160,384]{2,1,0:T(8,128)(2,1)S(1)}, bf16[3,160,384]{2,1,0:T(8,128)(2,1)S(1)}, u32[]{:S(2)}, u32[]{:S(2)}) %collective-permute-start) | collective-permute-done | bytes 368672 | tf_op jit(solution)/shard_map/ppermute | solution.py:10
  96.2 0.0 copy-done.2
  96.2 1.9 %collective-permute-start.1 = (bf16[3,160,384]{2,1,0:T(8,128)(2,1)S(1)}, bf16[3,160,384]{2,1,0:T(8,128)(2,1)S(1)}, u32[]{:S(2)}, u32[]{:S(2)}) collective-permute-start(bf16[3,160,384]{2,1,0:T(8,128)(2,1)S(1)} %bitcast_select_fusion), channel_id=1, source_target_pairs={{0,1},{1,2},{2,3},{4,5},{5,6},{6,7},{8,9},{9,10},{10,11},{12,13},{... | collective-permute-start | bytes 1105928 | tf_op jit(solution)/shard_map/ppermute | solution.py:10
  98.2 6.9 %collective-permute-done.1 = bf16[3,160,384]{2,1,0:T(8,128)(2,1)S(1)} collective-permute-done((bf16[3,160,384]{2,1,0:T(8,128)(2,1)S(1)}, bf16[3,160,384]{2,1,0:T(8,128)(2,1)S(1)}, u32[]{:S(2)}, u32[]{:S(2)}) %collective-permute-start.1) | collective-permute-done | bytes 368672 | tf_op jit(solution)/shard_map/ppermute | solution.py:10
  105.1 0.1 pad_maximum_fusion.3
  105.2 3.1 %collective-permute-start.2 = (bf16[3,1,160,384]{3,2,1,0:T(8,128)(2,1)S(1)}, bf16[3,1,160,384]{3,2,1,0:T(8,128)(2,1)S(1)}, u32[]{:S(2)}, u32[]{:S(2)}) collective-permute-start(bf16[3,1,160,384]{3,2,1,0:T(8,128)(2,1)S(1)} %get-tuple-element.16), channel_id=1, source_target_pairs={{0,4},{4,8},{8,12},{1,5},{5,9},{9,13},{2,6},{6,10},{10,14},{3,7},{... | collective-permute-start | bytes 1105928 | tf_op jit(solution)/shard_map/ppermute | solution.py:20
  108.3 2.9 %collective-permute-start.3 = (bf16[3,1,160,384]{3,2,1,0:T(8,128)(2,1)S(1)}, bf16[3,1,160,384]{3,2,1,0:T(8,128)(2,1)S(1)}, u32[]{:S(2)}, u32[]{:S(2)}) collective-permute-start(bf16[3,1,160,384]{3,2,1,0:T(8,128)(2,1)S(1)} %get-tuple-element.17), channel_id=1, source_target_pairs={{4,0},{8,4},{12,8},{5,1},{9,5},{13,9},{6,2},{10,6},{14,10},{7,3},{... | collective-permute-start | bytes 1105928 | tf_op jit(solution)/shard_map/ppermute | solution.py:21
  111.3 3.3 %collective-permute-done.2 = bf16[3,1,160,384]{3,2,1,0:T(8,128)(2,1)S(1)} collective-permute-done((bf16[3,1,160,384]{3,2,1,0:T(8,128)(2,1)S(1)}, bf16[3,1,160,384]{3,2,1,0:T(8,128)(2,1)S(1)}, u32[]{:S(2)}, u32[]{:S(2)}) %collective-permute-start.2) | collective-permute-done | bytes 368672 | tf_op jit(solution)/shard_map/ppermute | solution.py:20
  114.6 3.1 %collective-permute-done.3 = bf16[3,1,160,384]{3,2,1,0:T(8,128)(2,1)S(1)} collective-permute-done((bf16[3,1,160,384]{3,2,1,0:T(8,128)(2,1)S(1)}, bf16[3,1,160,384]{3,2,1,0:T(8,128)(2,1)S(1)}, u32[]{:S(2)}, u32[]{:S(2)}) %collective-permute-start.3) | collective-permute-done | bytes 368672 | tf_op jit(solution)/shard_map/ppermute | solution.py:21
  117.8 1.5 %select_maximum_fusion = bf16[3,5,162,384]{3,2,1,0:T(8,128)(2,1)S(1)} fusion(bf16[3,1,160,384]{3,2,1,0:T(8,128)(2,1)S(1)} %collective-permute-done.3, bf16[3,1,160,384]{3,2,1,0:T(8,128)(2,1)S(1)} %collective-permute-done.2, bf16[1,3,160,384]{3,2,1,0:T(8,128)(2,1)S(1)} %bitcast.76, bf16[1,3,160,384]{3,2,1,0:T(8,128)(2,1)S(1)} %bitcast.79, ...), kind=kLoop, calls=%fused_computation.8 | loop fusion | flops 16796160 | bytes 3709440 | tf_op jit(solution)/shard_map/concatenate | solution.py:22
  119.3 1.0 fusion.47
  120.3 0.0 slice-start
  120.3 0.6 pad_maximum_fusion
  120.9 0.0 slice-start.1
  120.9 1.0 fusion.46
  121.9 0.5 slice-done
  122.5 1.3 slice-done.1
  123.8 0.8 fusion.32
  124.6 0.8 fusion.33
  125.3 0.8 fusion.34
  126.1 0.8 fusion.35
  126.9 0.8 fusion.36
  127.6 0.8 fusion.37
  128.4 0.8 fusion.38
  129.2 0.8 fusion.39
  129.9 1.8 %fusion.20 = bf16[480,384]{1,0:T(8,128)(2,1)} fusion(f32[480,384]{1,0:T(8,128)S(1)} %fusion.32, f32[480,384]{1,0:T(8,128)S(1)} %fusion.33, f32[480,384]{1,0:T(8,128)S(1)} %fusion.34, f32[480,384]{1,0:T(8,128)S(1)} %fusion.35, f32[480,384]{1,0:T(8,128)S(1)} %fusion.36, f32[480,384]{1,0:T(8,128)S(1)} %fusion.37, f32[480,384]{1,0:T(8,128)S(1)} %fusion.38, ...), kind=kOutput, calls=%fused_computation.28 | convolution fusion | flops 426516480 | bytes 8994816 | tf_op jit(solution)/shard_map/dot_general | solution.py:98
  (11 shorter events, 0.1 us)
Async XLA Ops:
  6.5 40.5 %copy-start = (bf16[384,384]{1,0:T(8,128)(2,1)S(1)}, bf16[384,384]{1,0:T(8,128)(2,1)}, u32[]{:S(2)}) copy-start(bf16[384,384]{1,0:T(8,128)(2,1)} %param.12) | copy-start | bytes 884740
  6.5 4.6 %copy-start.3 = (bf16[384,384]{1,0:T(8,128)(2,1)S(1)}, bf16[384,384]{1,0:T(8,128)(2,1)}, u32[]{:S(2)}) copy-start(bf16[384,384]{1,0:T(8,128)(2,1)} %param.14) | copy-start | bytes 884740
  6.5 40.5 %all-gather.3.cloned.1.call-start = ((), (), s32[]{:S(2)}) async-start(), calls=%async_computation | async-start | bytes 1843200 | tf_op jit(solution)/shard_map/all_gather | solution.py:73
  11.1 71.8 %all-gather.5.cloned.1.call-start = ((), (), s32[]{:S(2)}) async-start(), calls=%async_computation.1 | async-start | bytes 1843200 | tf_op jit(solution)/shard_map/all_gather | solution.py:74
  51.6 31.3 %copy-start.1 = (bf16[1,3,160,384]{3,2,1,0:T(8,128)(2,1)S(1)}, bf16[1,3,160,384]{3,2,1,0:T(8,128)(2,1)}, u32[]{:S(2)}) copy-start(bf16[1,3,160,384]{3,2,1,0:T(8,128)(2,1)} %param.9) | copy-start | bytes 1105924
  51.6 31.3 %copy-start.5 = (bf16[384,384]{1,0:T(8,128)(2,1)S(1)}, bf16[384,384]{1,0:T(8,128)(2,1)}, u32[]{:S(2)}) copy-start(bf16[384,384]{1,0:T(8,128)(2,1)} %param.15) | copy-start | bytes 884740
  82.9 4.2 %copy-start.4 = (f32[384]{0:T(512)S(1)}, f32[384]{0:T(512)}, u32[]{:S(2)}) copy-start(f32[384]{0:T(512)} %param.16) | copy-start | bytes 4612
  82.9 13.3 %copy-start.2 = (bf16[2,3,160,384]{3,2,1,0:T(8,128)(2,1)S(1)}, bf16[2,3,160,384]{3,2,1,0:T(8,128)(2,1)}, u32[]{:S(2)}) copy-start(bf16[2,3,160,384]{3,2,1,0:T(8,128)(2,1)} %param.10) | copy-start | bytes 2211844
  87.4 8.8 %collective-permute-start = (bf16[3,160,384]{2,1,0:T(8,128)(2,1)S(1)}, bf16[3,160,384]{2,1,0:T(8,128)(2,1)S(1)}, u32[]{:S(2)}, u32[]{:S(2)}) collective-permute-start(bf16[3,160,384]{2,1,0:T(8,128)(2,1)S(1)} %bitcast.74), channel_id=1, source_target_pairs={{0,1},{1,2},{2,3},{4,5},{5,6},{6,7},{8,9},{9,10},{10,11},{12,13},{... | collective-permute-start | bytes 1105928 | tf_op jit(solution)/shard_map/ppermute | solution.py:10
  96.2 8.8 %collective-permute-start.1 = (bf16[3,160,384]{2,1,0:T(8,128)(2,1)S(1)}, bf16[3,160,384]{2,1,0:T(8,128)(2,1)S(1)}, u32[]{:S(2)}, u32[]{:S(2)}) collective-permute-start(bf16[3,160,384]{2,1,0:T(8,128)(2,1)S(1)} %bitcast_select_fusion), channel_id=1, source_target_pairs={{0,1},{1,2},{2,3},{4,5},{5,6},{6,7},{8,9},{9,10},{10,11},{12,13},{... | collective-permute-start | bytes 1105928 | tf_op jit(solution)/shard_map/ppermute | solution.py:10
  105.2 9.4 %collective-permute-start.2 = (bf16[3,1,160,384]{3,2,1,0:T(8,128)(2,1)S(1)}, bf16[3,1,160,384]{3,2,1,0:T(8,128)(2,1)S(1)}, u32[]{:S(2)}, u32[]{:S(2)}) collective-permute-start(bf16[3,1,160,384]{3,2,1,0:T(8,128)(2,1)S(1)} %get-tuple-element.16), channel_id=1, source_target_pairs={{0,4},{4,8},{8,12},{1,5},{5,9},{9,13},{2,6},{6,10},{10,14},{3,7},{... | collective-permute-start | bytes 1105928 | tf_op jit(solution)/shard_map/ppermute | solution.py:20
  108.3 9.4 %collective-permute-start.3 = (bf16[3,1,160,384]{3,2,1,0:T(8,128)(2,1)S(1)}, bf16[3,1,160,384]{3,2,1,0:T(8,128)(2,1)S(1)}, u32[]{:S(2)}, u32[]{:S(2)}) collective-permute-start(bf16[3,1,160,384]{3,2,1,0:T(8,128)(2,1)S(1)} %get-tuple-element.17), channel_id=1, source_target_pairs={{4,0},{8,4},{12,8},{5,1},{9,5},{13,9},{6,2},{10,6},{14,10},{7,3},{... | collective-permute-start | bytes 1105928 | tf_op jit(solution)/shard_map/ppermute | solution.py:21
  120.3 2.2 %slice-start = ((s8[7962624]{0:T(1024)(128)(4,1)}), s8[4194304]{0:T(1024)(128)(4,1)S(1)}, s32[]{:S(2)}) async-start(s8[7962624]{0:T(1024)(128)(4,1)} %bitcast.91), calls=%async_computation.2 | async-start | bytes 8388608
  120.9 2.9 %slice-start.1 = ((s8[7962624]{0:T(1024)(128)(4,1)}), s8[3768320]{0:T(1024)(128)(4,1)S(1)}, s32[]{:S(2)}) async-start(s8[7962624]{0:T(1024)(128)(4,1)} %bitcast.91), calls=%async_computation.3 | async-start | bytes 7536640
Sparse Core Ops, SparseCore 0:
  11.3 35.7 all-gather.2
  48.6 34.2 all-gather.4
where the time goes:
time: 139 us
  waiting for transfers between devices  83.4 us (60%)
  matrix products  19.8 us (14%)
  between operations  13.6 us (10%)
  starting transfers between devices  9.93 us (7%)
  other arithmetic  7.89 us (6%)
  local copies, waits for them, and re-layouts  3.93 us (3%)
    all_gather x1, waiting for transfers between devices, shards(): lax.all_gather(keys, 'strip', axis=0, tiled=True)  34.7 us
    all_gather x1, waiting for transfers between devices, shards(): lax.all_gather(values, 'strip', axis=0, tiled=True)  28.4 us
    ppermute x2, waiting for transfers between devices, passed_along(): return lax.ppermute(x, axis, pairs)  13.8 us
    dot_general x9, matrix products, shards(): jnp.dot(window, kernel[step_t, step_r], preferred_element_type=jnp.float32)  7.82 us
    dot_general x1, matrix products, attend(): lax.dot_general(query, keys, (((1,), (1,)), ((), ())), preferred_element_...  4.61 us
    dot_general x1, matrix products, shards(): jnp.dot(attended, out_weight, preferred_element_type=jnp.float32)  4.14 us
    ppermute x2, starting transfers between devices, passed_along(): return lax.ppermute(x, axis, pairs)  3.84 us
    ppermute x1, waiting for transfers between devices, with_halo(): before = lax.ppermute(last, axis, up)  3.35 us
  transfers between devices with their start and end apart: 6, of which 6 were waited for; matrix products, arithmetic and copies ran while one was open for 6% of the time, Pallas kernels for 0%

commit v1 on v0

--- a/solution.py
+++ b/solution.py
@@ -21,6 +21,25 @@
         after = lax.ppermute(leading, axis, down)
         x = jnp.concatenate([before, x, after], axis=dim)
     return x
+
+
+def strip_gather(x, axis):
+    n = lax.axis_size(axis)
+    if n == 1:
+        return x
+    m = x.shape[0]
+    up_pairs = [(i, i + 1) for i in range(n - 1)]
+    down_pairs = [(i + 1, i) for i in range(n - 1)]
+    ups, downs = [], []
+    up, down = x, x
+    for _ in range(n - 1):
+        up = lax.ppermute(up, axis, up_pairs)
+        down = lax.ppermute(down, axis, down_pairs)
+        ups.append(up)
+        downs.append(down)
+    stacked = jnp.concatenate(ups[::-1] + [x] + downs, axis=0)
+    me = lax.axis_index(axis)
+    return lax.dynamic_slice_in_dim(stacked, (n - 1 - me) * m, n * m, axis=0)
 
 
 def rms_scale(values, gain):
@@ -58,20 +77,22 @@
     flat = frames.reshape(-1, width)
     count = flat.shape[0]
     scale = 1.0 / jnp.sqrt(jnp.float32(width))
+    whole = strip_gather(flat, "strip")
     normed = rms_scale(flat, attn_gain).astype(jnp.bfloat16)
+    normed_all = rms_scale(whole, attn_gain).astype(jnp.bfloat16)
     query = jnp.dot(normed, query_weight, preferred_element_type=jnp.float32).astype(jnp.bfloat16)
     start_carry = (
         jnp.full((count,), -1e30, jnp.float32),
         jnp.zeros((count,), jnp.float32),
         jnp.zeros((count, width), jnp.float32),
     )
-    keys = jnp.dot(normed, key_weight, preferred_element_type=jnp.float32).astype(jnp.bfloat16)
-    values = jnp.dot(normed, value_weight, preferred_element_type=jnp.float32).astype(jnp.bfloat16)
+    keys = jnp.dot(normed_all, key_weight, preferred_element_type=jnp.float32).astype(jnp.bfloat16)
+    values = jnp.dot(normed_all, value_weight, preferred_element_type=jnp.float32).astype(jnp.bfloat16)
     peak, total, summed = attend(
         start_carry,
         query,
-        lax.all_gather(keys, "strip", axis=0, tiled=True),
-        lax.all_gather(values, "strip", axis=0, tiled=True),
+        keys,
+        values,
         scale,
     )
     attended = (summed / total[:, None]).astype(jnp.bfloat16)

time: 139 us -> 100 us (0.72)
  waiting for transfers between devices: 83.4 us -> 38.9 us
  starting transfers between devices: 9.93 us -> 27.6 us
  between operations: 13.6 us -> 0.41 us
  local copies, waits for them, and re-layouts: 3.93 us -> 5.81 us
    all_gather x2 -> x0, waiting for transfers between devices: 63.1 us -> none  [the longest x1 34.7 us: shards(): lax.all_gather(keys, 'strip', axis=0, tiled=True)]
    ppermute x0 -> x6, waiting for transfers between devices: none -> 18.3 us  [the longest x3 13.8 us: strip_gather(): up = lax.ppermute(up, axis, up_pairs)]
    ppermute x0 -> x6, starting transfers between devices: none -> 17.7 us  [the longest x3 10.6 us: strip_gather(): up = lax.ppermute(up, axis, up_pairs)]
    dot_general x1, matrix products: 4.14 us -> 0.49 us  [shards(): jnp.dot(attended, out_weight, preferred_element_type=jnp.float32)]
    dot_general x2, matrix products: 3.2 us -> 6.17 us  [the longest x1 4.64 us: attend(): jnp.dot(weights.astype(jnp.bfloat16), values, preferred_element_type=jnp....]
    unnamed x16 -> x26, local copies, waits for them, and re-layouts: 1.88 us -> 3.83 us
  transfers between devices with their start and end apart: 6 -> 10, of which waited for: 6 -> 8; matrix products, arithmetic and copies ran while one was open for 6% -> 3% of each run, Pallas kernels for 0% -> 0%
where the time goes in v1:
time: 100 us; the launch traced here: 99.6 us
  waiting for transfers between devices  38.9 us (39%)
  starting transfers between devices  27.6 us (28%)
  matrix products  19.8 us (20%)
  other arithmetic  7.03 us (7%)
  local copies, waits for them, and re-layouts  5.81 us (6%)
    ppermute x3, waiting for transfers between devices, strip_gather(): up = lax.ppermute(up, axis, up_pairs)  13.8 us
    ppermute x2, waiting for transfers between devices, passed_along(): return lax.ppermute(x, axis, pairs)  13.8 us
    ppermute x3, starting transfers between devices, strip_gather(): up = lax.ppermute(up, axis, up_pairs)  10.6 us
    dot_general x9, matrix products, shards(): jnp.dot(window, kernel[step_t, step_r], preferred_element_type=jnp.float32)  7.83 us
    ppermute x3, starting transfers between devices, strip_gather(): down = lax.ppermute(down, axis, down_pairs)  7.13 us
    dot_general x1, matrix products, attend(): lax.dot_general(query, keys, (((1,), (1,)), ((), ())), preferred_element_...  5.33 us
    dot_general x1, matrix products, attend(): jnp.dot(weights.astype(jnp.bfloat16), values, preferred_element_type=jnp....  4.64 us
    ppermute x3, waiting for transfers between devices, strip_gather(): down = lax.ppermute(down, axis, down_pairs)  4.46 us
  transfers between devices with their start and end apart: 10, of which 8 were waited for; matrix products, arithmetic and copies ran while one was open for 3% of the time, Pallas kernels for 0%

profile of v1, /device:TPU:10, one launch (start us, length us, event | category | flops | bytes accessed | tf_op | source)
XLA Modules:
  0.0 99.6 jit_solution(13722599372733570557)
XLA Ops:
  0.0 3.6 %collective-permute-start = (bf16[480,384]{1,0:T(8,128)(2,1)}, bf16[480,384]{1,0:T(8,128)(2,1)S(1)}, u32[]{:S(2)}, u32[]{:S(2)}) collective-permute-start(bf16[480,384]{1,0:T(8,128)(2,1)} %bitcast.73), channel_id=1, source_target_pairs={{0,4},{4,8},{8,12},{1,5},{5,9},{9,13},{2,6},{6,10},{10,14},{3,7},{... | collective-permute-start | bytes 1105928 | tf_op jit(solution)/shard_map/ppermute | solution.py:36
  3.6 2.4 %collective-permute-start.3 = (bf16[480,384]{1,0:T(8,128)(2,1)}, bf16[480,384]{1,0:T(8,128)(2,1)S(1)}, u32[]{:S(2)}, u32[]{:S(2)}) collective-permute-start(bf16[480,384]{1,0:T(8,128)(2,1)} %bitcast.74), channel_id=1, source_target_pairs={{4,0},{8,4},{12,8},{5,1},{9,5},{13,9},{6,2},{10,6},{14,10},{7,3},{... | collective-permute-start | bytes 1105928 | tf_op jit(solution)/shard_map/ppermute | solution.py:37
  6.0 6.6 %collective-permute-done = bf16[480,384]{1,0:T(8,128)(2,1)S(1)} collective-permute-done((bf16[480,384]{1,0:T(8,128)(2,1)}, bf16[480,384]{1,0:T(8,128)(2,1)S(1)}, u32[]{:S(2)}, u32[]{:S(2)}) %collective-permute-start) | collective-permute-done | bytes 368672 | tf_op jit(solution)/shard_map/ppermute | solution.py:36
  12.6 3.5 %collective-permute-start.1 = (bf16[480,384]{1,0:T(8,128)(2,1)S(1)}, bf16[480,384]{1,0:T(8,128)(2,1)S(1)}, u32[]{:S(2)}, u32[]{:S(2)}) collective-permute-start(bf16[480,384]{1,0:T(8,128)(2,1)S(1)} %collective-permute-done), channel_id=1, source_target_pairs={{0,4},{4,8},{8,12},{1,5},{5,9},{9,13},{2,6},{6,10},{10,14},{3,7},{... | collective-permute-start | bytes 1105928 | tf_op jit(solution)/shard_map/ppermute | solution.py:36
  16.0 1.2 %multiply_reduce_fusion.2 = f32[3,160]{1,0:T(4,128)S(1)} fusion(bf16[1,3,160,384]{3,2,1,0:T(8,128)(2,1)} %param.9), kind=kLoop, calls=%fused_computation.64 | loop fusion | flops 552480 | bytes 370560 | tf_op jit(solution)/shard_map/reduce_sum | solution.py:47
  17.2 2.4 %collective-permute-start.4 = (bf16[480,384]{1,0:T(8,128)(2,1)S(1)}, bf16[480,384]{1,0:T(8,128)(2,1)S(1)}, u32[]{:S(2)}, u32[]{:S(2)}) collective-permute-start(bf16[480,384]{1,0:T(8,128)(2,1)S(1)} %collective-permute-done.3), channel_id=1, source_target_pairs={{4,0},{8,4},{12,8},{5,1},{9,5},{13,9},{6,2},{10,6},{14,10},{7,3},{... | collective-permute-start | bytes 1105928 | tf_op jit(solution)/shard_map/ppermute | solution.py:37
  19.6 4.3 %collective-permute-done.1 = bf16[480,384]{1,0:T(8,128)(2,1)S(1)} collective-permute-done((bf16[480,384]{1,0:T(8,128)(2,1)S(1)}, bf16[480,384]{1,0:T(8,128)(2,1)S(1)}, u32[]{:S(2)}, u32[]{:S(2)}) %collective-permute-start.1) | collective-permute-done | bytes 368672 | tf_op jit(solution)/shard_map/ppermute | solution.py:36
  23.9 3.5 %collective-permute-start.2 = (bf16[480,384]{1,0:T(8,128)(2,1)S(1)}, bf16[480,384]{1,0:T(8,128)(2,1)S(1)}, u32[]{:S(2)}, u32[]{:S(2)}) collective-permute-start(bf16[480,384]{1,0:T(8,128)(2,1)S(1)} %collective-permute-done.1), channel_id=1, source_target_pairs={{0,4},{4,8},{8,12},{1,5},{5,9},{9,13},{2,6},{6,10},{10,14},{3,7},{... | collective-permute-start | bytes 1105928 | tf_op jit(solution)/shard_map/ppermute | solution.py:36
  27.4 0.1 rsqrt.28
  27.5 1.5 %convolution_convert_fusion.2 = bf16[480,384]{1,0:T(8,128)(2,1)S(1)} fusion(bf16[384,384]{1,0:T(8,128)(2,1)} %param.12, bf16[480,384]{1,0:T(8,128)(2,1)} %bitcast.75, f32[384]{0:T(512)} %param.11, f32[480]{0:T(512)S(1)} %rsqrt.28), kind=kOutput, calls=%fused_computation.39 | convolution fusion | flops 142479360 | bytes 1035648 | tf_op jit(solution)/shard_map/dot_general | solution.py:83
  29.0 2.4 %collective-permute-start.5 = (bf16[480,384]{1,0:T(8,128)(2,1)S(1)}, bf16[480,384]{1,0:T(8,128)(2,1)S(1)}, u32[]{:S(2)}, u32[]{:S(2)}) collective-permute-start(bf16[480,384]{1,0:T(8,128)(2,1)S(1)} %collective-permute-done.4), channel_id=1, source_target_pairs={{4,0},{8,4},{12,8},{5,1},{9,5},{13,9},{6,2},{10,6},{14,10},{7,3},{... | collective-permute-start | bytes 1105928 | tf_op jit(solution)/shard_map/ppermute | solution.py:37
  31.4 3.0 %collective-permute-done.2 = bf16[480,384]{1,0:T(8,128)(2,1)S(1)} collective-permute-done((bf16[480,384]{1,0:T(8,128)(2,1)S(1)}, bf16[480,384]{1,0:T(8,128)(2,1)S(1)}, u32[]{:S(2)}, u32[]{:S(2)}) %collective-permute-start.2) | collective-permute-done | bytes 368672 | tf_op jit(solution)/shard_map/ppermute | solution.py:36
  34.5 0.1 constant_dynamic-update-slice_fusion.5
  34.5 0.1 constant_dynamic-update-slice_fusion.4
  34.6 0.1 constant_dynamic-update-slice_fusion.3
  34.7 0.1 constant_dynamic-update-slice_fusion.2
  34.8 4.5 %collective-permute-done.5 = bf16[480,384]{1,0:T(8,128)(2,1)S(1)} collective-permute-done((bf16[480,384]{1,0:T(8,128)(2,1)S(1)}, bf16[480,384]{1,0:T(8,128)(2,1)S(1)}, u32[]{:S(2)}, u32[]{:S(2)}) %collective-permute-start.5) | collective-permute-done | bytes 368672 | tf_op jit(solution)/shard_map/ppermute | solution.py:37
  39.4 1.5 %copy-done.2 = bf16[3360,384]{1,0:T(8,128)(2,1)} copy-done((bf16[3360,384]{1,0:T(8,128)(2,1)}, bf16[3360,384]{1,0:T(8,128)(2,1)S(1)}, u32[]{:S(2)}) %copy-start.2) | copy-done | bytes 2580504
  40.8 0.4 fusion.3
  41.2 5.3 %multiply_reduce_fusion = (f32[480]{0:T(512)S(1)}, f32[480,1920]{1,0:T(8,128)}) fusion(bf16[480,384]{1,0:T(8,128)(2,1)S(1)} %convolution_convert_fusion.2, bf16[384,384]{1,0:T(8,128)(2,1)S(1)} %copy-done, f32[384]{0:T(512)S(1)} %copy-done.7, f32[1920]{0:T(1024)S(1)} %add_rsqrt_fusion, bf16[3360,384]{1,0:T(8,128)(2,1)} %copy-done.2, s32[]{:T(128)S(6)} %select_n.15), kind=kOutput, calls=%fused_computation.7 | convolution fusion | flops 1279548928 | bytes 5835652 | tf_op jit(solution)/shard_map/dot_general | solution.py:53
  46.5 2.8 %fusion.1 = f32[480]{0:T(512)S(1)} fusion(f32[480,1920]{1,0:T(8,128)} %get-tuple-element.19, f32[480]{0:T(512)S(1)} %broadcast_maximum_fusion), kind=kLoop, calls=%fused_computation.8 | loop fusion | flops 2764320 | bytes 3690240 | tf_op jit(solution)/shard_map/reduce_sum | solution.py:58
  49.4 4.6 %fusion.30 = bf16[480,384]{1,0:T(8,128)(2,1)S(1)} fusion(bf16[384,384]{1,0:T(8,128)(2,1)S(1)} %copy-done.6, f32[480,1920]{1,0:T(8,128)} %get-tuple-element.19, f32[480]{0:T(512)S(1)} %broadcast_maximum_fusion, f32[480]{0:T(512)S(1)} %fusion.1, f32[384]{0:T(512)S(1)} %copy-done.7, f32[1920]{0:T(1024)S(1)} %add_rsqrt_fusion, bf16[3360,384]{1,0:T(8,128)(2,1)} %copy-done.2, ...), kind=kOutput, calls=%fused_computation.41 | convolution fusion | flops 1280839680 | bytes 5837572 | tf_op jit(solution)/shard_map/dot_general | solution.py:59
  54.1 0.5 multiply_reduce_fusion.1
  54.6 0.3 multiply_convert_fusion
  54.9 1.9 %collective-permute-start.6 = (bf16[3,160,384]{2,1,0:T(8,128)(2,1)S(1)}, bf16[3,160,384]{2,1,0:T(8,128)(2,1)S(1)}, u32[]{:S(2)}, u32[]{:S(2)}) collective-permute-start(bf16[3,160,384]{2,1,0:T(8,128)(2,1)S(1)} %bitcast.65), channel_id=1, source_target_pairs={{0,1},{1,2},{2,3},{4,5},{5,6},{6,7},{8,9},{9,10},{10,11},{12,13},{... | collective-permute-start | bytes 1105928 | tf_op jit(solution)/shard_map/ppermute | solution.py:10
  56.8 6.9 %collective-permute-done.6 = bf16[3,160,384]{2,1,0:T(8,128)(2,1)S(1)} collective-permute-done((bf16[3,160,384]{2,1,0:T(8,128)(2,1)S(1)}, bf16[3,160,384]{2,1,0:T(8,128)(2,1)S(1)}, u32[]{:S(2)}, u32[]{:S(2)}) %collective-permute-start.6) | collective-permute-done | bytes 368672 | tf_op jit(solution)/shard_map/ppermute | solution.py:10
  63.8 1.9 %collective-permute-start.7 = (bf16[3,160,384]{2,1,0:T(8,128)(2,1)S(1)}, bf16[3,160,384]{2,1,0:T(8,128)(2,1)S(1)}, u32[]{:S(2)}, u32[]{:S(2)}) collective-permute-start(bf16[3,160,384]{2,1,0:T(8,128)(2,1)S(1)} %bitcast_select_fusion), channel_id=1, source_target_pairs={{0,1},{1,2},{2,3},{4,5},{5,6},{6,7},{8,9},{9,10},{10,11},{12,13},{... | collective-permute-start | bytes 1105928 | tf_op jit(solution)/shard_map/ppermute | solution.py:10
  65.7 6.9 %collective-permute-done.7 = bf16[3,160,384]{2,1,0:T(8,128)(2,1)S(1)} collective-permute-done((bf16[3,160,384]{2,1,0:T(8,128)(2,1)S(1)}, bf16[3,160,384]{2,1,0:T(8,128)(2,1)S(1)}, u32[]{:S(2)}, u32[]{:S(2)}) %collective-permute-start.7) | collective-permute-done | bytes 368672 | tf_op jit(solution)/shard_map/ppermute | solution.py:10
  72.6 0.1 pad_maximum_fusion.3
  72.7 3.5 %collective-permute-start.8 = (bf16[3,1,160,384]{3,2,1,0:T(8,128)(2,1)S(1)}, bf16[3,1,160,384]{3,2,1,0:T(8,128)(2,1)S(1)}, u32[]{:S(2)}, u32[]{:S(2)}) collective-permute-start(bf16[3,1,160,384]{3,2,1,0:T(8,128)(2,1)S(1)} %get-tuple-element.16), channel_id=1, source_target_pairs={{0,4},{4,8},{8,12},{1,5},{5,9},{9,13},{2,6},{6,10},{10,14},{3,7},{... | collective-permute-start | bytes 1105928 | tf_op jit(solution)/shard_map/ppermute | solution.py:20
  76.2 2.5 %collective-permute-start.9 = (bf16[3,1,160,384]{3,2,1,0:T(8,128)(2,1)S(1)}, bf16[3,1,160,384]{3,2,1,0:T(8,128)(2,1)S(1)}, u32[]{:S(2)}, u32[]{:S(2)}) collective-permute-start(bf16[3,1,160,384]{3,2,1,0:T(8,128)(2,1)S(1)} %get-tuple-element.17), channel_id=1, source_target_pairs={{4,0},{8,4},{12,8},{5,1},{9,5},{13,9},{6,2},{10,6},{14,10},{7,3},{... | collective-permute-start | bytes 1105928 | tf_op jit(solution)/shard_map/ppermute | solution.py:21
  78.8 3.3 %collective-permute-done.8 = bf16[3,1,160,384]{3,2,1,0:T(8,128)(2,1)S(1)} collective-permute-done((bf16[3,1,160,384]{3,2,1,0:T(8,128)(2,1)S(1)}, bf16[3,1,160,384]{3,2,1,0:T(8,128)(2,1)S(1)}, u32[]{:S(2)}, u32[]{:S(2)}) %collective-permute-start.8) | collective-permute-done | bytes 368672 | tf_op jit(solution)/shard_map/ppermute | solution.py:20
  82.2 3.5 %collective-permute-done.9 = bf16[3,1,160,384]{3,2,1,0:T(8,128)(2,1)S(1)} collective-permute-done((bf16[3,1,160,384]{3,2,1,0:T(8,128)(2,1)S(1)}, bf16[3,1,160,384]{3,2,1,0:T(8,128)(2,1)S(1)}, u32[]{:S(2)}, u32[]{:S(2)}) %collective-permute-start.9) | collective-permute-done | bytes 368672 | tf_op jit(solution)/shard_map/ppermute | solution.py:21
  85.7 1.5 %select_maximum_fusion = bf16[3,5,162,384]{3,2,1,0:T(8,128)(2,1)S(1)} fusion(bf16[3,1,160,384]{3,2,1,0:T(8,128)(2,1)S(1)} %collective-permute-done.9, bf16[3,1,160,384]{3,2,1,0:T(8,128)(2,1)S(1)} %collective-permute-done.8, bf16[1,3,160,384]{3,2,1,0:T(8,128)(2,1)S(1)} %bitcast.67, bf16[1,3,160,384]{3,2,1,0:T(8,128)(2,1)S(1)} %bitcast.70, ...), kind=kLoop, calls=%fused_computation.15 | loop fusion | flops 16796160 | bytes 3709440 | tf_op jit(solution)/shard_map/concatenate | solution.py:22
  87.2 1.0 fusion.57
  88.2 0.6 pad_maximum_fusion
  88.8 0.9 fusion.56
  89.7 0.7 slice-done
  90.4 1.3 %slice-done.1 = s8[3768320]{0:T(1024)(128)(4,1)S(1)} async-done(((s8[7962624]{0:T(1024)(128)(4,1)}), s8[3768320]{0:T(1024)(128)(4,1)S(1)}, s32[]{:S(2)}) %slice-start.1) | async-done | bytes 3768344
  91.7 0.8 fusion.33
  92.5 0.8 fusion.34
  93.2 0.8 fusion.35
  94.0 0.8 fusion.36
  94.8 0.8 fusion.37
  95.5 0.8 fusion.38
  96.3 0.8 fusion.39
  97.0 0.8 fusion.40
  97.8 1.8 %fusion.24 = bf16[480,384]{1,0:T(8,128)(2,1)} fusion(f32[480,384]{1,0:T(8,128)S(1)} %fusion.33, f32[480,384]{1,0:T(8,128)S(1)} %fusion.34, f32[480,384]{1,0:T(8,128)S(1)} %fusion.35, f32[480,384]{1,0:T(8,128)S(1)} %fusion.36, f32[480,384]{1,0:T(8,128)S(1)} %fusion.37, f32[480,384]{1,0:T(8,128)S(1)} %fusion.38, f32[480,384]{1,0:T(8,128)S(1)} %fusion.39, ...), kind=kOutput, calls=%fused_computation.36 | convolution fusion | flops 426516480 | bytes 8994816 | tf_op jit(solution)/shard_map/dot_general | solution.py:119
  (29 shorter events, 0.3 us)
Async XLA Ops:
  0.0 41.2 %copy-start = (bf16[384,384]{1,0:T(8,128)(2,1)S(1)}, bf16[384,384]{1,0:T(8,128)(2,1)}, u32[]{:S(2)}) copy-start(bf16[384,384]{1,0:T(8,128)(2,1)} %param.13) | copy-start | bytes 884740
  0.0 34.6 %copy-start.1 = (bf16[1,3,160,384]{3,2,1,0:T(8,128)(2,1)S(1)}, bf16[1,3,160,384]{3,2,1,0:T(8,128)(2,1)}, u32[]{:S(2)}) copy-start(bf16[1,3,160,384]{3,2,1,0:T(8,128)(2,1)} %param.9) | copy-start | bytes 1105924
  0.0 12.6 %collective-permute-start = (bf16[480,384]{1,0:T(8,128)(2,1)}, bf16[480,384]{1,0:T(8,128)(2,1)S(1)}, u32[]{:S(2)}, u32[]{:S(2)}) collective-permute-start(bf16[480,384]{1,0:T(8,128)(2,1)} %bitcast.73), channel_id=1, source_target_pairs={{0,4},{4,8},{8,12},{1,5},{5,9},{9,13},{2,6},{6,10},{10,14},{3,7},{... | collective-permute-start | bytes 1105928 | tf_op jit(solution)/shard_map/ppermute | solution.py:36
  3.6 13.6 %collective-permute-start.3 = (bf16[480,384]{1,0:T(8,128)(2,1)}, bf16[480,384]{1,0:T(8,128)(2,1)S(1)}, u32[]{:S(2)}, u32[]{:S(2)}) collective-permute-start(bf16[480,384]{1,0:T(8,128)(2,1)} %bitcast.74), channel_id=1, source_target_pairs={{4,0},{8,4},{12,8},{5,1},{9,5},{13,9},{6,2},{10,6},{14,10},{7,3},{... | collective-permute-start | bytes 1105928 | tf_op jit(solution)/shard_map/ppermute | solution.py:37
  12.6 11.4 %collective-permute-start.1 = (bf16[480,384]{1,0:T(8,128)(2,1)S(1)}, bf16[480,384]{1,0:T(8,128)(2,1)S(1)}, u32[]{:S(2)}, u32[]{:S(2)}) collective-permute-start(bf16[480,384]{1,0:T(8,128)(2,1)S(1)} %collective-permute-done), channel_id=1, source_target_pairs={{0,4},{4,8},{8,12},{1,5},{5,9},{9,13},{2,6},{6,10},{10,14},{3,7},{... | collective-permute-start | bytes 1105928 | tf_op jit(solution)/shard_map/ppermute | solution.py:36
  17.2 11.8 %collective-permute-start.4 = (bf16[480,384]{1,0:T(8,128)(2,1)S(1)}, bf16[480,384]{1,0:T(8,128)(2,1)S(1)}, u32[]{:S(2)}, u32[]{:S(2)}) collective-permute-start(bf16[480,384]{1,0:T(8,128)(2,1)S(1)} %collective-permute-done.3), channel_id=1, source_target_pairs={{4,0},{8,4},{12,8},{5,1},{9,5},{13,9},{6,2},{10,6},{14,10},{7,3},{... | collective-permute-start | bytes 1105928 | tf_op jit(solution)/shard_map/ppermute | solution.py:37
  23.9 10.5 %collective-permute-start.2 = (bf16[480,384]{1,0:T(8,128)(2,1)S(1)}, bf16[480,384]{1,0:T(8,128)(2,1)S(1)}, u32[]{:S(2)}, u32[]{:S(2)}) collective-permute-start(bf16[480,384]{1,0:T(8,128)(2,1)S(1)} %collective-permute-done.1), channel_id=1, source_target_pairs={{0,4},{4,8},{8,12},{1,5},{5,9},{9,13},{2,6},{6,10},{10,14},{3,7},{... | collective-permute-start | bytes 1105928 | tf_op jit(solution)/shard_map/ppermute | solution.py:36
  29.0 10.2 %collective-permute-start.5 = (bf16[480,384]{1,0:T(8,128)(2,1)S(1)}, bf16[480,384]{1,0:T(8,128)(2,1)S(1)}, u32[]{:S(2)}, u32[]{:S(2)}) collective-permute-start(bf16[480,384]{1,0:T(8,128)(2,1)S(1)} %collective-permute-done.4), channel_id=1, source_target_pairs={{4,0},{8,4},{12,8},{5,1},{9,5},{13,9},{6,2},{10,6},{14,10},{7,3},{... | collective-permute-start | bytes 1105928 | tf_op jit(solution)/shard_map/ppermute | solution.py:37
  34.5 6.7 %copy-start.7 = (f32[384]{0:T(512)S(1)}, f32[384]{0:T(512)}, u32[]{:S(2)}) copy-start(f32[384]{0:T(512)} %param.11) | copy-start | bytes 4612
  39.3 1.5 %copy-start.2 = (bf16[3360,384]{1,0:T(8,128)(2,1)}, bf16[3360,384]{1,0:T(8,128)(2,1)S(1)}, u32[]{:S(2)}) copy-start(bf16[3360,384]{1,0:T(8,128)(2,1)S(1)} %constant_dynamic-update-slice_fusion) | copy-start | bytes 7741444
  46.5 2.8 %copy-start.6 = (bf16[384,384]{1,0:T(8,128)(2,1)S(1)}, bf16[384,384]{1,0:T(8,128)(2,1)}, u32[]{:S(2)}) copy-start(bf16[384,384]{1,0:T(8,128)(2,1)} %param.14) | copy-start | bytes 884740
  49.4 4.7 %copy-start.4 = (bf16[384,384]{1,0:T(8,128)(2,1)S(1)}, bf16[384,384]{1,0:T(8,128)(2,1)}, u32[]{:S(2)}) copy-start(bf16[384,384]{1,0:T(8,128)(2,1)} %param.15) | copy-start | bytes 884740
  49.4 5.2 %copy-start.5 = (f32[384]{0:T(512)S(1)}, f32[384]{0:T(512)}, u32[]{:S(2)}) copy-start(f32[384]{0:T(512)} %param.16) | copy-start | bytes 4612
  54.1 9.6 %copy-start.3 = (bf16[2,3,160,384]{3,2,1,0:T(8,128)(2,1)S(1)}, bf16[2,3,160,384]{3,2,1,0:T(8,128)(2,1)}, u32[]{:S(2)}) copy-start(bf16[2,3,160,384]{3,2,1,0:T(8,128)(2,1)} %param.10) | copy-start | bytes 2211844
  54.9 8.8 %collective-permute-start.6 = (bf16[3,160,384]{2,1,0:T(8,128)(2,1)S(1)}, bf16[3,160,384]{2,1,0:T(8,128)(2,1)S(1)}, u32[]{:S(2)}, u32[]{:S(2)}) collective-permute-start(bf16[3,160,384]{2,1,0:T(8,128)(2,1)S(1)} %bitcast.65), channel_id=1, source_target_pairs={{0,1},{1,2},{2,3},{4,5},{5,6},{6,7},{8,9},{9,10},{10,11},{12,13},{... | collective-permute-start | bytes 1105928 | tf_op jit(solution)/shard_map/ppermute | solution.py:10
  63.8 8.8 %collective-permute-start.7 = (bf16[3,160,384]{2,1,0:T(8,128)(2,1)S(1)}, bf16[3,160,384]{2,1,0:T(8,128)(2,1)S(1)}, u32[]{:S(2)}, u32[]{:S(2)}) collective-permute-start(bf16[3,160,384]{2,1,0:T(8,128)(2,1)S(1)} %bitcast_select_fusion), channel_id=1, source_target_pairs={{0,1},{1,2},{2,3},{4,5},{5,6},{6,7},{8,9},{9,10},{10,11},{12,13},{... | collective-permute-start | bytes 1105928 | tf_op jit(solution)/shard_map/ppermute | solution.py:10
  72.7 9.4 %collective-permute-start.8 = (bf16[3,1,160,384]{3,2,1,0:T(8,128)(2,1)S(1)}, bf16[3,1,160,384]{3,2,1,0:T(8,128)(2,1)S(1)}, u32[]{:S(2)}, u32[]{:S(2)}) collective-permute-start(bf16[3,1,160,384]{3,2,1,0:T(8,128)(2,1)S(1)} %get-tuple-element.16), channel_id=1, source_target_pairs={{0,4},{4,8},{8,12},{1,5},{5,9},{9,13},{2,6},{6,10},{10,14},{3,7},{... | collective-permute-start | bytes 1105928 | tf_op jit(solution)/shard_map/ppermute | solution.py:20
  76.2 9.4 %collective-permute-start.9 = (bf16[3,1,160,384]{3,2,1,0:T(8,128)(2,1)S(1)}, bf16[3,1,160,384]{3,2,1,0:T(8,128)(2,1)S(1)}, u32[]{:S(2)}, u32[]{:S(2)}) collective-permute-start(bf16[3,1,160,384]{3,2,1,0:T(8,128)(2,1)S(1)} %get-tuple-element.17), channel_id=1, source_target_pairs={{4,0},{8,4},{12,8},{5,1},{9,5},{13,9},{6,2},{10,6},{14,10},{7,3},{... | collective-permute-start | bytes 1105928 | tf_op jit(solution)/shard_map/ppermute | solution.py:21
  88.2 2.2 %slice-start = ((s8[7962624]{0:T(1024)(128)(4,1)}), s8[4194304]{0:T(1024)(128)(4,1)S(1)}, s32[]{:S(2)}) async-start(s8[7962624]{0:T(1024)(128)(4,1)} %bitcast.86), calls=%async_computation | async-start | bytes 8388608
  88.8 2.9 %slice-start.1 = ((s8[7962624]{0:T(1024)(128)(4,1)}), s8[3768320]{0:T(1024)(128)(4,1)S(1)}, s32[]{:S(2)}) async-start(s8[7962624]{0:T(1024)(128)(4,1)} %bitcast.86), calls=%async_computation.1 | async-start | bytes 7536640

commit v2 on v1

v2 whole, which is shorter than its diff:
```python
import jax
import jax.numpy as jnp
from jax import lax
from jax.sharding import PartitionSpec as P


def relay_blocks(x, axis):
    n = lax.axis_size(axis)
    up_pairs = [(i, i + 1) for i in range(n - 1)]
    down_pairs = [(i + 1, i) for i in range(n - 1)]
    ups, downs = [], []
    up, down = x, x
    for _ in range(n - 1):
        up = lax.ppermute(up, axis, up_pairs)
        down = lax.ppermute(down, axis, down_pairs)
        ups.append(up)
        downs.append(down)
    return ups, downs


def with_halo(x, axis, dim):
    size, length = (lax.axis_size(axis), x.shape[dim])
    up = [(i, i + 1) for i in range(size - 1)]
    down = [(j, i) for i, j in up]
    last = lax.slice_in_dim(x, length - 1, length, axis=dim)
    leading = lax.slice_in_dim(x, 0, 1, axis=dim)
    before = lax.ppermute(last, axis, up)
    after = lax.ppermute(leading, axis, down)
    return jnp.concatenate([before, x, after], axis=dim)


def rms_scale(values, gain):
    wide = values.astype(jnp.float32)
    return wide * lax.rsqrt(jnp.mean(wide * wide, axis=-1, keepdims=True) + 1e-06) * gain


def frame_conv(padded, kernel, rows, cols, width):
    padded = jnp.pad(padded, ((0, 0), (1, 1), (0, 0)))
    widened = jnp.concatenate(
        [padded[:, 0:cols], padded[:, 1 : cols + 1], padded[:, 2 : cols + 2]], axis=-1
    )
    total = None
    for step_r in range(3):
        window = widened[step_r : step_r + rows].reshape(-1, 3 * width)
        part = jnp.dot(window, kernel[step_r], preferred_element_type=jnp.float32)
        total = part if total is None else total + part
    return total


def shards(
    frames,
    cache_frames,
    attn_gain,
    query_weight,
    key_weight,
    value_weight,
    out_weight,
    conv_gain,
    conv_weight,
):
    rows = frames.shape[1]
    cols = frames.shape[2]
    width = frames.shape[3]
    flat = frames.reshape(-1, width)
    count = flat.shape[0]
    scale = 1.0 / jnp.sqrt(jnp.float32(width))
    normed = rms_scale(flat, attn_gain).astype(jnp.bfloat16)
    query = jnp.dot(normed, query_weight, preferred_element_type=jnp.float32).astype(jnp.bfloat16)

    def block_parts(block):
        block_normed = rms_scale(block, attn_gain).astype(jnp.bfloat16)
        keys = jnp.dot(block_normed, key_weight, preferred_element_type=jnp.float32).astype(
            jnp.bfloat16
        )
        values = jnp.dot(block_normed, value_weight, preferred_element_type=jnp.float32).astype(
            jnp.bfloat16
        )
        scores_t = (
            lax.dot_general(keys, query, (((1,), (1,)), ((), ())), preferred_element_type=jnp.float32)
            * scale
        )
        return scores_t, values

    n = lax.axis_size("strip")
    ups, downs = relay_blocks(flat, "strip")
    parts = [block_parts(b) for b in ups[::-1] + [flat] + downs]
    scores_all = jnp.concatenate([p[0] for p in parts], axis=0)
    values_all = jnp.concatenate([p[1] for p in parts], axis=0)
    me = lax.axis_index("strip")
    start = (n - 1 - me) * count
    scores_t = lax.dynamic_slice_in_dim(scores_all, start, n * count, axis=0)
    values = lax.dynamic_slice_in_dim(values_all, start, n * count, axis=0)
    peak = jnp.max(scores_t, axis=0)
    weights = jnp.exp(scores_t - peak[None, :])
    total = jnp.sum(weights, axis=0)
    summed = lax.dot_general(
        weights.astype(jnp.bfloat16), values, (((0,), (0,)), ((), ())),
        preferred_element_type=jnp.float32,
    )
    attended = (summed / total[:, None]).astype(jnp.bfloat16)
    resid = (
        flat.astype(jnp.float32) + jnp.dot(attended, out_weight, preferred_element_type=jnp.float32)
    ).astype(jnp.bfloat16)
    act = jax.nn.silu(rms_scale(resid, conv_gain)).astype(jnp.bfloat16).reshape(rows, cols, width)

    cache = lax.optimization_barrier((cache_frames, scores_all))[0]
    cache_padded = with_halo(cache, "strip", 1)
    act_padded = with_halo(act, "strip", 0)

    kernel = conv_weight.reshape(3, 3, 3 * width, width)
    result = resid.astype(jnp.float32) + frame_conv(act_padded, kernel[2], rows, cols, width)

    nt = lax.axis_size("tm")
    frame_index = lax.axis_index("tm")
    prior = lax.ppermute(act_padded, "tm", [(i, i + 1) for i in range(nt - 1)])
    older_even = lax.ppermute(act_padded, "tm", [(i, i + 2) for i in range(0, nt - 2, 2)])
    older_odd = lax.ppermute(prior, "tm", [(i, i + 1) for i in range(2, nt - 1, 2)])
    prior = jnp.where(frame_index == 0, cache_padded[1], prior)
    result = result + frame_conv(prior, kernel[1], rows, cols, width)
    older = jnp.where(frame_index % 2 == 0, older_even, older_odd)
    older = jnp.where(frame_index == 0, cache_padded[0], older)
    older = jnp.where(frame_index == 1, cache_padded[1], older)
    result = result + frame_conv(older, kernel[0], rows, cols, width)
    return result.astype(jnp.bfloat16).reshape(1, rows, cols, width)


def solution(mesh):
    return jax.shard_map(
        shards,
        mesh=mesh,
        in_specs=(
            P(("clip", "tm"), "strip", None, None),
            P("clip", "strip", None, None),
            P(),
            P(),
            P(),
            P(),
            P(),
            P(),
            P(),
        ),
        out_specs=P(("clip", "tm"), "strip", None, None),
        check_vma=False,
    )
```

time: 100 us -> 131 us (1.31); the launches traced: 99.6 us -> 128 us
  waiting for transfers between devices: 38.9 us -> 9.48 us
  matrix products: 19.8 us -> 47.3 us
  local copies, waits for them, and re-layouts: 5.81 us -> 19 us
  other arithmetic: 7.03 us -> 16.1 us
  starting transfers between devices: 27.6 us -> 36 us
    dot_general x11 -> x23, matrix products: 17.8 us -> 41.9 us  [the longest x7 19.9 us: block_parts(): lax.dot_general(keys, query, (((1,), (1,)), ((), ())), preferred_element_...]
    ppermute x8 -> x9, waiting for transfers between devices: 32.1 us -> 9.47 us  [the longest x1 8.93 us: shards(): prior = lax.ppermute(act_padded, 'tm', [(i, i + 1) for i in range(nt - 1)])]
    concatenate x1 -> x2, local copies, waits for them, and re-layouts: 0.06 us -> 8.91 us  [the longest x1 8.87 us: shards(): scores_all = jnp.concatenate([p[0] for p in parts], axis=0)]
    reduce_sum x2 -> x7, other arithmetic: 1.54 us -> 8.02 us  [rms_scale(): jnp.mean(wide * wide, axis=-1, keepdims=True) + 1e-06]
    slice x2 -> x9, local copies, waits for them, and re-layouts: 1.85 us -> 7.23 us  [the longest x1 5.54 us: frame_conv(): part = jnp.dot(window, kernel[step_r], preferred_element_type=jnp.float32)]
    ppermute x1 -> x2, starting transfers between devices: 3.49 us -> 8.56 us  [with_halo(): before = lax.ppermute(last, axis, up)]
    dot_general x1, matrix products: 0.49 us -> 4.22 us  [shards(): jnp.dot(attended, out_weight, preferred_element_type=jnp.float32)]
    ppermute x1 -> x2, waiting for transfers between devices: 3.5 us -> 0.01 us  [with_halo(): after = lax.ppermute(leading, axis, down)]
  transfers between devices with their start and end apart: 10 -> 13, of which waited for: 8 -> 3; matrix products, arithmetic and copies ran while one was open for 3% -> 24% of each run, Pallas kernels for 0% -> 0%
where the time goes in v2:
time: 131 us; the launch traced here: 128 us
  matrix products  47.3 us (36%)
  starting transfers between devices  36 us (27%)
  local copies, waits for them, and re-layouts  19 us (15%)
  other arithmetic  16.1 us (12%)
  waiting for transfers between devices  9.48 us (7%)
    dot_general x7, matrix products, block_parts(): lax.dot_general(keys, query, (((1,), (1,)), ((), ())), preferred_element_...  19.9 us
    dot_general x7, matrix products, block_parts(): jnp.dot(block_normed, value_weight, preferred_element_type=jnp.float32)  14.3 us
    ppermute x3, starting transfers between devices, relay_blocks(): up = lax.ppermute(up, axis, up_pairs)  9.76 us
    ppermute x3, starting transfers between devices, relay_blocks(): down = lax.ppermute(down, axis, down_pairs)  9.09 us
    ppermute x1, waiting for transfers between devices, shards(): prior = lax.ppermute(act_padded, 'tm', [(i, i + 1) for i in range(nt - 1)])  8.93 us
    concatenate x1, local copies, waits for them, and re-layouts, shards(): scores_all = jnp.concatenate([p[0] for p in parts], axis=0)  8.87 us
    ppermute x2, starting transfers between devices, with_halo(): before = lax.ppermute(last, axis, up)  8.56 us
    reduce_sum x7, other arithmetic, rms_scale(): jnp.mean(wide * wide, axis=-1, keepdims=True) + 1e-06  8.02 us
  transfers between devices with their start and end apart: 13, of which 3 were waited for; matrix products, arithmetic and copies ran while one was open for 24% of the time, Pallas kernels for 0%

profile of v2, /device:TPU:10, one launch (start us, length us, event | category | flops | bytes accessed | tf_op | source)
XLA Modules:
  0.0 128.4 jit_solution(10597289211290596794)
XLA Ops:
  0.0 2.5 %collective-permute-start.3 = (bf16[480,384]{1,0:T(8,128)(2,1)}, bf16[480,384]{1,0:T(8,128)(2,1)}, u32[]{:S(2)}, u32[]{:S(2)}) collective-permute-start(bf16[480,384]{1,0:T(8,128)(2,1)} %bitcast.94), channel_id=1, source_target_pairs={{4,0},{8,4},{12,8},{5,1},{9,5},{13,9},{6,2},{10,6},{14,10},{7,3},{... | collective-permute-start | bytes 1105928 | tf_op jit(solution)/shard_map/ppermute | solution.py:15
  2.5 3.5 %collective-permute-start = (bf16[480,384]{1,0:T(8,128)(2,1)}, bf16[480,384]{1,0:T(8,128)(2,1)}, u32[]{:S(2)}, u32[]{:S(2)}) collective-permute-start(bf16[480,384]{1,0:T(8,128)(2,1)} %bitcast.95), channel_id=1, source_target_pairs={{0,4},{4,8},{8,12},{1,5},{5,9},{9,13},{2,6},{6,10},{10,14},{3,7},{... | collective-permute-start | bytes 1105928 | tf_op jit(solution)/shard_map/ppermute | solution.py:14
  6.0 1.2 multiply_reduce_fusion.1
  7.3 5.5 %fusion.77 = (bf16[1,1,3,384,384]{4,3,2,1,0:T(8,128)(2,1)S(1)}, bf16[1,1,3,384,384]{4,3,2,1,0:T(8,128)(2,1)}, bf16[1,1,3,384,384]{4,3,2,1,0:T(8,128)(2,1)}, bf16...) fusion(bf16[3,3,3,384,384]{4,3,2,1,0:T(8,128)(2,1)} %param.17), kind=kLoop, calls=%fused_computation.117 | loop fusion | bytes 15925248 | tf_op jit(solution)/shard_map/slice | solution.py:45
  13.0 1.1 convolution_convert_fusion.13
  14.1 1.9 %convolution_multiply_fusion.3 = f32[480,480]{0,1:T(8,128)S(1)} fusion(bf16[480,384]{1,0:T(8,128)(2,1)} %convolution_convert_fusion.13, bf16[480,384]{1,0:T(8,128)(2,1)S(1)} %fusion.35, bf16[384,384]{1,0:T(8,128)(2,1)} %param.13), kind=kOutput, calls=%fused_computation.13 | convolution fusion | flops 318919680 | bytes 1953792 | tf_op jit(solution)/shard_map/dot_general | solution.py:79
  16.0 3.1 %collective-permute-start.4 = (bf16[480,384]{1,0:T(8,128)(2,1)}, bf16[480,384]{1,0:T(8,128)(2,1)}, u32[]{:S(2)}, u32[]{:S(2)}) collective-permute-start(bf16[480,384]{1,0:T(8,128)(2,1)} %collective-permute-done.3), channel_id=1, source_target_pairs={{4,0},{8,4},{12,8},{5,1},{9,5},{13,9},{6,2},{10,6},{14,10},{7,3},{... | collective-permute-start | bytes 1105928 | tf_op jit(solution)/shard_map/ppermute | solution.py:15
  19.1 1.1 fusion.45
  20.3 3.0 %collective-permute-start.1 = (bf16[480,384]{1,0:T(8,128)(2,1)}, bf16[480,384]{1,0:T(8,128)(2,1)}, u32[]{:S(2)}, u32[]{:S(2)}) collective-permute-start(bf16[480,384]{1,0:T(8,128)(2,1)} %collective-permute-done), channel_id=1, source_target_pairs={{0,4},{4,8},{8,12},{1,5},{5,9},{9,13},{2,6},{6,10},{10,14},{3,7},{... | collective-permute-start | bytes 1105928 | tf_op jit(solution)/shard_map/ppermute | solution.py:14
  23.4 1.1 fusion.42
  24.5 3.1 %convolution_multiply_fusion.2 = f32[480,480]{0,1:T(8,128)} fusion(bf16[480,384]{1,0:T(8,128)(2,1)} %convolution_convert_fusion.13, bf16[384,384]{1,0:T(8,128)(2,1)} %param.13, bf16[480,384]{1,0:T(8,128)(2,1)} %collective-permute-done.3, f32[480]{0:T(512)S(1)} %add_rsqrt_fusion.4, f32[384]{0:T(512)S(1)} %copy-done.13), kind=kOutput, calls=%fused_computation.12 | convolution fusion | flops 319656960 | bytes 1957248 | tf_op jit(solution)/shard_map/dot_general | solution.py:79
  27.6 3.0 %convolution_multiply_fusion.4 = f32[480,480]{0,1:T(8,128)} fusion(bf16[480,384]{1,0:T(8,128)(2,1)} %convolution_convert_fusion.13, bf16[384,384]{1,0:T(8,128)(2,1)} %param.13, bf16[480,384]{1,0:T(8,128)(2,1)} %collective-permute-done, f32[480]{0:T(512)S(1)} %add_rsqrt_fusion.5, f32[384]{0:T(512)S(1)} %copy-done.13), kind=kOutput, calls=%fused_computation.14 | convolution fusion | flops 319656960 | bytes 1957248 | tf_op jit(solution)/shard_map/dot_general | solution.py:79
  30.6 3.5 %collective-permute-start.5 = (bf16[480,384]{1,0:T(8,128)(2,1)}, bf16[480,384]{1,0:T(8,128)(2,1)}, u32[]{:S(2)}, u32[]{:S(2)}) collective-permute-start(bf16[480,384]{1,0:T(8,128)(2,1)} %collective-permute-done.4), channel_id=1, source_target_pairs={{4,0},{8,4},{12,8},{5,1},{9,5},{13,9},{6,2},{10,6},{14,10},{7,3},{... | collective-permute-start | bytes 1105928 | tf_op jit(solution)/shard_map/ppermute | solution.py:15
  34.1 1.1 fusion.48
  35.3 3.2 %collective-permute-start.2 = (bf16[480,384]{1,0:T(8,128)(2,1)}, bf16[480,384]{1,0:T(8,128)(2,1)}, u32[]{:S(2)}, u32[]{:S(2)}) collective-permute-start(bf16[480,384]{1,0:T(8,128)(2,1)} %collective-permute-done.1), channel_id=1, source_target_pairs={{0,4},{4,8},{8,12},{1,5},{5,9},{9,13},{2,6},{6,10},{10,14},{3,7},{... | collective-permute-start | bytes 1105928 | tf_op jit(solution)/shard_map/ppermute | solution.py:14
  38.5 1.1 fusion.39
  39.6 3.0 %convolution_multiply_fusion.1 = f32[480,480]{0,1:T(8,128)} fusion(bf16[480,384]{1,0:T(8,128)(2,1)} %convolution_convert_fusion.13, bf16[384,384]{1,0:T(8,128)(2,1)} %param.13, bf16[480,384]{1,0:T(8,128)(2,1)} %collective-permute-done.4, f32[480]{0:T(512)S(1)} %add_rsqrt_fusion.3, f32[384]{0:T(512)S(1)} %copy-done.13), kind=kOutput, calls=%fused_computation.11 | convolution fusion | flops 319656960 | bytes 1957248 | tf_op jit(solution)/shard_map/dot_general | solution.py:79
  42.6 3.0 %convolution_multiply_fusion.5 = f32[480,480]{0,1:T(8,128)} fusion(bf16[480,384]{1,0:T(8,128)(2,1)} %convolution_convert_fusion.13, bf16[384,384]{1,0:T(8,128)(2,1)} %param.13, bf16[480,384]{1,0:T(8,128)(2,1)} %collective-permute-done.1, f32[480]{0:T(512)S(1)} %add_rsqrt_fusion.6, f32[384]{0:T(512)S(1)} %copy-done.13), kind=kOutput, calls=%fused_computation.15 | convolution fusion | flops 319656960 | bytes 1957248 | tf_op jit(solution)/shard_map/dot_general | solution.py:79
  45.6 1.1 fusion.51
  46.8 1.1 fusion.36
  47.9 3.0 %convolution_multiply_fusion = f32[480,480]{0,1:T(8,128)} fusion(bf16[480,384]{1,0:T(8,128)(2,1)} %convolution_convert_fusion.13, bf16[384,384]{1,0:T(8,128)(2,1)} %param.13, bf16[480,384]{1,0:T(8,128)(2,1)} %collective-permute-done.5, f32[480]{0:T(512)S(1)} %add_rsqrt_fusion.2, f32[384]{0:T(512)S(1)} %copy-done.13), kind=kOutput, calls=%fused_computation.10 | convolution fusion | flops 319656960 | bytes 1957248 | tf_op jit(solution)/shard_map/dot_general | solution.py:79
  50.9 3.1 %convolution_multiply_fusion.6 = f32[480,480]{0,1:T(8,128)} fusion(bf16[480,384]{1,0:T(8,128)(2,1)} %convolution_convert_fusion.13, bf16[384,384]{1,0:T(8,128)(2,1)} %param.13, bf16[480,384]{1,0:T(8,128)(2,1)} %collective-permute-done.2, f32[384]{0:T(512)S(1)} %copy-done.13, f32[480]{0:T(512)S(1)} %add_rsqrt_fusion.7), kind=kOutput, calls=%fused_computation.16 | convolution fusion | flops 319656960 | bytes 1957248 | tf_op jit(solution)/shard_map/dot_general | solution.py:79
  54.0 8.9 %concatenate.21 = f32[3360,480]{0,1:T(8,128)} concatenate(f32[480,480]{0,1:T(8,128)} %convolution_multiply_fusion.6, f32[480,480]{0,1:T(8,128)} %convolution_multiply_fusion.5, f32[480,480]{0,1:T(8,128)} %convolution_multiply_fusion.4, f32[480,480]{0,1:T(8,128)S(1)} %convolution_multiply_fusion.3, f32[480,480]{0,1:T(8,128)} %convolution_multiply_fusion.2, ...), dimensions={0} | concatenate | bytes 12902400 | tf_op jit(solution)/shard_map/concatenate | solution.py:87
  62.9 3.3 %dynamic-slice_reduce_fusion = f32[480]{0:T(512)S(1)} fusion(f32[3360,480]{0,1:T(8,128)} %concatenate.21, s32[]{:T(128)S(6)} %select_n.35), kind=kLoop, calls=%fused_computation.1 | loop fusion | flops 921120 | bytes 3688324 | tf_op jit(solution)/shard_map/reduce_max | solution.py:93
  66.2 3.4 %fusion = f32[480]{0:T(512)S(1)} fusion(f32[3360,480]{0,1:T(8,128)} %concatenate.21, s32[]{:T(128)S(6)} %select_n.35, f32[480]{0:T(512)S(1)} %dynamic-slice_reduce_fusion), kind=kLoop, calls=%fused_computation.2 | loop fusion | flops 1842720 | bytes 3690244 | tf_op jit(solution)/shard_map/reduce_sum | solution.py:95
  69.6 2.2 %fusion.19 = bf16[3360,384]{1,0:T(8,128)(2,1)} fusion(bf16[384,384]{1,0:T(8,128)(2,1)S(1)} %copy-done, bf16[480,384]{1,0:T(8,128)(2,1)} %collective-permute-done.2, f32[384]{0:T(512)S(1)} %copy-done.13, f32[480]{0:T(512)S(1)} %add_rsqrt_fusion.7), kind=kOutput, calls=%fused_computation.43 | convolution fusion | flops 142479360 | bytes 1035648 | tf_op jit(solution)/shard_map/dot_general | solution.py:75
  71.8 2.2 %fusion.18 = bf16[3360,384]{1,0:T(8,128)(2,1)} fusion(bf16[3360,384]{1,0:T(8,128)(2,1)} %fusion.19, bf16[384,384]{1,0:T(8,128)(2,1)S(1)} %copy-done, bf16[480,384]{1,0:T(8,128)(2,1)} %collective-permute-done.1, f32[480]{0:T(512)S(1)} %add_rsqrt_fusion.6, f32[384]{0:T(512)S(1)} %copy-done.13), kind=kOutput, calls=%fused_computation.41 | convolution fusion | flops 142479360 | bytes 1035648 | tf_op jit(solution)/shard_map/dot_general | solution.py:75
  74.0 2.2 %fusion.17 = bf16[3360,384]{1,0:T(8,128)(2,1)} fusion(bf16[3360,384]{1,0:T(8,128)(2,1)} %fusion.18, bf16[384,384]{1,0:T(8,128)(2,1)S(1)} %copy-done, bf16[480,384]{1,0:T(8,128)(2,1)} %collective-permute-done, f32[480]{0:T(512)S(1)} %add_rsqrt_fusion.5, f32[384]{0:T(512)S(1)} %copy-done.13), kind=kOutput, calls=%fused_computation.39 | convolution fusion | flops 142479360 | bytes 1035648 | tf_op jit(solution)/shard_map/dot_general | solution.py:75
  76.1 1.1 fusion.16
  77.3 2.3 %fusion.15 = bf16[3360,384]{1,0:T(8,128)(2,1)} fusion(bf16[3360,384]{1,0:T(8,128)(2,1)} %fusion.16, bf16[384,384]{1,0:T(8,128)(2,1)S(1)} %copy-done, bf16[480,384]{1,0:T(8,128)(2,1)} %collective-permute-done.3, f32[480]{0:T(512)S(1)} %add_rsqrt_fusion.4, f32[384]{0:T(512)S(1)} %copy-done.13), kind=kOutput, calls=%fused_computation.35 | convolution fusion | flops 142479360 | bytes 1035648 | tf_op jit(solution)/shard_map/dot_general | solution.py:75
  79.5 2.2 %fusion.14 = bf16[3360,384]{1,0:T(8,128)(2,1)} fusion(bf16[3360,384]{1,0:T(8,128)(2,1)} %fusion.15, bf16[384,384]{1,0:T(8,128)(2,1)S(1)} %copy-done, bf16[480,384]{1,0:T(8,128)(2,1)} %collective-permute-done.4, f32[480]{0:T(512)S(1)} %add_rsqrt_fusion.3, f32[384]{0:T(512)S(1)} %copy-done.13), kind=kOutput, calls=%fused_computation.33 | convolution fusion | flops 142479360 | bytes 1035648 | tf_op jit(solution)/shard_map/dot_general | solution.py:75
  81.7 2.2 %fusion.13 = bf16[3360,384]{1,0:T(8,128)(2,1)} fusion(bf16[3360,384]{1,0:T(8,128)(2,1)} %fusion.14, bf16[384,384]{1,0:T(8,128)(2,1)S(1)} %copy-done, bf16[480,384]{1,0:T(8,128)(2,1)} %collective-permute-done.5, f32[480]{0:T(512)S(1)} %add_rsqrt_fusion.2, f32[384]{0:T(512)S(1)} %copy-done.13), kind=kOutput, calls=%fused_computation.31 | convolution fusion | flops 142479360 | bytes 1035648 | tf_op jit(solution)/shard_map/dot_general | solution.py:75
  83.9 4.2 %multiply_reduce_fusion = (f32[480]{0:T(512)S(1)}, f32[480,384]{1,0:T(8,128)S(1)}) fusion(bf16[384,384]{1,0:T(8,128)(2,1)} %param.15, bf16[3360,384]{1,0:T(8,128)(2,1)} %fusion.13, s32[]{:T(128)S(6)} %select_n.35, f32[3360,480]{0,1:T(8,128)} %concatenate.21, f32[480]{0:T(512)S(1)} %dynamic-slice_reduce_fusion, f32[480]{0:T(512)S(1)} %fusion, ...), kind=kOutput, calls=%fused_computation.88 | convolution fusion | flops 852663808 | bytes 6568576 | tf_op jit(solution)/shard_map/dot_general | solution.py:102
  88.5 4.6 %collective-permute-start.6 = (bf16[1,160,384]{2,1,0:T(8,128)(2,1)S(1)}, bf16[1,160,384]{2,1,0:T(8,128)(2,1)S(1)}, u32[]{:S(2)}, u32[]{:S(2)}) collective-permute-start(bf16[1,160,384]{2,1,0:T(8,128)(2,1)S(1)} %get-tuple-element.35), channel_id=1, source_target_pairs={{0,4},{4,8},{8,12},{1,5},{5,9},{9,13},{2,6},{6,10},{10,14},{3,7},{... | collective-permute-start | bytes 368648 | tf_op jit(solution)/shard_map/ppermute | solution.py:27
  93.2 1.9 %collective-permute-start.7 = (bf16[1,160,384]{2,1,0:T(8,128)(2,1)S(1)}, bf16[1,160,384]{2,1,0:T(8,128)(2,1)S(1)}, u32[]{:S(2)}, u32[]{:S(2)}) collective-permute-start(bf16[1,160,384]{2,1,0:T(8,128)(2,1)S(1)} %get-tuple-element.36), channel_id=1, source_target_pairs={{4,0},{8,4},{12,8},{5,1},{9,5},{13,9},{6,2},{10,6},{14,10},{7,3},{... | collective-permute-start | bytes 368648 | tf_op jit(solution)/shard_map/ppermute | solution.py:28
  95.2 3.9 %collective-permute-start.8 = (bf16[2,1,160,384]{3,2,1,0:T(8,128)(2,1)S(1)}, bf16[2,1,160,384]{3,2,1,0:T(8,128)(2,1)S(1)}, u32[]{:S(2)}, u32[]{:S(2)}) collective-permute-start(bf16[2,1,160,384]{3,2,1,0:T(8,128)(2,1)S(1)} %get-tuple-element.28), channel_id=1, source_target_pairs={{0,4},{4,8},{8,12},{1,5},{5,9},{9,13},{2,6},{6,10},{10,14},{3,7},{... | collective-permute-start | bytes 737288 | tf_op jit(solution)/shard_map/ppermute | solution.py:27
  99.1 1.9 %collective-permute-start.9 = (bf16[2,1,160,384]{3,2,1,0:T(8,128)(2,1)S(1)}, bf16[2,1,160,384]{3,2,1,0:T(8,128)(2,1)S(1)}, u32[]{:S(2)}, u32[]{:S(2)}) collective-permute-start(bf16[2,1,160,384]{3,2,1,0:T(8,128)(2,1)S(1)} %get-tuple-element.27), channel_id=1, source_target_pairs={{4,0},{8,4},{12,8},{5,1},{9,5},{13,9},{6,2},{10,6},{14,10},{7,3},{... | collective-permute-start | bytes 737288 | tf_op jit(solution)/shard_map/ppermute | solution.py:28
  101.2 1.9 %collective-permute-start.10 = (bf16[5,160,384]{2,1,0:T(8,128)(2,1)S(1)}, bf16[5,160,384]{2,1,0:T(8,128)(2,1)S(1)}, u32[]{:S(2)}, u32[]{:S(2)}) collective-permute-start(bf16[5,160,384]{2,1,0:T(8,128)(2,1)S(1)} %pad_maximum_fusion.3), channel_id=1, source_target_pairs={{0,1},{1,2},{2,3},{4,5},{5,6},{6,7},{8,9},{9,10},{10,11},{12,13},{... | collective-permute-start | bytes 1843208 | tf_op jit(solution)/shard_map/ppermute | solution.py:115
  103.1 1.5 %collective-permute-start.11 = (bf16[5,160,384]{2,1,0:T(8,128)(2,1)S(1)}, bf16[5,160,384]{2,1,0:T(8,128)(2,1)S(1)}, u32[]{:S(2)}, u32[]{:S(2)}) collective-permute-start(bf16[5,160,384]{2,1,0:T(8,128)(2,1)S(1)} %pad_maximum_fusion.3), channel_id=1, source_target_pairs={{0,2},{4,6},{8,10},{12,14},{16,18},{20,22},{24,26},{28,30}} | collective-permute-start | bytes 1843208 | tf_op jit(solution)/shard_map/ppermute | solution.py:116
  105.3 0.9 copy-done.11
  107.8 8.9 %collective-permute-done.10 = bf16[5,160,384]{2,1,0:T(8,128)(2,1)S(1)} collective-permute-done((bf16[5,160,384]{2,1,0:T(8,128)(2,1)S(1)}, bf16[5,160,384]{2,1,0:T(8,128)(2,1)S(1)}, u32[]{:S(2)}, u32[]{:S(2)}) %collective-permute-start.10) | collective-permute-done | bytes 614432 | tf_op jit(solution)/shard_map/ppermute | solution.py:115
  116.7 1.3 %collective-permute-start.12 = (bf16[5,160,384]{2,1,0:T(8,128)(2,1)S(1)}, bf16[5,160,384]{2,1,0:T(8,128)(2,1)S(1)}, u32[]{:S(2)}, u32[]{:S(2)}) collective-permute-start(bf16[5,160,384]{2,1,0:T(8,128)(2,1)S(1)} %collective-permute-done.10), channel_id=1, source_target_pairs={{2,3},{6,7},{10,11},{14,15},{18,19},{22,23},{26,27},{30,31}} | collective-permute-start | bytes 1843208 | tf_op jit(solution)/shard_map/ppermute | solution.py:117
  118.0 0.8 fusion.9
  121.4 0.9 copy-done.9
  123.0 0.8 fusion.88
  124.2 0.8 convolution_add_fusion.2
  126.1 0.8 fusion.7
  126.9 1.5 %fusion.10 = bf16[480,384]{1,0:T(8,128)(2,1)} fusion(f32[480,384]{1,0:T(8,128)S(1)} %fusion.7, f32[480,384]{1,0:T(8,128)S(1)} %convolution_add_fusion.2, bf16[480,1152]{1,0:T(8,128)(2,1)S(1)} %bitcast.85, bf16[1152,384]{1,0:T(8,128)(2,1)S(1)} %bitcast.90), kind=kOutput, calls=%fused_computation.27 | convolution fusion | flops 425226240 | bytes 3833856 | tf_op jit(solution)/shard_map/dot_general | solution.py:45
  (70 shorter events, 7.7 us)
Async XLA Ops:
  0.0 69.6 %copy-start = (bf16[384,384]{1,0:T(8,128)(2,1)S(1)}, bf16[384,384]{1,0:T(8,128)(2,1)}, u32[]{:S(2)}) copy-start(bf16[384,384]{1,0:T(8,128)(2,1)} %param.14) | copy-start | bytes 884740
  0.0 16.0 %collective-permute-start.3 = (bf16[480,384]{1,0:T(8,128)(2,1)}, bf16[480,384]{1,0:T(8,128)(2,1)}, u32[]{:S(2)}, u32[]{:S(2)}) collective-permute-start(bf16[480,384]{1,0:T(8,128)(2,1)} %bitcast.94), channel_id=1, source_target_pairs={{4,0},{8,4},{12,8},{5,1},{9,5},{13,9},{6,2},{10,6},{14,10},{7,3},{... | collective-permute-start | bytes 1105928 | tf_op jit(solution)/shard_map/ppermute | solution.py:15
  2.5 17.8 %collective-permute-start = (bf16[480,384]{1,0:T(8,128)(2,1)}, bf16[480,384]{1,0:T(8,128)(2,1)}, u32[]{:S(2)}, u32[]{:S(2)}) collective-permute-start(bf16[480,384]{1,0:T(8,128)(2,1)} %bitcast.95), channel_id=1, source_target_pairs={{0,4},{4,8},{8,12},{1,5},{5,9},{9,13},{2,6},{6,10},{10,14},{3,7},{... | collective-permute-start | bytes 1105928 | tf_op jit(solution)/shard_map/ppermute | solution.py:14
  7.3 5.6 %copy-start.6 = (bf16[1,3,160,384]{3,2,1,0:T(8,128)(2,1)S(1)}, bf16[1,3,160,384]{3,2,1,0:T(8,128)(2,1)}, u32[]{:S(2)}) copy-start(bf16[1,3,160,384]{3,2,1,0:T(8,128)(2,1)} %param.9) | copy-start | bytes 1105924
  7.3 5.6 %copy-start.13 = (f32[384]{0:T(512)S(1)}, f32[384]{0:T(512)}, u32[]{:S(2)}) copy-start(f32[384]{0:T(512)} %param.11) | copy-start | bytes 4612
  7.3 5.7 %copy-start.12 = (bf16[384,384]{1,0:T(8,128)(2,1)S(1)}, bf16[384,384]{1,0:T(8,128)(2,1)}, u32[]{:S(2)}) copy-start(bf16[384,384]{1,0:T(8,128)(2,1)} %param.12) | copy-start | bytes 884740
  16.0 14.5 %collective-permute-start.4 = (bf16[480,384]{1,0:T(8,128)(2,1)}, bf16[480,384]{1,0:T(8,128)(2,1)}, u32[]{:S(2)}, u32[]{:S(2)}) collective-permute-start(bf16[480,384]{1,0:T(8,128)(2,1)} %collective-permute-done.3), channel_id=1, source_target_pairs={{4,0},{8,4},{12,8},{5,1},{9,5},{13,9},{6,2},{10,6},{14,10},{7,3},{... | collective-permute-start | bytes 1105928 | tf_op jit(solution)/shard_map/ppermute | solution.py:15
  20.3 14.9 %collective-permute-start.1 = (bf16[480,384]{1,0:T(8,128)(2,1)}, bf16[480,384]{1,0:T(8,128)(2,1)}, u32[]{:S(2)}, u32[]{:S(2)}) collective-permute-start(bf16[480,384]{1,0:T(8,128)(2,1)} %collective-permute-done), channel_id=1, source_target_pairs={{0,4},{4,8},{8,12},{1,5},{5,9},{9,13},{2,6},{6,10},{10,14},{3,7},{... | collective-permute-start | bytes 1105928 | tf_op jit(solution)/shard_map/ppermute | solution.py:14
  30.6 15.1 %collective-permute-start.5 = (bf16[480,384]{1,0:T(8,128)(2,1)}, bf16[480,384]{1,0:T(8,128)(2,1)}, u32[]{:S(2)}, u32[]{:S(2)}) collective-permute-start(bf16[480,384]{1,0:T(8,128)(2,1)} %collective-permute-done.4), channel_id=1, source_target_pairs={{4,0},{8,4},{12,8},{5,1},{9,5},{13,9},{6,2},{10,6},{14,10},{7,3},{... | collective-permute-start | bytes 1105928 | tf_op jit(solution)/shard_map/ppermute | solution.py:15
  35.3 11.5 %collective-permute-start.2 = (bf16[480,384]{1,0:T(8,128)(2,1)}, bf16[480,384]{1,0:T(8,128)(2,1)}, u32[]{:S(2)}, u32[]{:S(2)}) collective-permute-start(bf16[480,384]{1,0:T(8,128)(2,1)} %collective-permute-done.1), channel_id=1, source_target_pairs={{0,4},{4,8},{8,12},{1,5},{5,9},{9,13},{2,6},{6,10},{10,14},{3,7},{... | collective-permute-start | bytes 1105928 | tf_op jit(solution)/shard_map/ppermute | solution.py:14
  77.3 6.7 %copy-start.7 = (bf16[1,3,160,384]{3,2,1,0:T(8,128)(2,1)S(1)}, bf16[1,3,160,384]{3,2,1,0:T(8,128)(2,1)}, u32[]{:S(2)}) copy-start(bf16[1,3,160,384]{3,2,1,0:T(8,128)(2,1)} %param.9) | copy-start | bytes 1105924
  83.9 4.3 %copy-start.14 = (f32[384]{0:T(512)S(1)}, f32[384]{0:T(512)}, u32[]{:S(2)}) copy-start(f32[384]{0:T(512)} %param.16) | copy-start | bytes 4612
  88.2 6.9 %copy-start.5 = (bf16[2,3,160,384]{3,2,1,0:T(8,128)(2,1)S(1)}, bf16[2,3,160,384]{3,2,1,0:T(8,128)(2,1)}, u32[]{:S(2)}) copy-start(bf16[2,3,160,384]{3,2,1,0:T(8,128)(2,1)} %param.10) | copy-start | bytes 2211844
  88.5 12.5 %collective-permute-start.6 = (bf16[1,160,384]{2,1,0:T(8,128)(2,1)S(1)}, bf16[1,160,384]{2,1,0:T(8,128)(2,1)S(1)}, u32[]{:S(2)}, u32[]{:S(2)}) collective-permute-start(bf16[1,160,384]{2,1,0:T(8,128)(2,1)S(1)} %get-tuple-element.35), channel_id=1, source_target_pairs={{0,4},{4,8},{8,12},{1,5},{5,9},{9,13},{2,6},{6,10},{10,14},{3,7},{... | collective-permute-start | bytes 368648 | tf_op jit(solution)/shard_map/ppermute | solution.py:27
  93.2 7.9 %collective-permute-start.7 = (bf16[1,160,384]{2,1,0:T(8,128)(2,1)S(1)}, bf16[1,160,384]{2,1,0:T(8,128)(2,1)S(1)}, u32[]{:S(2)}, u32[]{:S(2)}) collective-permute-start(bf16[1,160,384]{2,1,0:T(8,128)(2,1)S(1)} %get-tuple-element.36), channel_id=1, source_target_pairs={{4,0},{8,4},{12,8},{5,1},{9,5},{13,9},{6,2},{10,6},{14,10},{7,3},{... | collective-permute-start | bytes 368648 | tf_op jit(solution)/shard_map/ppermute | solution.py:28
  95.2 23.7 %collective-permute-start.8 = (bf16[2,1,160,384]{3,2,1,0:T(8,128)(2,1)S(1)}, bf16[2,1,160,384]{3,2,1,0:T(8,128)(2,1)S(1)}, u32[]{:S(2)}, u32[]{:S(2)}) collective-permute-start(bf16[2,1,160,384]{3,2,1,0:T(8,128)(2,1)S(1)} %get-tuple-element.28), channel_id=1, source_target_pairs={{0,4},{4,8},{8,12},{1,5},{5,9},{9,13},{2,6},{6,10},{10,14},{3,7},{... | collective-permute-start | bytes 737288 | tf_op jit(solution)/shard_map/ppermute | solution.py:27
  99.1 20.0 %collective-permute-start.9 = (bf16[2,1,160,384]{3,2,1,0:T(8,128)(2,1)S(1)}, bf16[2,1,160,384]{3,2,1,0:T(8,128)(2,1)S(1)}, u32[]{:S(2)}, u32[]{:S(2)}) collective-permute-start(bf16[2,1,160,384]{3,2,1,0:T(8,128)(2,1)S(1)} %get-tuple-element.27), channel_id=1, source_target_pairs={{4,0},{8,4},{12,8},{5,1},{9,5},{13,9},{6,2},{10,6},{14,10},{7,3},{... | collective-permute-start | bytes 737288 | tf_op jit(solution)/shard_map/ppermute | solution.py:28
  101.2 15.5 %collective-permute-start.10 = (bf16[5,160,384]{2,1,0:T(8,128)(2,1)S(1)}, bf16[5,160,384]{2,1,0:T(8,128)(2,1)S(1)}, u32[]{:S(2)}, u32[]{:S(2)}) collective-permute-start(bf16[5,160,384]{2,1,0:T(8,128)(2,1)S(1)} %pad_maximum_fusion.3), channel_id=1, source_target_pairs={{0,1},{1,2},{2,3},{4,5},{5,6},{6,7},{8,9},{9,10},{10,11},{12,13},{... | collective-permute-start | bytes 1843208 | tf_op jit(solution)/shard_map/ppermute | solution.py:115
  103.1 16.1 %collective-permute-start.11 = (bf16[5,160,384]{2,1,0:T(8,128)(2,1)S(1)}, bf16[5,160,384]{2,1,0:T(8,128)(2,1)S(1)}, u32[]{:S(2)}, u32[]{:S(2)}) collective-permute-start(bf16[5,160,384]{2,1,0:T(8,128)(2,1)S(1)} %pad_maximum_fusion.3), channel_id=1, source_target_pairs={{0,2},{4,6},{8,10},{12,14},{16,18},{20,22},{24,26},{28,30}} | collective-permute-start | bytes 1843208 | tf_op jit(solution)/shard_map/ppermute | solution.py:116
  105.1 1.2 copy-start.11
  105.3 1.7 %copy-start.10 = (bf16[1,1,3,384,384]{4,3,2,1,0:T(8,128)(2,1)S(1)}, bf16[1,1,3,384,384]{4,3,2,1,0:T(8,128)(2,1)}, u32[]{:S(2)}) copy-start(bf16[1,1,3,384,384]{4,3,2,1,0:T(8,128)(2,1)} %get-tuple-element.12) | copy-start | bytes 2654212
  116.7 2.9 %collective-permute-start.12 = (bf16[5,160,384]{2,1,0:T(8,128)(2,1)S(1)}, bf16[5,160,384]{2,1,0:T(8,128)(2,1)S(1)}, u32[]{:S(2)}, u32[]{:S(2)}) collective-permute-start(bf16[5,160,384]{2,1,0:T(8,128)(2,1)S(1)} %collective-permute-done.10), channel_id=1, source_target_pairs={{2,3},{6,7},{10,11},{14,15},{18,19},{22,23},{26,27},{30,31}} | collective-permute-start | bytes 1843208 | tf_op jit(solution)/shard_map/ppermute | solution.py:117
  121.1 1.2 copy-start.9
  121.4 1.6 %copy-start.8 = (bf16[1,1,3,384,384]{4,3,2,1,0:T(8,128)(2,1)S(1)}, bf16[1,1,3,384,384]{4,3,2,1,0:T(8,128)(2,1)}, u32[]{:S(2)}) copy-start(bf16[1,1,3,384,384]{4,3,2,1,0:T(8,128)(2,1)} %get-tuple-element.10) | copy-start | bytes 2654212
  123.0 1.2 copy-start.3
  123.8 1.2 copy-start.2
  124.9 1.2 copy-start.4
  126.9 1.5 %copy-start.1 = (bf16[384,384]{1,0:T(8,128)(2,1)S(1)}, bf16[384,384]{1,0:T(8,128)(2,1)}, u32[]{:S(2)}) copy-start(bf16[384,384]{1,0:T(8,128)(2,1)} %param.14) | copy-start | bytes 884740

commit v3 on v1

--- a/solution.py
+++ b/solution.py
@@ -1,6 +1,11 @@
+import functools
+
 import jax
 import jax.numpy as jnp
+import numpy as np
 from jax import lax
+from jax.experimental import pallas as pl
+from jax.experimental.pallas import tpu as pltpu
 from jax.sharding import PartitionSpec as P
 
 
@@ -47,17 +52,42 @@
     return wide * lax.rsqrt(jnp.mean(wide * wide, axis=-1, keepdims=True) + 1e-06) * gain
 
 
-def attend(carry, query, keys, values, scale):
-    peak, total, summed = carry
+def attention_kernel(scale, q_ref, k_ref, v_ref, o_ref):
     scores = (
-        lax.dot_general(query, keys, (((1,), (1,)), ((), ())), preferred_element_type=jnp.float32)
+        lax.dot_general(
+            q_ref[...], k_ref[...], (((1,), (1,)), ((), ())), preferred_element_type=jnp.float32
+        )
         * scale
     )
-    fresh = jnp.maximum(peak, jnp.max(scores, axis=1))
-    weights = jnp.exp(scores - fresh[:, None])
-    total = jnp.sum(weights, axis=1)
-    summed = jnp.dot(weights.astype(jnp.bfloat16), values, preferred_element_type=jnp.float32)
-    return (fresh, total, summed)
+    peak = jnp.max(scores, axis=1, keepdims=True)
+    weights = jnp.exp(scores - peak)
+    total = jnp.sum(weights, axis=1, keepdims=True)
+    summed = jnp.dot(weights.astype(jnp.bfloat16), v_ref[...], preferred_element_type=jnp.float32)
+    o_ref[...] = (summed / total).astype(o_ref.dtype)
+
+
+def attend(query, keys, values, scale):
+    count, width = query.shape
+    total_keys = keys.shape[0]
+    block = 160 if count % 160 == 0 else count
+    flops = 4 * count * total_keys * width
+    return pl.pallas_call(
+        functools.partial(attention_kernel, scale),
+        out_shape=jax.ShapeDtypeStruct((count, width), jnp.bfloat16),
+        grid=(count // block,),
+        in_specs=[
+            pl.BlockSpec((block, width), lambda i: (i, 0)),
+            pl.BlockSpec((total_keys, width), lambda i: (0, 0)),
+            pl.BlockSpec((total_keys, width), lambda i: (0, 0)),
+        ],
+        out_specs=pl.BlockSpec((block, width), lambda i: (i, 0)),
+        compiler_params=pltpu.CompilerParams(vmem_limit_bytes=60 * 1024 * 1024),
+        cost_estimate=pl.CostEstimate(
+            flops=flops,
+            transcendentals=count * total_keys,
+            bytes_accessed=2 * width * (2 * count + 2 * total_keys),
+        ),
+    )(query, keys, values)
 
 
 def shards(
@@ -76,26 +106,14 @@
     width = frames.shape[3]
     flat = frames.reshape(-1, width)
     count = flat.shape[0]
-    scale = 1.0 / jnp.sqrt(jnp.float32(width))
+    scale = float(np.float32(1.0) / np.sqrt(np.float32(width)))
     whole = strip_gather(flat, "strip")
     normed = rms_scale(flat, attn_gain).astype(jnp.bfloat16)
     normed_all = rms_scale(whole, attn_gain).astype(jnp.bfloat16)
     query = jnp.dot(normed, query_weight, preferred_element_type=jnp.float32).astype(jnp.bfloat16)
-    start_carry = (
-        jnp.full((count,), -1e30, jnp.float32),
-        jnp.zeros((count,), jnp.float32),
-        jnp.zeros((count, width), jnp.float32),
-    )
     keys = jnp.dot(normed_all, key_weight, preferred_element_type=jnp.float32).astype(jnp.bfloat16)
     values = jnp.dot(normed_all, value_weight, preferred_element_type=jnp.float32).astype(jnp.bfloat16)
-    peak, total, summed = attend(
-        start_carry,
-        query,
-        keys,
-        values,
-        scale,
-    )
-    attended = (summed / total[:, None]).astype(jnp.bfloat16)
+    attended = attend(query, keys, values, scale)
     resid = (
         flat.astype(jnp.float32) + jnp.dot(attended, out_weight, preferred_element_type=jnp.float32)
     ).astype(jnp.bfloat16)

time: 100 us -> 98.7 us (0.987)
  Pallas kernels: 0 us -> 6.65 us
  matrix products: 19.8 us -> 16.2 us
  other arithmetic: 7.03 us -> 4.21 us
  local copies, waits for them, and re-layouts: 5.81 us -> 4.34 us
    pallas_call x0 -> x1, Pallas kernels: none -> 6.65 us  [attend(): pl.pallas_call(functools.partial(attention_kernel, scale), out_shape=jax....]
    dot_general x2, matrix products: 9.96 us -> 4.52 us  [the longest x1 2.27 us: shards(): jnp.dot(normed_all, value_weight, preferred_element_type=jnp.float32)]
    reduce_sum x1 -> x0, other arithmetic: 2.83 us -> none  [attend(): total = jnp.sum(weights, axis=1)]
    unnamed x26 -> x24, local copies, waits for them, and re-layouts: 3.83 us -> 2.23 us
    dot_general x1, matrix products: 0.49 us -> 1.54 us  [shards(): jnp.dot(attended, out_weight, preferred_element_type=jnp.float32)]
  transfers between devices with their start and end apart: 10 -> 10, of which waited for: 8 -> 8; matrix products, arithmetic and copies ran while one was open for 3% -> 4% of each run, Pallas kernels for 0% -> 0%
where the time goes in v3:
time: 98.7 us; the launch traced here: 98.2 us
  waiting for transfers between devices  39 us (40%)
  starting transfers between devices  27.6 us (28%)
  matrix products  16.2 us (16%)
  Pallas kernels  6.65 us (7%)
  local copies, waits for them, and re-layouts  4.34 us (4%)
  other arithmetic  4.21 us (4%)
    ppermute x2, waiting for transfers between devices, passed_along(): return lax.ppermute(x, axis, pairs)  13.8 us
    ppermute x3, waiting for transfers between devices, strip_gather(): up = lax.ppermute(up, axis, up_pairs)  13.1 us
    ppermute x3, starting transfers between devices, strip_gather(): up = lax.ppermute(up, axis, up_pairs)  10.6 us
    dot_general x9, matrix products, shards(): jnp.dot(window, kernel[step_t, step_r], preferred_element_type=jnp.float32)  7.82 us
    ppermute x3, starting transfers between devices, strip_gather(): down = lax.ppermute(down, axis, down_pairs)  7.12 us
    pallas_call x1, Pallas kernels, attend(): pl.pallas_call(functools.partial(attention_kernel, scale), out_shape=jax....  6.65 us
    ppermute x3, waiting for transfers between devices, strip_gather(): down = lax.ppermute(down, axis, down_pairs)  5.18 us
    ppermute x2, starting transfers between devices, passed_along(): return lax.ppermute(x, axis, pairs)  3.84 us
  transfers between devices with their start and end apart: 10, of which 8 were waited for; matrix products, arithmetic and copies ran while one was open for 4% of the time, Pallas kernels for 0%

profile of v3, /device:TPU:10, one launch (start us, length us, event | category | flops | bytes accessed | tf_op | source)
XLA Modules:
  0.0 98.2 jit_solution(7404766645912507468)
XLA Ops:
  0.0 3.6 %collective-permute-start = (bf16[480,384]{1,0:T(8,128)(2,1)}, bf16[480,384]{1,0:T(8,128)(2,1)S(1)}, u32[]{:S(2)}, u32[]{:S(2)}) collective-permute-start(bf16[480,384]{1,0:T(8,128)(2,1)} %bitcast.72), channel_id=1, source_target_pairs={{0,4},{4,8},{8,12},{1,5},{5,9},{9,13},{2,6},{6,10},{10,14},{3,7},{... | collective-permute-start | bytes 1105928 | tf_op jit(solution)/shard_map/ppermute | solution.py:41
  3.6 2.4 %collective-permute-start.3 = (bf16[480,384]{1,0:T(8,128)(2,1)}, bf16[480,384]{1,0:T(8,128)(2,1)S(1)}, u32[]{:S(2)}, u32[]{:S(2)}) collective-permute-start(bf16[480,384]{1,0:T(8,128)(2,1)} %bitcast.73), channel_id=1, source_target_pairs={{4,0},{8,4},{12,8},{5,1},{9,5},{13,9},{6,2},{10,6},{14,10},{7,3},{... | collective-permute-start | bytes 1105928 | tf_op jit(solution)/shard_map/ppermute | solution.py:42
  6.0 6.6 %collective-permute-done = bf16[480,384]{1,0:T(8,128)(2,1)S(1)} collective-permute-done((bf16[480,384]{1,0:T(8,128)(2,1)}, bf16[480,384]{1,0:T(8,128)(2,1)S(1)}, u32[]{:S(2)}, u32[]{:S(2)}) %collective-permute-start) | collective-permute-done | bytes 368672 | tf_op jit(solution)/shard_map/ppermute | solution.py:41
  12.6 3.5 %collective-permute-start.1 = (bf16[480,384]{1,0:T(8,128)(2,1)S(1)}, bf16[480,384]{1,0:T(8,128)(2,1)S(1)}, u32[]{:S(2)}, u32[]{:S(2)}) collective-permute-start(bf16[480,384]{1,0:T(8,128)(2,1)S(1)} %collective-permute-done), channel_id=1, source_target_pairs={{0,4},{4,8},{8,12},{1,5},{5,9},{9,13},{2,6},{6,10},{10,14},{3,7},{... | collective-permute-start | bytes 1105928 | tf_op jit(solution)/shard_map/ppermute | solution.py:41
  16.0 1.2 %multiply_reduce_fusion.1 = f32[3,160]{1,0:T(4,128)S(1)} fusion(bf16[1,3,160,384]{3,2,1,0:T(8,128)(2,1)} %param.9), kind=kLoop, calls=%fused_computation.54 | loop fusion | flops 552480 | bytes 370560 | tf_op jit(solution)/shard_map/reduce_sum | solution.py:52
  17.2 2.4 %collective-permute-start.4 = (bf16[480,384]{1,0:T(8,128)(2,1)S(1)}, bf16[480,384]{1,0:T(8,128)(2,1)S(1)}, u32[]{:S(2)}, u32[]{:S(2)}) collective-permute-start(bf16[480,384]{1,0:T(8,128)(2,1)S(1)} %collective-permute-done.3), channel_id=1, source_target_pairs={{4,0},{8,4},{12,8},{5,1},{9,5},{13,9},{6,2},{10,6},{14,10},{7,3},{... | collective-permute-start | bytes 1105928 | tf_op jit(solution)/shard_map/ppermute | solution.py:42
  19.6 4.3 %collective-permute-done.1 = bf16[480,384]{1,0:T(8,128)(2,1)S(1)} collective-permute-done((bf16[480,384]{1,0:T(8,128)(2,1)S(1)}, bf16[480,384]{1,0:T(8,128)(2,1)S(1)}, u32[]{:S(2)}, u32[]{:S(2)}) %collective-permute-start.1) | collective-permute-done | bytes 368672 | tf_op jit(solution)/shard_map/ppermute | solution.py:41
  23.9 3.5 %collective-permute-start.2 = (bf16[480,384]{1,0:T(8,128)(2,1)S(1)}, bf16[480,384]{1,0:T(8,128)(2,1)S(1)}, u32[]{:S(2)}, u32[]{:S(2)}) collective-permute-start(bf16[480,384]{1,0:T(8,128)(2,1)S(1)} %collective-permute-done.1), channel_id=1, source_target_pairs={{0,4},{4,8},{8,12},{1,5},{5,9},{9,13},{2,6},{6,10},{10,14},{3,7},{... | collective-permute-start | bytes 1105928 | tf_op jit(solution)/shard_map/ppermute | solution.py:41
  27.4 0.1 rsqrt.28
  27.5 2.3 %convolution_convert_fusion.2.q_ref = bf16[480,384]{1,0:T(8,128)(2,1)} fusion(bf16[384,384]{1,0:T(8,128)(2,1)} %param.12, bf16[480,384]{1,0:T(8,128)(2,1)} %bitcast.74, f32[384]{0:T(512)} %param.11, f32[480]{0:T(512)S(1)} %rsqrt.28), kind=kOutput, calls=%fused_computation.31 | convolution fusion | flops 142479360 | bytes 1035648 | tf_op jit(solution)/shard_map/dot_general | solution.py:113
  29.8 2.4 %collective-permute-start.5 = (bf16[480,384]{1,0:T(8,128)(2,1)S(1)}, bf16[480,384]{1,0:T(8,128)(2,1)S(1)}, u32[]{:S(2)}, u32[]{:S(2)}) collective-permute-start(bf16[480,384]{1,0:T(8,128)(2,1)S(1)} %collective-permute-done.4), channel_id=1, source_target_pairs={{4,0},{8,4},{12,8},{5,1},{9,5},{13,9},{6,2},{10,6},{14,10},{7,3},{... | collective-permute-start | bytes 1105928 | tf_op jit(solution)/shard_map/ppermute | solution.py:42
  32.1 2.3 %collective-permute-done.2 = bf16[480,384]{1,0:T(8,128)(2,1)S(1)} collective-permute-done((bf16[480,384]{1,0:T(8,128)(2,1)S(1)}, bf16[480,384]{1,0:T(8,128)(2,1)S(1)}, u32[]{:S(2)}, u32[]{:S(2)}) %collective-permute-start.2) | collective-permute-done | bytes 368672 | tf_op jit(solution)/shard_map/ppermute | solution.py:41
  34.5 0.1 constant_dynamic-update-slice_fusion.5
  34.5 0.1 constant_dynamic-update-slice_fusion.4
  34.6 0.1 constant_dynamic-update-slice_fusion.3
  34.7 0.1 constant_dynamic-update-slice_fusion.2
  34.8 0.1 constant_dynamic-update-slice_fusion.1
  34.8 5.2 %collective-permute-done.5 = bf16[480,384]{1,0:T(8,128)(2,1)S(1)} collective-permute-done((bf16[480,384]{1,0:T(8,128)(2,1)S(1)}, bf16[480,384]{1,0:T(8,128)(2,1)S(1)}, u32[]{:S(2)}, u32[]{:S(2)}) %collective-permute-start.5) | collective-permute-done | bytes 368672 | tf_op jit(solution)/shard_map/ppermute | solution.py:42
  40.1 0.4 fusion.1
  40.5 2.3 %convolution_convert_fusion.v_ref = bf16[1920,384]{1,0:T(8,128)(2,1)} fusion(bf16[384,384]{1,0:T(8,128)(2,1)S(1)} %copy-done, f32[384]{0:T(512)S(1)} %copy-done.6, f32[1920]{0:T(1024)S(1)} %add_rsqrt_fusion, bf16[3360,384]{1,0:T(8,128)(2,1)S(1)} %constant_dynamic-update-slice_fusion, s32[]{:T(128)S(6)} %select_n.15), kind=kOutput, calls=%fused_computation.9 | convolution fusion | flops 569917440 | bytes 3254276 | tf_op jit(solution)/shard_map/dot_general | solution.py:115
  42.7 2.3 %convolution_convert_fusion.1.k_ref = bf16[1920,384]{1,0:T(8,128)(2,1)} fusion(bf16[384,384]{1,0:T(8,128)(2,1)S(1)} %copy-done.5, f32[384]{0:T(512)S(1)} %copy-done.6, f32[1920]{0:T(1024)S(1)} %add_rsqrt_fusion, bf16[3360,384]{1,0:T(8,128)(2,1)S(1)} %constant_dynamic-update-slice_fusion, s32[]{:T(128)S(6)} %select_n.15), kind=kOutput, calls=%fused_computation.10 | convolution fusion | flops 569917440 | bytes 3254276 | tf_op jit(solution)/shard_map/dot_general | solution.py:114
  45.0 6.6 %shard_map.91 = bf16[480,384]{1,0:T(8,128)(2,1)} custom-call(bf16[480,384]{1,0:T(8,128)(2,1)} %convolution_convert_fusion.2.q_ref, bf16[1920,384]{1,0:T(8,128)(2,1)} %convolution_convert_fusion.1.k_ref, bf16[1920,384]{1,0:T(8,128)(2,1)} %convolution_convert_fusion.v_ref), custom_call_target="tpu_custom_call" | custom-call | flops 1415577600 | bytes 3686400 | tf_op jit(solution)/shard_map/pallas_call | solution.py:74
  51.7 1.5 %multiply_reduce_fusion = (f32[480]{0:T(512)S(1)}, f32[480,384]{1,0:T(8,128)S(1)}) fusion(bf16[480,384]{1,0:T(8,128)(2,1)} %shard_map.91, bf16[384,384]{1,0:T(8,128)(2,1)S(1)} %copy-done.3, bf16[480,384]{1,0:T(8,128)(2,1)S(1)} %bitcast.76), kind=kOutput, calls=%fused_computation.53 | convolution fusion | flops 142663200 | bytes 1771392 | tf_op jit(solution)/shard_map/dot_general | solution.py:118
  53.2 0.3 multiply_convert_fusion
  53.5 1.9 %collective-permute-start.6 = (bf16[3,160,384]{2,1,0:T(8,128)(2,1)S(1)}, bf16[3,160,384]{2,1,0:T(8,128)(2,1)S(1)}, u32[]{:S(2)}, u32[]{:S(2)}) collective-permute-start(bf16[3,160,384]{2,1,0:T(8,128)(2,1)S(1)} %bitcast.64), channel_id=1, source_target_pairs={{0,1},{1,2},{2,3},{4,5},{5,6},{6,7},{8,9},{9,10},{10,11},{12,13},{... | collective-permute-start | bytes 1105928 | tf_op jit(solution)/shard_map/ppermute | solution.py:15
  55.4 6.9 %collective-permute-done.6 = bf16[3,160,384]{2,1,0:T(8,128)(2,1)S(1)} collective-permute-done((bf16[3,160,384]{2,1,0:T(8,128)(2,1)S(1)}, bf16[3,160,384]{2,1,0:T(8,128)(2,1)S(1)}, u32[]{:S(2)}, u32[]{:S(2)}) %collective-permute-start.6) | collective-permute-done | bytes 368672 | tf_op jit(solution)/shard_map/ppermute | solution.py:15
  62.4 1.9 %collective-permute-start.7 = (bf16[3,160,384]{2,1,0:T(8,128)(2,1)S(1)}, bf16[3,160,384]{2,1,0:T(8,128)(2,1)S(1)}, u32[]{:S(2)}, u32[]{:S(2)}) collective-permute-start(bf16[3,160,384]{2,1,0:T(8,128)(2,1)S(1)} %bitcast_select_fusion), channel_id=1, source_target_pairs={{0,1},{1,2},{2,3},{4,5},{5,6},{6,7},{8,9},{9,10},{10,11},{12,13},{... | collective-permute-start | bytes 1105928 | tf_op jit(solution)/shard_map/ppermute | solution.py:15
  64.3 6.9 %collective-permute-done.7 = bf16[3,160,384]{2,1,0:T(8,128)(2,1)S(1)} collective-permute-done((bf16[3,160,384]{2,1,0:T(8,128)(2,1)S(1)}, bf16[3,160,384]{2,1,0:T(8,128)(2,1)S(1)}, u32[]{:S(2)}, u32[]{:S(2)}) %collective-permute-start.7) | collective-permute-done | bytes 368672 | tf_op jit(solution)/shard_map/ppermute | solution.py:15
  71.3 0.1 pad_maximum_fusion.3
  71.4 3.5 %collective-permute-start.8 = (bf16[3,1,160,384]{3,2,1,0:T(8,128)(2,1)S(1)}, bf16[3,1,160,384]{3,2,1,0:T(8,128)(2,1)S(1)}, u32[]{:S(2)}, u32[]{:S(2)}) collective-permute-start(bf16[3,1,160,384]{3,2,1,0:T(8,128)(2,1)S(1)} %get-tuple-element.16), channel_id=1, source_target_pairs={{0,4},{4,8},{8,12},{1,5},{5,9},{9,13},{2,6},{6,10},{10,14},{3,7},{... | collective-permute-start | bytes 1105928 | tf_op jit(solution)/shard_map/ppermute | solution.py:25
  74.9 2.5 %collective-permute-start.9 = (bf16[3,1,160,384]{3,2,1,0:T(8,128)(2,1)S(1)}, bf16[3,1,160,384]{3,2,1,0:T(8,128)(2,1)S(1)}, u32[]{:S(2)}, u32[]{:S(2)}) collective-permute-start(bf16[3,1,160,384]{3,2,1,0:T(8,128)(2,1)S(1)} %get-tuple-element.17), channel_id=1, source_target_pairs={{4,0},{8,4},{12,8},{5,1},{9,5},{13,9},{6,2},{10,6},{14,10},{7,3},{... | collective-permute-start | bytes 1105928 | tf_op jit(solution)/shard_map/ppermute | solution.py:26
  77.4 3.3 %collective-permute-done.8 = bf16[3,1,160,384]{3,2,1,0:T(8,128)(2,1)S(1)} collective-permute-done((bf16[3,1,160,384]{3,2,1,0:T(8,128)(2,1)S(1)}, bf16[3,1,160,384]{3,2,1,0:T(8,128)(2,1)S(1)}, u32[]{:S(2)}, u32[]{:S(2)}) %collective-permute-start.8) | collective-permute-done | bytes 368672 | tf_op jit(solution)/shard_map/ppermute | solution.py:25
  80.8 3.5 %collective-permute-done.9 = bf16[3,1,160,384]{3,2,1,0:T(8,128)(2,1)S(1)} collective-permute-done((bf16[3,1,160,384]{3,2,1,0:T(8,128)(2,1)S(1)}, bf16[3,1,160,384]{3,2,1,0:T(8,128)(2,1)S(1)}, u32[]{:S(2)}, u32[]{:S(2)}) %collective-permute-start.9) | collective-permute-done | bytes 368672 | tf_op jit(solution)/shard_map/ppermute | solution.py:26
  84.3 1.5 %select_maximum_fusion = bf16[3,5,162,384]{3,2,1,0:T(8,128)(2,1)S(1)} fusion(bf16[3,1,160,384]{3,2,1,0:T(8,128)(2,1)S(1)} %collective-permute-done.9, bf16[3,1,160,384]{3,2,1,0:T(8,128)(2,1)S(1)} %collective-permute-done.8, bf16[1,3,160,384]{3,2,1,0:T(8,128)(2,1)S(1)} %bitcast.66, bf16[1,3,160,384]{3,2,1,0:T(8,128)(2,1)S(1)} %bitcast.69, ...), kind=kLoop, calls=%fused_computation.11 | loop fusion | flops 16796160 | bytes 3709440 | tf_op jit(solution)/shard_map/concatenate | solution.py:27
  85.8 1.0 fusion.39
  86.8 0.6 pad_maximum_fusion
  87.5 1.0 %fusion.38 = (bf16[1,3,160,1152]{3,2,1,0:T(8,128)(2,1)S(1)}, bf16[1,3,160,1152]{3,2,1,0:T(8,128)(2,1)S(1)}, bf16[1,3,160,1152]{3,2,1,0:T(8,128)(2,1)S(1)}, bf16[...) fusion(bf16[3,5,160,1152]{3,2,1,0:T(8,128)(2,1)S(1)} %pad_maxim, ...), kind=kLoop, calls=%fused_computation.75 | loop fusion | bytes 19906560 | tf_op jit(solution)/shard_map/slice | solution.py:136
  88.5 0.5 slice-done
  89.0 1.3 %slice-done.1 = s8[3768320]{0:T(1024)(128)(4,1)S(1)} async-done(((s8[7962624]{0:T(1024)(128)(4,1)}), s8[3768320]{0:T(1024)(128)(4,1)S(1)}, s32[]{:S(2)}) %slice-start.1) | async-done | bytes 3768344
  90.3 0.8 fusion.20
  91.1 0.8 fusion.21
  91.9 0.8 fusion.22
  92.6 0.8 fusion.23
  93.4 0.8 fusion.24
  94.2 0.8 fusion.25
  94.9 0.8 fusion.26
  95.7 0.8 fusion.27
  96.5 1.8 %fusion.17 = bf16[480,384]{1,0:T(8,128)(2,1)} fusion(f32[480,384]{1,0:T(8,128)S(1)} %fusion.20, f32[480,384]{1,0:T(8,128)S(1)} %fusion.21, f32[480,384]{1,0:T(8,128)S(1)} %fusion.22, f32[480,384]{1,0:T(8,128)S(1)} %fusion.23, f32[480,384]{1,0:T(8,128)S(1)} %fusion.24, f32[480,384]{1,0:T(8,128)S(1)} %fusion.25, f32[480,384]{1,0:T(8,128)S(1)} %fusion.26, ...), kind=kOutput, calls=%fused_computation.28 | convolution fusion | flops 426516480 | bytes 8994816 | tf_op jit(solution)/shard_map/dot_general | solution.py:137
  (26 shorter events, 0.3 us)
Async XLA Ops:
  0.0 40.5 %copy-start = (bf16[384,384]{1,0:T(8,128)(2,1)S(1)}, bf16[384,384]{1,0:T(8,128)(2,1)}, u32[]{:S(2)}) copy-start(bf16[384,384]{1,0:T(8,128)(2,1)} %param.14) | copy-start | bytes 884740
  0.0 34.6 %copy-start.1 = (bf16[1,3,160,384]{3,2,1,0:T(8,128)(2,1)S(1)}, bf16[1,3,160,384]{3,2,1,0:T(8,128)(2,1)}, u32[]{:S(2)}) copy-start(bf16[1,3,160,384]{3,2,1,0:T(8,128)(2,1)} %param.9) | copy-start | bytes 1105924
  0.0 12.6 %collective-permute-start = (bf16[480,384]{1,0:T(8,128)(2,1)}, bf16[480,384]{1,0:T(8,128)(2,1)S(1)}, u32[]{:S(2)}, u32[]{:S(2)}) collective-permute-start(bf16[480,384]{1,0:T(8,128)(2,1)} %bitcast.72), channel_id=1, source_target_pairs={{0,4},{4,8},{8,12},{1,5},{5,9},{9,13},{2,6},{6,10},{10,14},{3,7},{... | collective-permute-start | bytes 1105928 | tf_op jit(solution)/shard_map/ppermute | solution.py:41
  3.6 13.6 %collective-permute-start.3 = (bf16[480,384]{1,0:T(8,128)(2,1)}, bf16[480,384]{1,0:T(8,128)(2,1)S(1)}, u32[]{:S(2)}, u32[]{:S(2)}) collective-permute-start(bf16[480,384]{1,0:T(8,128)(2,1)} %bitcast.73), channel_id=1, source_target_pairs={{4,0},{8,4},{12,8},{5,1},{9,5},{13,9},{6,2},{10,6},{14,10},{7,3},{... | collective-permute-start | bytes 1105928 | tf_op jit(solution)/shard_map/ppermute | solution.py:42
  12.6 11.4 %collective-permute-start.1 = (bf16[480,384]{1,0:T(8,128)(2,1)S(1)}, bf16[480,384]{1,0:T(8,128)(2,1)S(1)}, u32[]{:S(2)}, u32[]{:S(2)}) collective-permute-start(bf16[480,384]{1,0:T(8,128)(2,1)S(1)} %collective-permute-done), channel_id=1, source_target_pairs={{0,4},{4,8},{8,12},{1,5},{5,9},{9,13},{2,6},{6,10},{10,14},{3,7},{... | collective-permute-start | bytes 1105928 | tf_op jit(solution)/shard_map/ppermute | solution.py:41
  17.2 12.5 %collective-permute-start.4 = (bf16[480,384]{1,0:T(8,128)(2,1)S(1)}, bf16[480,384]{1,0:T(8,128)(2,1)S(1)}, u32[]{:S(2)}, u32[]{:S(2)}) collective-permute-start(bf16[480,384]{1,0:T(8,128)(2,1)S(1)} %collective-permute-done.3), channel_id=1, source_target_pairs={{4,0},{8,4},{12,8},{5,1},{9,5},{13,9},{6,2},{10,6},{14,10},{7,3},{... | collective-permute-start | bytes 1105928 | tf_op jit(solution)/shard_map/ppermute | solution.py:42
  23.9 10.5 %collective-permute-start.2 = (bf16[480,384]{1,0:T(8,128)(2,1)S(1)}, bf16[480,384]{1,0:T(8,128)(2,1)S(1)}, u32[]{:S(2)}, u32[]{:S(2)}) collective-permute-start(bf16[480,384]{1,0:T(8,128)(2,1)S(1)} %collective-permute-done.1), channel_id=1, source_target_pairs={{0,4},{4,8},{8,12},{1,5},{5,9},{9,13},{2,6},{6,10},{10,14},{3,7},{... | collective-permute-start | bytes 1105928 | tf_op jit(solution)/shard_map/ppermute | solution.py:41
  29.8 10.2 %collective-permute-start.5 = (bf16[480,384]{1,0:T(8,128)(2,1)S(1)}, bf16[480,384]{1,0:T(8,128)(2,1)S(1)}, u32[]{:S(2)}, u32[]{:S(2)}) collective-permute-start(bf16[480,384]{1,0:T(8,128)(2,1)S(1)} %collective-permute-done.4), channel_id=1, source_target_pairs={{4,0},{8,4},{12,8},{5,1},{9,5},{13,9},{6,2},{10,6},{14,10},{7,3},{... | collective-permute-start | bytes 1105928 | tf_op jit(solution)/shard_map/ppermute | solution.py:42
  34.5 5.9 %copy-start.6 = (f32[384]{0:T(512)S(1)}, f32[384]{0:T(512)}, u32[]{:S(2)}) copy-start(f32[384]{0:T(512)} %param.11) | copy-start | bytes 4612
  40.1 2.7 %copy-start.5 = (bf16[384,384]{1,0:T(8,128)(2,1)S(1)}, bf16[384,384]{1,0:T(8,128)(2,1)}, u32[]{:S(2)}) copy-start(bf16[384,384]{1,0:T(8,128)(2,1)} %param.13) | copy-start | bytes 884740
  45.0 6.7 %copy-start.3 = (bf16[384,384]{1,0:T(8,128)(2,1)S(1)}, bf16[384,384]{1,0:T(8,128)(2,1)}, u32[]{:S(2)}) copy-start(bf16[384,384]{1,0:T(8,128)(2,1)} %param.15) | copy-start | bytes 884740
  45.0 8.2 %copy-start.4 = (f32[384]{0:T(512)S(1)}, f32[384]{0:T(512)}, u32[]{:S(2)}) copy-start(f32[384]{0:T(512)} %param.16) | copy-start | bytes 4612
  51.7 10.7 %copy-start.2 = (bf16[2,3,160,384]{3,2,1,0:T(8,128)(2,1)S(1)}, bf16[2,3,160,384]{3,2,1,0:T(8,128)(2,1)}, u32[]{:S(2)}) copy-start(bf16[2,3,160,384]{3,2,1,0:T(8,128)(2,1)} %param.10) | copy-start | bytes 2211844
  53.5 8.8 %collective-permute-start.6 = (bf16[3,160,384]{2,1,0:T(8,128)(2,1)S(1)}, bf16[3,160,384]{2,1,0:T(8,128)(2,1)S(1)}, u32[]{:S(2)}, u32[]{:S(2)}) collective-permute-start(bf16[3,160,384]{2,1,0:T(8,128)(2,1)S(1)} %bitcast.64), channel_id=1, source_target_pairs={{0,1},{1,2},{2,3},{4,5},{5,6},{6,7},{8,9},{9,10},{10,11},{12,13},{... | collective-permute-start | bytes 1105928 | tf_op jit(solution)/shard_map/ppermute | solution.py:15
  62.4 8.8 %collective-permute-start.7 = (bf16[3,160,384]{2,1,0:T(8,128)(2,1)S(1)}, bf16[3,160,384]{2,1,0:T(8,128)(2,1)S(1)}, u32[]{:S(2)}, u32[]{:S(2)}) collective-permute-start(bf16[3,160,384]{2,1,0:T(8,128)(2,1)S(1)} %bitcast_select_fusion), channel_id=1, source_target_pairs={{0,1},{1,2},{2,3},{4,5},{5,6},{6,7},{8,9},{9,10},{10,11},{12,13},{... | collective-permute-start | bytes 1105928 | tf_op jit(solution)/shard_map/ppermute | solution.py:15
  71.4 9.4 %collective-permute-start.8 = (bf16[3,1,160,384]{3,2,1,0:T(8,128)(2,1)S(1)}, bf16[3,1,160,384]{3,2,1,0:T(8,128)(2,1)S(1)}, u32[]{:S(2)}, u32[]{:S(2)}) collective-permute-start(bf16[3,1,160,384]{3,2,1,0:T(8,128)(2,1)S(1)} %get-tuple-element.16), channel_id=1, source_target_pairs={{0,4},{4,8},{8,12},{1,5},{5,9},{9,13},{2,6},{6,10},{10,14},{3,7},{... | collective-permute-start | bytes 1105928 | tf_op jit(solution)/shard_map/ppermute | solution.py:25
  74.9 9.4 %collective-permute-start.9 = (bf16[3,1,160,384]{3,2,1,0:T(8,128)(2,1)S(1)}, bf16[3,1,160,384]{3,2,1,0:T(8,128)(2,1)S(1)}, u32[]{:S(2)}, u32[]{:S(2)}) collective-permute-start(bf16[3,1,160,384]{3,2,1,0:T(8,128)(2,1)S(1)} %get-tuple-element.17), channel_id=1, source_target_pairs={{4,0},{8,4},{12,8},{5,1},{9,5},{13,9},{6,2},{10,6},{14,10},{7,3},{... | collective-permute-start | bytes 1105928 | tf_op jit(solution)/shard_map/ppermute | solution.py:26
  86.8 2.2 %slice-start = ((s8[7962624]{0:T(1024)(128)(4,1)}), s8[4194304]{0:T(1024)(128)(4,1)S(1)}, s32[]{:S(2)}) async-start(s8[7962624]{0:T(1024)(128)(4,1)} %bitcast.85), calls=%async_computation | async-start | bytes 8388608
  87.5 2.9 %slice-start.1 = ((s8[7962624]{0:T(1024)(128)(4,1)}), s8[3768320]{0:T(1024)(128)(4,1)S(1)}, s32[]{:S(2)}) async-start(s8[7962624]{0:T(1024)(128)(4,1)} %bitcast.85), calls=%async_computation.1 | async-start | bytes 7536640

commit v4 on v3

--- a/solution.py
+++ b/solution.py
@@ -28,20 +28,26 @@
     return x
 
 
-def strip_gather(x, axis):
+def strip_gather(x, axis, chunks):
     n = lax.axis_size(axis)
     if n == 1:
         return x
     m = x.shape[0]
     up_pairs = [(i, i + 1) for i in range(n - 1)]
     down_pairs = [(i + 1, i) for i in range(n - 1)]
-    ups, downs = [], []
-    up, down = x, x
-    for _ in range(n - 1):
-        up = lax.ppermute(up, axis, up_pairs)
-        down = lax.ppermute(down, axis, down_pairs)
-        ups.append(up)
-        downs.append(down)
+    size = m // chunks
+    ups = [[] for _ in range(n - 1)]
+    downs = [[] for _ in range(n - 1)]
+    for c in range(chunks):
+        piece = x[c * size : (c + 1) * size]
+        up, down = piece, piece
+        for k in range(n - 1):
+            up = lax.ppermute(up, axis, up_pairs)
+            down = lax.ppermute(down, axis, down_pairs)
+            ups[k].append(up)
+            downs[k].append(down)
+    ups = [jnp.concatenate(p, axis=0) for p in ups]
+    downs = [jnp.concatenate(p, axis=0) for p in downs]
     stacked = jnp.concatenate(ups[::-1] + [x] + downs, axis=0)
     me = lax.axis_index(axis)
     return lax.dynamic_slice_in_dim(stacked, (n - 1 - me) * m, n * m, axis=0)
@@ -107,7 +113,7 @@
     flat = frames.reshape(-1, width)
     count = flat.shape[0]
     scale = float(np.float32(1.0) / np.sqrt(np.float32(width)))
-    whole = strip_gather(flat, "strip")
+    whole = strip_gather(flat, "strip", 2 if count % 16 == 0 else 1)
     normed = rms_scale(flat, attn_gain).astype(jnp.bfloat16)
     normed_all = rms_scale(whole, attn_gain).astype(jnp.bfloat16)
     query = jnp.dot(normed, query_weight, preferred_element_type=jnp.float32).astype(jnp.bfloat16)

time: 98.7 us -> 104 us (1.054)
  starting transfers between devices: 27.6 us -> 44.5 us
  waiting for transfers between devices: 39 us -> 25.7 us
  local copies, waits for them, and re-layouts: 4.34 us -> 5.51 us
    ppermute x3 -> x6, waiting for transfers between devices: 13.1 us -> 0.02 us  [strip_gather(): up = lax.ppermute(up, axis, up_pairs)]
    ppermute x3 -> x6, starting transfers between devices: 10.6 us -> 21.8 us  [strip_gather(): up = lax.ppermute(up, axis, up_pairs)]
    ppermute x3 -> x6, starting transfers between devices: 7.12 us -> 12.8 us  [strip_gather(): down = lax.ppermute(down, axis, down_pairs)]
    slice x0 -> x1, local copies, waits for them, and re-layouts: none -> 1.11 us  [strip_gather(): piece = x[c * size:(c + 1) * size]]
    ppermute x3 -> x6, waiting for transfers between devices: 5.18 us -> 5.02 us  [strip_gather(): down = lax.ppermute(down, axis, down_pairs)]
    unnamed x24 -> x30, local copies, waits for them, and re-layouts: 2.23 us -> 2.28 us
  transfers between devices with their start and end apart: 10 -> 16, of which waited for: 8 -> 5; matrix products, arithmetic and copies ran while one was open for 4% -> 4% of each run, Pallas kernels for 0% -> 0%
where the time goes in v4:
time: 104 us; the launch traced here: 103 us
  starting transfers between devices  44.5 us (43%)
  waiting for transfers between devices  25.7 us (25%)
  matrix products  16.2 us (16%)
  Pallas kernels  6.66 us (6%)
  local copies, waits for them, and re-layouts  5.51 us (5%)
  other arithmetic  4.23 us (4%)
    ppermute x6, starting transfers between devices, strip_gather(): up = lax.ppermute(up, axis, up_pairs)  21.8 us
    ppermute x2, waiting for transfers between devices, passed_along(): return lax.ppermute(x, axis, pairs)  13.8 us
    ppermute x6, starting transfers between devices, strip_gather(): down = lax.ppermute(down, axis, down_pairs)  12.8 us
    dot_general x9, matrix products, shards(): jnp.dot(window, kernel[step_t, step_r], preferred_element_type=jnp.float32)  7.8 us
    pallas_call x1, Pallas kernels, attend(): pl.pallas_call(functools.partial(attention_kernel, scale), out_shape=jax....  6.66 us
    ppermute x6, waiting for transfers between devices, strip_gather(): down = lax.ppermute(down, axis, down_pairs)  5.02 us
    ppermute x2, starting transfers between devices, passed_along(): return lax.ppermute(x, axis, pairs)  3.84 us
    ppermute x1, waiting for transfers between devices, with_halo(): after = lax.ppermute(leading, axis, down)  3.48 us
  transfers between devices with their start and end apart: 16, of which 5 were waited for; matrix products, arithmetic and copies ran while one was open for 4% of the time, Pallas kernels for 0%

profile of v4, /device:TPU:10, one launch (start us, length us, event | category | flops | bytes accessed | tf_op | source)
XLA Modules:
  0.0 103.3 jit_solution(13002906056893888163)
XLA Ops:
  0.0 1.1 %fusion.40 = (bf16[240,384]{1,0:T(8,128)(2,1)S(1)}, bf16[240,384]{1,0:T(8,128)(2,1)S(1)}) fusion(bf16[480,384]{1,0:T(8,128)(2,1)} %bitcast.64), kind=kLoop, calls=%fused_computation.83 | loop fusion | bytes 737280 | tf_op jit(solution)/shard_map/slice | solution.py:42
  1.1 3.5 %collective-permute-start.3 = (bf16[240,384]{1,0:T(8,128)(2,1)S(1)}, bf16[240,384]{1,0:T(8,128)(2,1)S(1)}, u32[]{:S(2)}, u32[]{:S(2)}) collective-permute-start(bf16[240,384]{1,0:T(8,128)(2,1)S(1)} %get-tuple-element.18), channel_id=1, source_target_pairs={{0,4},{4,8},{8,12},{1,5},{5,9},{9,13},{2,6},{6,10},{10,14},{3,7},{... | collective-permute-start | bytes 552968 | tf_op jit(solution)/shard_map/ppermute | solution.py:45
  4.6 3.5 %collective-permute-start = (bf16[240,384]{1,0:T(8,128)(2,1)S(1)}, bf16[240,384]{1,0:T(8,128)(2,1)S(1)}, u32[]{:S(2)}, u32[]{:S(2)}) collective-permute-start(bf16[240,384]{1,0:T(8,128)(2,1)S(1)} %get-tuple-element.19), channel_id=1, source_target_pairs={{0,4},{4,8},{8,12},{1,5},{5,9},{9,13},{2,6},{6,10},{10,14},{3,7},{... | collective-permute-start | bytes 552968 | tf_op jit(solution)/shard_map/ppermute | solution.py:45
  8.1 2.4 %collective-permute-start.7 = (bf16[240,384]{1,0:T(8,128)(2,1)S(1)}, bf16[240,384]{1,0:T(8,128)(2,1)S(1)}, u32[]{:S(2)}, u32[]{:S(2)}) collective-permute-start(bf16[240,384]{1,0:T(8,128)(2,1)S(1)} %get-tuple-element.18), channel_id=1, source_target_pairs={{4,0},{8,4},{12,8},{5,1},{9,5},{13,9},{6,2},{10,6},{14,10},{7,3},{... | collective-permute-start | bytes 552968 | tf_op jit(solution)/shard_map/ppermute | solution.py:46
  10.5 1.9 %collective-permute-start.6 = (bf16[240,384]{1,0:T(8,128)(2,1)S(1)}, bf16[240,384]{1,0:T(8,128)(2,1)S(1)}, u32[]{:S(2)}, u32[]{:S(2)}) collective-permute-start(bf16[240,384]{1,0:T(8,128)(2,1)S(1)} %get-tuple-element.19), channel_id=1, source_target_pairs={{4,0},{8,4},{12,8},{5,1},{9,5},{13,9},{6,2},{10,6},{14,10},{7,3},{... | collective-permute-start | bytes 552968 | tf_op jit(solution)/shard_map/ppermute | solution.py:46
  12.4 1.2 %multiply_reduce_fusion.1 = f32[3,160]{1,0:T(4,128)S(1)} fusion(bf16[1,3,160,384]{3,2,1,0:T(8,128)(2,1)} %param.9), kind=kLoop, calls=%fused_computation.54 | loop fusion | flops 552480 | bytes 370560 | tf_op jit(solution)/shard_map/reduce_sum | solution.py:58
  13.6 3.9 %collective-permute-start.4 = (bf16[240,384]{1,0:T(8,128)(2,1)S(1)}, bf16[240,384]{1,0:T(8,128)(2,1)S(1)}, u32[]{:S(2)}, u32[]{:S(2)}) collective-permute-start(bf16[240,384]{1,0:T(8,128)(2,1)S(1)} %collective-permute-done.3), channel_id=1, source_target_pairs={{0,4},{4,8},{8,12},{1,5},{5,9},{9,13},{2,6},{6,10},{10,14},{3,7},{... | collective-permute-start | bytes 552968 | tf_op jit(solution)/shard_map/ppermute | solution.py:45
  17.5 3.5 %collective-permute-start.1 = (bf16[240,384]{1,0:T(8,128)(2,1)S(1)}, bf16[240,384]{1,0:T(8,128)(2,1)S(1)}, u32[]{:S(2)}, u32[]{:S(2)}) collective-permute-start(bf16[240,384]{1,0:T(8,128)(2,1)S(1)} %collective-permute-done), channel_id=1, source_target_pairs={{0,4},{4,8},{8,12},{1,5},{5,9},{9,13},{2,6},{6,10},{10,14},{3,7},{... | collective-permute-start | bytes 552968 | tf_op jit(solution)/shard_map/ppermute | solution.py:45
  21.0 0.1 rsqrt.28
  21.1 2.4 %collective-permute-start.9 = (bf16[240,384]{1,0:T(8,128)(2,1)S(1)}, bf16[240,384]{1,0:T(8,128)(2,1)S(1)}, u32[]{:S(2)}, u32[]{:S(2)}) collective-permute-start(bf16[240,384]{1,0:T(8,128)(2,1)S(1)} %collective-permute-done.7), channel_id=1, source_target_pairs={{4,0},{8,4},{12,8},{5,1},{9,5},{13,9},{6,2},{10,6},{14,10},{7,3},{... | collective-permute-start | bytes 552968 | tf_op jit(solution)/shard_map/ppermute | solution.py:46
  23.5 1.9 %collective-permute-start.8 = (bf16[240,384]{1,0:T(8,128)(2,1)S(1)}, bf16[240,384]{1,0:T(8,128)(2,1)S(1)}, u32[]{:S(2)}, u32[]{:S(2)}) collective-permute-start(bf16[240,384]{1,0:T(8,128)(2,1)S(1)} %collective-permute-done.6), channel_id=1, source_target_pairs={{4,0},{8,4},{12,8},{5,1},{9,5},{13,9},{6,2},{10,6},{14,10},{7,3},{... | collective-permute-start | bytes 552968 | tf_op jit(solution)/shard_map/ppermute | solution.py:46
  25.4 3.9 %collective-permute-start.5 = (bf16[240,384]{1,0:T(8,128)(2,1)S(1)}, bf16[240,384]{1,0:T(8,128)(2,1)S(1)}, u32[]{:S(2)}, u32[]{:S(2)}) collective-permute-start(bf16[240,384]{1,0:T(8,128)(2,1)S(1)} %collective-permute-done.4), channel_id=1, source_target_pairs={{0,4},{4,8},{8,12},{1,5},{5,9},{9,13},{2,6},{6,10},{10,14},{3,7},{... | collective-permute-start | bytes 552968 | tf_op jit(solution)/shard_map/ppermute | solution.py:45
  29.4 3.5 %collective-permute-start.2 = (bf16[240,384]{1,0:T(8,128)(2,1)S(1)}, bf16[240,384]{1,0:T(8,128)(2,1)S(1)}, u32[]{:S(2)}, u32[]{:S(2)}) collective-permute-start(bf16[240,384]{1,0:T(8,128)(2,1)S(1)} %collective-permute-done.1), channel_id=1, source_target_pairs={{0,4},{4,8},{8,12},{1,5},{5,9},{9,13},{2,6},{6,10},{10,14},{3,7},{... | collective-permute-start | bytes 552968 | tf_op jit(solution)/shard_map/ppermute | solution.py:45
  32.9 2.3 %convolution_convert_fusion.2.q_ref = bf16[480,384]{1,0:T(8,128)(2,1)} fusion(bf16[384,384]{1,0:T(8,128)(2,1)} %param.12, bf16[480,384]{1,0:T(8,128)(2,1)} %bitcast.65, f32[384]{0:T(512)} %param.11, f32[480]{0:T(512)S(1)} %rsqrt.28), kind=kOutput, calls=%fused_computation.31 | convolution fusion | flops 142479360 | bytes 1035648 | tf_op jit(solution)/shard_map/dot_general | solution.py:119
  35.2 2.4 %collective-permute-start.11 = (bf16[240,384]{1,0:T(8,128)(2,1)S(1)}, bf16[240,384]{1,0:T(8,128)(2,1)S(1)}, u32[]{:S(2)}, u32[]{:S(2)}) collective-permute-start(bf16[240,384]{1,0:T(8,128)(2,1)S(1)} %collective-permute-done.9), channel_id=1, source_target_pairs={{4,0},{8,4},{12,8},{5,1},{9,5},{13,9},{6,2},{10,6},{14,10},{7,3},{... | collective-permute-start | bytes 552968 | tf_op jit(solution)/shard_map/ppermute | solution.py:46
  37.5 1.9 %collective-permute-start.10 = (bf16[240,384]{1,0:T(8,128)(2,1)S(1)}, bf16[240,384]{1,0:T(8,128)(2,1)S(1)}, u32[]{:S(2)}, u32[]{:S(2)}) collective-permute-start(bf16[240,384]{1,0:T(8,128)(2,1)S(1)} %collective-permute-done.8), channel_id=1, source_target_pairs={{4,0},{8,4},{12,8},{5,1},{9,5},{13,9},{6,2},{10,6},{14,10},{7,3},{... | collective-permute-start | bytes 552968 | tf_op jit(solution)/shard_map/ppermute | solution.py:46
  40.0 5.0 %collective-permute-done.10 = bf16[240,384]{1,0:T(8,128)(2,1)S(1)} collective-permute-done((bf16[240,384]{1,0:T(8,128)(2,1)S(1)}, bf16[240,384]{1,0:T(8,128)(2,1)S(1)}, u32[]{:S(2)}, u32[]{:S(2)}) %collective-permute-start.10) | collective-permute-done | bytes 184352 | tf_op jit(solution)/shard_map/ppermute | solution.py:46
  45.1 0.4 fusion.1
  45.5 2.3 %convolution_convert_fusion.v_ref = bf16[1920,384]{1,0:T(8,128)(2,1)} fusion(bf16[384,384]{1,0:T(8,128)(2,1)S(1)} %copy-done, f32[384]{0:T(512)S(1)} %copy-done.6, f32[1920]{0:T(1024)S(1)} %add_rsqrt_fusion, bf16[3360,384]{1,0:T(8,128)(2,1)S(1)} %constant_dynamic-update-slice_fusion, s32[]{:T(128)S(6)} %select_n.15), kind=kOutput, calls=%fused_computation.9 | convolution fusion | flops 569917440 | bytes 3254276 | tf_op jit(solution)/shard_map/dot_general | solution.py:121
  47.7 2.3 %convolution_convert_fusion.1.k_ref = bf16[1920,384]{1,0:T(8,128)(2,1)} fusion(bf16[384,384]{1,0:T(8,128)(2,1)S(1)} %copy-done.5, f32[384]{0:T(512)S(1)} %copy-done.6, f32[1920]{0:T(1024)S(1)} %add_rsqrt_fusion, bf16[3360,384]{1,0:T(8,128)(2,1)S(1)} %constant_dynamic-update-slice_fusion, s32[]{:T(128)S(6)} %select_n.15), kind=kOutput, calls=%fused_computation.10 | convolution fusion | flops 569917440 | bytes 3254276 | tf_op jit(solution)/shard_map/dot_general | solution.py:120
  50.0 6.7 %shard_map.91 = bf16[480,384]{1,0:T(8,128)(2,1)} custom-call(bf16[480,384]{1,0:T(8,128)(2,1)} %convolution_convert_fusion.2.q_ref, bf16[1920,384]{1,0:T(8,128)(2,1)} %convolution_convert_fusion.1.k_ref, bf16[1920,384]{1,0:T(8,128)(2,1)} %convolution_convert_fusion.v_ref), custom_call_target="tpu_custom_call" | custom-call | flops 1415577600 | bytes 3686400 | tf_op jit(solution)/shard_map/pallas_call | solution.py:80
  56.7 1.5 %multiply_reduce_fusion = (f32[480]{0:T(512)S(1)}, f32[480,384]{1,0:T(8,128)S(1)}) fusion(bf16[480,384]{1,0:T(8,128)(2,1)} %shard_map.91, bf16[384,384]{1,0:T(8,128)(2,1)S(1)} %copy-done.3, bf16[480,384]{1,0:T(8,128)(2,1)S(1)} %bitcast.67), kind=kOutput, calls=%fused_computation.53 | convolution fusion | flops 142663200 | bytes 1771392 | tf_op jit(solution)/shard_map/dot_general | solution.py:124
  58.3 0.3 multiply_convert_fusion
  58.5 1.9 %collective-permute-start.12 = (bf16[3,160,384]{2,1,0:T(8,128)(2,1)S(1)}, bf16[3,160,384]{2,1,0:T(8,128)(2,1)S(1)}, u32[]{:S(2)}, u32[]{:S(2)}) collective-permute-start(bf16[3,160,384]{2,1,0:T(8,128)(2,1)S(1)} %bitcast.68), channel_id=1, source_target_pairs={{0,1},{1,2},{2,3},{4,5},{5,6},{6,7},{8,9},{9,10},{10,11},{12,13},{... | collective-permute-start | bytes 1105928 | tf_op jit(solution)/shard_map/ppermute | solution.py:15
  60.5 6.9 %collective-permute-done.12 = bf16[3,160,384]{2,1,0:T(8,128)(2,1)S(1)} collective-permute-done((bf16[3,160,384]{2,1,0:T(8,128)(2,1)S(1)}, bf16[3,160,384]{2,1,0:T(8,128)(2,1)S(1)}, u32[]{:S(2)}, u32[]{:S(2)}) %collective-permute-start.12) | collective-permute-done | bytes 368672 | tf_op jit(solution)/shard_map/ppermute | solution.py:15
  67.4 1.9 %collective-permute-start.13 = (bf16[3,160,384]{2,1,0:T(8,128)(2,1)S(1)}, bf16[3,160,384]{2,1,0:T(8,128)(2,1)S(1)}, u32[]{:S(2)}, u32[]{:S(2)}) collective-permute-start(bf16[3,160,384]{2,1,0:T(8,128)(2,1)S(1)} %bitcast_select_fusion), channel_id=1, source_target_pairs={{0,1},{1,2},{2,3},{4,5},{5,6},{6,7},{8,9},{9,10},{10,11},{12,13},{... | collective-permute-start | bytes 1105928 | tf_op jit(solution)/shard_map/ppermute | solution.py:15
  69.4 6.9 %collective-permute-done.13 = bf16[3,160,384]{2,1,0:T(8,128)(2,1)S(1)} collective-permute-done((bf16[3,160,384]{2,1,0:T(8,128)(2,1)S(1)}, bf16[3,160,384]{2,1,0:T(8,128)(2,1)S(1)}, u32[]{:S(2)}, u32[]{:S(2)}) %collective-permute-start.13) | collective-permute-done | bytes 368672 | tf_op jit(solution)/shard_map/ppermute | solution.py:15
  76.3 0.1 fusion.31
  76.3 0.1 pad_maximum_fusion.3
  76.4 3.5 %collective-permute-start.14 = (bf16[3,1,160,384]{3,2,1,0:T(8,128)(2,1)S(1)}, bf16[3,1,160,384]{3,2,1,0:T(8,128)(2,1)S(1)}, u32[]{:S(2)}, u32[]{:S(2)}) collective-permute-start(bf16[3,1,160,384]{3,2,1,0:T(8,128)(2,1)S(1)} %get-tuple-element.16), channel_id=1, source_target_pairs={{0,4},{4,8},{8,12},{1,5},{5,9},{9,13},{2,6},{6,10},{10,14},{3,7},{... | collective-permute-start | bytes 1105928 | tf_op jit(solution)/shard_map/ppermute | solution.py:25
  79.9 2.6 %collective-permute-start.15 = (bf16[3,1,160,384]{3,2,1,0:T(8,128)(2,1)S(1)}, bf16[3,1,160,384]{3,2,1,0:T(8,128)(2,1)S(1)}, u32[]{:S(2)}, u32[]{:S(2)}) collective-permute-start(bf16[3,1,160,384]{3,2,1,0:T(8,128)(2,1)S(1)} %get-tuple-element.17), channel_id=1, source_target_pairs={{4,0},{8,4},{12,8},{5,1},{9,5},{13,9},{6,2},{10,6},{14,10},{7,3},{... | collective-permute-start | bytes 1105928 | tf_op jit(solution)/shard_map/ppermute | solution.py:26
  82.5 3.3 %collective-permute-done.14 = bf16[3,1,160,384]{3,2,1,0:T(8,128)(2,1)S(1)} collective-permute-done((bf16[3,1,160,384]{3,2,1,0:T(8,128)(2,1)S(1)}, bf16[3,1,160,384]{3,2,1,0:T(8,128)(2,1)S(1)}, u32[]{:S(2)}, u32[]{:S(2)}) %collective-permute-start.14) | collective-permute-done | bytes 368672 | tf_op jit(solution)/shard_map/ppermute | solution.py:25
  85.8 3.5 %collective-permute-done.15 = bf16[3,1,160,384]{3,2,1,0:T(8,128)(2,1)S(1)} collective-permute-done((bf16[3,1,160,384]{3,2,1,0:T(8,128)(2,1)S(1)}, bf16[3,1,160,384]{3,2,1,0:T(8,128)(2,1)S(1)}, u32[]{:S(2)}, u32[]{:S(2)}) %collective-permute-start.15) | collective-permute-done | bytes 368672 | tf_op jit(solution)/shard_map/ppermute | solution.py:26
  89.3 1.5 %select_maximum_fusion = bf16[3,5,162,384]{3,2,1,0:T(8,128)(2,1)S(1)} fusion(bf16[3,1,160,384]{3,2,1,0:T(8,128)(2,1)S(1)} %collective-permute-done.15, bf16[3,1,160,384]{3,2,1,0:T(8,128)(2,1)S(1)} %collective-permute-done.14, bf16[1,3,160,384]{3,2,1,0:T(8,128)(2,1)S(1)} %bitcast.70, bf16[1,3,160,384]{3,2,1,0:T(8,128)(2,1)S(1)} %bitcast.73, ...), kind=kLoop, calls=%fused_computation.11 | loop fusion | flops 16796160 | bytes 3709440 | tf_op jit(solution)/shard_map/concatenate | solution.py:27
  90.9 1.0 fusion.39
  91.9 0.6 pad_maximum_fusion
  92.5 1.0 fusion.38
  93.6 0.5 slice-done
  94.1 1.3 %slice-done.1 = s8[3768320]{0:T(1024)(128)(4,1)S(1)} async-done(((s8[7962624]{0:T(1024)(128)(4,1)}), s8[3768320]{0:T(1024)(128)(4,1)S(1)}, s32[]{:S(2)}) %slice-start.1) | async-done | bytes 3768344
  95.4 0.8 fusion.20
  96.2 0.8 fusion.21
  96.9 0.8 fusion.22
  97.7 0.8 fusion.23
  98.5 0.8 fusion.24
  99.2 0.8 fusion.25
  100.0 0.8 fusion.26
  100.8 0.8 fusion.27
  101.5 1.7 %fusion.17 = bf16[480,384]{1,0:T(8,128)(2,1)} fusion(f32[480,384]{1,0:T(8,128)S(1)} %fusion.20, f32[480,384]{1,0:T(8,128)S(1)} %fusion.21, f32[480,384]{1,0:T(8,128)S(1)} %fusion.22, f32[480,384]{1,0:T(8,128)S(1)} %fusion.23, f32[480,384]{1,0:T(8,128)S(1)} %fusion.24, f32[480,384]{1,0:T(8,128)S(1)} %fusion.25, f32[480,384]{1,0:T(8,128)S(1)} %fusion.26, ...), kind=kOutput, calls=%fused_computation.28 | convolution fusion | flops 426516480 | bytes 8994816 | tf_op jit(solution)/shard_map/dot_general | solution.py:143
  (45 shorter events, 0.6 us)
Async XLA Ops:
  0.0 45.4 %copy-start = (bf16[384,384]{1,0:T(8,128)(2,1)S(1)}, bf16[384,384]{1,0:T(8,128)(2,1)}, u32[]{:S(2)}) copy-start(bf16[384,384]{1,0:T(8,128)(2,1)} %param.14) | copy-start | bytes 884740
  0.0 39.7 %copy-start.1 = (bf16[1,3,160,384]{3,2,1,0:T(8,128)(2,1)S(1)}, bf16[1,3,160,384]{3,2,1,0:T(8,128)(2,1)}, u32[]{:S(2)}) copy-start(bf16[1,3,160,384]{3,2,1,0:T(8,128)(2,1)} %param.9) | copy-start | bytes 1105924
  1.1 12.5 %collective-permute-start.3 = (bf16[240,384]{1,0:T(8,128)(2,1)S(1)}, bf16[240,384]{1,0:T(8,128)(2,1)S(1)}, u32[]{:S(2)}, u32[]{:S(2)}) collective-permute-start(bf16[240,384]{1,0:T(8,128)(2,1)S(1)} %get-tuple-element.18), channel_id=1, source_target_pairs={{0,4},{4,8},{8,12},{1,5},{5,9},{9,13},{2,6},{6,10},{10,14},{3,7},{... | collective-permute-start | bytes 552968 | tf_op jit(solution)/shard_map/ppermute | solution.py:45
  4.6 12.9 %collective-permute-start = (bf16[240,384]{1,0:T(8,128)(2,1)S(1)}, bf16[240,384]{1,0:T(8,128)(2,1)S(1)}, u32[]{:S(2)}, u32[]{:S(2)}) collective-permute-start(bf16[240,384]{1,0:T(8,128)(2,1)S(1)} %get-tuple-element.19), channel_id=1, source_target_pairs={{0,4},{4,8},{8,12},{1,5},{5,9},{9,13},{2,6},{6,10},{10,14},{3,7},{... | collective-permute-start | bytes 552968 | tf_op jit(solution)/shard_map/ppermute | solution.py:45
  8.1 13.0 %collective-permute-start.7 = (bf16[240,384]{1,0:T(8,128)(2,1)S(1)}, bf16[240,384]{1,0:T(8,128)(2,1)S(1)}, u32[]{:S(2)}, u32[]{:S(2)}) collective-permute-start(bf16[240,384]{1,0:T(8,128)(2,1)S(1)} %get-tuple-element.18), channel_id=1, source_target_pairs={{4,0},{8,4},{12,8},{5,1},{9,5},{13,9},{6,2},{10,6},{14,10},{7,3},{... | collective-permute-start | bytes 552968 | tf_op jit(solution)/shard_map/ppermute | solution.py:46
  10.5 13.0 %collective-permute-start.6 = (bf16[240,384]{1,0:T(8,128)(2,1)S(1)}, bf16[240,384]{1,0:T(8,128)(2,1)S(1)}, u32[]{:S(2)}, u32[]{:S(2)}) collective-permute-start(bf16[240,384]{1,0:T(8,128)(2,1)S(1)} %get-tuple-element.19), channel_id=1, source_target_pairs={{4,0},{8,4},{12,8},{5,1},{9,5},{13,9},{6,2},{10,6},{14,10},{7,3},{... | collective-permute-start | bytes 552968 | tf_op jit(solution)/shard_map/ppermute | solution.py:46
  13.6 11.8 %collective-permute-start.4 = (bf16[240,384]{1,0:T(8,128)(2,1)S(1)}, bf16[240,384]{1,0:T(8,128)(2,1)S(1)}, u32[]{:S(2)}, u32[]{:S(2)}) collective-permute-start(bf16[240,384]{1,0:T(8,128)(2,1)S(1)} %collective-permute-done.3), channel_id=1, source_target_pairs={{0,4},{4,8},{8,12},{1,5},{5,9},{9,13},{2,6},{6,10},{10,14},{3,7},{... | collective-permute-start | bytes 552968 | tf_op jit(solution)/shard_map/ppermute | solution.py:45
  17.5 11.8 %collective-permute-start.1 = (bf16[240,384]{1,0:T(8,128)(2,1)S(1)}, bf16[240,384]{1,0:T(8,128)(2,1)S(1)}, u32[]{:S(2)}, u32[]{:S(2)}) collective-permute-start(bf16[240,384]{1,0:T(8,128)(2,1)S(1)} %collective-permute-done), channel_id=1, source_target_pairs={{0,4},{4,8},{8,12},{1,5},{5,9},{9,13},{2,6},{6,10},{10,14},{3,7},{... | collective-permute-start | bytes 552968 | tf_op jit(solution)/shard_map/ppermute | solution.py:45
  21.1 14.0 %collective-permute-start.9 = (bf16[240,384]{1,0:T(8,128)(2,1)S(1)}, bf16[240,384]{1,0:T(8,128)(2,1)S(1)}, u32[]{:S(2)}, u32[]{:S(2)}) collective-permute-start(bf16[240,384]{1,0:T(8,128)(2,1)S(1)} %collective-permute-done.7), channel_id=1, source_target_pairs={{4,0},{8,4},{12,8},{5,1},{9,5},{13,9},{6,2},{10,6},{14,10},{7,3},{... | collective-permute-start | bytes 552968 | tf_op jit(solution)/shard_map/ppermute | solution.py:46
  23.5 14.0 %collective-permute-start.8 = (bf16[240,384]{1,0:T(8,128)(2,1)S(1)}, bf16[240,384]{1,0:T(8,128)(2,1)S(1)}, u32[]{:S(2)}, u32[]{:S(2)}) collective-permute-start(bf16[240,384]{1,0:T(8,128)(2,1)S(1)} %collective-permute-done.6), channel_id=1, source_target_pairs={{4,0},{8,4},{12,8},{5,1},{9,5},{13,9},{6,2},{10,6},{14,10},{7,3},{... | collective-permute-start | bytes 552968 | tf_op jit(solution)/shard_map/ppermute | solution.py:46
  25.4 14.1 %collective-permute-start.5 = (bf16[240,384]{1,0:T(8,128)(2,1)S(1)}, bf16[240,384]{1,0:T(8,128)(2,1)S(1)}, u32[]{:S(2)}, u32[]{:S(2)}) collective-permute-start(bf16[240,384]{1,0:T(8,128)(2,1)S(1)} %collective-permute-done.4), channel_id=1, source_target_pairs={{0,4},{4,8},{8,12},{1,5},{5,9},{9,13},{2,6},{6,10},{10,14},{3,7},{... | collective-permute-start | bytes 552968 | tf_op jit(solution)/shard_map/ppermute | solution.py:45
  29.4 10.1 %collective-permute-start.2 = (bf16[240,384]{1,0:T(8,128)(2,1)S(1)}, bf16[240,384]{1,0:T(8,128)(2,1)S(1)}, u32[]{:S(2)}, u32[]{:S(2)}) collective-permute-start(bf16[240,384]{1,0:T(8,128)(2,1)S(1)} %collective-permute-done.1), channel_id=1, source_target_pairs={{0,4},{4,8},{8,12},{1,5},{5,9},{9,13},{2,6},{6,10},{10,14},{3,7},{... | collective-permute-start | bytes 552968 | tf_op jit(solution)/shard_map/ppermute | solution.py:45
  35.2 9.8 %collective-permute-start.11 = (bf16[240,384]{1,0:T(8,128)(2,1)S(1)}, bf16[240,384]{1,0:T(8,128)(2,1)S(1)}, u32[]{:S(2)}, u32[]{:S(2)}) collective-permute-start(bf16[240,384]{1,0:T(8,128)(2,1)S(1)} %collective-permute-done.9), channel_id=1, source_target_pairs={{4,0},{8,4},{12,8},{5,1},{9,5},{13,9},{6,2},{10,6},{14,10},{7,3},{... | collective-permute-start | bytes 552968 | tf_op jit(solution)/shard_map/ppermute | solution.py:46
  37.5 7.4 %collective-permute-start.10 = (bf16[240,384]{1,0:T(8,128)(2,1)S(1)}, bf16[240,384]{1,0:T(8,128)(2,1)S(1)}, u32[]{:S(2)}, u32[]{:S(2)}) collective-permute-start(bf16[240,384]{1,0:T(8,128)(2,1)S(1)} %collective-permute-done.8), channel_id=1, source_target_pairs={{4,0},{8,4},{12,8},{5,1},{9,5},{13,9},{6,2},{10,6},{14,10},{7,3},{... | collective-permute-start | bytes 552968 | tf_op jit(solution)/shard_map/ppermute | solution.py:46
  39.6 5.8 %copy-start.6 = (f32[384]{0:T(512)S(1)}, f32[384]{0:T(512)}, u32[]{:S(2)}) copy-start(f32[384]{0:T(512)} %param.11) | copy-start | bytes 4612
  45.0 2.7 %copy-start.5 = (bf16[384,384]{1,0:T(8,128)(2,1)S(1)}, bf16[384,384]{1,0:T(8,128)(2,1)}, u32[]{:S(2)}) copy-start(bf16[384,384]{1,0:T(8,128)(2,1)} %param.13) | copy-start | bytes 884740
  50.0 6.7 %copy-start.3 = (bf16[384,384]{1,0:T(8,128)(2,1)S(1)}, bf16[384,384]{1,0:T(8,128)(2,1)}, u32[]{:S(2)}) copy-start(bf16[384,384]{1,0:T(8,128)(2,1)} %param.15) | copy-start | bytes 884740
  50.0 8.2 %copy-start.4 = (f32[384]{0:T(512)S(1)}, f32[384]{0:T(512)}, u32[]{:S(2)}) copy-start(f32[384]{0:T(512)} %param.16) | copy-start | bytes 4612
  56.7 10.7 %copy-start.2 = (bf16[2,3,160,384]{3,2,1,0:T(8,128)(2,1)S(1)}, bf16[2,3,160,384]{3,2,1,0:T(8,128)(2,1)}, u32[]{:S(2)}) copy-start(bf16[2,3,160,384]{3,2,1,0:T(8,128)(2,1)} %param.10) | copy-start | bytes 2211844
  58.5 8.8 %collective-permute-start.12 = (bf16[3,160,384]{2,1,0:T(8,128)(2,1)S(1)}, bf16[3,160,384]{2,1,0:T(8,128)(2,1)S(1)}, u32[]{:S(2)}, u32[]{:S(2)}) collective-permute-start(bf16[3,160,384]{2,1,0:T(8,128)(2,1)S(1)} %bitcast.68), channel_id=1, source_target_pairs={{0,1},{1,2},{2,3},{4,5},{5,6},{6,7},{8,9},{9,10},{10,11},{12,13},{... | collective-permute-start | bytes 1105928 | tf_op jit(solution)/shard_map/ppermute | solution.py:15
  67.4 8.8 %collective-permute-start.13 = (bf16[3,160,384]{2,1,0:T(8,128)(2,1)S(1)}, bf16[3,160,384]{2,1,0:T(8,128)(2,1)S(1)}, u32[]{:S(2)}, u32[]{:S(2)}) collective-permute-start(bf16[3,160,384]{2,1,0:T(8,128)(2,1)S(1)} %bitcast_select_fusion), channel_id=1, source_target_pairs={{0,1},{1,2},{2,3},{4,5},{5,6},{6,7},{8,9},{9,10},{10,11},{12,13},{... | collective-permute-start | bytes 1105928 | tf_op jit(solution)/shard_map/ppermute | solution.py:15
  76.4 9.4 %collective-permute-start.14 = (bf16[3,1,160,384]{3,2,1,0:T(8,128)(2,1)S(1)}, bf16[3,1,160,384]{3,2,1,0:T(8,128)(2,1)S(1)}, u32[]{:S(2)}, u32[]{:S(2)}) collective-permute-start(bf16[3,1,160,384]{3,2,1,0:T(8,128)(2,1)S(1)} %get-tuple-element.16), channel_id=1, source_target_pairs={{0,4},{4,8},{8,12},{1,5},{5,9},{9,13},{2,6},{6,10},{10,14},{3,7},{... | collective-permute-start | bytes 1105928 | tf_op jit(solution)/shard_map/ppermute | solution.py:25
  79.9 9.4 %collective-permute-start.15 = (bf16[3,1,160,384]{3,2,1,0:T(8,128)(2,1)S(1)}, bf16[3,1,160,384]{3,2,1,0:T(8,128)(2,1)S(1)}, u32[]{:S(2)}, u32[]{:S(2)}) collective-permute-start(bf16[3,1,160,384]{3,2,1,0:T(8,128)(2,1)S(1)} %get-tuple-element.17), channel_id=1, source_target_pairs={{4,0},{8,4},{12,8},{5,1},{9,5},{13,9},{6,2},{10,6},{14,10},{7,3},{... | collective-permute-start | bytes 1105928 | tf_op jit(solution)/shard_map/ppermute | solution.py:26
  91.9 2.2 %slice-start = ((s8[7962624]{0:T(1024)(128)(4,1)}), s8[4194304]{0:T(1024)(128)(4,1)S(1)}, s32[]{:S(2)}) async-start(s8[7962624]{0:T(1024)(128)(4,1)} %bitcast.84), calls=%async_computation | async-start | bytes 8388608
  92.5 2.9 %slice-start.1 = ((s8[7962624]{0:T(1024)(128)(4,1)}), s8[3768320]{0:T(1024)(128)(4,1)S(1)}, s32[]{:S(2)}) async-start(s8[7962624]{0:T(1024)(128)(4,1)} %bitcast.84), calls=%async_computation.1 | async-start | bytes 7536640

commit v5 on v3

--- a/solution.py
+++ b/solution.py
@@ -7,12 +7,6 @@
 from jax.experimental import pallas as pl
 from jax.experimental.pallas import tpu as pltpu
 from jax.sharding import PartitionSpec as P
-
-
-def passed_along(x, axis, by):
-    size = lax.axis_size(axis)
-    pairs = [(i, i + by) for i in range(size) if 0 <= i + by < size]
-    return lax.ppermute(x, axis, pairs)
 
 
 def with_halo(x, sides, width):
@@ -118,25 +112,47 @@
         flat.astype(jnp.float32) + jnp.dot(attended, out_weight, preferred_element_type=jnp.float32)
     ).astype(jnp.bfloat16)
     act = jax.nn.silu(rms_scale(resid, conv_gain)).astype(jnp.bfloat16).reshape(rows, cols, width)
+    kernel = conv_weight.reshape(3, 3, 3 * width, width)
+
+    def frame_conv(padded, step_t):
+        padded = jnp.pad(padded, ((0, 0), (1, 1), (0, 0)))
+        widened = jnp.concatenate(
+            [padded[:, 0:cols], padded[:, 1 : cols + 1], padded[:, 2 : cols + 2]], axis=-1
+        )
+        total = None
+        for step_r in range(3):
+            window = widened[step_r : step_r + rows].reshape(-1, 3 * width)
+            part = jnp.dot(window, kernel[step_t, step_r], preferred_element_type=jnp.float32)
+            total = part if total is None else total + part
+        return total
+
+    act_padded = with_halo(act, (("strip", 0),), 1)
+    nt = lax.axis_size("tm")
     frame_index = lax.axis_index("tm")
-    prior = passed_along(act, "tm", 1)
-    prior = jnp.where(frame_index == 0, cache_frames[1], prior)
-    older = passed_along(prior, "tm", 1)
-    older = jnp.where(frame_index == 0, cache_frames[0], older)
-    stacked = jnp.stack([older, prior, act])
-    padded = with_halo(stacked, (("strip", 1),), 1)
-    padded = jnp.pad(padded, ((0, 0), (0, 0), (1, 1), (0, 0)))
-    widened = jnp.concatenate(
-        [padded[:, :, 0:cols], padded[:, :, 1 : cols + 1], padded[:, :, 2 : cols + 2]], axis=-1
+    to_next = frame_conv(act_padded, 1).astype(jnp.bfloat16)
+    to_after = frame_conv(act_padded, 0).astype(jnp.bfloat16)
+    from_prior = lax.ppermute(to_next, "tm", [(i, i + 1) for i in range(nt - 1)])
+    from_older = lax.ppermute(to_after, "tm", [(i, i + 2) for i in range(nt - 2)])
+    own = frame_conv(act_padded, 2)
+
+    cache = lax.optimization_barrier((cache_frames, keys))[0]
+    cache_padded = with_halo(cache, (("strip", 1),), 1)
+    cache_part = lax.cond(
+        frame_index == 0,
+        lambda: frame_conv(cache_padded[1], 1) + frame_conv(cache_padded[0], 0),
+        lambda: lax.cond(
+            frame_index == 1,
+            lambda: frame_conv(cache_padded[1], 0),
+            lambda: jnp.zeros((count, width), jnp.float32),
+        ),
     )
-    kernel = conv_weight.reshape(3, 3, 3 * width, width)
-    result = resid.astype(jnp.float32)
-    for step_t in range(3):
-        for step_r in range(3):
-            window = widened[step_t, step_r : step_r + rows].reshape(-1, 3 * width)
-            result = result + jnp.dot(
-                window, kernel[step_t, step_r], preferred_element_type=jnp.float32
-            )
+    result = (
+        resid.astype(jnp.float32)
+        + own
+        + from_prior.astype(jnp.float32)
+        + from_older.astype(jnp.float32)
+        + cache_part
+    )
     return result.astype(jnp.bfloat16).reshape(1, rows, cols, width)
 
 

time: 98.7 us -> 110 us (1.11)
  the two profiles are of different devices: /device:TPU:10 before, /device:TPU:0 now
where the time goes in v5:
time: 110 us; the launch traced here: 109 us
  matrix products  42.2 us (38%)
  starting transfers between devices  35 us (32%)
  waiting for transfers between devices  19.7 us (18%)
  Pallas kernels  6.66 us (6%)
  other arithmetic  2.65 us (2%)
  local copies, waits for them, and re-layouts  2.46 us (2%)
    dot_general x15, matrix products, frame_conv(): jnp.dot(window, kernel[step_t, step_r], preferred_element_type=jnp.float32)  33.8 us
    ppermute x3, starting transfers between devices, strip_gather(): up = lax.ppermute(up, axis, up_pairs)  13.8 us
    ppermute x3, waiting for transfers between devices, strip_gather(): up = lax.ppermute(up, axis, up_pairs)  13.6 us
    ppermute x2, starting transfers between devices, with_halo(): before = lax.ppermute(last, axis, up)  8.63 us
    pallas_call x1, Pallas kernels, attend(): pl.pallas_call(functools.partial(attention_kernel, scale), out_shape=jax....  6.66 us
    ppermute x3, waiting for transfers between devices, strip_gather(): down = lax.ppermute(down, axis, down_pairs)  6.1 us
    ppermute x1, starting transfers between devices, shards(): lax.ppermute(to_after, 'tm', [(i, i + 2) for i in range(nt - 2)])  4.14 us
    ppermute x3, starting transfers between devices, strip_gather(): down = lax.ppermute(down, axis, down_pairs)  3.87 us
  transfers between devices with their start and end apart: 12, of which 4 were waited for; matrix products, arithmetic and copies ran while one was open for 34% of the time, Pallas kernels for 0%

profile of v5, /device:TPU:0, one launch (start us, length us, event | category | flops | bytes accessed | tf_op | source)
XLA Modules:
  0.0 109.2 jit_solution(16120182380534730902)
XLA Ops:
  0.0 5.1 %collective-permute-start = (bf16[480,384]{1,0:T(8,128)(2,1)}, bf16[480,384]{1,0:T(8,128)(2,1)S(1)}, u32[]{:S(2)}, u32[]{:S(2)}) collective-permute-start(bf16[480,384]{1,0:T(8,128)(2,1)} %bitcast.114), channel_id=1, source_target_pairs={{0,4},{4,8},{8,12},{1,5},{5,9},{9,13},{2,6},{6,10},{10,14},{3,7},{... | collective-permute-start | bytes 1105928 | tf_op jit(solution)/shard_map/ppermute | solution.py:35
  5.1 1.3 %collective-permute-start.3 = (bf16[480,384]{1,0:T(8,128)(2,1)}, bf16[480,384]{1,0:T(8,128)(2,1)S(1)}, u32[]{:S(2)}, u32[]{:S(2)}) collective-permute-start(bf16[480,384]{1,0:T(8,128)(2,1)} %bitcast.115), channel_id=1, source_target_pairs={{4,0},{8,4},{12,8},{5,1},{9,5},{13,9},{6,2},{10,6},{14,10},{7,3},{... | collective-permute-start | bytes 1105928 | tf_op jit(solution)/shard_map/ppermute | solution.py:36
  6.4 6.8 %collective-permute-done = bf16[480,384]{1,0:T(8,128)(2,1)S(1)} collective-permute-done((bf16[480,384]{1,0:T(8,128)(2,1)}, bf16[480,384]{1,0:T(8,128)(2,1)S(1)}, u32[]{:S(2)}, u32[]{:S(2)}) %collective-permute-start) | collective-permute-done | bytes 368672 | tf_op jit(solution)/shard_map/ppermute | solution.py:35
  13.2 4.3 %collective-permute-start.1 = (bf16[480,384]{1,0:T(8,128)(2,1)S(1)}, bf16[480,384]{1,0:T(8,128)(2,1)S(1)}, u32[]{:S(2)}, u32[]{:S(2)}) collective-permute-start(bf16[480,384]{1,0:T(8,128)(2,1)S(1)} %collective-permute-done), channel_id=1, source_target_pairs={{0,4},{4,8},{8,12},{1,5},{5,9},{9,13},{2,6},{6,10},{10,14},{3,7},{... | collective-permute-start | bytes 1105928 | tf_op jit(solution)/shard_map/ppermute | solution.py:35
  17.6 1.2 %multiply_reduce_fusion.1 = f32[3,160]{1,0:T(4,128)S(1)} fusion(bf16[1,3,160,384]{3,2,1,0:T(8,128)(2,1)} %param.13), kind=kLoop, calls=%fused_computation.91 | loop fusion | flops 552480 | bytes 370560 | tf_op jit(solution)/shard_map/reduce_sum | solution.py:46
  18.8 1.3 %collective-permute-start.4 = (bf16[480,384]{1,0:T(8,128)(2,1)S(1)}, bf16[480,384]{1,0:T(8,128)(2,1)S(1)}, u32[]{:S(2)}, u32[]{:S(2)}) collective-permute-start(bf16[480,384]{1,0:T(8,128)(2,1)S(1)} %collective-permute-done.3), channel_id=1, source_target_pairs={{4,0},{8,4},{12,8},{5,1},{9,5},{13,9},{6,2},{10,6},{14,10},{7,3},{... | collective-permute-start | bytes 1105928 | tf_op jit(solution)/shard_map/ppermute | solution.py:36
  20.1 4.4 %collective-permute-done.1 = bf16[480,384]{1,0:T(8,128)(2,1)S(1)} collective-permute-done((bf16[480,384]{1,0:T(8,128)(2,1)S(1)}, bf16[480,384]{1,0:T(8,128)(2,1)S(1)}, u32[]{:S(2)}, u32[]{:S(2)}) %collective-permute-start.1) | collective-permute-done | bytes 368672 | tf_op jit(solution)/shard_map/ppermute | solution.py:35
  24.5 4.4 %collective-permute-start.2 = (bf16[480,384]{1,0:T(8,128)(2,1)S(1)}, bf16[480,384]{1,0:T(8,128)(2,1)S(1)}, u32[]{:S(2)}, u32[]{:S(2)}) collective-permute-start(bf16[480,384]{1,0:T(8,128)(2,1)S(1)} %collective-permute-done.1), channel_id=1, source_target_pairs={{0,4},{4,8},{8,12},{1,5},{5,9},{9,13},{2,6},{6,10},{10,14},{3,7},{... | collective-permute-start | bytes 1105928 | tf_op jit(solution)/shard_map/ppermute | solution.py:35
  29.0 2.3 %convolution_convert_fusion.2.q_ref = bf16[480,384]{1,0:T(8,128)(2,1)} fusion(bf16[384,384]{1,0:T(8,128)(2,1)} %param.16, bf16[480,384]{1,0:T(8,128)(2,1)} %bitcast.116, f32[384]{0:T(512)} %param.15, f32[480]{0:T(512)S(1)} %rsqrt.28), kind=kOutput, calls=%fused_computation.67 | convolution fusion | flops 142479360 | bytes 1035648 | tf_op jit(solution)/shard_map/dot_general | solution.py:107
  31.3 1.3 %collective-permute-start.5 = (bf16[480,384]{1,0:T(8,128)(2,1)S(1)}, bf16[480,384]{1,0:T(8,128)(2,1)S(1)}, u32[]{:S(2)}, u32[]{:S(2)}) collective-permute-start(bf16[480,384]{1,0:T(8,128)(2,1)S(1)} %collective-permute-done.4), channel_id=1, source_target_pairs={{4,0},{8,4},{12,8},{5,1},{9,5},{13,9},{6,2},{10,6},{14,10},{7,3},{... | collective-permute-start | bytes 1105928 | tf_op jit(solution)/shard_map/ppermute | solution.py:36
  32.6 2.4 %collective-permute-done.2 = bf16[480,384]{1,0:T(8,128)(2,1)S(1)} collective-permute-done((bf16[480,384]{1,0:T(8,128)(2,1)S(1)}, bf16[480,384]{1,0:T(8,128)(2,1)S(1)}, u32[]{:S(2)}, u32[]{:S(2)}) %collective-permute-start.2) | collective-permute-done | bytes 368672 | tf_op jit(solution)/shard_map/ppermute | solution.py:35
  35.4 6.1 %collective-permute-done.5 = bf16[480,384]{1,0:T(8,128)(2,1)S(1)} collective-permute-done((bf16[480,384]{1,0:T(8,128)(2,1)S(1)}, bf16[480,384]{1,0:T(8,128)(2,1)S(1)}, u32[]{:S(2)}, u32[]{:S(2)}) %collective-permute-start.5) | collective-permute-done | bytes 368672 | tf_op jit(solution)/shard_map/ppermute | solution.py:36
  41.5 0.4 fusion.22
  42.0 2.3 %convolution_convert_fusion.1.k_ref = bf16[1920,384]{1,0:T(8,128)(2,1)} fusion(bf16[384,384]{1,0:T(8,128)(2,1)S(1)} %copy-done, f32[384]{0:T(512)S(1)} %copy-done.6, f32[1920]{0:T(1024)S(1)} %add_rsqrt_fusion, bf16[3360,384]{1,0:T(8,128)(2,1)S(1)} %constant_dynamic-update-slice_fusion, s32[]{:T(128)S(6)} %select_n.3), kind=kOutput, calls=%fused_computation.46 | convolution fusion | flops 569917440 | bytes 3254276 | tf_op jit(solution)/shard_map/dot_general | solution.py:108
  44.3 2.3 %convolution_convert_fusion.v_ref = bf16[1920,384]{1,0:T(8,128)(2,1)} fusion(bf16[384,384]{1,0:T(8,128)(2,1)S(1)} %copy-done.5, f32[384]{0:T(512)S(1)} %copy-done.6, f32[1920]{0:T(1024)S(1)} %add_rsqrt_fusion, bf16[3360,384]{1,0:T(8,128)(2,1)S(1)} %constant_dynamic-update-slice_fusion, s32[]{:T(128)S(6)} %select_n.3), kind=kOutput, calls=%fused_computation.45 | convolution fusion | flops 569917440 | bytes 3254276 | tf_op jit(solution)/shard_map/dot_general | solution.py:109
  46.5 6.7 %shard_map.91 = bf16[480,384]{1,0:T(8,128)(2,1)} custom-call(bf16[480,384]{1,0:T(8,128)(2,1)} %convolution_convert_fusion.2.q_ref, bf16[1920,384]{1,0:T(8,128)(2,1)} %convolution_convert_fusion.1.k_ref, bf16[1920,384]{1,0:T(8,128)(2,1)} %convolution_convert_fusion.v_ref), custom_call_target="tpu_custom_call" | custom-call | flops 1415577600 | bytes 3686400 | tf_op jit(solution)/shard_map/pallas_call | solution.py:68
  53.2 1.5 %multiply_reduce_fusion = (f32[480]{0:T(512)S(1)}, f32[480,384]{1,0:T(8,128)S(1)}) fusion(bf16[480,384]{1,0:T(8,128)(2,1)} %shard_map.91, bf16[384,384]{1,0:T(8,128)(2,1)S(1)} %copy-done.3, bf16[480,384]{1,0:T(8,128)(2,1)S(1)} %bitcast.118), kind=kOutput, calls=%fused_computation.90 | convolution fusion | flops 142663200 | bytes 1771392 | tf_op jit(solution)/shard_map/dot_general | solution.py:112
  54.8 0.3 multiply_convert_fusion
  55.1 3.4 %collective-permute-start.6 = (bf16[1,160,384]{2,1,0:T(8,128)(2,1)S(1)}, bf16[1,160,384]{2,1,0:T(8,128)(2,1)S(1)}, u32[]{:S(2)}, u32[]{:S(2)}) collective-permute-start(bf16[1,160,384]{2,1,0:T(8,128)(2,1)S(1)} %get-tuple-element.60), channel_id=1, source_target_pairs={{0,4},{4,8},{8,12},{1,5},{5,9},{9,13},{2,6},{6,10},{10,14},{3,7},{... | collective-permute-start | bytes 368648 | tf_op jit(solution)/shard_map/ppermute | solution.py:19
  58.5 1.3 %collective-permute-start.7 = (bf16[1,160,384]{2,1,0:T(8,128)(2,1)S(1)}, bf16[1,160,384]{2,1,0:T(8,128)(2,1)S(1)}, u32[]{:S(2)}, u32[]{:S(2)}) collective-permute-start(bf16[1,160,384]{2,1,0:T(8,128)(2,1)S(1)} %get-tuple-element.61), channel_id=1, source_target_pairs={{4,0},{8,4},{12,8},{5,1},{9,5},{13,9},{6,2},{10,6},{14,10},{7,3},{... | collective-permute-start | bytes 368648 | tf_op jit(solution)/shard_map/ppermute | solution.py:20
  59.9 1.3 %collective-permute-start.11 = (bf16[2,1,160,384]{3,2,1,0:T(8,128)(2,1)S(1)}, bf16[2,1,160,384]{3,2,1,0:T(8,128)(2,1)S(1)}, u32[]{:S(2)}, u32[]{:S(2)}) collective-permute-start(bf16[2,1,160,384]{3,2,1,0:T(8,128)(2,1)S(1)} %get-tuple-element.56), channel_id=1, source_target_pairs={{4,0},{8,4},{12,8},{5,1},{9,5},{13,9},{6,2},{10,6},{14,10},{7,3},{... | collective-permute-start | bytes 737288 | tf_op jit(solution)/shard_map/ppermute | solution.py:20
  61.2 5.2 %collective-permute-start.10 = (bf16[2,1,160,384]{3,2,1,0:T(8,128)(2,1)S(1)}, bf16[2,1,160,384]{3,2,1,0:T(8,128)(2,1)S(1)}, u32[]{:S(2)}, u32[]{:S(2)}) collective-permute-start(bf16[2,1,160,384]{3,2,1,0:T(8,128)(2,1)S(1)} %get-tuple-element.57), channel_id=1, source_target_pairs={{0,4},{4,8},{8,12},{1,5},{5,9},{9,13},{2,6},{6,10},{10,14},{3,7},{... | collective-permute-start | bytes 737288 | tf_op jit(solution)/shard_map/ppermute | solution.py:19
  66.6 0.2 fusion.63
  66.8 0.2 pad_maximum_fusion.3
  67.0 0.2 fusion.61
  67.2 1.9 %fusion.38 = f32[480,384]{1,0:T(8,128)S(1)} fusion(bf16[480,1152]{1,0:T(8,128)(2,1)S(1)} %bitcast.122, bf16[3,3,1152,384]{3,2,1,0:T(8,128)(2,1)} %bitcast.26), kind=kOutput, calls=%fused_computation.70 | convolution fusion | flops 424673280 | bytes 2727936 | tf_op jit(solution)/shard_map/dot_general | solution.py:125
  69.2 1.9 %fusion.40 = f32[480,384]{1,0:T(8,128)S(1)} fusion(bf16[480,1152]{1,0:T(8,128)(2,1)S(1)} %bitcast.123, bf16[3,3,1152,384]{3,2,1,0:T(8,128)(2,1)} %bitcast.26), kind=kOutput, calls=%fused_computation.75 | convolution fusion | flops 424673280 | bytes 2727936 | tf_op jit(solution)/shard_map/dot_general | solution.py:125
  71.1 2.8 %fusion.42 = f32[480,384]{1,0:T(8,128)} fusion(bf16[480,1152]{1,0:T(8,128)(2,1)S(1)} %bitcast.124, bf16[3,3,1152,384]{3,2,1,0:T(8,128)(2,1)} %bitcast.26), kind=kOutput, calls=%fused_computation.80 | convolution fusion | flops 424673280 | bytes 2727936 | tf_op jit(solution)/shard_map/dot_general | solution.py:125
  73.9 1.9 %fusion.39 = f32[480,384]{1,0:T(8,128)S(1)} fusion(bf16[480,1152]{1,0:T(8,128)(2,1)S(1)} %bitcast.119, bf16[3,3,1152,384]{3,2,1,0:T(8,128)(2,1)} %bitcast.26), kind=kOutput, calls=%fused_computation.72 | convolution fusion | flops 424673280 | bytes 2727936 | tf_op jit(solution)/shard_map/dot_general | solution.py:125
  75.9 1.9 %fusion.41 = f32[480,384]{1,0:T(8,128)S(1)} fusion(bf16[480,1152]{1,0:T(8,128)(2,1)S(1)} %bitcast.120, bf16[3,3,1152,384]{3,2,1,0:T(8,128)(2,1)} %bitcast.26), kind=kOutput, calls=%fused_computation.77 | convolution fusion | flops 424673280 | bytes 2727936 | tf_op jit(solution)/shard_map/dot_general | solution.py:125
  77.8 2.7 %fusion.35 = bf16[480,384]{1,0:T(8,128)(2,1)} fusion(f32[480,384]{1,0:T(8,128)S(1)} %fusion.38, f32[480,384]{1,0:T(8,128)S(1)} %fusion.39, bf16[480,1152]{1,0:T(8,128)(2,1)S(1)} %bitcast.103, bf16[3,3,1152,384]{3,2,1,0:T(8,128)(2,1)} %bitcast.26), kind=kOutput, calls=%fused_computation.64 | convolution fusion | flops 425226240 | bytes 3833856 | tf_op jit(solution)/shard_map/dot_general | solution.py:125
  80.5 4.1 %collective-permute-start.9 = (bf16[480,384]{1,0:T(8,128)(2,1)}, bf16[480,384]{1,0:T(8,128)(2,1)}, u32[]{:S(2)}, u32[]{:S(2)}) collective-permute-start(bf16[480,384]{1,0:T(8,128)(2,1)} %fusion.35), channel_id=1, source_target_pairs={{0,2},{1,3},{4,6},{5,7},{8,10},{9,11},{12,14},{13,15},{16,18},{17,... | collective-permute-start | bytes 1105928 | tf_op jit(solution)/shard_map/ppermute | solution.py:135
  84.6 2.7 %fusion.34 = bf16[480,384]{1,0:T(8,128)(2,1)} fusion(f32[480,384]{1,0:T(8,128)S(1)} %fusion.40, f32[480,384]{1,0:T(8,128)S(1)} %fusion.41, bf16[480,1152]{1,0:T(8,128)(2,1)S(1)} %bitcast.104, bf16[3,3,1152,384]{3,2,1,0:T(8,128)(2,1)} %bitcast.26), kind=kOutput, calls=%fused_computation.63 | convolution fusion | flops 425226240 | bytes 3833856 | tf_op jit(solution)/shard_map/dot_general | solution.py:125
  87.3 2.0 %collective-permute-start.8 = (bf16[480,384]{1,0:T(8,128)(2,1)}, bf16[480,384]{1,0:T(8,128)(2,1)}, u32[]{:S(2)}, u32[]{:S(2)}) collective-permute-start(bf16[480,384]{1,0:T(8,128)(2,1)} %fusion.34), channel_id=1, source_target_pairs={{0,1},{1,2},{2,3},{4,5},{5,6},{6,7},{8,9},{9,10},{10,11},{12,13},{... | collective-permute-start | bytes 1105928 | tf_op jit(solution)/shard_map/ppermute | solution.py:134
  89.3 2.8 %fusion.43 = f32[480,384]{1,0:T(8,128)} fusion(bf16[480,1152]{1,0:T(8,128)(2,1)S(1)} %bitcast.121, bf16[3,3,1152,384]{3,2,1,0:T(8,128)(2,1)} %bitcast.26), kind=kOutput, calls=%fused_computation.82 | convolution fusion | flops 424673280 | bytes 2727936 | tf_op jit(solution)/shard_map/dot_general | solution.py:125
  92.4 13.4 %conditional.2 = (f32[480,384]{1,0:T(8,128)S(1)}) conditional(s32[]{:T(128)} %convert_element_type.78, (s32[]{:T(128)}, bf16[2,5,160,384]{3,2,1,0:T(8,128)(2,1)S(1)}, bf16[3,3,1152,384]{3,2,1,0:T(8,128)(2,1)}) %tuple.19, (bf16[2,5,160,384]{3,2,1,0:T(8,128)(2,1)S(1)}, bf16[3,3,1152,384]{3,2,1,0:T(8,128)(2,1)}) %tuple.20), branch_computations={%region_3.6_spmd, %region_6.7_spmd} | conditional | flops 2560020480 | bytes 46841864 | solution.py:140
  92.5 0.3 pad_slice_fusion.3
  92.8 0.3 pad_slice_fusion.5
  93.1 0.4 pad_maximum_fusion.1
  93.5 0.3 fusion.60
  93.8 1.9 %fusion.14 = f32[480,384]{1,0:T(8,128)S(1)} fusion(bf16[480,1152]{1,0:T(8,128)(2,1)S(1)} %bitcast.126, bf16[3,3,1152,384]{3,2,1,0:T(8,128)(2,1)} %get-tuple-element.31), kind=kOutput, calls=%fused_computation.26 | convolution fusion | flops 424673280 | bytes 2727936 | tf_op jit(solution)/shard_map/cond/branch_1_fun/dot_general | solution.py:125
  95.7 2.0 %convolution_add_fusion.5 = f32[480,384]{1,0:T(8,128)S(1)} fusion(f32[480,384]{1,0:T(8,128)S(1)} %fusion.14, bf16[480,1152]{1,0:T(8,128)(2,1)S(1)} %bitcast.112, bf16[3,3,1152,384]{3,2,1,0:T(8,128)(2,1)} %get-tuple-element.31), kind=kOutput, calls=%fused_computation.19 | convolution fusion | flops 424857600 | bytes 3465216 | tf_op jit(solution)/shard_map/cond/branch_1_fun/dot_general | solution.py:125
  97.7 1.9 %convolution_add_fusion.4 = f32[480,384]{1,0:T(8,128)S(1)} fusion(f32[480,384]{1,0:T(8,128)S(1)} %convolution_add_fusion.5, bf16[480,1152]{1,0:T(8,128)(2,1)S(1)} %bitcast.110, bf16[3,3,1152,384]{3,2,1,0:T(8,128)(2,1)} %get-tuple-element.31), kind=kOutput, calls=%fused_computation.18 | convolution fusion | flops 424857600 | bytes 3465216 | tf_op jit(solution)/shard_map/cond/branch_1_fun/dot_general | solution.py:125
  99.6 0.3 fusion.59
  99.9 1.9 %fusion.10 = f32[480,384]{1,0:T(8,128)S(1)} fusion(bf16[480,1152]{1,0:T(8,128)(2,1)S(1)} %bitcast.127, bf16[3,3,1152,384]{3,2,1,0:T(8,128)(2,1)} %get-tuple-element.31), kind=kOutput, calls=%fused_computation.22 | convolution fusion | flops 424673280 | bytes 2727936 | tf_op jit(solution)/shard_map/cond/branch_1_fun/dot_general | solution.py:125
  101.8 1.9 %convolution_add_fusion.3 = f32[480,384]{1,0:T(8,128)S(1)} fusion(f32[480,384]{1,0:T(8,128)S(1)} %fusion.10, bf16[480,1152]{1,0:T(8,128)(2,1)S(1)} %bitcast.113, bf16[3,3,1152,384]{3,2,1,0:T(8,128)(2,1)} %get-tuple-element.31), kind=kOutput, calls=%fused_computation.17 | convolution fusion | flops 424857600 | bytes 3465216 | tf_op jit(solution)/shard_map/cond/branch_1_fun/dot_general | solution.py:125
  103.8 2.0 %fusion.7 = f32[480,384]{1,0:T(8,128)S(1)} fusion(f32[480,384]{1,0:T(8,128)S(1)} %convolution_add_fusion.4, f32[480,384]{1,0:T(8,128)S(1)} %convolution_add_fusion.3, bf16[480,1152]{1,0:T(8,128)(2,1)S(1)} %bitcast.108, bf16[3,3,1152,384]{3,2,1,0:T(8,128)(2,1)} %get-tuple-element.31), kind=kOutput, calls=%fused_computation.16 | convolution fusion | flops 425041920 | bytes 4202496 | tf_op jit(solution)/shard_map/cond/branch_1_fun/dot_general | solution.py:125
  105.8 3.5 %fusion.33 = bf16[480,384]{1,0:T(8,128)(2,1)} fusion(f32[480,384]{1,0:T(8,128)S(1)} %get-tuple-element.65, f32[480,384]{1,0:T(8,128)S(1)} %get-tuple-element.63, f32[480,384]{1,0:T(8,128)} %fusion.42, f32[480,384]{1,0:T(8,128)} %fusion.43, bf16[480,1152]{1,0:T(8,128)(2,1)S(1)} %bitcast.105, bf16[3,3,1152,384]{3,2,1,0:T(8,128)(2,1)} %bitcast.26, ...), kind=kOutput, calls=%fused_computation.62 | convolution fusion | flops 426332160 | bytes 6045696 | tf_op jit(solution)/shard_map/dot_general | solution.py:125
  (40 shorter events, 1.1 us)
Async XLA Ops:
  0.0 41.9 %copy-start = (bf16[384,384]{1,0:T(8,128)(2,1)S(1)}, bf16[384,384]{1,0:T(8,128)(2,1)}, u32[]{:S(2)}) copy-start(bf16[384,384]{1,0:T(8,128)(2,1)} %param.17) | copy-start | bytes 884740
  0.0 13.2 %collective-permute-start = (bf16[480,384]{1,0:T(8,128)(2,1)}, bf16[480,384]{1,0:T(8,128)(2,1)S(1)}, u32[]{:S(2)}, u32[]{:S(2)}) collective-permute-start(bf16[480,384]{1,0:T(8,128)(2,1)} %bitcast.114), channel_id=1, source_target_pairs={{0,4},{4,8},{8,12},{1,5},{5,9},{9,13},{2,6},{6,10},{10,14},{3,7},{... | collective-permute-start | bytes 1105928 | tf_op jit(solution)/shard_map/ppermute | solution.py:35
  5.1 13.7 %collective-permute-start.3 = (bf16[480,384]{1,0:T(8,128)(2,1)}, bf16[480,384]{1,0:T(8,128)(2,1)S(1)}, u32[]{:S(2)}, u32[]{:S(2)}) collective-permute-start(bf16[480,384]{1,0:T(8,128)(2,1)} %bitcast.115), channel_id=1, source_target_pairs={{4,0},{8,4},{12,8},{5,1},{9,5},{13,9},{6,2},{10,6},{14,10},{7,3},{... | collective-permute-start | bytes 1105928 | tf_op jit(solution)/shard_map/ppermute | solution.py:36
  13.2 11.2 %collective-permute-start.1 = (bf16[480,384]{1,0:T(8,128)(2,1)S(1)}, bf16[480,384]{1,0:T(8,128)(2,1)S(1)}, u32[]{:S(2)}, u32[]{:S(2)}) collective-permute-start(bf16[480,384]{1,0:T(8,128)(2,1)S(1)} %collective-permute-done), channel_id=1, source_target_pairs={{0,4},{4,8},{8,12},{1,5},{5,9},{9,13},{2,6},{6,10},{10,14},{3,7},{... | collective-permute-start | bytes 1105928 | tf_op jit(solution)/shard_map/ppermute | solution.py:35
  17.5 17.6 %copy-start.1 = (bf16[1,3,160,384]{3,2,1,0:T(8,128)(2,1)S(1)}, bf16[1,3,160,384]{3,2,1,0:T(8,128)(2,1)}, u32[]{:S(2)}) copy-start(bf16[1,3,160,384]{3,2,1,0:T(8,128)(2,1)} %param.13) | copy-start | bytes 1105924
  18.8 12.5 %collective-permute-start.4 = (bf16[480,384]{1,0:T(8,128)(2,1)S(1)}, bf16[480,384]{1,0:T(8,128)(2,1)S(1)}, u32[]{:S(2)}, u32[]{:S(2)}) collective-permute-start(bf16[480,384]{1,0:T(8,128)(2,1)S(1)} %collective-permute-done.3), channel_id=1, source_target_pairs={{4,0},{8,4},{12,8},{5,1},{9,5},{13,9},{6,2},{10,6},{14,10},{7,3},{... | collective-permute-start | bytes 1105928 | tf_op jit(solution)/shard_map/ppermute | solution.py:36
  24.5 10.5 %collective-permute-start.2 = (bf16[480,384]{1,0:T(8,128)(2,1)S(1)}, bf16[480,384]{1,0:T(8,128)(2,1)S(1)}, u32[]{:S(2)}, u32[]{:S(2)}) collective-permute-start(bf16[480,384]{1,0:T(8,128)(2,1)S(1)} %collective-permute-done.1), channel_id=1, source_target_pairs={{0,4},{4,8},{8,12},{1,5},{5,9},{9,13},{2,6},{6,10},{10,14},{3,7},{... | collective-permute-start | bytes 1105928 | tf_op jit(solution)/shard_map/ppermute | solution.py:35
  31.3 10.2 %collective-permute-start.5 = (bf16[480,384]{1,0:T(8,128)(2,1)S(1)}, bf16[480,384]{1,0:T(8,128)(2,1)S(1)}, u32[]{:S(2)}, u32[]{:S(2)}) collective-permute-start(bf16[480,384]{1,0:T(8,128)(2,1)S(1)} %collective-permute-done.4), channel_id=1, source_target_pairs={{4,0},{8,4},{12,8},{5,1},{9,5},{13,9},{6,2},{10,6},{14,10},{7,3},{... | collective-permute-start | bytes 1105928 | tf_op jit(solution)/shard_map/ppermute | solution.py:36
  35.2 6.7 %copy-start.6 = (f32[384]{0:T(512)S(1)}, f32[384]{0:T(512)}, u32[]{:S(2)}) copy-start(f32[384]{0:T(512)} %param.15) | copy-start | bytes 4612
  42.0 2.3 %copy-start.5 = (bf16[384,384]{1,0:T(8,128)(2,1)S(1)}, bf16[384,384]{1,0:T(8,128)(2,1)}, u32[]{:S(2)}) copy-start(bf16[384,384]{1,0:T(8,128)(2,1)} %param.18) | copy-start | bytes 884740
  46.5 6.7 %copy-start.3 = (bf16[384,384]{1,0:T(8,128)(2,1)S(1)}, bf16[384,384]{1,0:T(8,128)(2,1)}, u32[]{:S(2)}) copy-start(bf16[384,384]{1,0:T(8,128)(2,1)} %param.19) | copy-start | bytes 884740
  46.5 8.2 %copy-start.4 = (f32[384]{0:T(512)S(1)}, f32[384]{0:T(512)}, u32[]{:S(2)}) copy-start(f32[384]{0:T(512)} %param.20) | copy-start | bytes 4612
  53.2 6.6 %copy-start.2 = (bf16[2,3,160,384]{3,2,1,0:T(8,128)(2,1)S(1)}, bf16[2,3,160,384]{3,2,1,0:T(8,128)(2,1)}, u32[]{:S(2)}) copy-start(bf16[2,3,160,384]{3,2,1,0:T(8,128)(2,1)} %param.14) | copy-start | bytes 2211844
  55.1 11.3 %collective-permute-start.6 = (bf16[1,160,384]{2,1,0:T(8,128)(2,1)S(1)}, bf16[1,160,384]{2,1,0:T(8,128)(2,1)S(1)}, u32[]{:S(2)}, u32[]{:S(2)}) collective-permute-start(bf16[1,160,384]{2,1,0:T(8,128)(2,1)S(1)} %get-tuple-element.60), channel_id=1, source_target_pairs={{0,4},{4,8},{8,12},{1,5},{5,9},{9,13},{2,6},{6,10},{10,14},{3,7},{... | collective-permute-start | bytes 368648 | tf_op jit(solution)/shard_map/ppermute | solution.py:19
  58.5 7.9 %collective-permute-start.7 = (bf16[1,160,384]{2,1,0:T(8,128)(2,1)S(1)}, bf16[1,160,384]{2,1,0:T(8,128)(2,1)S(1)}, u32[]{:S(2)}, u32[]{:S(2)}) collective-permute-start(bf16[1,160,384]{2,1,0:T(8,128)(2,1)S(1)} %get-tuple-element.61), channel_id=1, source_target_pairs={{4,0},{8,4},{12,8},{5,1},{9,5},{13,9},{6,2},{10,6},{14,10},{7,3},{... | collective-permute-start | bytes 368648 | tf_op jit(solution)/shard_map/ppermute | solution.py:20
  59.9 32.5 %collective-permute-start.11 = (bf16[2,1,160,384]{3,2,1,0:T(8,128)(2,1)S(1)}, bf16[2,1,160,384]{3,2,1,0:T(8,128)(2,1)S(1)}, u32[]{:S(2)}, u32[]{:S(2)}) collective-permute-start(bf16[2,1,160,384]{3,2,1,0:T(8,128)(2,1)S(1)} %get-tuple-element.56), channel_id=1, source_target_pairs={{4,0},{8,4},{12,8},{5,1},{9,5},{13,9},{6,2},{10,6},{14,10},{7,3},{... | collective-permute-start | bytes 737288 | tf_op jit(solution)/shard_map/ppermute | solution.py:20
  61.2 31.0 %collective-permute-start.10 = (bf16[2,1,160,384]{3,2,1,0:T(8,128)(2,1)S(1)}, bf16[2,1,160,384]{3,2,1,0:T(8,128)(2,1)S(1)}, u32[]{:S(2)}, u32[]{:S(2)}) collective-permute-start(bf16[2,1,160,384]{3,2,1,0:T(8,128)(2,1)S(1)} %get-tuple-element.57), channel_id=1, source_target_pairs={{0,4},{4,8},{8,12},{1,5},{5,9},{9,13},{2,6},{6,10},{10,14},{3,7},{... | collective-permute-start | bytes 737288 | tf_op jit(solution)/shard_map/ppermute | solution.py:19
  80.5 25.3 %collective-permute-start.9 = (bf16[480,384]{1,0:T(8,128)(2,1)}, bf16[480,384]{1,0:T(8,128)(2,1)}, u32[]{:S(2)}, u32[]{:S(2)}) collective-permute-start(bf16[480,384]{1,0:T(8,128)(2,1)} %fusion.35), channel_id=1, source_target_pairs={{0,2},{1,3},{4,6},{5,7},{8,10},{9,11},{12,14},{13,15},{16,18},{17,... | collective-permute-start | bytes 1105928 | tf_op jit(solution)/shard_map/ppermute | solution.py:135
  87.3 18.5 %collective-permute-start.8 = (bf16[480,384]{1,0:T(8,128)(2,1)}, bf16[480,384]{1,0:T(8,128)(2,1)}, u32[]{:S(2)}, u32[]{:S(2)}) collective-permute-start(bf16[480,384]{1,0:T(8,128)(2,1)} %fusion.34), channel_id=1, source_target_pairs={{0,1},{1,2},{2,3},{4,5},{5,6},{6,7},{8,9},{9,10},{10,11},{12,13},{... | collective-permute-start | bytes 1105928 | tf_op jit(solution)/shard_map/ppermute | solution.py:134

commit v6 on v3

--- a/solution.py
+++ b/solution.py
@@ -120,9 +120,10 @@
     act = jax.nn.silu(rms_scale(resid, conv_gain)).astype(jnp.bfloat16).reshape(rows, cols, width)
     frame_index = lax.axis_index("tm")
     prior = passed_along(act, "tm", 1)
+    older = passed_along(act, "tm", 2)
     prior = jnp.where(frame_index == 0, cache_frames[1], prior)
-    older = passed_along(prior, "tm", 1)
     older = jnp.where(frame_index == 0, cache_frames[0], older)
+    older = jnp.where(frame_index == 1, cache_frames[1], older)
     stacked = jnp.stack([older, prior, act])
     padded = with_halo(stacked, (("strip", 1),), 1)
     padded = jnp.pad(padded, ((0, 0), (0, 0), (1, 1), (0, 0)))

time: 98.7 us -> 101 us (1.023)
  waiting for transfers between devices: 39 us -> 41.1 us
    ppermute x1, waiting for transfers between devices: 3.35 us -> 7 us  [with_halo(): before = lax.ppermute(last, axis, up)]
    ppermute x2, waiting for transfers between devices: 13.8 us -> 12 us  [passed_along(): return lax.ppermute(x, axis, pairs)]
where the time goes in v6:
time: 101 us; the launch traced here: 99.8 us
  waiting for transfers between devices  41.1 us (41%)
  starting transfers between devices  26.9 us (27%)
  matrix products  16.2 us (16%)
  Pallas kernels  6.66 us (7%)
  local copies, waits for them, and re-layouts  4.34 us (4%)
  other arithmetic  4.23 us (4%)
    ppermute x3, waiting for transfers between devices, strip_gather(): up = lax.ppermute(up, axis, up_pairs)  13.1 us
    ppermute x2, waiting for transfers between devices, passed_along(): return lax.ppermute(x, axis, pairs)  12 us
    ppermute x3, starting transfers between devices, strip_gather(): up = lax.ppermute(up, axis, up_pairs)  10.6 us
    dot_general x9, matrix products, shards(): jnp.dot(window, kernel[step_t, step_r], preferred_element_type=jnp.float32)  7.82 us
    ppermute x3, starting transfers between devices, strip_gather(): down = lax.ppermute(down, axis, down_pairs)  7.12 us
    ppermute x1, waiting for transfers between devices, with_halo(): before = lax.ppermute(last, axis, up)  7 us
    pallas_call x1, Pallas kernels, attend(): pl.pallas_call(functools.partial(attention_kernel, scale), out_shape=jax....  6.66 us
    ppermute x3, waiting for transfers between devices, strip_gather(): down = lax.ppermute(down, axis, down_pairs)  5.18 us
  transfers between devices with their start and end apart: 10, of which 8 were waited for; matrix products, arithmetic and copies ran while one was open for 4% of the time, Pallas kernels for 0%

profile of v6, /device:TPU:10, one launch (start us, length us, event | category | flops | bytes accessed | tf_op | source)
XLA Modules:
  0.0 99.8 jit_solution(4733306819143544478)
XLA Ops:
  0.0 3.6 %collective-permute-start = (bf16[480,384]{1,0:T(8,128)(2,1)}, bf16[480,384]{1,0:T(8,128)(2,1)S(1)}, u32[]{:S(2)}, u32[]{:S(2)}) collective-permute-start(bf16[480,384]{1,0:T(8,128)(2,1)} %bitcast.76), channel_id=1, source_target_pairs={{0,4},{4,8},{8,12},{1,5},{5,9},{9,13},{2,6},{6,10},{10,14},{3,7},{... | collective-permute-start | bytes 1105928 | tf_op jit(solution)/shard_map/ppermute | solution.py:41
  3.6 2.4 %collective-permute-start.3 = (bf16[480,384]{1,0:T(8,128)(2,1)}, bf16[480,384]{1,0:T(8,128)(2,1)S(1)}, u32[]{:S(2)}, u32[]{:S(2)}) collective-permute-start(bf16[480,384]{1,0:T(8,128)(2,1)} %bitcast.77), channel_id=1, source_target_pairs={{4,0},{8,4},{12,8},{5,1},{9,5},{13,9},{6,2},{10,6},{14,10},{7,3},{... | collective-permute-start | bytes 1105928 | tf_op jit(solution)/shard_map/ppermute | solution.py:42
  6.0 6.6 %collective-permute-done = bf16[480,384]{1,0:T(8,128)(2,1)S(1)} collective-permute-done((bf16[480,384]{1,0:T(8,128)(2,1)}, bf16[480,384]{1,0:T(8,128)(2,1)S(1)}, u32[]{:S(2)}, u32[]{:S(2)}) %collective-permute-start) | collective-permute-done | bytes 368672 | tf_op jit(solution)/shard_map/ppermute | solution.py:41
  12.6 3.5 %collective-permute-start.1 = (bf16[480,384]{1,0:T(8,128)(2,1)S(1)}, bf16[480,384]{1,0:T(8,128)(2,1)S(1)}, u32[]{:S(2)}, u32[]{:S(2)}) collective-permute-start(bf16[480,384]{1,0:T(8,128)(2,1)S(1)} %collective-permute-done), channel_id=1, source_target_pairs={{0,4},{4,8},{8,12},{1,5},{5,9},{9,13},{2,6},{6,10},{10,14},{3,7},{... | collective-permute-start | bytes 1105928 | tf_op jit(solution)/shard_map/ppermute | solution.py:41
  16.0 1.2 %multiply_reduce_fusion.1 = f32[3,160]{1,0:T(4,128)S(1)} fusion(bf16[1,3,160,384]{3,2,1,0:T(8,128)(2,1)} %param.9), kind=kLoop, calls=%fused_computation.54 | loop fusion | flops 552480 | bytes 370560 | tf_op jit(solution)/shard_map/reduce_sum | solution.py:52
  17.2 2.4 %collective-permute-start.4 = (bf16[480,384]{1,0:T(8,128)(2,1)S(1)}, bf16[480,384]{1,0:T(8,128)(2,1)S(1)}, u32[]{:S(2)}, u32[]{:S(2)}) collective-permute-start(bf16[480,384]{1,0:T(8,128)(2,1)S(1)} %collective-permute-done.3), channel_id=1, source_target_pairs={{4,0},{8,4},{12,8},{5,1},{9,5},{13,9},{6,2},{10,6},{14,10},{7,3},{... | collective-permute-start | bytes 1105928 | tf_op jit(solution)/shard_map/ppermute | solution.py:42
  19.6 4.3 %collective-permute-done.1 = bf16[480,384]{1,0:T(8,128)(2,1)S(1)} collective-permute-done((bf16[480,384]{1,0:T(8,128)(2,1)S(1)}, bf16[480,384]{1,0:T(8,128)(2,1)S(1)}, u32[]{:S(2)}, u32[]{:S(2)}) %collective-permute-start.1) | collective-permute-done | bytes 368672 | tf_op jit(solution)/shard_map/ppermute | solution.py:41
  23.9 3.5 %collective-permute-start.2 = (bf16[480,384]{1,0:T(8,128)(2,1)S(1)}, bf16[480,384]{1,0:T(8,128)(2,1)S(1)}, u32[]{:S(2)}, u32[]{:S(2)}) collective-permute-start(bf16[480,384]{1,0:T(8,128)(2,1)S(1)} %collective-permute-done.1), channel_id=1, source_target_pairs={{0,4},{4,8},{8,12},{1,5},{5,9},{9,13},{2,6},{6,10},{10,14},{3,7},{... | collective-permute-start | bytes 1105928 | tf_op jit(solution)/shard_map/ppermute | solution.py:41
  27.4 0.1 rsqrt.28
  27.5 2.3 %convolution_convert_fusion.2.q_ref = bf16[480,384]{1,0:T(8,128)(2,1)} fusion(bf16[384,384]{1,0:T(8,128)(2,1)} %param.12, bf16[480,384]{1,0:T(8,128)(2,1)} %bitcast.78, f32[384]{0:T(512)} %param.11, f32[480]{0:T(512)S(1)} %rsqrt.28), kind=kOutput, calls=%fused_computation.31 | convolution fusion | flops 142479360 | bytes 1035648 | tf_op jit(solution)/shard_map/dot_general | solution.py:113
  29.8 2.4 %collective-permute-start.5 = (bf16[480,384]{1,0:T(8,128)(2,1)S(1)}, bf16[480,384]{1,0:T(8,128)(2,1)S(1)}, u32[]{:S(2)}, u32[]{:S(2)}) collective-permute-start(bf16[480,384]{1,0:T(8,128)(2,1)S(1)} %collective-permute-done.4), channel_id=1, source_target_pairs={{4,0},{8,4},{12,8},{5,1},{9,5},{13,9},{6,2},{10,6},{14,10},{7,3},{... | collective-permute-start | bytes 1105928 | tf_op jit(solution)/shard_map/ppermute | solution.py:42
  32.1 2.3 %collective-permute-done.2 = bf16[480,384]{1,0:T(8,128)(2,1)S(1)} collective-permute-done((bf16[480,384]{1,0:T(8,128)(2,1)S(1)}, bf16[480,384]{1,0:T(8,128)(2,1)S(1)}, u32[]{:S(2)}, u32[]{:S(2)}) %collective-permute-start.2) | collective-permute-done | bytes 368672 | tf_op jit(solution)/shard_map/ppermute | solution.py:41
  34.5 0.1 constant_dynamic-update-slice_fusion.5
  34.5 0.1 constant_dynamic-update-slice_fusion.4
  34.6 0.1 constant_dynamic-update-slice_fusion.3
  34.7 0.1 constant_dynamic-update-slice_fusion.2
  34.8 5.2 %collective-permute-done.5 = bf16[480,384]{1,0:T(8,128)(2,1)S(1)} collective-permute-done((bf16[480,384]{1,0:T(8,128)(2,1)S(1)}, bf16[480,384]{1,0:T(8,128)(2,1)S(1)}, u32[]{:S(2)}, u32[]{:S(2)}) %collective-permute-start.5) | collective-permute-done | bytes 368672 | tf_op jit(solution)/shard_map/ppermute | solution.py:42
  40.1 0.4 fusion.1
  40.5 2.3 %convolution_convert_fusion.v_ref = bf16[1920,384]{1,0:T(8,128)(2,1)} fusion(bf16[384,384]{1,0:T(8,128)(2,1)S(1)} %copy-done, f32[384]{0:T(512)S(1)} %copy-done.6, f32[1920]{0:T(1024)S(1)} %add_rsqrt_fusion, bf16[3360,384]{1,0:T(8,128)(2,1)S(1)} %constant_dynamic-update-slice_fusion, s32[]{:T(128)S(6)} %select_n.21), kind=kOutput, calls=%fused_computation.9 | convolution fusion | flops 569917440 | bytes 3254276 | tf_op jit(solution)/shard_map/dot_general | solution.py:115
  42.7 2.3 %convolution_convert_fusion.1.k_ref = bf16[1920,384]{1,0:T(8,128)(2,1)} fusion(bf16[384,384]{1,0:T(8,128)(2,1)S(1)} %copy-done.5, f32[384]{0:T(512)S(1)} %copy-done.6, f32[1920]{0:T(1024)S(1)} %add_rsqrt_fusion, bf16[3360,384]{1,0:T(8,128)(2,1)S(1)} %constant_dynamic-update-slice_fusion, s32[]{:T(128)S(6)} %select_n.21), kind=kOutput, calls=%fused_computation.10 | convolution fusion | flops 569917440 | bytes 3254276 | tf_op jit(solution)/shard_map/dot_general | solution.py:114
  45.0 6.7 %shard_map.91 = bf16[480,384]{1,0:T(8,128)(2,1)} custom-call(bf16[480,384]{1,0:T(8,128)(2,1)} %convolution_convert_fusion.2.q_ref, bf16[1920,384]{1,0:T(8,128)(2,1)} %convolution_convert_fusion.1.k_ref, bf16[1920,384]{1,0:T(8,128)(2,1)} %convolution_convert_fusion.v_ref), custom_call_target="tpu_custom_call" | custom-call | flops 1415577600 | bytes 3686400 | tf_op jit(solution)/shard_map/pallas_call | solution.py:74
  51.7 1.5 %multiply_reduce_fusion = (f32[480]{0:T(512)S(1)}, f32[480,384]{1,0:T(8,128)S(1)}) fusion(bf16[480,384]{1,0:T(8,128)(2,1)} %shard_map.91, bf16[384,384]{1,0:T(8,128)(2,1)S(1)} %copy-done.3, bf16[480,384]{1,0:T(8,128)(2,1)S(1)} %bitcast.80), kind=kOutput, calls=%fused_computation.53 | convolution fusion | flops 142663200 | bytes 1771392 | tf_op jit(solution)/shard_map/dot_general | solution.py:118
  53.2 0.3 multiply_convert_fusion
  53.5 1.9 %collective-permute-start.7 = (bf16[3,160,384]{2,1,0:T(8,128)(2,1)S(1)}, bf16[3,160,384]{2,1,0:T(8,128)(2,1)S(1)}, u32[]{:S(2)}, u32[]{:S(2)}) collective-permute-start(bf16[3,160,384]{2,1,0:T(8,128)(2,1)S(1)} %bitcast.70), channel_id=1, source_target_pairs={{0,1},{1,2},{2,3},{4,5},{5,6},{6,7},{8,9},{9,10},{10,11},{12,13},{... | collective-permute-start | bytes 1105928 | tf_op jit(solution)/shard_map/ppermute | solution.py:15
  55.4 1.3 %collective-permute-start.6 = (bf16[3,160,384]{2,1,0:T(8,128)(2,1)S(1)}, bf16[3,160,384]{2,1,0:T(8,128)(2,1)S(1)}, u32[]{:S(2)}, u32[]{:S(2)}) collective-permute-start(bf16[3,160,384]{2,1,0:T(8,128)(2,1)S(1)} %bitcast.71), channel_id=1, source_target_pairs={{0,2},{1,3},{4,6},{5,7},{8,10},{9,11},{12,14},{13,15},{16,18},{17,... | collective-permute-start | bytes 1105928 | tf_op jit(solution)/shard_map/ppermute | solution.py:15
  56.7 7.0 %collective-permute-done.7 = bf16[3,160,384]{2,1,0:T(8,128)(2,1)S(1)} collective-permute-done((bf16[3,160,384]{2,1,0:T(8,128)(2,1)S(1)}, bf16[3,160,384]{2,1,0:T(8,128)(2,1)S(1)}, u32[]{:S(2)}, u32[]{:S(2)}) %collective-permute-start.7) | collective-permute-done | bytes 368672 | tf_op jit(solution)/shard_map/ppermute | solution.py:15
  63.8 5.0 %collective-permute-done.6 = bf16[3,160,384]{2,1,0:T(8,128)(2,1)S(1)} collective-permute-done((bf16[3,160,384]{2,1,0:T(8,128)(2,1)S(1)}, bf16[3,160,384]{2,1,0:T(8,128)(2,1)S(1)}, u32[]{:S(2)}, u32[]{:S(2)}) %collective-permute-start.6) | collective-permute-done | bytes 368672 | tf_op jit(solution)/shard_map/ppermute | solution.py:15
  68.8 0.1 fusion.32
  68.9 0.1 pad_maximum_fusion.3
  69.0 3.5 %collective-permute-start.8 = (bf16[3,1,160,384]{3,2,1,0:T(8,128)(2,1)S(1)}, bf16[3,1,160,384]{3,2,1,0:T(8,128)(2,1)S(1)}, u32[]{:S(2)}, u32[]{:S(2)}) collective-permute-start(bf16[3,1,160,384]{3,2,1,0:T(8,128)(2,1)S(1)} %get-tuple-element.16), channel_id=1, source_target_pairs={{0,4},{4,8},{8,12},{1,5},{5,9},{9,13},{2,6},{6,10},{10,14},{3,7},{... | collective-permute-start | bytes 1105928 | tf_op jit(solution)/shard_map/ppermute | solution.py:25
  72.5 2.5 %collective-permute-start.9 = (bf16[3,1,160,384]{3,2,1,0:T(8,128)(2,1)S(1)}, bf16[3,1,160,384]{3,2,1,0:T(8,128)(2,1)S(1)}, u32[]{:S(2)}, u32[]{:S(2)}) collective-permute-start(bf16[3,1,160,384]{3,2,1,0:T(8,128)(2,1)S(1)} %get-tuple-element.17), channel_id=1, source_target_pairs={{4,0},{8,4},{12,8},{5,1},{9,5},{13,9},{6,2},{10,6},{14,10},{7,3},{... | collective-permute-start | bytes 1105928 | tf_op jit(solution)/shard_map/ppermute | solution.py:26
  75.1 7.0 %collective-permute-done.8 = bf16[3,1,160,384]{3,2,1,0:T(8,128)(2,1)S(1)} collective-permute-done((bf16[3,1,160,384]{3,2,1,0:T(8,128)(2,1)S(1)}, bf16[3,1,160,384]{3,2,1,0:T(8,128)(2,1)S(1)}, u32[]{:S(2)}, u32[]{:S(2)}) %collective-permute-start.8) | collective-permute-done | bytes 368672 | tf_op jit(solution)/shard_map/ppermute | solution.py:25
  82.1 3.8 %collective-permute-done.9 = bf16[3,1,160,384]{3,2,1,0:T(8,128)(2,1)S(1)} collective-permute-done((bf16[3,1,160,384]{3,2,1,0:T(8,128)(2,1)S(1)}, bf16[3,1,160,384]{3,2,1,0:T(8,128)(2,1)S(1)}, u32[]{:S(2)}, u32[]{:S(2)}) %collective-permute-start.9) | collective-permute-done | bytes 368672 | tf_op jit(solution)/shard_map/ppermute | solution.py:26
  85.9 1.5 %select_maximum_fusion = bf16[3,5,162,384]{3,2,1,0:T(8,128)(2,1)S(1)} fusion(bf16[3,1,160,384]{3,2,1,0:T(8,128)(2,1)S(1)} %collective-permute-done.9, bf16[3,1,160,384]{3,2,1,0:T(8,128)(2,1)S(1)} %collective-permute-done.8, bf16[1,3,160,384]{3,2,1,0:T(8,128)(2,1)S(1)} %bitcast.73, bf16[1,3,160,384]{3,2,1,0:T(8,128)(2,1)S(1)} %get-tuple-element.19, ...), kind=kLoop, calls=%fused_computation.11 | loop fusion | flops 16796160 | bytes 3709440 | tf_op jit(solution)/shard_map/concatenate | solution.py:27
  87.4 1.0 fusion.41
  88.4 0.6 pad_maximum_fusion
  89.1 1.0 fusion.40
  90.1 0.5 slice-done
  90.6 1.3 %slice-done.1 = s8[3768320]{0:T(1024)(128)(4,1)S(1)} async-done(((s8[7962624]{0:T(1024)(128)(4,1)}), s8[3768320]{0:T(1024)(128)(4,1)S(1)}, s32[]{:S(2)}) %slice-start.1) | async-done | bytes 3768344
  91.9 0.8 fusion.20
  92.7 0.8 fusion.21
  93.4 0.8 fusion.22
  94.2 0.8 fusion.23
  95.0 0.8 fusion.24
  95.7 0.8 fusion.25
  96.5 0.8 fusion.26
  97.3 0.8 fusion.27
  98.0 1.8 %fusion.17 = bf16[480,384]{1,0:T(8,128)(2,1)} fusion(f32[480,384]{1,0:T(8,128)S(1)} %fusion.20, f32[480,384]{1,0:T(8,128)S(1)} %fusion.21, f32[480,384]{1,0:T(8,128)S(1)} %fusion.22, f32[480,384]{1,0:T(8,128)S(1)} %fusion.23, f32[480,384]{1,0:T(8,128)S(1)} %fusion.24, f32[480,384]{1,0:T(8,128)S(1)} %fusion.25, f32[480,384]{1,0:T(8,128)S(1)} %fusion.26, ...), kind=kOutput, calls=%fused_computation.28 | convolution fusion | flops 426516480 | bytes 8994816 | tf_op jit(solution)/shard_map/dot_general | solution.py:138
  (25 shorter events, 0.2 us)
Async XLA Ops:
  0.0 40.5 %copy-start = (bf16[384,384]{1,0:T(8,128)(2,1)S(1)}, bf16[384,384]{1,0:T(8,128)(2,1)}, u32[]{:S(2)}) copy-start(bf16[384,384]{1,0:T(8,128)(2,1)} %param.14) | copy-start | bytes 884740
  0.0 34.6 %copy-start.1 = (bf16[1,3,160,384]{3,2,1,0:T(8,128)(2,1)S(1)}, bf16[1,3,160,384]{3,2,1,0:T(8,128)(2,1)}, u32[]{:S(2)}) copy-start(bf16[1,3,160,384]{3,2,1,0:T(8,128)(2,1)} %param.9) | copy-start | bytes 1105924
  0.0 12.6 %collective-permute-start = (bf16[480,384]{1,0:T(8,128)(2,1)}, bf16[480,384]{1,0:T(8,128)(2,1)S(1)}, u32[]{:S(2)}, u32[]{:S(2)}) collective-permute-start(bf16[480,384]{1,0:T(8,128)(2,1)} %bitcast.76), channel_id=1, source_target_pairs={{0,4},{4,8},{8,12},{1,5},{5,9},{9,13},{2,6},{6,10},{10,14},{3,7},{... | collective-permute-start | bytes 1105928 | tf_op jit(solution)/shard_map/ppermute | solution.py:41
  3.6 13.6 %collective-permute-start.3 = (bf16[480,384]{1,0:T(8,128)(2,1)}, bf16[480,384]{1,0:T(8,128)(2,1)S(1)}, u32[]{:S(2)}, u32[]{:S(2)}) collective-permute-start(bf16[480,384]{1,0:T(8,128)(2,1)} %bitcast.77), channel_id=1, source_target_pairs={{4,0},{8,4},{12,8},{5,1},{9,5},{13,9},{6,2},{10,6},{14,10},{7,3},{... | collective-permute-start | bytes 1105928 | tf_op jit(solution)/shard_map/ppermute | solution.py:42
  12.6 11.4 %collective-permute-start.1 = (bf16[480,384]{1,0:T(8,128)(2,1)S(1)}, bf16[480,384]{1,0:T(8,128)(2,1)S(1)}, u32[]{:S(2)}, u32[]{:S(2)}) collective-permute-start(bf16[480,384]{1,0:T(8,128)(2,1)S(1)} %collective-permute-done), channel_id=1, source_target_pairs={{0,4},{4,8},{8,12},{1,5},{5,9},{9,13},{2,6},{6,10},{10,14},{3,7},{... | collective-permute-start | bytes 1105928 | tf_op jit(solution)/shard_map/ppermute | solution.py:41
  17.2 12.5 %collective-permute-start.4 = (bf16[480,384]{1,0:T(8,128)(2,1)S(1)}, bf16[480,384]{1,0:T(8,128)(2,1)S(1)}, u32[]{:S(2)}, u32[]{:S(2)}) collective-permute-start(bf16[480,384]{1,0:T(8,128)(2,1)S(1)} %collective-permute-done.3), channel_id=1, source_target_pairs={{4,0},{8,4},{12,8},{5,1},{9,5},{13,9},{6,2},{10,6},{14,10},{7,3},{... | collective-permute-start | bytes 1105928 | tf_op jit(solution)/shard_map/ppermute | solution.py:42
  23.9 10.5 %collective-permute-start.2 = (bf16[480,384]{1,0:T(8,128)(2,1)S(1)}, bf16[480,384]{1,0:T(8,128)(2,1)S(1)}, u32[]{:S(2)}, u32[]{:S(2)}) collective-permute-start(bf16[480,384]{1,0:T(8,128)(2,1)S(1)} %collective-permute-done.1), channel_id=1, source_target_pairs={{0,4},{4,8},{8,12},{1,5},{5,9},{9,13},{2,6},{6,10},{10,14},{3,7},{... | collective-permute-start | bytes 1105928 | tf_op jit(solution)/shard_map/ppermute | solution.py:41
  29.8 10.2 %collective-permute-start.5 = (bf16[480,384]{1,0:T(8,128)(2,1)S(1)}, bf16[480,384]{1,0:T(8,128)(2,1)S(1)}, u32[]{:S(2)}, u32[]{:S(2)}) collective-permute-start(bf16[480,384]{1,0:T(8,128)(2,1)S(1)} %collective-permute-done.4), channel_id=1, source_target_pairs={{4,0},{8,4},{12,8},{5,1},{9,5},{13,9},{6,2},{10,6},{14,10},{7,3},{... | collective-permute-start | bytes 1105928 | tf_op jit(solution)/shard_map/ppermute | solution.py:42
  34.5 5.9 %copy-start.6 = (f32[384]{0:T(512)S(1)}, f32[384]{0:T(512)}, u32[]{:S(2)}) copy-start(f32[384]{0:T(512)} %param.11) | copy-start | bytes 4612
  40.1 2.7 %copy-start.5 = (bf16[384,384]{1,0:T(8,128)(2,1)S(1)}, bf16[384,384]{1,0:T(8,128)(2,1)}, u32[]{:S(2)}) copy-start(bf16[384,384]{1,0:T(8,128)(2,1)} %param.13) | copy-start | bytes 884740
  45.0 6.7 %copy-start.3 = (bf16[384,384]{1,0:T(8,128)(2,1)S(1)}, bf16[384,384]{1,0:T(8,128)(2,1)}, u32[]{:S(2)}) copy-start(bf16[384,384]{1,0:T(8,128)(2,1)} %param.15) | copy-start | bytes 884740
  45.0 8.2 %copy-start.4 = (f32[384]{0:T(512)S(1)}, f32[384]{0:T(512)}, u32[]{:S(2)}) copy-start(f32[384]{0:T(512)} %param.16) | copy-start | bytes 4612
  51.7 17.1 %copy-start.2 = (bf16[2,3,160,384]{3,2,1,0:T(8,128)(2,1)S(1)}, bf16[2,3,160,384]{3,2,1,0:T(8,128)(2,1)}, u32[]{:S(2)}) copy-start(bf16[2,3,160,384]{3,2,1,0:T(8,128)(2,1)} %param.10) | copy-start | bytes 2211844
  53.5 10.3 %collective-permute-start.7 = (bf16[3,160,384]{2,1,0:T(8,128)(2,1)S(1)}, bf16[3,160,384]{2,1,0:T(8,128)(2,1)S(1)}, u32[]{:S(2)}, u32[]{:S(2)}) collective-permute-start(bf16[3,160,384]{2,1,0:T(8,128)(2,1)S(1)} %bitcast.70), channel_id=1, source_target_pairs={{0,1},{1,2},{2,3},{4,5},{5,6},{6,7},{8,9},{9,10},{10,11},{12,13},{... | collective-permute-start | bytes 1105928 | tf_op jit(solution)/shard_map/ppermute | solution.py:15
  55.4 13.4 %collective-permute-start.6 = (bf16[3,160,384]{2,1,0:T(8,128)(2,1)S(1)}, bf16[3,160,384]{2,1,0:T(8,128)(2,1)S(1)}, u32[]{:S(2)}, u32[]{:S(2)}) collective-permute-start(bf16[3,160,384]{2,1,0:T(8,128)(2,1)S(1)} %bitcast.71), channel_id=1, source_target_pairs={{0,2},{1,3},{4,6},{5,7},{8,10},{9,11},{12,14},{13,15},{16,18},{17,... | collective-permute-start | bytes 1105928 | tf_op jit(solution)/shard_map/ppermute | solution.py:15
  69.0 13.1 %collective-permute-start.8 = (bf16[3,1,160,384]{3,2,1,0:T(8,128)(2,1)S(1)}, bf16[3,1,160,384]{3,2,1,0:T(8,128)(2,1)S(1)}, u32[]{:S(2)}, u32[]{:S(2)}) collective-permute-start(bf16[3,1,160,384]{3,2,1,0:T(8,128)(2,1)S(1)} %get-tuple-element.16), channel_id=1, source_target_pairs={{0,4},{4,8},{8,12},{1,5},{5,9},{9,13},{2,6},{6,10},{10,14},{3,7},{... | collective-permute-start | bytes 1105928 | tf_op jit(solution)/shard_map/ppermute | solution.py:25
  72.5 13.3 %collective-permute-start.9 = (bf16[3,1,160,384]{3,2,1,0:T(8,128)(2,1)S(1)}, bf16[3,1,160,384]{3,2,1,0:T(8,128)(2,1)S(1)}, u32[]{:S(2)}, u32[]{:S(2)}) collective-permute-start(bf16[3,1,160,384]{3,2,1,0:T(8,128)(2,1)S(1)} %get-tuple-element.17), channel_id=1, source_target_pairs={{4,0},{8,4},{12,8},{5,1},{9,5},{13,9},{6,2},{10,6},{14,10},{7,3},{... | collective-permute-start | bytes 1105928 | tf_op jit(solution)/shard_map/ppermute | solution.py:26
  88.4 2.2 %slice-start = ((s8[7962624]{0:T(1024)(128)(4,1)}), s8[4194304]{0:T(1024)(128)(4,1)S(1)}, s32[]{:S(2)}) async-start(s8[7962624]{0:T(1024)(128)(4,1)} %bitcast.89), calls=%async_computation | async-start | bytes 8388608
  89.0 2.9 %slice-start.1 = ((s8[7962624]{0:T(1024)(128)(4,1)}), s8[3768320]{0:T(1024)(128)(4,1)S(1)}, s32[]{:S(2)}) async-start(s8[7962624]{0:T(1024)(128)(4,1)} %bitcast.89), calls=%async_computation.1 | async-start | bytes 7536640

commit v7 on v3

--- a/solution.py
+++ b/solution.py
@@ -107,7 +107,7 @@
     flat = frames.reshape(-1, width)
     count = flat.shape[0]
     scale = float(np.float32(1.0) / np.sqrt(np.float32(width)))
-    whole = strip_gather(flat, "strip")
+    whole = lax.all_gather(flat, "strip", axis=0, tiled=True)
     normed = rms_scale(flat, attn_gain).astype(jnp.bfloat16)
     normed_all = rms_scale(whole, attn_gain).astype(jnp.bfloat16)
     query = jnp.dot(normed, query_weight, preferred_element_type=jnp.float32).astype(jnp.bfloat16)

time: 98.7 us -> 113 us (1.14)
  starting transfers between devices: 27.6 us -> 9.88 us
  waiting for transfers between devices: 39 us -> 54.8 us
  between operations: 0.36 us -> 13.6 us
  matrix products: 16.2 us -> 17.6 us
  other arithmetic: 4.21 us -> 5.57 us
    all_gather x0 -> x1, waiting for transfers between devices: none -> 33.8 us  [shards(): whole = lax.all_gather(flat, 'strip', axis=0, tiled=True)]
    ppermute x6 -> x0, waiting for transfers between devices: 18.3 us -> none  [the longest x3 13.1 us: strip_gather(): up = lax.ppermute(up, axis, up_pairs)]
    ppermute x6 -> x0, starting transfers between devices: 17.7 us -> none  [the longest x3 10.6 us: strip_gather(): up = lax.ppermute(up, axis, up_pairs)]
    dot_general x1, matrix products: 2.27 us -> 3.74 us  [shards(): jnp.dot(normed_all, value_weight, preferred_element_type=jnp.float32)]
    reduce_sum x2, other arithmetic: 1.55 us -> 2.92 us  [rms_scale(): jnp.mean(wide * wide, axis=-1, keepdims=True) + 1e-06]
  transfers between devices with their start and end apart: 10 -> 5, of which waited for: 8 -> 5; matrix products, arithmetic and copies ran while one was open for 4% -> 3% of each run, Pallas kernels for 0% -> 0%
where the time goes in v7:
time: 113 us; the launch traced here: 112 us
  waiting for transfers between devices  54.8 us (48%)
  matrix products  17.6 us (16%)
  between operations  13.6 us (12%)
  starting transfers between devices  9.88 us (9%)
  Pallas kernels  6.69 us (6%)
  other arithmetic  5.57 us (5%)
  local copies, waits for them, and re-layouts  3.94 us (3%)
    all_gather x1, waiting for transfers between devices, shards(): whole = lax.all_gather(flat, 'strip', axis=0, tiled=True)  33.8 us
    ppermute x2, waiting for transfers between devices, passed_along(): return lax.ppermute(x, axis, pairs)  13.8 us
    dot_general x9, matrix products, shards(): jnp.dot(window, kernel[step_t, step_r], preferred_element_type=jnp.float32)  7.82 us
    pallas_call x1, Pallas kernels, attend(): pl.pallas_call(functools.partial(attention_kernel, scale), out_shape=jax....  6.69 us
    ppermute x2, starting transfers between devices, passed_along(): return lax.ppermute(x, axis, pairs)  3.84 us
    dot_general x1, matrix products, shards(): jnp.dot(normed_all, value_weight, preferred_element_type=jnp.float32)  3.74 us
    ppermute x1, waiting for transfers between devices, with_halo(): before = lax.ppermute(last, axis, up)  3.35 us
    ppermute x1, waiting for transfers between devices, with_halo(): after = lax.ppermute(leading, axis, down)  3.11 us
  transfers between devices with their start and end apart: 5, of which 5 were waited for; matrix products, arithmetic and copies ran while one was open for 3% of the time, Pallas kernels for 0%

profile of v7, /device:TPU:10, one launch (start us, length us, event | category | flops | bytes accessed | tf_op | source)
XLA Modules:
  0.0 112.2 jit_solution(7165917692814101840)
XLA Ops:
  6.5 0.0 copy-start
  6.5 0.0 all-gather.2.cloned.1.call-start
  6.5 0.7 all-gather.2.cloned.1.call-update
  7.3 1.2 %multiply_reduce_fusion.1 = f32[3,160]{1,0:T(4,128)S(1)} fusion(bf16[1,3,160,384]{3,2,1,0:T(8,128)(2,1)} %param.9), kind=kLoop, calls=%fused_computation.54 | loop fusion | flops 552480 | bytes 370560 | tf_op jit(solution)/shard_map/reduce_sum | solution.py:52
  8.5 0.1 rsqrt.28
  8.5 2.3 %convolution_convert_fusion.2.q_ref = bf16[480,384]{1,0:T(8,128)(2,1)} fusion(bf16[384,384]{1,0:T(8,128)(2,1)} %param.12, bf16[480,384]{1,0:T(8,128)(2,1)} %bitcast.73, f32[384]{0:T(512)} %param.11, f32[480]{0:T(512)S(1)} %rsqrt.28), kind=kOutput, calls=%fused_computation.31 | convolution fusion | flops 142479360 | bytes 1035648 | tf_op jit(solution)/shard_map/dot_general | solution.py:113
  10.8 33.8 %all-gather.2.cloned.1.call-done = bf16[1920,384]{1,0:T(8,128)(2,1)} async-done(((bf16[480,384]{1,0:T(8,128)(2,1)}), bf16[1920,384]{1,0:T(8,128)(2,1)}) %all-gather.2.cloned.1.call-update) | async-done | bytes 1474576 | tf_op jit(solution)/shard_map/all_gather | solution.py:110
  44.7 1.7 %fusion.1 = f32[1920]{0:T(1024)S(1)} fusion(bf16[1920,384]{1,0:T(8,128)(2,1)} %all-gather.2.cloned.1.call-done), kind=kLoop, calls=%fused_computation.6 | loop fusion | flops 2209920 | bytes 1482240 | tf_op jit(solution)/shard_map/reduce_sum | solution.py:52
  46.4 0.0 copy-done
  46.4 0.0 copy-done.7
  46.4 0.0 copy-start.2
  46.4 0.0 copy-start.6
  46.5 3.7 %convolution_convert_fusion.v_ref = bf16[1920,384]{1,0:T(8,128)(2,1)} fusion(bf16[384,384]{1,0:T(8,128)(2,1)S(1)} %copy-done, bf16[1920,384]{1,0:T(8,128)(2,1)} %all-gather.2.cloned.1.call-done, f32[384]{0:T(512)S(1)} %copy-done.7, f32[1920]{0:T(1024)S(1)} %add_rsqrt_fusion), kind=kOutput, calls=%fused_computation.9 | convolution fusion | flops 569917440 | bytes 3253248 | tf_op jit(solution)/shard_map/dot_general | solution.py:115
  50.2 0.0 copy-done.2
  50.2 0.0 copy-done.6
  50.2 2.3 %convolution_convert_fusion.1.k_ref = bf16[1920,384]{1,0:T(8,128)(2,1)} fusion(bf16[384,384]{1,0:T(8,128)(2,1)S(1)} %copy-done.6, bf16[1920,384]{1,0:T(8,128)(2,1)S(1)} %copy-done.2, f32[384]{0:T(512)S(1)} %copy-done.7, f32[1920]{0:T(1024)S(1)} %add_rsqrt_fusion), kind=kOutput, calls=%fused_computation.10 | convolution fusion | flops 569917440 | bytes 3253248 | tf_op jit(solution)/shard_map/dot_general | solution.py:114
  52.5 6.7 %shard_map.91 = bf16[480,384]{1,0:T(8,128)(2,1)} custom-call(bf16[480,384]{1,0:T(8,128)(2,1)} %convolution_convert_fusion.2.q_ref, bf16[1920,384]{1,0:T(8,128)(2,1)} %convolution_convert_fusion.1.k_ref, bf16[1920,384]{1,0:T(8,128)(2,1)} %convolution_convert_fusion.v_ref), custom_call_target="tpu_custom_call" | custom-call | flops 1415577600 | bytes 3686400 | tf_op jit(solution)/shard_map/pallas_call | solution.py:74
  59.2 0.0 copy-done.1
  59.2 0.0 copy-done.4
  59.2 1.5 %multiply_reduce_fusion = (f32[480]{0:T(512)S(1)}, f32[480,384]{1,0:T(8,128)S(1)}) fusion(bf16[480,384]{1,0:T(8,128)(2,1)} %shard_map.91, bf16[384,384]{1,0:T(8,128)(2,1)S(1)} %copy-done.4, bf16[480,384]{1,0:T(8,128)(2,1)S(1)} %bitcast.74), kind=kOutput, calls=%fused_computation.53 | convolution fusion | flops 142663200 | bytes 1771392 | tf_op jit(solution)/shard_map/dot_general | solution.py:118
  60.7 0.3 multiply_convert_fusion
  61.0 1.9 %collective-permute-start = (bf16[3,160,384]{2,1,0:T(8,128)(2,1)S(1)}, bf16[3,160,384]{2,1,0:T(8,128)(2,1)S(1)}, u32[]{:S(2)}, u32[]{:S(2)}) collective-permute-start(bf16[3,160,384]{2,1,0:T(8,128)(2,1)S(1)} %bitcast.64), channel_id=1, source_target_pairs={{0,1},{1,2},{2,3},{4,5},{5,6},{6,7},{8,9},{9,10},{10,11},{12,13},{... | collective-permute-start | bytes 1105928 | tf_op jit(solution)/shard_map/ppermute | solution.py:15
  63.0 6.9 %collective-permute-done = bf16[3,160,384]{2,1,0:T(8,128)(2,1)S(1)} collective-permute-done((bf16[3,160,384]{2,1,0:T(8,128)(2,1)S(1)}, bf16[3,160,384]{2,1,0:T(8,128)(2,1)S(1)}, u32[]{:S(2)}, u32[]{:S(2)}) %collective-permute-start) | collective-permute-done | bytes 368672 | tf_op jit(solution)/shard_map/ppermute | solution.py:15
  69.9 0.0 copy-done.3
  69.9 1.9 %collective-permute-start.1 = (bf16[3,160,384]{2,1,0:T(8,128)(2,1)S(1)}, bf16[3,160,384]{2,1,0:T(8,128)(2,1)S(1)}, u32[]{:S(2)}, u32[]{:S(2)}) collective-permute-start(bf16[3,160,384]{2,1,0:T(8,128)(2,1)S(1)} %bitcast_select_fusion), channel_id=1, source_target_pairs={{0,1},{1,2},{2,3},{4,5},{5,6},{6,7},{8,9},{9,10},{10,11},{12,13},{... | collective-permute-start | bytes 1105928 | tf_op jit(solution)/shard_map/ppermute | solution.py:15
  71.8 6.9 %collective-permute-done.1 = bf16[3,160,384]{2,1,0:T(8,128)(2,1)S(1)} collective-permute-done((bf16[3,160,384]{2,1,0:T(8,128)(2,1)S(1)}, bf16[3,160,384]{2,1,0:T(8,128)(2,1)S(1)}, u32[]{:S(2)}, u32[]{:S(2)}) %collective-permute-start.1) | collective-permute-done | bytes 368672 | tf_op jit(solution)/shard_map/ppermute | solution.py:15
  78.8 0.1 pad_maximum_fusion.3
  78.9 3.1 %collective-permute-start.2 = (bf16[3,1,160,384]{3,2,1,0:T(8,128)(2,1)S(1)}, bf16[3,1,160,384]{3,2,1,0:T(8,128)(2,1)S(1)}, u32[]{:S(2)}, u32[]{:S(2)}) collective-permute-start(bf16[3,1,160,384]{3,2,1,0:T(8,128)(2,1)S(1)} %get-tuple-element.16), channel_id=1, source_target_pairs={{0,4},{4,8},{8,12},{1,5},{5,9},{9,13},{2,6},{6,10},{10,14},{3,7},{... | collective-permute-start | bytes 1105928 | tf_op jit(solution)/shard_map/ppermute | solution.py:25
  82.0 2.9 %collective-permute-start.3 = (bf16[3,1,160,384]{3,2,1,0:T(8,128)(2,1)S(1)}, bf16[3,1,160,384]{3,2,1,0:T(8,128)(2,1)S(1)}, u32[]{:S(2)}, u32[]{:S(2)}) collective-permute-start(bf16[3,1,160,384]{3,2,1,0:T(8,128)(2,1)S(1)} %get-tuple-element.17), channel_id=1, source_target_pairs={{4,0},{8,4},{12,8},{5,1},{9,5},{13,9},{6,2},{10,6},{14,10},{7,3},{... | collective-permute-start | bytes 1105928 | tf_op jit(solution)/shard_map/ppermute | solution.py:26
  85.0 3.3 %collective-permute-done.2 = bf16[3,1,160,384]{3,2,1,0:T(8,128)(2,1)S(1)} collective-permute-done((bf16[3,1,160,384]{3,2,1,0:T(8,128)(2,1)S(1)}, bf16[3,1,160,384]{3,2,1,0:T(8,128)(2,1)S(1)}, u32[]{:S(2)}, u32[]{:S(2)}) %collective-permute-start.2) | collective-permute-done | bytes 368672 | tf_op jit(solution)/shard_map/ppermute | solution.py:25
  88.3 3.1 %collective-permute-done.3 = bf16[3,1,160,384]{3,2,1,0:T(8,128)(2,1)S(1)} collective-permute-done((bf16[3,1,160,384]{3,2,1,0:T(8,128)(2,1)S(1)}, bf16[3,1,160,384]{3,2,1,0:T(8,128)(2,1)S(1)}, u32[]{:S(2)}, u32[]{:S(2)}) %collective-permute-start.3) | collective-permute-done | bytes 368672 | tf_op jit(solution)/shard_map/ppermute | solution.py:26
  91.4 1.5 %select_maximum_fusion = bf16[3,5,162,384]{3,2,1,0:T(8,128)(2,1)S(1)} fusion(bf16[3,1,160,384]{3,2,1,0:T(8,128)(2,1)S(1)} %collective-permute-done.3, bf16[3,1,160,384]{3,2,1,0:T(8,128)(2,1)S(1)} %collective-permute-done.2, bf16[1,3,160,384]{3,2,1,0:T(8,128)(2,1)S(1)} %bitcast.66, bf16[1,3,160,384]{3,2,1,0:T(8,128)(2,1)S(1)} %bitcast.69, ...), kind=kLoop, calls=%fused_computation.11 | loop fusion | flops 16796160 | bytes 3709440 | tf_op jit(solution)/shard_map/concatenate | solution.py:27
  93.0 1.0 fusion.37
  94.0 0.0 slice-start
  94.0 0.6 pad_maximum_fusion
  94.6 0.0 slice-start.1
  94.6 1.0 fusion.36
  95.6 0.5 slice-done
  96.1 1.3 %slice-done.1 = s8[3768320]{0:T(1024)(128)(4,1)S(1)} async-done(((s8[7962624]{0:T(1024)(128)(4,1)}), s8[3768320]{0:T(1024)(128)(4,1)S(1)}, s32[]{:S(2)}) %slice-start.1) | async-done | bytes 3768344
  97.5 0.8 fusion.20
  98.2 0.8 fusion.21
  99.0 0.8 fusion.22
  99.8 0.8 fusion.23
  100.5 0.8 fusion.24
  101.3 0.8 fusion.25
  102.1 0.8 fusion.26
  102.8 0.8 fusion.27
  103.6 1.8 %fusion.17 = bf16[480,384]{1,0:T(8,128)(2,1)} fusion(f32[480,384]{1,0:T(8,128)S(1)} %fusion.20, f32[480,384]{1,0:T(8,128)S(1)} %fusion.21, f32[480,384]{1,0:T(8,128)S(1)} %fusion.22, f32[480,384]{1,0:T(8,128)S(1)} %fusion.23, f32[480,384]{1,0:T(8,128)S(1)} %fusion.24, f32[480,384]{1,0:T(8,128)S(1)} %fusion.25, f32[480,384]{1,0:T(8,128)S(1)} %fusion.26, ...), kind=kOutput, calls=%fused_computation.28 | convolution fusion | flops 426516480 | bytes 8994816 | tf_op jit(solution)/shard_map/dot_general | solution.py:137
  (12 shorter events, 0.1 us)
Async XLA Ops:
  6.5 39.9 %copy-start = (bf16[384,384]{1,0:T(8,128)(2,1)S(1)}, bf16[384,384]{1,0:T(8,128)(2,1)}, u32[]{:S(2)}) copy-start(bf16[384,384]{1,0:T(8,128)(2,1)} %param.14) | copy-start | bytes 884740
  6.5 39.9 %copy-start.7 = (f32[384]{0:T(512)S(1)}, f32[384]{0:T(512)}, u32[]{:S(2)}) copy-start(f32[384]{0:T(512)} %param.11) | copy-start | bytes 4612
  6.5 38.1 %all-gather.2.cloned.1.call-start = ((), (), s32[]{:S(2)}) async-start(), calls=%async_computation | async-start | bytes 1843200 | tf_op jit(solution)/shard_map/all_gather | solution.py:110
  46.4 3.8 %copy-start.2 = (bf16[1920,384]{1,0:T(8,128)(2,1)S(1)}, bf16[1920,384]{1,0:T(8,128)(2,1)}, u32[]{:S(2)}) copy-start(bf16[1920,384]{1,0:T(8,128)(2,1)} %all-gather.2.cloned.1.call-done) | copy-start | bytes 4423684
  46.4 3.8 %copy-start.6 = (bf16[384,384]{1,0:T(8,128)(2,1)S(1)}, bf16[384,384]{1,0:T(8,128)(2,1)}, u32[]{:S(2)}) copy-start(bf16[384,384]{1,0:T(8,128)(2,1)} %param.13) | copy-start | bytes 884740
  52.5 6.7 %copy-start.1 = (bf16[1,3,160,384]{3,2,1,0:T(8,128)(2,1)S(1)}, bf16[1,3,160,384]{3,2,1,0:T(8,128)(2,1)}, u32[]{:S(2)}) copy-start(bf16[1,3,160,384]{3,2,1,0:T(8,128)(2,1)} %param.9) | copy-start | bytes 1105924
  52.5 6.7 %copy-start.4 = (bf16[384,384]{1,0:T(8,128)(2,1)S(1)}, bf16[384,384]{1,0:T(8,128)(2,1)}, u32[]{:S(2)}) copy-start(bf16[384,384]{1,0:T(8,128)(2,1)} %param.15) | copy-start | bytes 884740
  52.5 8.3 %copy-start.5 = (f32[384]{0:T(512)S(1)}, f32[384]{0:T(512)}, u32[]{:S(2)}) copy-start(f32[384]{0:T(512)} %param.16) | copy-start | bytes 4612
  59.2 10.7 %copy-start.3 = (bf16[2,3,160,384]{3,2,1,0:T(8,128)(2,1)S(1)}, bf16[2,3,160,384]{3,2,1,0:T(8,128)(2,1)}, u32[]{:S(2)}) copy-start(bf16[2,3,160,384]{3,2,1,0:T(8,128)(2,1)} %param.10) | copy-start | bytes 2211844
  61.0 8.8 %collective-permute-start = (bf16[3,160,384]{2,1,0:T(8,128)(2,1)S(1)}, bf16[3,160,384]{2,1,0:T(8,128)(2,1)S(1)}, u32[]{:S(2)}, u32[]{:S(2)}) collective-permute-start(bf16[3,160,384]{2,1,0:T(8,128)(2,1)S(1)} %bitcast.64), channel_id=1, source_target_pairs={{0,1},{1,2},{2,3},{4,5},{5,6},{6,7},{8,9},{9,10},{10,11},{12,13},{... | collective-permute-start | bytes 1105928 | tf_op jit(solution)/shard_map/ppermute | solution.py:15
  69.9 8.8 %collective-permute-start.1 = (bf16[3,160,384]{2,1,0:T(8,128)(2,1)S(1)}, bf16[3,160,384]{2,1,0:T(8,128)(2,1)S(1)}, u32[]{:S(2)}, u32[]{:S(2)}) collective-permute-start(bf16[3,160,384]{2,1,0:T(8,128)(2,1)S(1)} %bitcast_select_fusion), channel_id=1, source_target_pairs={{0,1},{1,2},{2,3},{4,5},{5,6},{6,7},{8,9},{9,10},{10,11},{12,13},{... | collective-permute-start | bytes 1105928 | tf_op jit(solution)/shard_map/ppermute | solution.py:15
  78.9 9.4 %collective-permute-start.2 = (bf16[3,1,160,384]{3,2,1,0:T(8,128)(2,1)S(1)}, bf16[3,1,160,384]{3,2,1,0:T(8,128)(2,1)S(1)}, u32[]{:S(2)}, u32[]{:S(2)}) collective-permute-start(bf16[3,1,160,384]{3,2,1,0:T(8,128)(2,1)S(1)} %get-tuple-element.16), channel_id=1, source_target_pairs={{0,4},{4,8},{8,12},{1,5},{5,9},{9,13},{2,6},{6,10},{10,14},{3,7},{... | collective-permute-start | bytes 1105928 | tf_op jit(solution)/shard_map/ppermute | solution.py:25
  82.0 9.4 %collective-permute-start.3 = (bf16[3,1,160,384]{3,2,1,0:T(8,128)(2,1)S(1)}, bf16[3,1,160,384]{3,2,1,0:T(8,128)(2,1)S(1)}, u32[]{:S(2)}, u32[]{:S(2)}) collective-permute-start(bf16[3,1,160,384]{3,2,1,0:T(8,128)(2,1)S(1)} %get-tuple-element.17), channel_id=1, source_target_pairs={{4,0},{8,4},{12,8},{5,1},{9,5},{13,9},{6,2},{10,6},{14,10},{7,3},{... | collective-permute-start | bytes 1105928 | tf_op jit(solution)/shard_map/ppermute | solution.py:26
  94.0 2.2 %slice-start = ((s8[7962624]{0:T(1024)(128)(4,1)}), s8[4194304]{0:T(1024)(128)(4,1)S(1)}, s32[]{:S(2)}) async-start(s8[7962624]{0:T(1024)(128)(4,1)} %bitcast.83), calls=%async_computation.1 | async-start | bytes 8388608
  94.6 2.9 %slice-start.1 = ((s8[7962624]{0:T(1024)(128)(4,1)}), s8[3768320]{0:T(1024)(128)(4,1)S(1)}, s32[]{:S(2)}) async-start(s8[7962624]{0:T(1024)(128)(4,1)} %bitcast.83), calls=%async_computation.2 | async-start | bytes 7536640
Sparse Core Ops, SparseCore 0:
  8.9 35.7 all-gather.1

commit v8 on v3

--- a/solution.py
+++ b/solution.py
@@ -123,8 +123,9 @@
     prior = jnp.where(frame_index == 0, cache_frames[1], prior)
     older = passed_along(prior, "tm", 1)
     older = jnp.where(frame_index == 0, cache_frames[0], older)
-    stacked = jnp.stack([older, prior, act])
-    padded = with_halo(stacked, (("strip", 1),), 1)
+    own_padded = with_halo(act[None], (("strip", 1),), 1)
+    earlier = with_halo(jnp.stack([older, prior]), (("strip", 1),), 1)
+    padded = jnp.concatenate([earlier, own_padded], axis=0)
     padded = jnp.pad(padded, ((0, 0), (0, 0), (1, 1), (0, 0)))
     widened = jnp.concatenate(
         [padded[:, :, 0:cols], padded[:, :, 1 : cols + 1], padded[:, :, 2 : cols + 2]], axis=-1

time: 98.7 us -> 101 us (1.023)
  starting transfers between devices: 27.6 us -> 33.4 us
  waiting for transfers between devices: 39 us -> 36.3 us
    ppermute x1 -> x2, starting transfers between devices: 3.5 us -> 6.99 us  [with_halo(): before = lax.ppermute(last, axis, up)]
    ppermute x1 -> x2, waiting for transfers between devices: 3.35 us -> 0.73 us  [with_halo(): before = lax.ppermute(last, axis, up)]
    ppermute x1 -> x2, starting transfers between devices: 2.54 us -> 4.88 us  [with_halo(): after = lax.ppermute(leading, axis, down)]
    ppermute x1 -> x2, waiting for transfers between devices: 3.51 us -> 3.5 us  [with_halo(): after = lax.ppermute(leading, axis, down)]
  transfers between devices with their start and end apart: 10 -> 12, of which waited for: 8 -> 8; matrix products, arithmetic and copies ran while one was open for 4% -> 4% of each run, Pallas kernels for 0% -> 0%
where the time goes in v8:
time: 101 us
  waiting for transfers between devices  36.3 us (36%)
  starting transfers between devices  33.4 us (33%)
  matrix products  16.2 us (16%)
  Pallas kernels  6.64 us (7%)
  local copies, waits for them, and re-layouts  4.36 us (4%)
  other arithmetic  3.49 us (3%)
    ppermute x2, waiting for transfers between devices, passed_along(): return lax.ppermute(x, axis, pairs)  13.8 us
    ppermute x3, waiting for transfers between devices, strip_gather(): up = lax.ppermute(up, axis, up_pairs)  13.1 us
    ppermute x3, starting transfers between devices, strip_gather(): up = lax.ppermute(up, axis, up_pairs)  10.6 us
    dot_general x9, matrix products, shards(): jnp.dot(window, kernel[step_t, step_r], preferred_element_type=jnp.float32)  7.82 us
    ppermute x3, starting transfers between devices, strip_gather(): down = lax.ppermute(down, axis, down_pairs)  7.12 us
    ppermute x2, starting transfers between devices, with_halo(): before = lax.ppermute(last, axis, up)  6.99 us
    pallas_call x1, Pallas kernels, attend(): pl.pallas_call(functools.partial(attention_kernel, scale), out_shape=jax....  6.64 us
    ppermute x3, waiting for transfers between devices, strip_gather(): down = lax.ppermute(down, axis, down_pairs)  5.18 us
  transfers between devices with their start and end apart: 12, of which 8 were waited for; matrix products, arithmetic and copies ran while one was open for 4% of the time, Pallas kernels for 0%

profile of v8, /device:TPU:10, one launch (start us, length us, event | category | flops | bytes accessed | tf_op | source)
XLA Modules:
  0.0 100.8 jit_solution(15104220841419537828)
XLA Ops:
  0.0 3.6 %collective-permute-start = (bf16[480,384]{1,0:T(8,128)(2,1)}, bf16[480,384]{1,0:T(8,128)(2,1)S(1)}, u32[]{:S(2)}, u32[]{:S(2)}) collective-permute-start(bf16[480,384]{1,0:T(8,128)(2,1)} %bitcast.72), channel_id=1, source_target_pairs={{0,4},{4,8},{8,12},{1,5},{5,9},{9,13},{2,6},{6,10},{10,14},{3,7},{... | collective-permute-start | bytes 1105928 | tf_op jit(solution)/shard_map/ppermute | solution.py:41
  3.6 2.4 %collective-permute-start.3 = (bf16[480,384]{1,0:T(8,128)(2,1)}, bf16[480,384]{1,0:T(8,128)(2,1)S(1)}, u32[]{:S(2)}, u32[]{:S(2)}) collective-permute-start(bf16[480,384]{1,0:T(8,128)(2,1)} %bitcast.73), channel_id=1, source_target_pairs={{4,0},{8,4},{12,8},{5,1},{9,5},{13,9},{6,2},{10,6},{14,10},{7,3},{... | collective-permute-start | bytes 1105928 | tf_op jit(solution)/shard_map/ppermute | solution.py:42
  6.0 6.6 %collective-permute-done = bf16[480,384]{1,0:T(8,128)(2,1)S(1)} collective-permute-done((bf16[480,384]{1,0:T(8,128)(2,1)}, bf16[480,384]{1,0:T(8,128)(2,1)S(1)}, u32[]{:S(2)}, u32[]{:S(2)}) %collective-permute-start) | collective-permute-done | bytes 368672 | tf_op jit(solution)/shard_map/ppermute | solution.py:41
  12.6 3.5 %collective-permute-start.1 = (bf16[480,384]{1,0:T(8,128)(2,1)S(1)}, bf16[480,384]{1,0:T(8,128)(2,1)S(1)}, u32[]{:S(2)}, u32[]{:S(2)}) collective-permute-start(bf16[480,384]{1,0:T(8,128)(2,1)S(1)} %collective-permute-done), channel_id=1, source_target_pairs={{0,4},{4,8},{8,12},{1,5},{5,9},{9,13},{2,6},{6,10},{10,14},{3,7},{... | collective-permute-start | bytes 1105928 | tf_op jit(solution)/shard_map/ppermute | solution.py:41
  16.0 1.2 %multiply_reduce_fusion.1 = f32[3,160]{1,0:T(4,128)S(1)} fusion(bf16[1,3,160,384]{3,2,1,0:T(8,128)(2,1)} %param.9), kind=kLoop, calls=%fused_computation.55 | loop fusion | flops 552480 | bytes 370560 | tf_op jit(solution)/shard_map/reduce_sum | solution.py:52
  17.2 2.4 %collective-permute-start.4 = (bf16[480,384]{1,0:T(8,128)(2,1)S(1)}, bf16[480,384]{1,0:T(8,128)(2,1)S(1)}, u32[]{:S(2)}, u32[]{:S(2)}) collective-permute-start(bf16[480,384]{1,0:T(8,128)(2,1)S(1)} %collective-permute-done.3), channel_id=1, source_target_pairs={{4,0},{8,4},{12,8},{5,1},{9,5},{13,9},{6,2},{10,6},{14,10},{7,3},{... | collective-permute-start | bytes 1105928 | tf_op jit(solution)/shard_map/ppermute | solution.py:42
  19.6 4.3 %collective-permute-done.1 = bf16[480,384]{1,0:T(8,128)(2,1)S(1)} collective-permute-done((bf16[480,384]{1,0:T(8,128)(2,1)S(1)}, bf16[480,384]{1,0:T(8,128)(2,1)S(1)}, u32[]{:S(2)}, u32[]{:S(2)}) %collective-permute-start.1) | collective-permute-done | bytes 368672 | tf_op jit(solution)/shard_map/ppermute | solution.py:41
  23.9 3.5 %collective-permute-start.2 = (bf16[480,384]{1,0:T(8,128)(2,1)S(1)}, bf16[480,384]{1,0:T(8,128)(2,1)S(1)}, u32[]{:S(2)}, u32[]{:S(2)}) collective-permute-start(bf16[480,384]{1,0:T(8,128)(2,1)S(1)} %collective-permute-done.1), channel_id=1, source_target_pairs={{0,4},{4,8},{8,12},{1,5},{5,9},{9,13},{2,6},{6,10},{10,14},{3,7},{... | collective-permute-start | bytes 1105928 | tf_op jit(solution)/shard_map/ppermute | solution.py:41
  27.4 0.1 rsqrt.28
  27.5 2.3 %convolution_convert_fusion.2.q_ref = bf16[480,384]{1,0:T(8,128)(2,1)} fusion(bf16[384,384]{1,0:T(8,128)(2,1)} %param.12, bf16[480,384]{1,0:T(8,128)(2,1)} %bitcast.74, f32[384]{0:T(512)} %param.11, f32[480]{0:T(512)S(1)} %rsqrt.28), kind=kOutput, calls=%fused_computation.32 | convolution fusion | flops 142479360 | bytes 1035648 | tf_op jit(solution)/shard_map/dot_general | solution.py:113
  29.8 2.4 %collective-permute-start.5 = (bf16[480,384]{1,0:T(8,128)(2,1)S(1)}, bf16[480,384]{1,0:T(8,128)(2,1)S(1)}, u32[]{:S(2)}, u32[]{:S(2)}) collective-permute-start(bf16[480,384]{1,0:T(8,128)(2,1)S(1)} %collective-permute-done.4), channel_id=1, source_target_pairs={{4,0},{8,4},{12,8},{5,1},{9,5},{13,9},{6,2},{10,6},{14,10},{7,3},{... | collective-permute-start | bytes 1105928 | tf_op jit(solution)/shard_map/ppermute | solution.py:42
  32.1 2.3 %collective-permute-done.2 = bf16[480,384]{1,0:T(8,128)(2,1)S(1)} collective-permute-done((bf16[480,384]{1,0:T(8,128)(2,1)S(1)}, bf16[480,384]{1,0:T(8,128)(2,1)S(1)}, u32[]{:S(2)}, u32[]{:S(2)}) %collective-permute-start.2) | collective-permute-done | bytes 368672 | tf_op jit(solution)/shard_map/ppermute | solution.py:41
  34.5 0.1 constant_dynamic-update-slice_fusion.5
  34.5 0.1 constant_dynamic-update-slice_fusion.4
  34.6 0.1 constant_dynamic-update-slice_fusion.3
  34.7 0.1 constant_dynamic-update-slice_fusion.2
  34.8 5.2 %collective-permute-done.5 = bf16[480,384]{1,0:T(8,128)(2,1)S(1)} collective-permute-done((bf16[480,384]{1,0:T(8,128)(2,1)S(1)}, bf16[480,384]{1,0:T(8,128)(2,1)S(1)}, u32[]{:S(2)}, u32[]{:S(2)}) %collective-permute-start.5) | collective-permute-done | bytes 368672 | tf_op jit(solution)/shard_map/ppermute | solution.py:42
  40.1 0.4 fusion.1
  40.5 2.3 %convolution_convert_fusion.v_ref = bf16[1920,384]{1,0:T(8,128)(2,1)} fusion(bf16[384,384]{1,0:T(8,128)(2,1)S(1)} %copy-done, f32[384]{0:T(512)S(1)} %copy-done.6, f32[1920]{0:T(1024)S(1)} %add_rsqrt_fusion, bf16[3360,384]{1,0:T(8,128)(2,1)S(1)} %constant_dynamic-update-slice_fusion, s32[]{:T(128)S(6)} %select_n.15), kind=kOutput, calls=%fused_computation.9 | convolution fusion | flops 569917440 | bytes 3254276 | tf_op jit(solution)/shard_map/dot_general | solution.py:115
  42.8 2.3 %convolution_convert_fusion.1.k_ref = bf16[1920,384]{1,0:T(8,128)(2,1)} fusion(bf16[384,384]{1,0:T(8,128)(2,1)S(1)} %copy-done.5, f32[384]{0:T(512)S(1)} %copy-done.6, f32[1920]{0:T(1024)S(1)} %add_rsqrt_fusion, bf16[3360,384]{1,0:T(8,128)(2,1)S(1)} %constant_dynamic-update-slice_fusion, s32[]{:T(128)S(6)} %select_n.15), kind=kOutput, calls=%fused_computation.10 | convolution fusion | flops 569917440 | bytes 3254276 | tf_op jit(solution)/shard_map/dot_general | solution.py:114
  45.0 6.6 %shard_map.91 = bf16[480,384]{1,0:T(8,128)(2,1)} custom-call(bf16[480,384]{1,0:T(8,128)(2,1)} %convolution_convert_fusion.2.q_ref, bf16[1920,384]{1,0:T(8,128)(2,1)} %convolution_convert_fusion.1.k_ref, bf16[1920,384]{1,0:T(8,128)(2,1)} %convolution_convert_fusion.v_ref), custom_call_target="tpu_custom_call" | custom-call | flops 1415577600 | bytes 3686400 | tf_op jit(solution)/shard_map/pallas_call | solution.py:74
  51.7 1.5 %multiply_reduce_fusion = (f32[480]{0:T(512)S(1)}, f32[480,384]{1,0:T(8,128)S(1)}) fusion(bf16[480,384]{1,0:T(8,128)(2,1)} %shard_map.91, bf16[384,384]{1,0:T(8,128)(2,1)S(1)} %copy-done.3, bf16[480,384]{1,0:T(8,128)(2,1)S(1)} %bitcast.76), kind=kOutput, calls=%fused_computation.54 | convolution fusion | flops 142663200 | bytes 1771392 | tf_op jit(solution)/shard_map/dot_general | solution.py:118
  53.2 0.3 multiply_convert_fusion
  53.5 1.9 %collective-permute-start.6 = (bf16[3,160,384]{2,1,0:T(8,128)(2,1)S(1)}, bf16[3,160,384]{2,1,0:T(8,128)(2,1)S(1)}, u32[]{:S(2)}, u32[]{:S(2)}) collective-permute-start(bf16[3,160,384]{2,1,0:T(8,128)(2,1)S(1)} %bitcast.67), channel_id=1, source_target_pairs={{0,1},{1,2},{2,3},{4,5},{5,6},{6,7},{8,9},{9,10},{10,11},{12,13},{... | collective-permute-start | bytes 1105928 | tf_op jit(solution)/shard_map/ppermute | solution.py:15
  55.4 6.9 %collective-permute-done.6 = bf16[3,160,384]{2,1,0:T(8,128)(2,1)S(1)} collective-permute-done((bf16[3,160,384]{2,1,0:T(8,128)(2,1)S(1)}, bf16[3,160,384]{2,1,0:T(8,128)(2,1)S(1)}, u32[]{:S(2)}, u32[]{:S(2)}) %collective-permute-start.6) | collective-permute-done | bytes 368672 | tf_op jit(solution)/shard_map/ppermute | solution.py:15
  62.4 1.9 %collective-permute-start.7 = (bf16[3,160,384]{2,1,0:T(8,128)(2,1)S(1)}, bf16[3,160,384]{2,1,0:T(8,128)(2,1)S(1)}, u32[]{:S(2)}, u32[]{:S(2)}) collective-permute-start(bf16[3,160,384]{2,1,0:T(8,128)(2,1)S(1)} %bitcast_select_fusion), channel_id=1, source_target_pairs={{0,1},{1,2},{2,3},{4,5},{5,6},{6,7},{8,9},{9,10},{10,11},{12,13},{... | collective-permute-start | bytes 1105928 | tf_op jit(solution)/shard_map/ppermute | solution.py:15
  64.3 6.9 %collective-permute-done.7 = bf16[3,160,384]{2,1,0:T(8,128)(2,1)S(1)} collective-permute-done((bf16[3,160,384]{2,1,0:T(8,128)(2,1)S(1)}, bf16[3,160,384]{2,1,0:T(8,128)(2,1)S(1)}, u32[]{:S(2)}, u32[]{:S(2)}) %collective-permute-start.7) | collective-permute-done | bytes 368672 | tf_op jit(solution)/shard_map/ppermute | solution.py:15
  71.3 3.5 %collective-permute-start.8 = (bf16[2,1,160,384]{3,2,1,0:T(8,128)(2,1)S(1)}, bf16[2,1,160,384]{3,2,1,0:T(8,128)(2,1)S(1)}, u32[]{:S(2)}, u32[]{:S(2)}) collective-permute-start(bf16[2,1,160,384]{3,2,1,0:T(8,128)(2,1)S(1)} %get-tuple-element.16), channel_id=1, source_target_pairs={{0,4},{4,8},{8,12},{1,5},{5,9},{9,13},{2,6},{6,10},{10,14},{3,7},{... | collective-permute-start | bytes 737288 | tf_op jit(solution)/shard_map/ppermute | solution.py:25
  74.9 2.4 %collective-permute-start.9 = (bf16[2,1,160,384]{3,2,1,0:T(8,128)(2,1)S(1)}, bf16[2,1,160,384]{3,2,1,0:T(8,128)(2,1)S(1)}, u32[]{:S(2)}, u32[]{:S(2)}) collective-permute-start(bf16[2,1,160,384]{3,2,1,0:T(8,128)(2,1)S(1)} %get-tuple-element.17), channel_id=1, source_target_pairs={{4,0},{8,4},{12,8},{5,1},{9,5},{13,9},{6,2},{10,6},{14,10},{7,3},{... | collective-permute-start | bytes 737288 | tf_op jit(solution)/shard_map/ppermute | solution.py:26
  77.2 3.5 %collective-permute-start.10 = (bf16[1,1,160,384]{3,2,1,0:T(8,128)(2,1)S(1)}, bf16[1,1,160,384]{3,2,1,0:T(8,128)(2,1)S(1)}, u32[]{:S(2)}, u32[]{:S(2)}) collective-permute-start(bf16[1,1,160,384]{3,2,1,0:T(8,128)(2,1)S(1)} %get-tuple-element.18), channel_id=1, source_target_pairs={{0,4},{4,8},{8,12},{1,5},{5,9},{9,13},{2,6},{6,10},{10,14},{3,7},{... | collective-permute-start | bytes 368648 | tf_op jit(solution)/shard_map/ppermute | solution.py:25
  80.7 2.5 %collective-permute-start.11 = (bf16[1,1,160,384]{3,2,1,0:T(8,128)(2,1)S(1)}, bf16[1,1,160,384]{3,2,1,0:T(8,128)(2,1)S(1)}, u32[]{:S(2)}, u32[]{:S(2)}) collective-permute-start(bf16[1,1,160,384]{3,2,1,0:T(8,128)(2,1)S(1)} %get-tuple-element.19), channel_id=1, source_target_pairs={{4,0},{8,4},{12,8},{5,1},{9,5},{13,9},{6,2},{10,6},{14,10},{7,3},{... | collective-permute-start | bytes 368648 | tf_op jit(solution)/shard_map/ppermute | solution.py:26
  83.3 0.7 collective-permute-done.10
  84.0 3.5 %collective-permute-done.11 = bf16[1,1,160,384]{3,2,1,0:T(8,128)(2,1)S(1)} collective-permute-done((bf16[1,1,160,384]{3,2,1,0:T(8,128)(2,1)S(1)}, bf16[1,1,160,384]{3,2,1,0:T(8,128)(2,1)S(1)}, u32[]{:S(2)}, u32[]{:S(2)}) %collective-permute-start.11) | collective-permute-done | bytes 122912 | tf_op jit(solution)/shard_map/ppermute | solution.py:26
  87.5 0.9 fusion.4
  88.4 1.0 fusion.38
  89.4 0.6 pad_maximum_fusion
  90.0 1.0 fusion.37
  91.0 0.5 slice-done
  91.6 1.3 %slice-done.1 = s8[3768320]{0:T(1024)(128)(4,1)S(1)} async-done(((s8[7962624]{0:T(1024)(128)(4,1)}), s8[3768320]{0:T(1024)(128)(4,1)S(1)}, s32[]{:S(2)}) %slice-start.1) | async-done | bytes 3768344
  92.9 0.8 fusion.19
  93.6 0.8 fusion.20
  94.4 0.8 fusion.21
  95.2 0.8 fusion.22
  95.9 0.8 fusion.23
  96.7 0.8 fusion.24
  97.5 0.8 fusion.25
  98.2 0.8 fusion.26
  99.0 1.8 %fusion.16 = bf16[480,384]{1,0:T(8,128)(2,1)} fusion(f32[480,384]{1,0:T(8,128)S(1)} %fusion.19, f32[480,384]{1,0:T(8,128)S(1)} %fusion.20, f32[480,384]{1,0:T(8,128)S(1)} %fusion.21, f32[480,384]{1,0:T(8,128)S(1)} %fusion.22, f32[480,384]{1,0:T(8,128)S(1)} %fusion.23, f32[480,384]{1,0:T(8,128)S(1)} %fusion.24, f32[480,384]{1,0:T(8,128)S(1)} %fusion.25, ...), kind=kOutput, calls=%fused_computation.29 | convolution fusion | flops 426516480 | bytes 8994816 | tf_op jit(solution)/shard_map/dot_general | solution.py:138
  (31 shorter events, 0.4 us)
Async XLA Ops:
  0.0 40.5 %copy-start = (bf16[384,384]{1,0:T(8,128)(2,1)S(1)}, bf16[384,384]{1,0:T(8,128)(2,1)}, u32[]{:S(2)}) copy-start(bf16[384,384]{1,0:T(8,128)(2,1)} %param.14) | copy-start | bytes 884740
  0.0 34.6 %copy-start.1 = (bf16[1,3,160,384]{3,2,1,0:T(8,128)(2,1)S(1)}, bf16[1,3,160,384]{3,2,1,0:T(8,128)(2,1)}, u32[]{:S(2)}) copy-start(bf16[1,3,160,384]{3,2,1,0:T(8,128)(2,1)} %param.9) | copy-start | bytes 1105924
  0.0 12.6 %collective-permute-start = (bf16[480,384]{1,0:T(8,128)(2,1)}, bf16[480,384]{1,0:T(8,128)(2,1)S(1)}, u32[]{:S(2)}, u32[]{:S(2)}) collective-permute-start(bf16[480,384]{1,0:T(8,128)(2,1)} %bitcast.72), channel_id=1, source_target_pairs={{0,4},{4,8},{8,12},{1,5},{5,9},{9,13},{2,6},{6,10},{10,14},{3,7},{... | collective-permute-start | bytes 1105928 | tf_op jit(solution)/shard_map/ppermute | solution.py:41
  3.6 13.6 %collective-permute-start.3 = (bf16[480,384]{1,0:T(8,128)(2,1)}, bf16[480,384]{1,0:T(8,128)(2,1)S(1)}, u32[]{:S(2)}, u32[]{:S(2)}) collective-permute-start(bf16[480,384]{1,0:T(8,128)(2,1)} %bitcast.73), channel_id=1, source_target_pairs={{4,0},{8,4},{12,8},{5,1},{9,5},{13,9},{6,2},{10,6},{14,10},{7,3},{... | collective-permute-start | bytes 1105928 | tf_op jit(solution)/shard_map/ppermute | solution.py:42
  12.6 11.4 %collective-permute-start.1 = (bf16[480,384]{1,0:T(8,128)(2,1)S(1)}, bf16[480,384]{1,0:T(8,128)(2,1)S(1)}, u32[]{:S(2)}, u32[]{:S(2)}) collective-permute-start(bf16[480,384]{1,0:T(8,128)(2,1)S(1)} %collective-permute-done), channel_id=1, source_target_pairs={{0,4},{4,8},{8,12},{1,5},{5,9},{9,13},{2,6},{6,10},{10,14},{3,7},{... | collective-permute-start | bytes 1105928 | tf_op jit(solution)/shard_map/ppermute | solution.py:41
  17.2 12.5 %collective-permute-start.4 = (bf16[480,384]{1,0:T(8,128)(2,1)S(1)}, bf16[480,384]{1,0:T(8,128)(2,1)S(1)}, u32[]{:S(2)}, u32[]{:S(2)}) collective-permute-start(bf16[480,384]{1,0:T(8,128)(2,1)S(1)} %collective-permute-done.3), channel_id=1, source_target_pairs={{4,0},{8,4},{12,8},{5,1},{9,5},{13,9},{6,2},{10,6},{14,10},{7,3},{... | collective-permute-start | bytes 1105928 | tf_op jit(solution)/shard_map/ppermute | solution.py:42
  23.9 10.5 %collective-permute-start.2 = (bf16[480,384]{1,0:T(8,128)(2,1)S(1)}, bf16[480,384]{1,0:T(8,128)(2,1)S(1)}, u32[]{:S(2)}, u32[]{:S(2)}) collective-permute-start(bf16[480,384]{1,0:T(8,128)(2,1)S(1)} %collective-permute-done.1), channel_id=1, source_target_pairs={{0,4},{4,8},{8,12},{1,5},{5,9},{9,13},{2,6},{6,10},{10,14},{3,7},{... | collective-permute-start | bytes 1105928 | tf_op jit(solution)/shard_map/ppermute | solution.py:41
  29.8 10.2 %collective-permute-start.5 = (bf16[480,384]{1,0:T(8,128)(2,1)S(1)}, bf16[480,384]{1,0:T(8,128)(2,1)S(1)}, u32[]{:S(2)}, u32[]{:S(2)}) collective-permute-start(bf16[480,384]{1,0:T(8,128)(2,1)S(1)} %collective-permute-done.4), channel_id=1, source_target_pairs={{4,0},{8,4},{12,8},{5,1},{9,5},{13,9},{6,2},{10,6},{14,10},{7,3},{... | collective-permute-start | bytes 1105928 | tf_op jit(solution)/shard_map/ppermute | solution.py:42
  34.5 5.9 %copy-start.6 = (f32[384]{0:T(512)S(1)}, f32[384]{0:T(512)}, u32[]{:S(2)}) copy-start(f32[384]{0:T(512)} %param.11) | copy-start | bytes 4612
  40.1 2.7 %copy-start.5 = (bf16[384,384]{1,0:T(8,128)(2,1)S(1)}, bf16[384,384]{1,0:T(8,128)(2,1)}, u32[]{:S(2)}) copy-start(bf16[384,384]{1,0:T(8,128)(2,1)} %param.13) | copy-start | bytes 884740
  45.0 6.6 %copy-start.3 = (bf16[384,384]{1,0:T(8,128)(2,1)S(1)}, bf16[384,384]{1,0:T(8,128)(2,1)}, u32[]{:S(2)}) copy-start(bf16[384,384]{1,0:T(8,128)(2,1)} %param.15) | copy-start | bytes 884740
  45.0 8.2 %copy-start.4 = (f32[384]{0:T(512)S(1)}, f32[384]{0:T(512)}, u32[]{:S(2)}) copy-start(f32[384]{0:T(512)} %param.16) | copy-start | bytes 4612
  51.7 10.7 %copy-start.2 = (bf16[2,3,160,384]{3,2,1,0:T(8,128)(2,1)S(1)}, bf16[2,3,160,384]{3,2,1,0:T(8,128)(2,1)}, u32[]{:S(2)}) copy-start(bf16[2,3,160,384]{3,2,1,0:T(8,128)(2,1)} %param.10) | copy-start | bytes 2211844
  53.5 8.8 %collective-permute-start.6 = (bf16[3,160,384]{2,1,0:T(8,128)(2,1)S(1)}, bf16[3,160,384]{2,1,0:T(8,128)(2,1)S(1)}, u32[]{:S(2)}, u32[]{:S(2)}) collective-permute-start(bf16[3,160,384]{2,1,0:T(8,128)(2,1)S(1)} %bitcast.67), channel_id=1, source_target_pairs={{0,1},{1,2},{2,3},{4,5},{5,6},{6,7},{8,9},{9,10},{10,11},{12,13},{... | collective-permute-start | bytes 1105928 | tf_op jit(solution)/shard_map/ppermute | solution.py:15
  62.4 8.8 %collective-permute-start.7 = (bf16[3,160,384]{2,1,0:T(8,128)(2,1)S(1)}, bf16[3,160,384]{2,1,0:T(8,128)(2,1)S(1)}, u32[]{:S(2)}, u32[]{:S(2)}) collective-permute-start(bf16[3,160,384]{2,1,0:T(8,128)(2,1)S(1)} %bitcast_select_fusion), channel_id=1, source_target_pairs={{0,1},{1,2},{2,3},{4,5},{5,6},{6,7},{8,9},{9,10},{10,11},{12,13},{... | collective-permute-start | bytes 1105928 | tf_op jit(solution)/shard_map/ppermute | solution.py:15
  71.3 16.2 %collective-permute-start.8 = (bf16[2,1,160,384]{3,2,1,0:T(8,128)(2,1)S(1)}, bf16[2,1,160,384]{3,2,1,0:T(8,128)(2,1)S(1)}, u32[]{:S(2)}, u32[]{:S(2)}) collective-permute-start(bf16[2,1,160,384]{3,2,1,0:T(8,128)(2,1)S(1)} %get-tuple-element.16), channel_id=1, source_target_pairs={{0,4},{4,8},{8,12},{1,5},{5,9},{9,13},{2,6},{6,10},{10,14},{3,7},{... | collective-permute-start | bytes 737288 | tf_op jit(solution)/shard_map/ppermute | solution.py:25
  74.9 12.7 %collective-permute-start.9 = (bf16[2,1,160,384]{3,2,1,0:T(8,128)(2,1)S(1)}, bf16[2,1,160,384]{3,2,1,0:T(8,128)(2,1)S(1)}, u32[]{:S(2)}, u32[]{:S(2)}) collective-permute-start(bf16[2,1,160,384]{3,2,1,0:T(8,128)(2,1)S(1)} %get-tuple-element.17), channel_id=1, source_target_pairs={{4,0},{8,4},{12,8},{5,1},{9,5},{13,9},{6,2},{10,6},{14,10},{7,3},{... | collective-permute-start | bytes 737288 | tf_op jit(solution)/shard_map/ppermute | solution.py:26
  77.2 6.8 %collective-permute-start.10 = (bf16[1,1,160,384]{3,2,1,0:T(8,128)(2,1)S(1)}, bf16[1,1,160,384]{3,2,1,0:T(8,128)(2,1)S(1)}, u32[]{:S(2)}, u32[]{:S(2)}) collective-permute-start(bf16[1,1,160,384]{3,2,1,0:T(8,128)(2,1)S(1)} %get-tuple-element.18), channel_id=1, source_target_pairs={{0,4},{4,8},{8,12},{1,5},{5,9},{9,13},{2,6},{6,10},{10,14},{3,7},{... | collective-permute-start | bytes 368648 | tf_op jit(solution)/shard_map/ppermute | solution.py:25
  80.7 6.8 %collective-permute-start.11 = (bf16[1,1,160,384]{3,2,1,0:T(8,128)(2,1)S(1)}, bf16[1,1,160,384]{3,2,1,0:T(8,128)(2,1)S(1)}, u32[]{:S(2)}, u32[]{:S(2)}) collective-permute-start(bf16[1,1,160,384]{3,2,1,0:T(8,128)(2,1)S(1)} %get-tuple-element.19), channel_id=1, source_target_pairs={{4,0},{8,4},{12,8},{5,1},{9,5},{13,9},{6,2},{10,6},{14,10},{7,3},{... | collective-permute-start | bytes 368648 | tf_op jit(solution)/shard_map/ppermute | solution.py:26
  89.4 2.2 %slice-start = ((s8[7962624]{0:T(1024)(128)(4,1)}), s8[4194304]{0:T(1024)(128)(4,1)S(1)}, s32[]{:S(2)}) async-start(s8[7962624]{0:T(1024)(128)(4,1)} %bitcast.85), calls=%async_computation | async-start | bytes 8388608
  90.0 2.9 %slice-start.1 = ((s8[7962624]{0:T(1024)(128)(4,1)}), s8[3768320]{0:T(1024)(128)(4,1)S(1)}, s32[]{:S(2)}) async-start(s8[7962624]{0:T(1024)(128)(4,1)} %bitcast.85), calls=%async_computation.1 | async-start | bytes 7536640

commit v9 on v3

--- a/solution.py
+++ b/solution.py
@@ -13,19 +13,6 @@
     size = lax.axis_size(axis)
     pairs = [(i, i + by) for i in range(size) if 0 <= i + by < size]
     return lax.ppermute(x, axis, pairs)
-
-
-def with_halo(x, sides, width):
-    for axis, dim in sides:
-        size, length = (lax.axis_size(axis), x.shape[dim])
-        up = [(i, (i + 1) % size) for i in range(size - 1)]
-        down = [(j, i) for i, j in up]
-        last = lax.slice_in_dim(x, length - width, length, axis=dim)
-        leading = lax.slice_in_dim(x, 0, width, axis=dim)
-        before = lax.ppermute(last, axis, up)
-        after = lax.ppermute(leading, axis, down)
-        x = jnp.concatenate([before, x, after], axis=dim)
-    return x
 
 
 def strip_gather(x, axis):
@@ -124,12 +111,25 @@
     older = passed_along(prior, "tm", 1)
     older = jnp.where(frame_index == 0, cache_frames[0], older)
     stacked = jnp.stack([older, prior, act])
-    padded = with_halo(stacked, (("strip", 1),), 1)
-    padded = jnp.pad(padded, ((0, 0), (0, 0), (1, 1), (0, 0)))
+    padded = jnp.pad(stacked, ((0, 0), (1, 1), (1, 1), (0, 0)))
     widened = jnp.concatenate(
         [padded[:, :, 0:cols], padded[:, :, 1 : cols + 1], padded[:, :, 2 : cols + 2]], axis=-1
     )
     kernel = conv_weight.reshape(3, 3, 3 * width, width)
+    to_prev = None
+    to_next = None
+    for step_t in range(3):
+        first = jnp.dot(widened[step_t, 1], kernel[step_t, 2], preferred_element_type=jnp.float32)
+        last = jnp.dot(widened[step_t, rows], kernel[step_t, 0], preferred_element_type=jnp.float32)
+        to_prev = first if to_prev is None else to_prev + first
+        to_next = last if to_next is None else to_next + last
+    n = lax.axis_size("strip")
+    from_next = lax.ppermute(
+        to_prev.astype(jnp.bfloat16), "strip", [(i + 1, i) for i in range(n - 1)]
+    )
+    from_prev = lax.ppermute(
+        to_next.astype(jnp.bfloat16), "strip", [(i, i + 1) for i in range(n - 1)]
+    )
     result = resid.astype(jnp.float32)
     for step_t in range(3):
         for step_r in range(3):
@@ -137,6 +137,15 @@
             result = result + jnp.dot(
                 window, kernel[step_t, step_r], preferred_element_type=jnp.float32
             )
+    edges = jnp.concatenate(
+        [
+            from_prev[None].astype(jnp.float32),
+            jnp.zeros((rows - 2, cols, width), jnp.float32),
+            from_next[None].astype(jnp.float32),
+        ],
+        axis=0,
+    )
+    result = result + edges.reshape(-1, width)
     return result.astype(jnp.bfloat16).reshape(1, rows, cols, width)
 
 

time: 98.7 us -> 93.4 us (0.946)
  waiting for transfers between devices: 39 us -> 32 us
  matrix products: 16.2 us -> 18.1 us
    ppermute x2, waiting for transfers between devices: 6.86 us -> 0.01 us  [the longest x1 0.01 us: shards(): lax.ppermute(to_next.astype(jnp.bfloat16), 'strip', [(i, i + 1) for i in...]
    dot_general x0 -> x6, matrix products: none -> 2.16 us  [the longest x3 1.08 us: shards(): jnp.dot(widened[step_t, rows], kernel[step_t, 0], preferred_element_type=...]
    concatenate x1, other arithmetic: 1.54 us -> 0.12 us  [shards(): jnp.concatenate([from_prev[None].astype(jnp.float32), jnp.zeros((rows - 2...]
  transfers between devices with their start and end apart: 10 -> 10, of which waited for: 8 -> 6; matrix products, arithmetic and copies ran while one was open for 4% -> 12% of each run, Pallas kernels for 0% -> 0%
where the time goes in v9:
time: 93.4 us; the launch traced here: 92.9 us
  waiting for transfers between devices  32 us (34%)
  starting transfers between devices  27.5 us (29%)
  matrix products  18.1 us (19%)
  Pallas kernels  6.67 us (7%)
  local copies, waits for them, and re-layouts  4.61 us (5%)
  other arithmetic  3.5 us (4%)
    ppermute x2, waiting for transfers between devices, passed_along(): return lax.ppermute(x, axis, pairs)  13.7 us
    ppermute x3, waiting for transfers between devices, strip_gather(): up = lax.ppermute(up, axis, up_pairs)  13.1 us
    ppermute x3, starting transfers between devices, strip_gather(): up = lax.ppermute(up, axis, up_pairs)  10.6 us
    dot_general x9, matrix products, shards(): jnp.dot(window, kernel[step_t, step_r], preferred_element_type=jnp.float32)  7.6 us
    ppermute x3, starting transfers between devices, strip_gather(): down = lax.ppermute(down, axis, down_pairs)  7.12 us
    pallas_call x1, Pallas kernels, attend(): pl.pallas_call(functools.partial(attention_kernel, scale), out_shape=jax....  6.67 us
    ppermute x3, waiting for transfers between devices, strip_gather(): down = lax.ppermute(down, axis, down_pairs)  5.18 us
    ppermute x2, starting transfers between devices, passed_along(): return lax.ppermute(x, axis, pairs)  3.84 us
  transfers between devices with their start and end apart: 10, of which 6 were waited for; matrix products, arithmetic and copies ran while one was open for 12% of the time, Pallas kernels for 0%

profile of v9, /device:TPU:10, one launch (start us, length us, event | category | flops | bytes accessed | tf_op | source)
XLA Modules:
  0.0 92.9 jit_solution(1979554509062356539)
XLA Ops:
  0.0 3.6 %collective-permute-start = (bf16[480,384]{1,0:T(8,128)(2,1)}, bf16[480,384]{1,0:T(8,128)(2,1)S(1)}, u32[]{:S(2)}, u32[]{:S(2)}) collective-permute-start(bf16[480,384]{1,0:T(8,128)(2,1)} %bitcast.127), channel_id=1, source_target_pairs={{0,4},{4,8},{8,12},{1,5},{5,9},{9,13},{2,6},{6,10},{10,14},{3,7},{... | collective-permute-start | bytes 1105928 | tf_op jit(solution)/shard_map/ppermute | solution.py:28
  3.6 2.4 %collective-permute-start.3 = (bf16[480,384]{1,0:T(8,128)(2,1)}, bf16[480,384]{1,0:T(8,128)(2,1)S(1)}, u32[]{:S(2)}, u32[]{:S(2)}) collective-permute-start(bf16[480,384]{1,0:T(8,128)(2,1)} %bitcast.128), channel_id=1, source_target_pairs={{4,0},{8,4},{12,8},{5,1},{9,5},{13,9},{6,2},{10,6},{14,10},{7,3},{... | collective-permute-start | bytes 1105928 | tf_op jit(solution)/shard_map/ppermute | solution.py:29
  6.0 6.6 %collective-permute-done = bf16[480,384]{1,0:T(8,128)(2,1)S(1)} collective-permute-done((bf16[480,384]{1,0:T(8,128)(2,1)}, bf16[480,384]{1,0:T(8,128)(2,1)S(1)}, u32[]{:S(2)}, u32[]{:S(2)}) %collective-permute-start) | collective-permute-done | bytes 368672 | tf_op jit(solution)/shard_map/ppermute | solution.py:28
  12.6 3.5 %collective-permute-start.1 = (bf16[480,384]{1,0:T(8,128)(2,1)S(1)}, bf16[480,384]{1,0:T(8,128)(2,1)S(1)}, u32[]{:S(2)}, u32[]{:S(2)}) collective-permute-start(bf16[480,384]{1,0:T(8,128)(2,1)S(1)} %collective-permute-done), channel_id=1, source_target_pairs={{0,4},{4,8},{8,12},{1,5},{5,9},{9,13},{2,6},{6,10},{10,14},{3,7},{... | collective-permute-start | bytes 1105928 | tf_op jit(solution)/shard_map/ppermute | solution.py:28
  16.0 1.2 %multiply_reduce_fusion.1 = f32[3,160]{1,0:T(4,128)S(1)} fusion(bf16[1,3,160,384]{3,2,1,0:T(8,128)(2,1)} %param.9), kind=kLoop, calls=%fused_computation.58 | loop fusion | flops 552480 | bytes 370560 | tf_op jit(solution)/shard_map/reduce_sum | solution.py:39
  17.2 2.4 %collective-permute-start.4 = (bf16[480,384]{1,0:T(8,128)(2,1)S(1)}, bf16[480,384]{1,0:T(8,128)(2,1)S(1)}, u32[]{:S(2)}, u32[]{:S(2)}) collective-permute-start(bf16[480,384]{1,0:T(8,128)(2,1)S(1)} %collective-permute-done.3), channel_id=1, source_target_pairs={{4,0},{8,4},{12,8},{5,1},{9,5},{13,9},{6,2},{10,6},{14,10},{7,3},{... | collective-permute-start | bytes 1105928 | tf_op jit(solution)/shard_map/ppermute | solution.py:29
  19.6 4.3 %collective-permute-done.1 = bf16[480,384]{1,0:T(8,128)(2,1)S(1)} collective-permute-done((bf16[480,384]{1,0:T(8,128)(2,1)S(1)}, bf16[480,384]{1,0:T(8,128)(2,1)S(1)}, u32[]{:S(2)}, u32[]{:S(2)}) %collective-permute-start.1) | collective-permute-done | bytes 368672 | tf_op jit(solution)/shard_map/ppermute | solution.py:28
  23.9 3.5 %collective-permute-start.2 = (bf16[480,384]{1,0:T(8,128)(2,1)S(1)}, bf16[480,384]{1,0:T(8,128)(2,1)S(1)}, u32[]{:S(2)}, u32[]{:S(2)}) collective-permute-start(bf16[480,384]{1,0:T(8,128)(2,1)S(1)} %collective-permute-done.1), channel_id=1, source_target_pairs={{0,4},{4,8},{8,12},{1,5},{5,9},{9,13},{2,6},{6,10},{10,14},{3,7},{... | collective-permute-start | bytes 1105928 | tf_op jit(solution)/shard_map/ppermute | solution.py:28
  27.4 0.1 rsqrt.28
  27.5 2.3 %convolution_convert_fusion.2.q_ref = bf16[480,384]{1,0:T(8,128)(2,1)} fusion(bf16[384,384]{1,0:T(8,128)(2,1)} %param.12, bf16[480,384]{1,0:T(8,128)(2,1)} %bitcast.129, f32[384]{0:T(512)} %param.11, f32[480]{0:T(512)S(1)} %rsqrt.28), kind=kOutput, calls=%fused_computation.32 | convolution fusion | flops 142479360 | bytes 1035648 | tf_op jit(solution)/shard_map/dot_general | solution.py:100
  29.8 2.4 %collective-permute-start.5 = (bf16[480,384]{1,0:T(8,128)(2,1)S(1)}, bf16[480,384]{1,0:T(8,128)(2,1)S(1)}, u32[]{:S(2)}, u32[]{:S(2)}) collective-permute-start(bf16[480,384]{1,0:T(8,128)(2,1)S(1)} %collective-permute-done.4), channel_id=1, source_target_pairs={{4,0},{8,4},{12,8},{5,1},{9,5},{13,9},{6,2},{10,6},{14,10},{7,3},{... | collective-permute-start | bytes 1105928 | tf_op jit(solution)/shard_map/ppermute | solution.py:29
  32.1 2.3 %collective-permute-done.2 = bf16[480,384]{1,0:T(8,128)(2,1)S(1)} collective-permute-done((bf16[480,384]{1,0:T(8,128)(2,1)S(1)}, bf16[480,384]{1,0:T(8,128)(2,1)S(1)}, u32[]{:S(2)}, u32[]{:S(2)}) %collective-permute-start.2) | collective-permute-done | bytes 368672 | tf_op jit(solution)/shard_map/ppermute | solution.py:28
  34.8 5.2 %collective-permute-done.5 = bf16[480,384]{1,0:T(8,128)(2,1)S(1)} collective-permute-done((bf16[480,384]{1,0:T(8,128)(2,1)S(1)}, bf16[480,384]{1,0:T(8,128)(2,1)S(1)}, u32[]{:S(2)}, u32[]{:S(2)}) %collective-permute-start.5) | collective-permute-done | bytes 368672 | tf_op jit(solution)/shard_map/ppermute | solution.py:29
  40.1 0.4 fusion.3
  40.5 2.3 %convolution_convert_fusion.v_ref = bf16[1920,384]{1,0:T(8,128)(2,1)} fusion(bf16[384,384]{1,0:T(8,128)(2,1)S(1)} %copy-done, f32[384]{0:T(512)S(1)} %copy-done.6, f32[1920]{0:T(1024)S(1)} %add_rsqrt_fusion, bf16[3360,384]{1,0:T(8,128)(2,1)S(1)} %constant_dynamic-update-slice_fusion, s32[]{:T(128)S(6)} %select_n.15), kind=kOutput, calls=%fused_computation.13 | convolution fusion | flops 569917440 | bytes 3254276 | tf_op jit(solution)/shard_map/dot_general | solution.py:102
  42.8 2.2 %convolution_convert_fusion.1.k_ref = bf16[1920,384]{1,0:T(8,128)(2,1)} fusion(bf16[384,384]{1,0:T(8,128)(2,1)S(1)} %copy-done.5, f32[384]{0:T(512)S(1)} %copy-done.6, f32[1920]{0:T(1024)S(1)} %add_rsqrt_fusion, bf16[3360,384]{1,0:T(8,128)(2,1)S(1)} %constant_dynamic-update-slice_fusion, s32[]{:T(128)S(6)} %select_n.15), kind=kOutput, calls=%fused_computation.14 | convolution fusion | flops 569917440 | bytes 3254276 | tf_op jit(solution)/shard_map/dot_general | solution.py:101
  45.0 6.7 %shard_map.91 = bf16[480,384]{1,0:T(8,128)(2,1)} custom-call(bf16[480,384]{1,0:T(8,128)(2,1)} %convolution_convert_fusion.2.q_ref, bf16[1920,384]{1,0:T(8,128)(2,1)} %convolution_convert_fusion.1.k_ref, bf16[1920,384]{1,0:T(8,128)(2,1)} %convolution_convert_fusion.v_ref), custom_call_target="tpu_custom_call" | custom-call | flops 1415577600 | bytes 3686400 | tf_op jit(solution)/shard_map/pallas_call | solution.py:61
  51.7 1.5 %multiply_reduce_fusion = (f32[480]{0:T(512)S(1)}, f32[480,384]{1,0:T(8,128)S(1)}) fusion(bf16[480,384]{1,0:T(8,128)(2,1)} %shard_map.91, bf16[384,384]{1,0:T(8,128)(2,1)S(1)} %copy-done.3, bf16[480,384]{1,0:T(8,128)(2,1)S(1)} %bitcast.131), kind=kOutput, calls=%fused_computation.57 | convolution fusion | flops 142663200 | bytes 1771392 | tf_op jit(solution)/shard_map/dot_general | solution.py:105
  53.3 0.3 multiply_convert_fusion
  53.5 1.9 %collective-permute-start.6 = (bf16[3,160,384]{2,1,0:T(8,128)(2,1)S(1)}, bf16[3,160,384]{2,1,0:T(8,128)(2,1)S(1)}, u32[]{:S(2)}, u32[]{:S(2)}) collective-permute-start(bf16[3,160,384]{2,1,0:T(8,128)(2,1)S(1)} %bitcast.132), channel_id=1, source_target_pairs={{0,1},{1,2},{2,3},{4,5},{5,6},{6,7},{8,9},{9,10},{10,11},{12,13},{... | collective-permute-start | bytes 1105928 | tf_op jit(solution)/shard_map/ppermute | solution.py:15
  55.5 6.9 %collective-permute-done.6 = bf16[3,160,384]{2,1,0:T(8,128)(2,1)S(1)} collective-permute-done((bf16[3,160,384]{2,1,0:T(8,128)(2,1)S(1)}, bf16[3,160,384]{2,1,0:T(8,128)(2,1)S(1)}, u32[]{:S(2)}, u32[]{:S(2)}) %collective-permute-start.6) | collective-permute-done | bytes 368672 | tf_op jit(solution)/shard_map/ppermute | solution.py:15
  62.4 1.9 %collective-permute-start.7 = (bf16[3,160,384]{2,1,0:T(8,128)(2,1)S(1)}, bf16[3,160,384]{2,1,0:T(8,128)(2,1)S(1)}, u32[]{:S(2)}, u32[]{:S(2)}) collective-permute-start(bf16[3,160,384]{2,1,0:T(8,128)(2,1)S(1)} %bitcast_select_fusion), channel_id=1, source_target_pairs={{0,1},{1,2},{2,3},{4,5},{5,6},{6,7},{8,9},{9,10},{10,11},{12,13},{... | collective-permute-start | bytes 1105928 | tf_op jit(solution)/shard_map/ppermute | solution.py:15
  64.3 0.1 pad.6.clone
  64.4 6.8 %collective-permute-done.7 = bf16[3,160,384]{2,1,0:T(8,128)(2,1)S(1)} collective-permute-done((bf16[3,160,384]{2,1,0:T(8,128)(2,1)S(1)}, bf16[3,160,384]{2,1,0:T(8,128)(2,1)S(1)}, u32[]{:S(2)}, u32[]{:S(2)}) %collective-permute-start.7) | collective-permute-done | bytes 368672 | tf_op jit(solution)/shard_map/ppermute | solution.py:15
  71.3 0.8 select_maximum_fusion
  72.2 1.0 %fusion.27 = (bf16[3,5,160,384]{3,2,1,0:T(8,128)(2,1)S(1)}, bf16[3,5,160,384]{3,2,1,0:T(8,128)(2,1)S(1)}, bf16[3,5,160,384]{3,2,1,0:T(8,128)(2,1)S(1)}) fusion(bf16[3,5,162,384]{3,2,1,0:T(8,128)(2,1)S(1)} %select_maximum_fusion), kind=kLoop, calls=%fused_computation.85 | loop fusion | bytes 11059200 | tf_op jit(solution)/shard_map/slice | solution.py:116
  73.2 0.6 pad_maximum_fusion
  73.8 0.4 slice-done
  74.2 1.5 %slice-done.1 = s8[4194304]{0:T(1024)(128)(4,1)S(1)} async-done(((s8[7962624]{0:T(1024)(128)(4,1)}), s8[4194304]{0:T(1024)(128)(4,1)S(1)}, s32[]{:S(2)}) %slice-start.1) | async-done | bytes 4194328
  75.7 0.4 fusion.14
  76.1 0.4 fusion.13
  76.5 1.0 %fusion.26 = (bf16[1,3,160,1152]{3,2,1,0:T(8,128)(2,1)S(1)}, bf16[1,3,160,1152]{3,2,1,0:T(8,128)(2,1)S(1)}, bf16[1,3,160,1152]{3,2,1,0:T(8,128)(2,1)S(1)}, bf16[...) fusion(bf16[3,5,160,1152]{3,2,1,0:T(8,128)(2,1)S(1)} %pad_maxim, ...), kind=kLoop, calls=%fused_computation.84 | loop fusion | bytes 19906560 | tf_op jit(solution)/shard_map/slice | solution.py:136
  77.5 0.4 convolution_add_fusion.11
  77.9 0.4 fusion.12
  78.2 2.4 %collective-permute-start.9 = (bf16[160,384]{1,0:T(8,128)(2,1)S(1)}, bf16[160,384]{1,0:T(8,128)(2,1)S(1)}, u32[]{:S(2)}, u32[]{:S(2)}) collective-permute-start(bf16[160,384]{1,0:T(8,128)(2,1)S(1)} %fusion.12), channel_id=1, source_target_pairs={{4,0},{8,4},{12,8},{5,1},{9,5},{13,9},{6,2},{10,6},{14,10},{7,3},{... | collective-permute-start | bytes 368648 | tf_op jit(solution)/shard_map/ppermute | solution.py:127
  80.6 0.4 convolution_add_fusion.13
  81.0 0.4 fusion.11
  81.4 3.6 %collective-permute-start.8 = (bf16[160,384]{1,0:T(8,128)(2,1)S(1)}, bf16[160,384]{1,0:T(8,128)(2,1)S(1)}, u32[]{:S(2)}, u32[]{:S(2)}) collective-permute-start(bf16[160,384]{1,0:T(8,128)(2,1)S(1)} %fusion.11), channel_id=1, source_target_pairs={{0,4},{4,8},{8,12},{1,5},{5,9},{9,13},{2,6},{6,10},{10,14},{3,7},{... | collective-permute-start | bytes 368648 | tf_op jit(solution)/shard_map/ppermute | solution.py:130
  85.0 0.8 convolution_add_fusion.9
  85.8 0.8 convolution_add_fusion.8
  86.6 0.8 convolution_add_fusion.7
  87.3 0.8 convolution_add_fusion.6
  88.1 0.8 convolution_add_fusion.5
  88.9 0.8 convolution_add_fusion.4
  89.6 0.8 convolution_add_fusion.3
  90.4 0.8 convolution_add_fusion.2
  91.2 0.1 pad_maximum_fusion.1
  91.4 1.5 %fusion.17 = bf16[480,384]{1,0:T(8,128)(2,1)} fusion(f32[3,160,384]{2,1,0:T(8,128)S(1)} %pad_maximum_fusion.1, f32[480,384]{1,0:T(8,128)S(1)} %convolution_add_fusion.2, bf16[480,1152]{1,0:T(8,128)(2,1)S(1)} %bitcast.118, bf16[3,3,1152,384]{3,2,1,0:T(8,128)(2,1)S(1)} %bitcast.117), kind=kOutput, calls=%fused_computation.55 | convolution fusion | flops 425226240 | bytes 3833856 | tf_op jit(solution)/shard_map/dot_general | solution.py:137
  (35 shorter events, 0.6 us)
Async XLA Ops:
  0.0 40.5 %copy-start = (bf16[384,384]{1,0:T(8,128)(2,1)S(1)}, bf16[384,384]{1,0:T(8,128)(2,1)}, u32[]{:S(2)}) copy-start(bf16[384,384]{1,0:T(8,128)(2,1)} %param.14) | copy-start | bytes 884740
  0.0 34.6 %copy-start.1 = (bf16[1,3,160,384]{3,2,1,0:T(8,128)(2,1)S(1)}, bf16[1,3,160,384]{3,2,1,0:T(8,128)(2,1)}, u32[]{:S(2)}) copy-start(bf16[1,3,160,384]{3,2,1,0:T(8,128)(2,1)} %param.9) | copy-start | bytes 1105924
  0.0 12.6 %collective-permute-start = (bf16[480,384]{1,0:T(8,128)(2,1)}, bf16[480,384]{1,0:T(8,128)(2,1)S(1)}, u32[]{:S(2)}, u32[]{:S(2)}) collective-permute-start(bf16[480,384]{1,0:T(8,128)(2,1)} %bitcast.127), channel_id=1, source_target_pairs={{0,4},{4,8},{8,12},{1,5},{5,9},{9,13},{2,6},{6,10},{10,14},{3,7},{... | collective-permute-start | bytes 1105928 | tf_op jit(solution)/shard_map/ppermute | solution.py:28
  3.6 13.6 %collective-permute-start.3 = (bf16[480,384]{1,0:T(8,128)(2,1)}, bf16[480,384]{1,0:T(8,128)(2,1)S(1)}, u32[]{:S(2)}, u32[]{:S(2)}) collective-permute-start(bf16[480,384]{1,0:T(8,128)(2,1)} %bitcast.128), channel_id=1, source_target_pairs={{4,0},{8,4},{12,8},{5,1},{9,5},{13,9},{6,2},{10,6},{14,10},{7,3},{... | collective-permute-start | bytes 1105928 | tf_op jit(solution)/shard_map/ppermute | solution.py:29
  12.6 11.4 %collective-permute-start.1 = (bf16[480,384]{1,0:T(8,128)(2,1)S(1)}, bf16[480,384]{1,0:T(8,128)(2,1)S(1)}, u32[]{:S(2)}, u32[]{:S(2)}) collective-permute-start(bf16[480,384]{1,0:T(8,128)(2,1)S(1)} %collective-permute-done), channel_id=1, source_target_pairs={{0,4},{4,8},{8,12},{1,5},{5,9},{9,13},{2,6},{6,10},{10,14},{3,7},{... | collective-permute-start | bytes 1105928 | tf_op jit(solution)/shard_map/ppermute | solution.py:28
  17.2 12.5 %collective-permute-start.4 = (bf16[480,384]{1,0:T(8,128)(2,1)S(1)}, bf16[480,384]{1,0:T(8,128)(2,1)S(1)}, u32[]{:S(2)}, u32[]{:S(2)}) collective-permute-start(bf16[480,384]{1,0:T(8,128)(2,1)S(1)} %collective-permute-done.3), channel_id=1, source_target_pairs={{4,0},{8,4},{12,8},{5,1},{9,5},{13,9},{6,2},{10,6},{14,10},{7,3},{... | collective-permute-start | bytes 1105928 | tf_op jit(solution)/shard_map/ppermute | solution.py:29
  23.9 10.5 %collective-permute-start.2 = (bf16[480,384]{1,0:T(8,128)(2,1)S(1)}, bf16[480,384]{1,0:T(8,128)(2,1)S(1)}, u32[]{:S(2)}, u32[]{:S(2)}) collective-permute-start(bf16[480,384]{1,0:T(8,128)(2,1)S(1)} %collective-permute-done.1), channel_id=1, source_target_pairs={{0,4},{4,8},{8,12},{1,5},{5,9},{9,13},{2,6},{6,10},{10,14},{3,7},{... | collective-permute-start | bytes 1105928 | tf_op jit(solution)/shard_map/ppermute | solution.py:28
  29.8 10.2 %collective-permute-start.5 = (bf16[480,384]{1,0:T(8,128)(2,1)S(1)}, bf16[480,384]{1,0:T(8,128)(2,1)S(1)}, u32[]{:S(2)}, u32[]{:S(2)}) collective-permute-start(bf16[480,384]{1,0:T(8,128)(2,1)S(1)} %collective-permute-done.4), channel_id=1, source_target_pairs={{4,0},{8,4},{12,8},{5,1},{9,5},{13,9},{6,2},{10,6},{14,10},{7,3},{... | collective-permute-start | bytes 1105928 | tf_op jit(solution)/shard_map/ppermute | solution.py:29
  34.5 5.9 %copy-start.6 = (f32[384]{0:T(512)S(1)}, f32[384]{0:T(512)}, u32[]{:S(2)}) copy-start(f32[384]{0:T(512)} %param.11) | copy-start | bytes 4612
  40.1 2.7 %copy-start.5 = (bf16[384,384]{1,0:T(8,128)(2,1)S(1)}, bf16[384,384]{1,0:T(8,128)(2,1)}, u32[]{:S(2)}) copy-start(bf16[384,384]{1,0:T(8,128)(2,1)} %param.13) | copy-start | bytes 884740
  45.0 6.7 %copy-start.3 = (bf16[384,384]{1,0:T(8,128)(2,1)S(1)}, bf16[384,384]{1,0:T(8,128)(2,1)}, u32[]{:S(2)}) copy-start(bf16[384,384]{1,0:T(8,128)(2,1)} %param.15) | copy-start | bytes 884740
  45.0 8.2 %copy-start.4 = (f32[384]{0:T(512)S(1)}, f32[384]{0:T(512)}, u32[]{:S(2)}) copy-start(f32[384]{0:T(512)} %param.16) | copy-start | bytes 4612
  51.7 10.7 %copy-start.2 = (bf16[2,3,160,384]{3,2,1,0:T(8,128)(2,1)S(1)}, bf16[2,3,160,384]{3,2,1,0:T(8,128)(2,1)}, u32[]{:S(2)}) copy-start(bf16[2,3,160,384]{3,2,1,0:T(8,128)(2,1)} %param.10) | copy-start | bytes 2211844
  53.5 8.8 %collective-permute-start.6 = (bf16[3,160,384]{2,1,0:T(8,128)(2,1)S(1)}, bf16[3,160,384]{2,1,0:T(8,128)(2,1)S(1)}, u32[]{:S(2)}, u32[]{:S(2)}) collective-permute-start(bf16[3,160,384]{2,1,0:T(8,128)(2,1)S(1)} %bitcast.132), channel_id=1, source_target_pairs={{0,1},{1,2},{2,3},{4,5},{5,6},{6,7},{8,9},{9,10},{10,11},{12,13},{... | collective-permute-start | bytes 1105928 | tf_op jit(solution)/shard_map/ppermute | solution.py:15
  62.4 8.8 %collective-permute-start.7 = (bf16[3,160,384]{2,1,0:T(8,128)(2,1)S(1)}, bf16[3,160,384]{2,1,0:T(8,128)(2,1)S(1)}, u32[]{:S(2)}, u32[]{:S(2)}) collective-permute-start(bf16[3,160,384]{2,1,0:T(8,128)(2,1)S(1)} %bitcast_select_fusion), channel_id=1, source_target_pairs={{0,1},{1,2},{2,3},{4,5},{5,6},{6,7},{8,9},{9,10},{10,11},{12,13},{... | collective-permute-start | bytes 1105928 | tf_op jit(solution)/shard_map/ppermute | solution.py:15
  72.1 2.1 %slice-start = ((s8[7962624]{0:T(1024)(128)(4,1)}), s8[3768320]{0:T(1024)(128)(4,1)S(1)}, s32[]{:S(2)}) async-start(s8[7962624]{0:T(1024)(128)(4,1)} %bitcast.101), calls=%async_computation | async-start | bytes 7536640
  73.2 2.5 %slice-start.1 = ((s8[7962624]{0:T(1024)(128)(4,1)}), s8[4194304]{0:T(1024)(128)(4,1)S(1)}, s32[]{:S(2)}) async-start(s8[7962624]{0:T(1024)(128)(4,1)} %bitcast.101), calls=%async_computation.1 | async-start | bytes 8388608
  78.2 12.9 %collective-permute-start.9 = (bf16[160,384]{1,0:T(8,128)(2,1)S(1)}, bf16[160,384]{1,0:T(8,128)(2,1)S(1)}, u32[]{:S(2)}, u32[]{:S(2)}) collective-permute-start(bf16[160,384]{1,0:T(8,128)(2,1)S(1)} %fusion.12), channel_id=1, source_target_pairs={{4,0},{8,4},{12,8},{5,1},{9,5},{13,9},{6,2},{10,6},{14,10},{7,3},{... | collective-permute-start | bytes 368648 | tf_op jit(solution)/shard_map/ppermute | solution.py:127
  81.4 9.8 %collective-permute-start.8 = (bf16[160,384]{1,0:T(8,128)(2,1)S(1)}, bf16[160,384]{1,0:T(8,128)(2,1)S(1)}, u32[]{:S(2)}, u32[]{:S(2)}) collective-permute-start(bf16[160,384]{1,0:T(8,128)(2,1)S(1)} %fusion.11), channel_id=1, source_target_pairs={{0,4},{4,8},{8,12},{1,5},{5,9},{9,13},{2,6},{6,10},{10,14},{3,7},{... | collective-permute-start | bytes 368648 | tf_op jit(solution)/shard_map/ppermute | solution.py:130

commit v10 on v9

--- a/solution.py
+++ b/solution.py
@@ -39,42 +39,88 @@
     return wide * lax.rsqrt(jnp.mean(wide * wide, axis=-1, keepdims=True) + 1e-06) * gain
 
 
-def attention_kernel(scale, q_ref, k_ref, v_ref, o_ref):
+def scaled(x, gain):
+    wide = x.astype(jnp.float32)
+    return wide * lax.rsqrt(jnp.mean(wide * wide, axis=-1, keepdims=True) + 1e-06) * gain
+
+
+def attention_kernel(
+    scale, whole_ref, flat_ref, query_ref, again_ref, wk_ref, wv_ref, wo_ref, cgain_ref,
+    resid_ref, act_ref, keys_ref, values_ref,
+):
+    @pl.when(pl.program_id(0) == 0)
+    def _():
+        normed_all = scaled(whole_ref[...], again_ref[...]).astype(jnp.bfloat16)
+        keys_ref[...] = jnp.dot(
+            normed_all, wk_ref[...], preferred_element_type=jnp.float32
+        ).astype(jnp.bfloat16)
+        values_ref[...] = jnp.dot(
+            normed_all, wv_ref[...], preferred_element_type=jnp.float32
+        ).astype(jnp.bfloat16)
+
     scores = (
         lax.dot_general(
-            q_ref[...], k_ref[...], (((1,), (1,)), ((), ())), preferred_element_type=jnp.float32
+            query_ref[...], keys_ref[...], (((1,), (1,)), ((), ())),
+            preferred_element_type=jnp.float32,
         )
         * scale
     )
     peak = jnp.max(scores, axis=1, keepdims=True)
     weights = jnp.exp(scores - peak)
     total = jnp.sum(weights, axis=1, keepdims=True)
-    summed = jnp.dot(weights.astype(jnp.bfloat16), v_ref[...], preferred_element_type=jnp.float32)
-    o_ref[...] = (summed / total).astype(o_ref.dtype)
-
-
-def attend(query, keys, values, scale):
+    summed = jnp.dot(
+        weights.astype(jnp.bfloat16), values_ref[...], preferred_element_type=jnp.float32
+    )
+    attended = (summed / total).astype(jnp.bfloat16)
+    resid = (
+        flat_ref[...].astype(jnp.float32)
+        + jnp.dot(attended, wo_ref[...], preferred_element_type=jnp.float32)
+    ).astype(jnp.bfloat16)
+    resid_ref[...] = resid
+    shown = scaled(resid, cgain_ref[...])
+    act_ref[...] = (shown / (1.0 + jnp.exp(-shown))).astype(jnp.bfloat16)
+
+
+def attend(whole, flat, query, attn_gain, key_weight, value_weight, out_weight, conv_gain, scale):
     count, width = query.shape
-    total_keys = keys.shape[0]
+    total_keys = whole.shape[0]
     block = 160 if count % 160 == 0 else count
-    flops = 4 * count * total_keys * width
+    full = lambda shape: pl.BlockSpec(shape, lambda i: (0, 0))
+    rows_of = pl.BlockSpec((block, width), lambda i: (i, 0))
+    flops = 4 * count * total_keys * width + 4 * total_keys * width * width
+    flops += 2 * count * width * width
     return pl.pallas_call(
         functools.partial(attention_kernel, scale),
-        out_shape=jax.ShapeDtypeStruct((count, width), jnp.bfloat16),
+        out_shape=(
+            jax.ShapeDtypeStruct((count, width), jnp.bfloat16),
+            jax.ShapeDtypeStruct((count, width), jnp.bfloat16),
+        ),
         grid=(count // block,),
         in_specs=[
-            pl.BlockSpec((block, width), lambda i: (i, 0)),
-            pl.BlockSpec((total_keys, width), lambda i: (0, 0)),
-            pl.BlockSpec((total_keys, width), lambda i: (0, 0)),
+            full((total_keys, width)),
+            rows_of,
+            rows_of,
+            full((1, width)),
+            full((width, width)),
+            full((width, width)),
+            full((width, width)),
+            full((1, width)),
         ],
-        out_specs=pl.BlockSpec((block, width), lambda i: (i, 0)),
+        out_specs=(rows_of, rows_of),
+        scratch_shapes=[
+            pltpu.VMEM((total_keys, width), jnp.bfloat16),
+            pltpu.VMEM((total_keys, width), jnp.bfloat16),
+        ],
         compiler_params=pltpu.CompilerParams(vmem_limit_bytes=60 * 1024 * 1024),
         cost_estimate=pl.CostEstimate(
             flops=flops,
-            transcendentals=count * total_keys,
-            bytes_accessed=2 * width * (2 * count + 2 * total_keys),
+            transcendentals=count * total_keys + count * width,
+            bytes_accessed=2 * width * (total_keys + 4 * count + 3 * width),
         ),
-    )(query, keys, values)
+    )(
+        whole, flat, query, attn_gain.reshape(1, width), key_weight, value_weight, out_weight,
+        conv_gain.reshape(1, width),
+    )
 
 
 def shards(
@@ -96,15 +142,11 @@
     scale = float(np.float32(1.0) / np.sqrt(np.float32(width)))
     whole = strip_gather(flat, "strip")
     normed = rms_scale(flat, attn_gain).astype(jnp.bfloat16)
-    normed_all = rms_scale(whole, attn_gain).astype(jnp.bfloat16)
     query = jnp.dot(normed, query_weight, preferred_element_type=jnp.float32).astype(jnp.bfloat16)
-    keys = jnp.dot(normed_all, key_weight, preferred_element_type=jnp.float32).astype(jnp.bfloat16)
-    values = jnp.dot(normed_all, value_weight, preferred_element_type=jnp.float32).astype(jnp.bfloat16)
-    attended = attend(query, keys, values, scale)
-    resid = (
-        flat.astype(jnp.float32) + jnp.dot(attended, out_weight, preferred_element_type=jnp.float32)
-    ).astype(jnp.bfloat16)
-    act = jax.nn.silu(rms_scale(resid, conv_gain)).astype(jnp.bfloat16).reshape(rows, cols, width)
+    resid, act = attend(
+        whole, flat, query, attn_gain, key_weight, value_weight, out_weight, conv_gain, scale
+    )
+    act = act.reshape(rows, cols, width)
     frame_index = lax.axis_index("tm")
     prior = passed_along(act, "tm", 1)
     prior = jnp.where(frame_index == 0, cache_frames[1], prior)

time: 93.4 us -> 93 us (level)
  matrix products: 18.1 us -> 12 us
  local copies, waits for them, and re-layouts: 4.61 us -> 8.23 us
  Pallas kernels: 6.67 us -> 9.61 us
  waiting for transfers between devices: 32 us -> 30.9 us
    dot_general x3 -> x0, matrix products: 6.06 us -> none  [the longest x1 2.27 us: shards(): jnp.dot(normed_all, value_weight, preferred_element_type=jnp.float32)]
    ppermute x3, waiting for transfers between devices: 13.1 us -> 9.68 us  [strip_gather(): up = lax.ppermute(up, axis, up_pairs)]
    pallas_call x1, Pallas kernels: 6.67 us -> 9.61 us  [attend(): pl.pallas_call(functools.partial(attention_kernel, scale), out_shape=(jax...]
    ppermute x3, waiting for transfers between devices: 5.18 us -> 7.27 us  [strip_gather(): down = lax.ppermute(down, axis, down_pairs)]
    dynamic_slice x0 -> x1, local copies, waits for them, and re-layouts: none -> 1.29 us  [strip_gather(): return lax.dynamic_slice_in_dim(stacked, (n - 1 - me) * m, n * m, axis=0)]
    reshape x0 -> x1, local copies, waits for them, and re-layouts: none -> 1.23 us  [attend(): conv_gain.reshape(1, width)]
    broadcast_in_dim x0 -> x1, local copies, waits for them, and re-layouts: none -> 1.22 us  [rms_scale(): wide * lax.rsqrt(jnp.mean(wide * wide, axis=-1, keepdims=True) + 1e-06)]
    unnamed x24 -> x18, local copies, waits for them, and re-layouts: 2.32 us -> 2.32 us
  transfers between devices with their start and end apart: 10 -> 10, of which waited for: 6 -> 7; matrix products, arithmetic and copies ran while one was open for 12% -> 14% of each run, Pallas kernels for 0% -> 0%
where the time goes in v10:
time: 93 us; the launch traced here: 92.4 us
  waiting for transfers between devices  30.9 us (33%)
  starting transfers between devices  27.5 us (30%)
  matrix products  12 us (13%)
  Pallas kernels  9.61 us (10%)
  local copies, waits for them, and re-layouts  8.23 us (9%)
  other arithmetic  3.77 us (4%)
    ppermute x2, waiting for transfers between devices, passed_along(): return lax.ppermute(x, axis, pairs)  13.9 us
    ppermute x3, starting transfers between devices, strip_gather(): up = lax.ppermute(up, axis, up_pairs)  10.6 us
    ppermute x3, waiting for transfers between devices, strip_gather(): up = lax.ppermute(up, axis, up_pairs)  9.68 us
    pallas_call x1, Pallas kernels, attend(): pl.pallas_call(functools.partial(attention_kernel, scale), out_shape=(jax...  9.61 us
    dot_general x9, matrix products, shards(): jnp.dot(window, kernel[step_t, step_r], preferred_element_type=jnp.float32)  7.67 us
    ppermute x3, waiting for transfers between devices, strip_gather(): down = lax.ppermute(down, axis, down_pairs)  7.27 us
    ppermute x3, starting transfers between devices, strip_gather(): down = lax.ppermute(down, axis, down_pairs)  7.12 us
    ppermute x2, starting transfers between devices, passed_along(): return lax.ppermute(x, axis, pairs)  3.83 us
  transfers between devices with their start and end apart: 10, of which 7 were waited for; matrix products, arithmetic and copies ran while one was open for 14% of the time, Pallas kernels for 0%

profile of v10, /device:TPU:10, one launch (start us, length us, event | category | flops | bytes accessed | tf_op | source)
XLA Modules:
  0.0 92.4 jit_solution(9401991728207200714)
XLA Ops:
  0.0 3.6 %collective-permute-start = (bf16[480,384]{1,0:T(8,128)(2,1)}, bf16[480,384]{1,0:T(8,128)(2,1)S(1)}, u32[]{:S(2)}, u32[]{:S(2)}) collective-permute-start(bf16[480,384]{1,0:T(8,128)(2,1)} %bitcast.122), channel_id=1, source_target_pairs={{0,4},{4,8},{8,12},{1,5},{5,9},{9,13},{2,6},{6,10},{10,14},{3,7},{... | collective-permute-start | bytes 1105928 | tf_op jit(solution)/shard_map/ppermute | solution.py:28
  3.6 2.4 %collective-permute-start.3 = (bf16[480,384]{1,0:T(8,128)(2,1)}, bf16[480,384]{1,0:T(8,128)(2,1)S(1)}, u32[]{:S(2)}, u32[]{:S(2)}) collective-permute-start(bf16[480,384]{1,0:T(8,128)(2,1)} %bitcast.123), channel_id=1, source_target_pairs={{4,0},{8,4},{12,8},{5,1},{9,5},{13,9},{6,2},{10,6},{14,10},{7,3},{... | collective-permute-start | bytes 1105928 | tf_op jit(solution)/shard_map/ppermute | solution.py:29
  6.0 6.6 %collective-permute-done = bf16[480,384]{1,0:T(8,128)(2,1)S(1)} collective-permute-done((bf16[480,384]{1,0:T(8,128)(2,1)}, bf16[480,384]{1,0:T(8,128)(2,1)S(1)}, u32[]{:S(2)}, u32[]{:S(2)}) %collective-permute-start) | collective-permute-done | bytes 368672 | tf_op jit(solution)/shard_map/ppermute | solution.py:28
  12.6 3.5 %collective-permute-start.1 = (bf16[480,384]{1,0:T(8,128)(2,1)S(1)}, bf16[480,384]{1,0:T(8,128)(2,1)S(1)}, u32[]{:S(2)}, u32[]{:S(2)}) collective-permute-start(bf16[480,384]{1,0:T(8,128)(2,1)S(1)} %collective-permute-done), channel_id=1, source_target_pairs={{0,4},{4,8},{8,12},{1,5},{5,9},{9,13},{2,6},{6,10},{10,14},{3,7},{... | collective-permute-start | bytes 1105928 | tf_op jit(solution)/shard_map/ppermute | solution.py:28
  16.0 1.2 %reshape.42.cgain_ref = f32[1,384]{1,0:T(1,128)} reshape(f32[384]{0:T(512)} %param.16) | data formatting | bytes 3072 | tf_op jit(solution)/shard_map/reshape | solution.py:122
  17.3 1.2 %broadcast_in_dim.4.again_ref = f32[1,384]{1,0:T(1,128)} reshape(f32[384]{0:T(512)} %param.11) | data formatting | bytes 3072 | tf_op jit(solution)/shard_map/broadcast_in_dim | solution.py:39
  18.5 1.2 %multiply_reduce_fusion = f32[3,160]{1,0:T(4,128)S(1)} fusion(bf16[1,3,160,384]{3,2,1,0:T(8,128)(2,1)} %param.9), kind=kLoop, calls=%fused_computation.44 | loop fusion | flops 552480 | bytes 370560 | tf_op jit(solution)/shard_map/reduce_sum | solution.py:39
  19.7 2.4 %collective-permute-start.4 = (bf16[480,384]{1,0:T(8,128)(2,1)S(1)}, bf16[480,384]{1,0:T(8,128)(2,1)S(1)}, u32[]{:S(2)}, u32[]{:S(2)}) collective-permute-start(bf16[480,384]{1,0:T(8,128)(2,1)S(1)} %collective-permute-done.3), channel_id=1, source_target_pairs={{4,0},{8,4},{12,8},{5,1},{9,5},{13,9},{6,2},{10,6},{14,10},{7,3},{... | collective-permute-start | bytes 1105928 | tf_op jit(solution)/shard_map/ppermute | solution.py:29
  22.1 1.9 %collective-permute-done.1 = bf16[480,384]{1,0:T(8,128)(2,1)S(1)} collective-permute-done((bf16[480,384]{1,0:T(8,128)(2,1)S(1)}, bf16[480,384]{1,0:T(8,128)(2,1)S(1)}, u32[]{:S(2)}, u32[]{:S(2)}) %collective-permute-start.1) | collective-permute-done | bytes 368672 | tf_op jit(solution)/shard_map/ppermute | solution.py:28
  23.9 3.5 %collective-permute-start.2 = (bf16[480,384]{1,0:T(8,128)(2,1)S(1)}, bf16[480,384]{1,0:T(8,128)(2,1)S(1)}, u32[]{:S(2)}, u32[]{:S(2)}) collective-permute-start(bf16[480,384]{1,0:T(8,128)(2,1)S(1)} %collective-permute-done.1), channel_id=1, source_target_pairs={{0,4},{4,8},{8,12},{1,5},{5,9},{9,13},{2,6},{6,10},{10,14},{3,7},{... | collective-permute-start | bytes 1105928 | tf_op jit(solution)/shard_map/ppermute | solution.py:28
  27.4 0.1 rsqrt.12
  27.5 2.2 %convolution_convert_fusion.query_ref = bf16[480,384]{1,0:T(8,128)(2,1)} fusion(bf16[384,384]{1,0:T(8,128)(2,1)S(1)} %copy-done, bf16[480,384]{1,0:T(8,128)(2,1)} %bitcast.124, f32[384]{0:T(512)} %param.11, f32[480]{0:T(512)S(1)} %rsqrt.12), kind=kOutput, calls=%fused_computation.21 | convolution fusion | flops 142479360 | bytes 1035648 | tf_op jit(solution)/shard_map/dot_general | solution.py:145
  29.7 1.1 %collective-permute-done.4 = bf16[480,384]{1,0:T(8,128)(2,1)S(1)} collective-permute-done((bf16[480,384]{1,0:T(8,128)(2,1)S(1)}, bf16[480,384]{1,0:T(8,128)(2,1)S(1)}, u32[]{:S(2)}, u32[]{:S(2)}) %collective-permute-start.4) | collective-permute-done | bytes 368672 | tf_op jit(solution)/shard_map/ppermute | solution.py:29
  30.8 2.4 %collective-permute-start.5 = (bf16[480,384]{1,0:T(8,128)(2,1)S(1)}, bf16[480,384]{1,0:T(8,128)(2,1)S(1)}, u32[]{:S(2)}, u32[]{:S(2)}) collective-permute-start(bf16[480,384]{1,0:T(8,128)(2,1)S(1)} %collective-permute-done.4), channel_id=1, source_target_pairs={{4,0},{8,4},{12,8},{5,1},{9,5},{13,9},{6,2},{10,6},{14,10},{7,3},{... | collective-permute-start | bytes 1105928 | tf_op jit(solution)/shard_map/ppermute | solution.py:29
  33.1 1.3 %collective-permute-done.2 = bf16[480,384]{1,0:T(8,128)(2,1)S(1)} collective-permute-done((bf16[480,384]{1,0:T(8,128)(2,1)S(1)}, bf16[480,384]{1,0:T(8,128)(2,1)S(1)}, u32[]{:S(2)}, u32[]{:S(2)}) %collective-permute-start.2) | collective-permute-done | bytes 368672 | tf_op jit(solution)/shard_map/ppermute | solution.py:28
  34.8 6.2 %collective-permute-done.5 = bf16[480,384]{1,0:T(8,128)(2,1)S(1)} collective-permute-done((bf16[480,384]{1,0:T(8,128)(2,1)S(1)}, bf16[480,384]{1,0:T(8,128)(2,1)S(1)}, u32[]{:S(2)}, u32[]{:S(2)}) %collective-permute-start.5) | collective-permute-done | bytes 368672 | tf_op jit(solution)/shard_map/ppermute | solution.py:29
  41.0 1.3 %constant_dynamic-slice_fusion.whole_ref = bf16[1920,384]{1,0:T(8,128)(2,1)} fusion(bf16[3360,384]{1,0:T(8,128)(2,1)S(1)} %constant_dynamic-update-slice_fusion, s32[]{:T(128)S(6)} %select_n.15), kind=kLoop, calls=%fused_computation.66 | loop fusion | bytes 2949124 | tf_op jit(solution)/shard_map/dynamic_slice | solution.py:34
  42.3 9.6 %shard_map.91 = (bf16[480,384]{1,0:T(8,128)(2,1)}, bf16[480,384]{1,0:T(8,128)(2,1)}) custom-call(bf16[1920,384]{1,0:T(8,128)(2,1)} %constant_dynamic-slice_fusion.whole_ref, bf16[480,384]{1,0:T(8,128)(2,1)} %bitcast.125, bf16[480,384]{1,0:T(8,128)(2,1)} %convolution_convert_fusion.query_ref, f32[1,384]{1,0:T(1,128)} %broadcast_in_dim.4.again_ref, ...), custom_call_target="tpu_custom_call" | custom-call | flops 2689597440 | bytes 3833856 | tf_op jit(solution)/shard_map/pallas_call | solution.py:92
  52.0 1.9 %collective-permute-start.6 = (bf16[3,160,384]{2,1,0:T(8,128)(2,1)}, bf16[3,160,384]{2,1,0:T(8,128)(2,1)S(1)}, u32[]{:S(2)}, u32[]{:S(2)}) collective-permute-start(bf16[3,160,384]{2,1,0:T(8,128)(2,1)} %bitcast.129), channel_id=1, source_target_pairs={{0,1},{1,2},{2,3},{4,5},{5,6},{6,7},{8,9},{9,10},{10,11},{12,13},{... | collective-permute-start | bytes 1105928 | tf_op jit(solution)/shard_map/ppermute | solution.py:15
  53.9 7.1 %collective-permute-done.6 = bf16[3,160,384]{2,1,0:T(8,128)(2,1)S(1)} collective-permute-done((bf16[3,160,384]{2,1,0:T(8,128)(2,1)}, bf16[3,160,384]{2,1,0:T(8,128)(2,1)S(1)}, u32[]{:S(2)}, u32[]{:S(2)}) %collective-permute-start.6) | collective-permute-done | bytes 368672 | tf_op jit(solution)/shard_map/ppermute | solution.py:15
  61.0 1.9 %collective-permute-start.7 = (bf16[3,160,384]{2,1,0:T(8,128)(2,1)S(1)}, bf16[3,160,384]{2,1,0:T(8,128)(2,1)S(1)}, u32[]{:S(2)}, u32[]{:S(2)}) collective-permute-start(bf16[3,160,384]{2,1,0:T(8,128)(2,1)S(1)} %bitcast_select_fusion), channel_id=1, source_target_pairs={{0,1},{1,2},{2,3},{4,5},{5,6},{6,7},{8,9},{9,10},{10,11},{12,13},{... | collective-permute-start | bytes 1105928 | tf_op jit(solution)/shard_map/ppermute | solution.py:15
  63.0 0.1 pad.6.clone
  63.0 6.8 %collective-permute-done.7 = bf16[3,160,384]{2,1,0:T(8,128)(2,1)S(1)} collective-permute-done((bf16[3,160,384]{2,1,0:T(8,128)(2,1)S(1)}, bf16[3,160,384]{2,1,0:T(8,128)(2,1)S(1)}, u32[]{:S(2)}, u32[]{:S(2)}) %collective-permute-start.7) | collective-permute-done | bytes 368672 | tf_op jit(solution)/shard_map/ppermute | solution.py:15
  69.9 0.1 fusion.12
  69.9 1.8 %select_maximum_fusion = bf16[3,5,162,384]{3,2,1,0:T(8,128)(2,1)S(1)} fusion(bf16[1,3,160,384]{3,2,1,0:T(8,128)(2,1)} %bitcast.130, bf16[1,3,160,384]{3,2,1,0:T(8,128)(2,1)S(1)} %bitcast.127, bf16[1,3,160,384]{3,2,1,0:T(8,128)(2,1)S(1)} %fusion.12), kind=kLoop, calls=%fused_computation.8 | loop fusion | flops 17729280 | bytes 2972160 | tf_op jit(solution)/shard_map/stack | solution.py:155
  71.7 1.0 %fusion.16 = (bf16[3,5,160,384]{3,2,1,0:T(8,128)(2,1)S(1)}, bf16[3,5,160,384]{3,2,1,0:T(8,128)(2,1)S(1)}, bf16[3,5,160,384]{3,2,1,0:T(8,128)(2,1)S(1)}) fusion(bf16[3,5,162,384]{3,2,1,0:T(8,128)(2,1)S(1)} %select_maximum_fusion), kind=kLoop, calls=%fused_computation.68 | loop fusion | bytes 11059200 | tf_op jit(solution)/shard_map/slice | solution.py:158
  72.7 0.6 pad_maximum_fusion
  73.3 0.6 slice-done
  73.9 1.4 %slice-done.1 = s8[3768320]{0:T(1024)(128)(4,1)S(1)} async-done(((s8[7962624]{0:T(1024)(128)(4,1)}), s8[3768320]{0:T(1024)(128)(4,1)S(1)}, s32[]{:S(2)}) %slice-start.1) | async-done | bytes 3768344
  75.3 0.4 fusion.10
  75.6 0.4 fusion.8
  76.0 0.9 %fusion.15 = (bf16[1,3,160,1152]{3,2,1,0:T(8,128)(2,1)S(1)}, bf16[1,3,160,1152]{3,2,1,0:T(8,128)(2,1)S(1)}, bf16[1,3,160,1152]{3,2,1,0:T(8,128)(2,1)S(1)}, bf16[...) fusion(bf16[3,5,160,1152]{3,2,1,0:T(8,128)(2,1)S(1)} %pad_maxim, ...), kind=kLoop, calls=%fused_computation.67 | loop fusion | bytes 19906560 | tf_op jit(solution)/shard_map/slice | solution.py:178
  77.0 0.4 convolution_add_fusion.9
  77.3 0.4 fusion.7
  77.7 2.4 %collective-permute-start.9 = (bf16[160,384]{1,0:T(8,128)(2,1)S(1)}, bf16[160,384]{1,0:T(8,128)(2,1)S(1)}, u32[]{:S(2)}, u32[]{:S(2)}) collective-permute-start(bf16[160,384]{1,0:T(8,128)(2,1)S(1)} %fusion.7), channel_id=1, source_target_pairs={{4,0},{8,4},{12,8},{5,1},{9,5},{13,9},{6,2},{10,6},{14,10},{7,3},{... | collective-permute-start | bytes 368648 | tf_op jit(solution)/shard_map/ppermute | solution.py:169
  80.1 0.4 convolution_add_fusion.11
  80.5 0.4 fusion.6
  80.8 3.6 %collective-permute-start.8 = (bf16[160,384]{1,0:T(8,128)(2,1)S(1)}, bf16[160,384]{1,0:T(8,128)(2,1)S(1)}, u32[]{:S(2)}, u32[]{:S(2)}) collective-permute-start(bf16[160,384]{1,0:T(8,128)(2,1)S(1)} %fusion.6), channel_id=1, source_target_pairs={{0,4},{4,8},{8,12},{1,5},{5,9},{9,13},{2,6},{6,10},{10,14},{3,7},{... | collective-permute-start | bytes 368648 | tf_op jit(solution)/shard_map/ppermute | solution.py:172
  84.5 0.8 fusion.9
  85.3 0.8 convolution_add_fusion.7
  86.1 0.8 convolution_add_fusion.6
  86.8 0.8 convolution_add_fusion.5
  87.6 0.8 convolution_add_fusion.4
  88.4 0.8 convolution_add_fusion.3
  89.2 0.8 convolution_add_fusion.2
  89.9 0.8 convolution_add_fusion.1
  90.8 0.1 pad_maximum_fusion.1
  90.9 1.5 %fusion.11 = bf16[480,384]{1,0:T(8,128)(2,1)} fusion(f32[3,160,384]{2,1,0:T(8,128)S(1)} %pad_maximum_fusion.1, f32[480,384]{1,0:T(8,128)S(1)} %convolution_add_fusion.1, bf16[480,1152]{1,0:T(8,128)(2,1)S(1)} %bitcast.114, bf16[3,3,1152,384]{3,2,1,0:T(8,128)(2,1)S(1)} %bitcast.113), kind=kOutput, calls=%fused_computation.42 | convolution fusion | flops 425226240 | bytes 3833856 | tf_op jit(solution)/shard_map/dot_general | solution.py:179
  (25 shorter events, 0.5 us)
Async XLA Ops:
  0.0 27.5 %copy-start = (bf16[384,384]{1,0:T(8,128)(2,1)S(1)}, bf16[384,384]{1,0:T(8,128)(2,1)}, u32[]{:S(2)}) copy-start(bf16[384,384]{1,0:T(8,128)(2,1)} %param.12) | copy-start | bytes 884740
  0.0 34.6 %copy-start.1 = (bf16[1,3,160,384]{3,2,1,0:T(8,128)(2,1)S(1)}, bf16[1,3,160,384]{3,2,1,0:T(8,128)(2,1)}, u32[]{:S(2)}) copy-start(bf16[1,3,160,384]{3,2,1,0:T(8,128)(2,1)} %param.9) | copy-start | bytes 1105924
  0.0 12.6 %collective-permute-start = (bf16[480,384]{1,0:T(8,128)(2,1)}, bf16[480,384]{1,0:T(8,128)(2,1)S(1)}, u32[]{:S(2)}, u32[]{:S(2)}) collective-permute-start(bf16[480,384]{1,0:T(8,128)(2,1)} %bitcast.122), channel_id=1, source_target_pairs={{0,4},{4,8},{8,12},{1,5},{5,9},{9,13},{2,6},{6,10},{10,14},{3,7},{... | collective-permute-start | bytes 1105928 | tf_op jit(solution)/shard_map/ppermute | solution.py:28
  3.6 16.1 %collective-permute-start.3 = (bf16[480,384]{1,0:T(8,128)(2,1)}, bf16[480,384]{1,0:T(8,128)(2,1)S(1)}, u32[]{:S(2)}, u32[]{:S(2)}) collective-permute-start(bf16[480,384]{1,0:T(8,128)(2,1)} %bitcast.123), channel_id=1, source_target_pairs={{4,0},{8,4},{12,8},{5,1},{9,5},{13,9},{6,2},{10,6},{14,10},{7,3},{... | collective-permute-start | bytes 1105928 | tf_op jit(solution)/shard_map/ppermute | solution.py:29
  12.6 11.4 %collective-permute-start.1 = (bf16[480,384]{1,0:T(8,128)(2,1)S(1)}, bf16[480,384]{1,0:T(8,128)(2,1)S(1)}, u32[]{:S(2)}, u32[]{:S(2)}) collective-permute-start(bf16[480,384]{1,0:T(8,128)(2,1)S(1)} %collective-permute-done), channel_id=1, source_target_pairs={{0,4},{4,8},{8,12},{1,5},{5,9},{9,13},{2,6},{6,10},{10,14},{3,7},{... | collective-permute-start | bytes 1105928 | tf_op jit(solution)/shard_map/ppermute | solution.py:28
  19.7 11.1 %collective-permute-start.4 = (bf16[480,384]{1,0:T(8,128)(2,1)S(1)}, bf16[480,384]{1,0:T(8,128)(2,1)S(1)}, u32[]{:S(2)}, u32[]{:S(2)}) collective-permute-start(bf16[480,384]{1,0:T(8,128)(2,1)S(1)} %collective-permute-done.3), channel_id=1, source_target_pairs={{4,0},{8,4},{12,8},{5,1},{9,5},{13,9},{6,2},{10,6},{14,10},{7,3},{... | collective-permute-start | bytes 1105928 | tf_op jit(solution)/shard_map/ppermute | solution.py:29
  23.9 10.5 %collective-permute-start.2 = (bf16[480,384]{1,0:T(8,128)(2,1)S(1)}, bf16[480,384]{1,0:T(8,128)(2,1)S(1)}, u32[]{:S(2)}, u32[]{:S(2)}) collective-permute-start(bf16[480,384]{1,0:T(8,128)(2,1)S(1)} %collective-permute-done.1), channel_id=1, source_target_pairs={{0,4},{4,8},{8,12},{1,5},{5,9},{9,13},{2,6},{6,10},{10,14},{3,7},{... | collective-permute-start | bytes 1105928 | tf_op jit(solution)/shard_map/ppermute | solution.py:28
  30.8 10.2 %collective-permute-start.5 = (bf16[480,384]{1,0:T(8,128)(2,1)S(1)}, bf16[480,384]{1,0:T(8,128)(2,1)S(1)}, u32[]{:S(2)}, u32[]{:S(2)}) collective-permute-start(bf16[480,384]{1,0:T(8,128)(2,1)S(1)} %collective-permute-done.4), channel_id=1, source_target_pairs={{4,0},{8,4},{12,8},{5,1},{9,5},{13,9},{6,2},{10,6},{14,10},{7,3},{... | collective-permute-start | bytes 1105928 | tf_op jit(solution)/shard_map/ppermute | solution.py:29
  42.3 18.6 %copy-start.2 = (bf16[2,3,160,384]{3,2,1,0:T(8,128)(2,1)S(1)}, bf16[2,3,160,384]{3,2,1,0:T(8,128)(2,1)}, u32[]{:S(2)}) copy-start(bf16[2,3,160,384]{3,2,1,0:T(8,128)(2,1)} %param.10) | copy-start | bytes 2211844
  52.0 9.0 %collective-permute-start.6 = (bf16[3,160,384]{2,1,0:T(8,128)(2,1)}, bf16[3,160,384]{2,1,0:T(8,128)(2,1)S(1)}, u32[]{:S(2)}, u32[]{:S(2)}) collective-permute-start(bf16[3,160,384]{2,1,0:T(8,128)(2,1)} %bitcast.129), channel_id=1, source_target_pairs={{0,1},{1,2},{2,3},{4,5},{5,6},{6,7},{8,9},{9,10},{10,11},{12,13},{... | collective-permute-start | bytes 1105928 | tf_op jit(solution)/shard_map/ppermute | solution.py:15
  61.0 8.8 %collective-permute-start.7 = (bf16[3,160,384]{2,1,0:T(8,128)(2,1)S(1)}, bf16[3,160,384]{2,1,0:T(8,128)(2,1)S(1)}, u32[]{:S(2)}, u32[]{:S(2)}) collective-permute-start(bf16[3,160,384]{2,1,0:T(8,128)(2,1)S(1)} %bitcast_select_fusion), channel_id=1, source_target_pairs={{0,1},{1,2},{2,3},{4,5},{5,6},{6,7},{8,9},{9,10},{10,11},{12,13},{... | collective-permute-start | bytes 1105928 | tf_op jit(solution)/shard_map/ppermute | solution.py:15
  71.7 2.2 %slice-start = ((s8[7962624]{0:T(1024)(128)(4,1)}), s8[4194304]{0:T(1024)(128)(4,1)S(1)}, s32[]{:S(2)}) async-start(s8[7962624]{0:T(1024)(128)(4,1)} %bitcast.97), calls=%async_computation | async-start | bytes 8388608
  72.7 2.5 %slice-start.1 = ((s8[7962624]{0:T(1024)(128)(4,1)}), s8[3768320]{0:T(1024)(128)(4,1)S(1)}, s32[]{:S(2)}) async-start(s8[7962624]{0:T(1024)(128)(4,1)} %bitcast.97), calls=%async_computation.1 | async-start | bytes 7536640
  77.7 13.0 %collective-permute-start.9 = (bf16[160,384]{1,0:T(8,128)(2,1)S(1)}, bf16[160,384]{1,0:T(8,128)(2,1)S(1)}, u32[]{:S(2)}, u32[]{:S(2)}) collective-permute-start(bf16[160,384]{1,0:T(8,128)(2,1)S(1)} %fusion.7), channel_id=1, source_target_pairs={{4,0},{8,4},{12,8},{5,1},{9,5},{13,9},{6,2},{10,6},{14,10},{7,3},{... | collective-permute-start | bytes 368648 | tf_op jit(solution)/shard_map/ppermute | solution.py:169
  80.5 4.8 %copy-start.3 = (bf16[480,384]{1,0:T(8,128)(2,1)S(1)}, bf16[480,384]{1,0:T(8,128)(2,1)}, u32[]{:S(2)}) copy-start(bf16[480,384]{1,0:T(8,128)(2,1)} %get-tuple-element.7) | copy-start | bytes 1105924
  80.8 9.9 %collective-permute-start.8 = (bf16[160,384]{1,0:T(8,128)(2,1)S(1)}, bf16[160,384]{1,0:T(8,128)(2,1)S(1)}, u32[]{:S(2)}, u32[]{:S(2)}) collective-permute-start(bf16[160,384]{1,0:T(8,128)(2,1)S(1)} %fusion.6), channel_id=1, source_target_pairs={{0,4},{4,8},{8,12},{1,5},{5,9},{9,13},{2,6},{6,10},{10,14},{3,7},{... | collective-permute-start | bytes 368648 | tf_op jit(solution)/shard_map/ppermute | solution.py:172

commit v11 on v10

--- a/solution.py
+++ b/solution.py
@@ -152,19 +152,29 @@
     prior = jnp.where(frame_index == 0, cache_frames[1], prior)
     older = passed_along(prior, "tm", 1)
     older = jnp.where(frame_index == 0, cache_frames[0], older)
-    stacked = jnp.stack([older, prior, act])
-    padded = jnp.pad(stacked, ((0, 0), (1, 1), (1, 1), (0, 0)))
-    widened = jnp.concatenate(
-        [padded[:, :, 0:cols], padded[:, :, 1 : cols + 1], padded[:, :, 2 : cols + 2]], axis=-1
-    )
     kernel = conv_weight.reshape(3, 3, 3 * width, width)
-    to_prev = None
-    to_next = None
-    for step_t in range(3):
-        first = jnp.dot(widened[step_t, 1], kernel[step_t, 2], preferred_element_type=jnp.float32)
-        last = jnp.dot(widened[step_t, rows], kernel[step_t, 0], preferred_element_type=jnp.float32)
-        to_prev = first if to_prev is None else to_prev + first
-        to_next = last if to_next is None else to_next + last
+
+    def widen(frame):
+        padded = jnp.pad(frame, ((1, 1), (1, 1), (0, 0)))
+        return jnp.concatenate(
+            [padded[:, 0:cols], padded[:, 1 : cols + 1], padded[:, 2 : cols + 2]], axis=-1
+        )
+
+    def frame_terms(wide, step_t):
+        main = None
+        for step_r in range(3):
+            window = wide[step_r : step_r + rows].reshape(-1, 3 * width)
+            part = jnp.dot(window, kernel[step_t, step_r], preferred_element_type=jnp.float32)
+            main = part if main is None else main + part
+        first = jnp.dot(wide[1], kernel[step_t, 2], preferred_element_type=jnp.float32)
+        last = jnp.dot(wide[rows], kernel[step_t, 0], preferred_element_type=jnp.float32)
+        return main, first, last
+
+    own_main, own_first, own_last = frame_terms(widen(act), 2)
+    prior_main, prior_first, prior_last = frame_terms(widen(prior), 1)
+    older_main, older_first, older_last = frame_terms(widen(older), 0)
+    to_prev = own_first + prior_first + older_first
+    to_next = own_last + prior_last + older_last
     n = lax.axis_size("strip")
     from_next = lax.ppermute(
         to_prev.astype(jnp.bfloat16), "strip", [(i + 1, i) for i in range(n - 1)]
@@ -172,13 +182,7 @@
     from_prev = lax.ppermute(
         to_next.astype(jnp.bfloat16), "strip", [(i, i + 1) for i in range(n - 1)]
     )
-    result = resid.astype(jnp.float32)
-    for step_t in range(3):
-        for step_r in range(3):
-            window = widened[step_t, step_r : step_r + rows].reshape(-1, 3 * width)
-            result = result + jnp.dot(
-                window, kernel[step_t, step_r], preferred_element_type=jnp.float32
-            )
+    result = resid.astype(jnp.float32) + own_main + prior_main + older_main
     edges = jnp.concatenate(
         [
             from_prev[None].astype(jnp.float32),

time: 93 us -> 83.3 us (0.90)
  waiting for transfers between devices: 30.9 us -> 23.6 us
  other arithmetic: 3.77 us -> 2.04 us
  local copies, waits for them, and re-layouts: 8.23 us -> 7.17 us
    ppermute x2, waiting for transfers between devices: 13.9 us -> 5 us  [passed_along(): return lax.ppermute(x, axis, pairs)]
    unnamed x18, local copies, waits for them, and re-layouts: 2.32 us -> 0.37 us
    another operation x2 -> x0, other arithmetic: 1.82 us -> none  [shards(): stacked = jnp.stack([older, prior, act])]
    ppermute x1, waiting for transfers between devices: 0.01 us -> 1.71 us  [shards(): lax.ppermute(to_next.astype(jnp.bfloat16), 'strip', [(i, i + 1) for i in...]
    slice x2 -> x6, local copies, waits for them, and re-layouts: 1.96 us -> 2.75 us  [the longest x3 1.97 us: widen(): padded[:, 0:cols]]
  transfers between devices with their start and end apart: 10 -> 10, of which waited for: 7 -> 8; matrix products, arithmetic and copies ran while one was open for 14% -> 21% of each run, Pallas kernels for 0% -> 0%
where the time goes in v11:
time: 83.3 us; the launch traced here: 82.8 us
  starting transfers between devices  27.8 us (33%)
  waiting for transfers between devices  23.6 us (28%)
  matrix products  12.1 us (15%)
  Pallas kernels  9.71 us (12%)
  local copies, waits for them, and re-layouts  7.17 us (9%)
  other arithmetic  2.04 us (2%)
    ppermute x3, starting transfers between devices, strip_gather(): up = lax.ppermute(up, axis, up_pairs)  10.6 us
    pallas_call x1, Pallas kernels, attend(): pl.pallas_call(functools.partial(attention_kernel, scale), out_shape=(jax...  9.71 us
    ppermute x3, waiting for transfers between devices, strip_gather(): up = lax.ppermute(up, axis, up_pairs)  9.35 us
    dot_general x9, matrix products, frame_terms(): jnp.dot(window, kernel[step_t, step_r], preferred_element_type=jnp.float32)  7.77 us
    ppermute x3, waiting for transfers between devices, strip_gather(): down = lax.ppermute(down, axis, down_pairs)  7.53 us
    ppermute x3, starting transfers between devices, strip_gather(): down = lax.ppermute(down, axis, down_pairs)  7.12 us
    ppermute x2, waiting for transfers between devices, passed_along(): return lax.ppermute(x, axis, pairs)  5 us
    ppermute x2, starting transfers between devices, passed_along(): return lax.ppermute(x, axis, pairs)  4.28 us
  transfers between devices with their start and end apart: 10, of which 8 were waited for; matrix products, arithmetic and copies ran while one was open for 21% of the time, Pallas kernels for 0%

profile of v11, /device:TPU:10, one launch (start us, length us, event | category | flops | bytes accessed | tf_op | source)
XLA Modules:
  0.0 82.8 jit_solution(761056465621053704)
XLA Ops:
  0.0 3.6 %collective-permute-start = (bf16[480,384]{1,0:T(8,128)(2,1)}, bf16[480,384]{1,0:T(8,128)(2,1)S(1)}, u32[]{:S(2)}, u32[]{:S(2)}) collective-permute-start(bf16[480,384]{1,0:T(8,128)(2,1)} %bitcast.114), channel_id=1, source_target_pairs={{0,4},{4,8},{8,12},{1,5},{5,9},{9,13},{2,6},{6,10},{10,14},{3,7},{... | collective-permute-start | bytes 1105928 | tf_op jit(solution)/shard_map/ppermute | solution.py:28
  3.6 2.4 %collective-permute-start.3 = (bf16[480,384]{1,0:T(8,128)(2,1)}, bf16[480,384]{1,0:T(8,128)(2,1)S(1)}, u32[]{:S(2)}, u32[]{:S(2)}) collective-permute-start(bf16[480,384]{1,0:T(8,128)(2,1)} %bitcast.115), channel_id=1, source_target_pairs={{4,0},{8,4},{12,8},{5,1},{9,5},{13,9},{6,2},{10,6},{14,10},{7,3},{... | collective-permute-start | bytes 1105928 | tf_op jit(solution)/shard_map/ppermute | solution.py:29
  6.0 6.6 %collective-permute-done = bf16[480,384]{1,0:T(8,128)(2,1)S(1)} collective-permute-done((bf16[480,384]{1,0:T(8,128)(2,1)}, bf16[480,384]{1,0:T(8,128)(2,1)S(1)}, u32[]{:S(2)}, u32[]{:S(2)}) %collective-permute-start) | collective-permute-done | bytes 368672 | tf_op jit(solution)/shard_map/ppermute | solution.py:28
  12.6 3.5 %collective-permute-start.1 = (bf16[480,384]{1,0:T(8,128)(2,1)S(1)}, bf16[480,384]{1,0:T(8,128)(2,1)S(1)}, u32[]{:S(2)}, u32[]{:S(2)}) collective-permute-start(bf16[480,384]{1,0:T(8,128)(2,1)S(1)} %collective-permute-done), channel_id=1, source_target_pairs={{0,4},{4,8},{8,12},{1,5},{5,9},{9,13},{2,6},{6,10},{10,14},{3,7},{... | collective-permute-start | bytes 1105928 | tf_op jit(solution)/shard_map/ppermute | solution.py:28
  16.0 1.3 %reshape.69.cgain_ref = f32[1,384]{1,0:T(1,128)} reshape(f32[384]{0:T(512)} %param.16) | data formatting | bytes 3072 | tf_op jit(solution)/shard_map/reshape | solution.py:122
  17.3 1.3 %broadcast_in_dim.4.again_ref = f32[1,384]{1,0:T(1,128)} reshape(f32[384]{0:T(512)} %param.11) | data formatting | bytes 3072 | tf_op jit(solution)/shard_map/broadcast_in_dim | solution.py:39
  18.6 1.2 %multiply_reduce_fusion = f32[3,160]{1,0:T(4,128)S(1)} fusion(bf16[1,3,160,384]{3,2,1,0:T(8,128)(2,1)} %param.9), kind=kLoop, calls=%fused_computation.45 | loop fusion | flops 552480 | bytes 370560 | tf_op jit(solution)/shard_map/reduce_sum | solution.py:39
  19.8 2.4 %collective-permute-start.4 = (bf16[480,384]{1,0:T(8,128)(2,1)S(1)}, bf16[480,384]{1,0:T(8,128)(2,1)S(1)}, u32[]{:S(2)}, u32[]{:S(2)}) collective-permute-start(bf16[480,384]{1,0:T(8,128)(2,1)S(1)} %collective-permute-done.3), channel_id=1, source_target_pairs={{4,0},{8,4},{12,8},{5,1},{9,5},{13,9},{6,2},{10,6},{14,10},{7,3},{... | collective-permute-start | bytes 1105928 | tf_op jit(solution)/shard_map/ppermute | solution.py:29
  22.2 1.7 %collective-permute-done.1 = bf16[480,384]{1,0:T(8,128)(2,1)S(1)} collective-permute-done((bf16[480,384]{1,0:T(8,128)(2,1)S(1)}, bf16[480,384]{1,0:T(8,128)(2,1)S(1)}, u32[]{:S(2)}, u32[]{:S(2)}) %collective-permute-start.1) | collective-permute-done | bytes 368672 | tf_op jit(solution)/shard_map/ppermute | solution.py:28
  23.9 3.5 %collective-permute-start.2 = (bf16[480,384]{1,0:T(8,128)(2,1)S(1)}, bf16[480,384]{1,0:T(8,128)(2,1)S(1)}, u32[]{:S(2)}, u32[]{:S(2)}) collective-permute-start(bf16[480,384]{1,0:T(8,128)(2,1)S(1)} %collective-permute-done.1), channel_id=1, source_target_pairs={{0,4},{4,8},{8,12},{1,5},{5,9},{9,13},{2,6},{6,10},{10,14},{3,7},{... | collective-permute-start | bytes 1105928 | tf_op jit(solution)/shard_map/ppermute | solution.py:28
  27.6 2.2 %convolution_convert_fusion.query_ref = bf16[480,384]{1,0:T(8,128)(2,1)} fusion(bf16[384,384]{1,0:T(8,128)(2,1)S(1)} %copy-done, bf16[480,384]{1,0:T(8,128)(2,1)} %bitcast.116, f32[384]{0:T(512)} %param.11, f32[480]{0:T(512)S(1)} %rsqrt.12), kind=kOutput, calls=%fused_computation.11 | convolution fusion | flops 142479360 | bytes 1035648 | tf_op jit(solution)/shard_map/dot_general | solution.py:145
  29.7 1.2 %collective-permute-done.4 = bf16[480,384]{1,0:T(8,128)(2,1)S(1)} collective-permute-done((bf16[480,384]{1,0:T(8,128)(2,1)S(1)}, bf16[480,384]{1,0:T(8,128)(2,1)S(1)}, u32[]{:S(2)}, u32[]{:S(2)}) %collective-permute-start.4) | collective-permute-done | bytes 368672 | tf_op jit(solution)/shard_map/ppermute | solution.py:29
  30.9 2.4 %collective-permute-start.5 = (bf16[480,384]{1,0:T(8,128)(2,1)S(1)}, bf16[480,384]{1,0:T(8,128)(2,1)S(1)}, u32[]{:S(2)}, u32[]{:S(2)}) collective-permute-start(bf16[480,384]{1,0:T(8,128)(2,1)S(1)} %collective-permute-done.4), channel_id=1, source_target_pairs={{4,0},{8,4},{12,8},{5,1},{9,5},{13,9},{6,2},{10,6},{14,10},{7,3},{... | collective-permute-start | bytes 1105928 | tf_op jit(solution)/shard_map/ppermute | solution.py:29
  33.3 1.1 %collective-permute-done.2 = bf16[480,384]{1,0:T(8,128)(2,1)S(1)} collective-permute-done((bf16[480,384]{1,0:T(8,128)(2,1)S(1)}, bf16[480,384]{1,0:T(8,128)(2,1)S(1)}, u32[]{:S(2)}, u32[]{:S(2)}) %collective-permute-start.2) | collective-permute-done | bytes 368672 | tf_op jit(solution)/shard_map/ppermute | solution.py:28
  34.8 6.3 %collective-permute-done.5 = bf16[480,384]{1,0:T(8,128)(2,1)S(1)} collective-permute-done((bf16[480,384]{1,0:T(8,128)(2,1)S(1)}, bf16[480,384]{1,0:T(8,128)(2,1)S(1)}, u32[]{:S(2)}, u32[]{:S(2)}) %collective-permute-start.5) | collective-permute-done | bytes 368672 | tf_op jit(solution)/shard_map/ppermute | solution.py:29
  41.2 1.3 %constant_dynamic-slice_fusion.whole_ref = bf16[1920,384]{1,0:T(8,128)(2,1)} fusion(bf16[3360,384]{1,0:T(8,128)(2,1)S(1)} %constant_dynamic-update-slice_fusion, s32[]{:T(128)S(6)} %select_n.15), kind=kLoop, calls=%fused_computation.66 | loop fusion | bytes 2949124 | tf_op jit(solution)/shard_map/dynamic_slice | solution.py:34
  42.5 9.7 %shard_map.91 = (bf16[480,384]{1,0:T(8,128)(2,1)}, bf16[480,384]{1,0:T(8,128)(2,1)}) custom-call(bf16[1920,384]{1,0:T(8,128)(2,1)} %constant_dynamic-slice_fusion.whole_ref, bf16[480,384]{1,0:T(8,128)(2,1)} %bitcast.117, bf16[480,384]{1,0:T(8,128)(2,1)} %convolution_convert_fusion.query_ref, f32[1,384]{1,0:T(1,128)} %broadcast_in_dim.4.again_ref, ...), custom_call_target="tpu_custom_call" | custom-call | flops 2689597440 | bytes 3833856 | tf_op jit(solution)/shard_map/pallas_call | solution.py:92
  52.2 2.2 %collective-permute-start.6 = (bf16[3,160,384]{2,1,0:T(8,128)(2,1)}, bf16[3,160,384]{2,1,0:T(8,128)(2,1)S(1)}, u32[]{:S(2)}, u32[]{:S(2)}) collective-permute-start(bf16[3,160,384]{2,1,0:T(8,128)(2,1)} %bitcast.122), channel_id=1, source_target_pairs={{0,1},{1,2},{2,3},{4,5},{5,6},{6,7},{8,9},{9,10},{10,11},{12,13},{... | collective-permute-start | bytes 1105928 | tf_op jit(solution)/shard_map/ppermute | solution.py:15
  54.4 1.5 %pad_slice_fusion.8 = (bf16[5,160,384]{2,1,0:T(8,128)(2,1)S(1)}, bf16[5,160,384]{2,1,0:T(8,128)(2,1)S(1)}, bf16[5,160,384]{2,1,0:T(8,128)(2,1)S(1)}) fusion(bf16[3,160,384]{2,1,0:T(8,128)(2,1)} %bitcast.123), kind=kLoop, calls=%fused_computation.40 | loop fusion | bytes 2211840 | tf_op jit(solution)/shard_map/slice | solution.py:160
  55.9 0.2 pad_maximum_fusion
  56.0 0.3 fusion.13
  56.3 0.4 fusion.6
  56.7 0.8 fusion.5
  57.5 0.8 convolution_add_fusion.5
  58.2 0.4 fusion.4
  58.6 0.8 convolution_add_fusion.4
  59.4 2.1 %collective-permute-done.6 = bf16[3,160,384]{2,1,0:T(8,128)(2,1)S(1)} collective-permute-done((bf16[3,160,384]{2,1,0:T(8,128)(2,1)}, bf16[3,160,384]{2,1,0:T(8,128)(2,1)S(1)}, u32[]{:S(2)}, u32[]{:S(2)}) %collective-permute-start.6) | collective-permute-done | bytes 368672 | tf_op jit(solution)/shard_map/ppermute | solution.py:15
  61.6 2.1 %collective-permute-start.7 = (bf16[3,160,384]{2,1,0:T(8,128)(2,1)S(1)}, bf16[3,160,384]{2,1,0:T(8,128)(2,1)S(1)}, u32[]{:S(2)}, u32[]{:S(2)}) collective-permute-start(bf16[3,160,384]{2,1,0:T(8,128)(2,1)S(1)} %bitcast_select_fusion.1), channel_id=1, source_target_pairs={{0,1},{1,2},{2,3},{4,5},{5,6},{6,7},{8,9},{9,10},{10,11},{12,13},{... | collective-permute-start | bytes 1105928 | tf_op jit(solution)/shard_map/ppermute | solution.py:15
  63.7 0.3 pad_slice_fusion.5
  64.0 0.2 pad_maximum_fusion.1
  64.1 0.3 fusion.14
  64.4 0.4 convolution_add_fusion.7
  64.8 0.8 fusion.7
  65.6 0.8 convolution_add_fusion.3
  66.3 0.4 convolution_add_fusion.9
  66.7 0.8 fusion.1
  67.5 2.9 %collective-permute-done.7 = bf16[3,160,384]{2,1,0:T(8,128)(2,1)S(1)} collective-permute-done((bf16[3,160,384]{2,1,0:T(8,128)(2,1)S(1)}, bf16[3,160,384]{2,1,0:T(8,128)(2,1)S(1)}, u32[]{:S(2)}, u32[]{:S(2)}) %collective-permute-start.7) | collective-permute-done | bytes 368672 | tf_op jit(solution)/shard_map/ppermute | solution.py:15
  70.5 0.3 pad_slice_fusion.2
  70.7 0.2 pad_maximum_fusion.2
  70.9 0.3 fusion.12
  71.2 0.4 fusion.3
  71.6 2.4 %collective-permute-start.9 = (bf16[160,384]{1,0:T(8,128)(2,1)S(1)}, bf16[160,384]{1,0:T(8,128)(2,1)S(1)}, u32[]{:S(2)}, u32[]{:S(2)}) collective-permute-start(bf16[160,384]{1,0:T(8,128)(2,1)S(1)} %fusion.3), channel_id=1, source_target_pairs={{4,0},{8,4},{12,8},{5,1},{9,5},{13,9},{6,2},{10,6},{14,10},{7,3},{... | collective-permute-start | bytes 368648 | tf_op jit(solution)/shard_map/ppermute | solution.py:179
  74.0 0.4 fusion.2
  74.3 3.5 %collective-permute-start.8 = (bf16[160,384]{1,0:T(8,128)(2,1)S(1)}, bf16[160,384]{1,0:T(8,128)(2,1)S(1)}, u32[]{:S(2)}, u32[]{:S(2)}) collective-permute-start(bf16[160,384]{1,0:T(8,128)(2,1)S(1)} %fusion.2), channel_id=1, source_target_pairs={{0,4},{4,8},{8,12},{1,5},{5,9},{9,13},{2,6},{6,10},{10,14},{3,7},{... | collective-permute-start | bytes 368648 | tf_op jit(solution)/shard_map/ppermute | solution.py:182
  77.8 0.8 fusion.8
  78.6 0.8 convolution_add_fusion.1
  79.4 1.7 %collective-permute-done.8 = bf16[160,384]{1,0:T(8,128)(2,1)S(1)} collective-permute-done((bf16[160,384]{1,0:T(8,128)(2,1)S(1)}, bf16[160,384]{1,0:T(8,128)(2,1)S(1)}, u32[]{:S(2)}, u32[]{:S(2)}) %collective-permute-start.8) | collective-permute-done | bytes 122912 | tf_op jit(solution)/shard_map/ppermute | solution.py:182
  81.2 1.6 %fusion.9 = bf16[480,384]{1,0:T(8,128)(2,1)} fusion(f32[3,160,384]{2,1,0:T(8,128)S(1)} %pad_maximum_fusion.3, f32[480,384]{1,0:T(8,128)S(1)} %fusion.1, f32[480,384]{1,0:T(8,128)S(1)} %convolution_add_fusion.1, bf16[480,1152]{1,0:T(8,128)(2,1)S(1)} %bitcast.91, bf16[3,3,1152,384]{3,2,1,0:T(8,128)(2,1)S(1)} %bitcast.113), kind=kOutput, calls=%fused_computation.43 | convolution fusion | flops 425410560 | bytes 4571136 | tf_op jit(solution)/shard_map/dot_general | solution.py:167
  (30 shorter events, 0.9 us)
Async XLA Ops:
  0.0 27.6 %copy-start = (bf16[384,384]{1,0:T(8,128)(2,1)S(1)}, bf16[384,384]{1,0:T(8,128)(2,1)}, u32[]{:S(2)}) copy-start(bf16[384,384]{1,0:T(8,128)(2,1)} %param.12) | copy-start | bytes 884740
  0.0 12.6 %collective-permute-start = (bf16[480,384]{1,0:T(8,128)(2,1)}, bf16[480,384]{1,0:T(8,128)(2,1)S(1)}, u32[]{:S(2)}, u32[]{:S(2)}) collective-permute-start(bf16[480,384]{1,0:T(8,128)(2,1)} %bitcast.114), channel_id=1, source_target_pairs={{0,4},{4,8},{8,12},{1,5},{5,9},{9,13},{2,6},{6,10},{10,14},{3,7},{... | collective-permute-start | bytes 1105928 | tf_op jit(solution)/shard_map/ppermute | solution.py:28
  3.6 16.2 %collective-permute-start.3 = (bf16[480,384]{1,0:T(8,128)(2,1)}, bf16[480,384]{1,0:T(8,128)(2,1)S(1)}, u32[]{:S(2)}, u32[]{:S(2)}) collective-permute-start(bf16[480,384]{1,0:T(8,128)(2,1)} %bitcast.115), channel_id=1, source_target_pairs={{4,0},{8,4},{12,8},{5,1},{9,5},{13,9},{6,2},{10,6},{14,10},{7,3},{... | collective-permute-start | bytes 1105928 | tf_op jit(solution)/shard_map/ppermute | solution.py:29
  12.6 11.4 %collective-permute-start.1 = (bf16[480,384]{1,0:T(8,128)(2,1)S(1)}, bf16[480,384]{1,0:T(8,128)(2,1)S(1)}, u32[]{:S(2)}, u32[]{:S(2)}) collective-permute-start(bf16[480,384]{1,0:T(8,128)(2,1)S(1)} %collective-permute-done), channel_id=1, source_target_pairs={{0,4},{4,8},{8,12},{1,5},{5,9},{9,13},{2,6},{6,10},{10,14},{3,7},{... | collective-permute-start | bytes 1105928 | tf_op jit(solution)/shard_map/ppermute | solution.py:28
  18.6 16.0 %copy-start.1 = (bf16[1,3,160,384]{3,2,1,0:T(8,128)(2,1)S(1)}, bf16[1,3,160,384]{3,2,1,0:T(8,128)(2,1)}, u32[]{:S(2)}) copy-start(bf16[1,3,160,384]{3,2,1,0:T(8,128)(2,1)} %param.9) | copy-start | bytes 1105924
  19.8 11.1 %collective-permute-start.4 = (bf16[480,384]{1,0:T(8,128)(2,1)S(1)}, bf16[480,384]{1,0:T(8,128)(2,1)S(1)}, u32[]{:S(2)}, u32[]{:S(2)}) collective-permute-start(bf16[480,384]{1,0:T(8,128)(2,1)S(1)} %collective-permute-done.3), channel_id=1, source_target_pairs={{4,0},{8,4},{12,8},{5,1},{9,5},{13,9},{6,2},{10,6},{14,10},{7,3},{... | collective-permute-start | bytes 1105928 | tf_op jit(solution)/shard_map/ppermute | solution.py:29
  23.9 10.5 %collective-permute-start.2 = (bf16[480,384]{1,0:T(8,128)(2,1)S(1)}, bf16[480,384]{1,0:T(8,128)(2,1)S(1)}, u32[]{:S(2)}, u32[]{:S(2)}) collective-permute-start(bf16[480,384]{1,0:T(8,128)(2,1)S(1)} %collective-permute-done.1), channel_id=1, source_target_pairs={{0,4},{4,8},{8,12},{1,5},{5,9},{9,13},{2,6},{6,10},{10,14},{3,7},{... | collective-permute-start | bytes 1105928 | tf_op jit(solution)/shard_map/ppermute | solution.py:28
  30.9 10.2 %collective-permute-start.5 = (bf16[480,384]{1,0:T(8,128)(2,1)S(1)}, bf16[480,384]{1,0:T(8,128)(2,1)S(1)}, u32[]{:S(2)}, u32[]{:S(2)}) collective-permute-start(bf16[480,384]{1,0:T(8,128)(2,1)S(1)} %collective-permute-done.4), channel_id=1, source_target_pairs={{4,0},{8,4},{12,8},{5,1},{9,5},{13,9},{6,2},{10,6},{14,10},{7,3},{... | collective-permute-start | bytes 1105928 | tf_op jit(solution)/shard_map/ppermute | solution.py:29
  42.5 13.8 %slice-start = ((s8[7962624]{0:T(1024)(128)(4,1)}), s8[3768320]{0:T(1024)(128)(4,1)S(1)}, s32[]{:S(2)}) async-start(s8[7962624]{0:T(1024)(128)(4,1)} %bitcast.97), calls=%async_computation | async-start | bytes 7536640
  52.2 4.1 %slice-start.1 = ((s8[7962624]{0:T(1024)(128)(4,1)}), s8[4194304]{0:T(1024)(128)(4,1)S(1)}, s32[]{:S(2)}) async-start(s8[7962624]{0:T(1024)(128)(4,1)} %bitcast.97), calls=%async_computation.1 | async-start | bytes 8388608
  52.2 9.3 %collective-permute-start.6 = (bf16[3,160,384]{2,1,0:T(8,128)(2,1)}, bf16[3,160,384]{2,1,0:T(8,128)(2,1)S(1)}, u32[]{:S(2)}, u32[]{:S(2)}) collective-permute-start(bf16[3,160,384]{2,1,0:T(8,128)(2,1)} %bitcast.122), channel_id=1, source_target_pairs={{0,1},{1,2},{2,3},{4,5},{5,6},{6,7},{8,9},{9,10},{10,11},{12,13},{... | collective-permute-start | bytes 1105928 | tf_op jit(solution)/shard_map/ppermute | solution.py:15
  58.6 2.9 %copy-start.2 = (bf16[2,3,160,384]{3,2,1,0:T(8,128)(2,1)S(1)}, bf16[2,3,160,384]{3,2,1,0:T(8,128)(2,1)}, u32[]{:S(2)}) copy-start(bf16[2,3,160,384]{3,2,1,0:T(8,128)(2,1)} %param.10) | copy-start | bytes 2211844
  61.6 8.8 %collective-permute-start.7 = (bf16[3,160,384]{2,1,0:T(8,128)(2,1)S(1)}, bf16[3,160,384]{2,1,0:T(8,128)(2,1)S(1)}, u32[]{:S(2)}, u32[]{:S(2)}) collective-permute-start(bf16[3,160,384]{2,1,0:T(8,128)(2,1)S(1)} %bitcast_select_fusion.1), channel_id=1, source_target_pairs={{0,1},{1,2},{2,3},{4,5},{5,6},{6,7},{8,9},{9,10},{10,11},{12,13},{... | collective-permute-start | bytes 1105928 | tf_op jit(solution)/shard_map/ppermute | solution.py:15
  65.5 1.2 %copy-start.3 = (bf16[480,384]{1,0:T(8,128)(2,1)S(1)}, bf16[480,384]{1,0:T(8,128)(2,1)}, u32[]{:S(2)}) copy-start(bf16[480,384]{1,0:T(8,128)(2,1)} %get-tuple-element.7) | copy-start | bytes 1105924
  71.6 7.8 %collective-permute-start.9 = (bf16[160,384]{1,0:T(8,128)(2,1)S(1)}, bf16[160,384]{1,0:T(8,128)(2,1)S(1)}, u32[]{:S(2)}, u32[]{:S(2)}) collective-permute-start(bf16[160,384]{1,0:T(8,128)(2,1)S(1)} %fusion.3), channel_id=1, source_target_pairs={{4,0},{8,4},{12,8},{5,1},{9,5},{13,9},{6,2},{10,6},{14,10},{7,3},{... | collective-permute-start | bytes 368648 | tf_op jit(solution)/shard_map/ppermute | solution.py:179
  74.3 6.8 %collective-permute-start.8 = (bf16[160,384]{1,0:T(8,128)(2,1)S(1)}, bf16[160,384]{1,0:T(8,128)(2,1)S(1)}, u32[]{:S(2)}, u32[]{:S(2)}) collective-permute-start(bf16[160,384]{1,0:T(8,128)(2,1)S(1)} %fusion.2), channel_id=1, source_target_pairs={{0,4},{4,8},{8,12},{1,5},{5,9},{9,13},{2,6},{6,10},{10,14},{3,7},{... | collective-permute-start | bytes 368648 | tf_op jit(solution)/shard_map/ppermute | solution.py:182

commit v12 on v11

--- a/solution.py
+++ b/solution.py
@@ -17,9 +17,9 @@
 
 def strip_gather(x, axis):
     n = lax.axis_size(axis)
+    m = x.shape[0]
     if n == 1:
-        return x
-    m = x.shape[0]
+        return x, jnp.zeros((1,), jnp.int32)
     up_pairs = [(i, i + 1) for i in range(n - 1)]
     down_pairs = [(i + 1, i) for i in range(n - 1)]
     ups, downs = [], []
@@ -31,7 +31,7 @@
         downs.append(down)
     stacked = jnp.concatenate(ups[::-1] + [x] + downs, axis=0)
     me = lax.axis_index(axis)
-    return lax.dynamic_slice_in_dim(stacked, (n - 1 - me) * m, n * m, axis=0)
+    return stacked, ((n - 1 - me) * m).astype(jnp.int32).reshape(1)
 
 
 def rms_scale(values, gain):
@@ -45,11 +45,13 @@
 
 
 def attention_kernel(
-    scale, whole_ref, flat_ref, query_ref, again_ref, wk_ref, wv_ref, wo_ref, cgain_ref,
-    resid_ref, act_ref, keys_ref, values_ref,
+    scale, start_ref, stacked_ref, flat_ref, query_ref, again_ref, wk_ref, wv_ref, wo_ref,
+    cgain_ref, resid_ref, act_ref, whole_ref, keys_ref, values_ref,
 ):
     @pl.when(pl.program_id(0) == 0)
     def _():
+        first = pl.multiple_of(start_ref[0], 16)
+        pltpu.sync_copy(stacked_ref.at[pl.ds(first, whole_ref.shape[0])], whole_ref)
         normed_all = scaled(whole_ref[...], again_ref[...]).astype(jnp.bfloat16)
         keys_ref[...] = jnp.dot(
             normed_all, wk_ref[...], preferred_element_type=jnp.float32
@@ -81,12 +83,15 @@
     act_ref[...] = (shown / (1.0 + jnp.exp(-shown))).astype(jnp.bfloat16)
 
 
-def attend(whole, flat, query, attn_gain, key_weight, value_weight, out_weight, conv_gain, scale):
+def attend(
+    stacked, start, parts, flat, query, attn_gain, key_weight, value_weight, out_weight, conv_gain,
+    scale,
+):
     count, width = query.shape
-    total_keys = whole.shape[0]
+    total_keys = parts * count
     block = 160 if count % 160 == 0 else count
-    full = lambda shape: pl.BlockSpec(shape, lambda i: (0, 0))
-    rows_of = pl.BlockSpec((block, width), lambda i: (i, 0))
+    full = lambda shape: pl.BlockSpec(shape, lambda i, start: (0, 0))
+    rows_of = pl.BlockSpec((block, width), lambda i, start: (i, 0))
     flops = 4 * count * total_keys * width + 4 * total_keys * width * width
     flops += 2 * count * width * width
     return pl.pallas_call(
@@ -95,9 +100,11 @@
             jax.ShapeDtypeStruct((count, width), jnp.bfloat16),
             jax.ShapeDtypeStruct((count, width), jnp.bfloat16),
         ),
-        grid=(count // block,),
-        in_specs=[
-            full((total_keys, width)),
+        grid_spec=pltpu.PrefetchScalarGridSpec(
+            num_scalar_prefetch=1,
+            grid=(count // block,),
+            in_specs=[
+            pl.BlockSpec(memory_space=pl.ANY),
             rows_of,
             rows_of,
             full((1, width)),
@@ -105,12 +112,14 @@
             full((width, width)),
             full((width, width)),
             full((1, width)),
-        ],
-        out_specs=(rows_of, rows_of),
-        scratch_shapes=[
-            pltpu.VMEM((total_keys, width), jnp.bfloat16),
-            pltpu.VMEM((total_keys, width), jnp.bfloat16),
-        ],
+            ],
+            out_specs=(rows_of, rows_of),
+            scratch_shapes=[
+                pltpu.VMEM((total_keys, width), jnp.bfloat16),
+                pltpu.VMEM((total_keys, width), jnp.bfloat16),
+                pltpu.VMEM((total_keys, width), jnp.bfloat16),
+            ],
+        ),
         compiler_params=pltpu.CompilerParams(vmem_limit_bytes=60 * 1024 * 1024),
         cost_estimate=pl.CostEstimate(
             flops=flops,
@@ -118,8 +127,8 @@
             bytes_accessed=2 * width * (total_keys + 4 * count + 3 * width),
         ),
     )(
-        whole, flat, query, attn_gain.reshape(1, width), key_weight, value_weight, out_weight,
-        conv_gain.reshape(1, width),
+        start, stacked, flat, query, attn_gain.reshape(1, width), key_weight, value_weight,
+        out_weight, conv_gain.reshape(1, width),
     )
 
 
@@ -140,18 +149,20 @@
     flat = frames.reshape(-1, width)
     count = flat.shape[0]
     scale = float(np.float32(1.0) / np.sqrt(np.float32(width)))
-    whole = strip_gather(flat, "strip")
+    stacked, start = strip_gather(flat, "strip")
     normed = rms_scale(flat, attn_gain).astype(jnp.bfloat16)
     query = jnp.dot(normed, query_weight, preferred_element_type=jnp.float32).astype(jnp.bfloat16)
     resid, act = attend(
-        whole, flat, query, attn_gain, key_weight, value_weight, out_weight, conv_gain, scale
+        stacked, start, lax.axis_size("strip"), flat, query, attn_gain, key_weight, value_weight,
+        out_weight, conv_gain, scale,
     )
     act = act.reshape(rows, cols, width)
     frame_index = lax.axis_index("tm")
     prior = passed_along(act, "tm", 1)
     prior = jnp.where(frame_index == 0, cache_frames[1], prior)
-    older = passed_along(prior, "tm", 1)
+    older = lax.ppermute(prior, "tm", [(i, i + 1) for i in range(1, lax.axis_size("tm") - 1)])
     older = jnp.where(frame_index == 0, cache_frames[0], older)
+    older = jnp.where(frame_index == 1, cache_frames[1], older)
     kernel = conv_weight.reshape(3, 3, 3 * width, width)
 
     def widen(frame):

time: 83.3 us -> 84.7 us (1.017)
  Pallas kernels: 9.71 us -> 10.8 us
    ppermute x0 -> x1, waiting for transfers between devices: none -> 2.94 us  [shards(): lax.ppermute(prior, 'tm', [(i, i + 1) for i in range(1, lax.axis_size('tm...]
    ppermute x2 -> x1, waiting for transfers between devices: 5 us -> 2.1 us  [passed_along(): return lax.ppermute(x, axis, pairs)]
    ppermute x2 -> x1, starting transfers between devices: 4.28 us -> 2.17 us  [passed_along(): return lax.ppermute(x, axis, pairs)]
    ppermute x0 -> x1, starting transfers between devices: none -> 2.1 us  [shards(): lax.ppermute(prior, 'tm', [(i, i + 1) for i in range(1, lax.axis_size('tm...]
    unnamed x18 -> x20, local copies, waits for them, and re-layouts: 0.37 us -> 1.84 us
    dynamic_slice x1 -> x0, local copies, waits for them, and re-layouts: 1.3 us -> none  [strip_gather(): return lax.dynamic_slice_in_dim(stacked, (n - 1 - me) * m, n * m, axis=0)]
    pallas_call x1, Pallas kernels: 9.71 us -> 10.8 us  [attend(): pl.pallas_call(functools.partial(attention_kernel, scale), out_shape=(jax...]
  transfers between devices with their start and end apart: 10 -> 10, of which waited for: 8 -> 8; matrix products, arithmetic and copies ran while one was open for 21% -> 20% of each run, Pallas kernels for 0% -> 0%
where the time goes in v12:
time: 84.7 us; the launch traced here: 84.2 us
  starting transfers between devices  27.8 us (33%)
  waiting for transfers between devices  23.6 us (28%)
  matrix products  12.2 us (14%)
  Pallas kernels  10.8 us (13%)
  local copies, waits for them, and re-layouts  7.35 us (9%)
  other arithmetic  2.06 us (2%)
    pallas_call x1, Pallas kernels, attend(): pl.pallas_call(functools.partial(attention_kernel, scale), out_shape=(jax...  10.8 us
    ppermute x3, starting transfers between devices, strip_gather(): up = lax.ppermute(up, axis, up_pairs)  10.6 us
    ppermute x3, waiting for transfers between devices, strip_gather(): up = lax.ppermute(up, axis, up_pairs)  9.33 us
    dot_general x9, matrix products, frame_terms(): jnp.dot(window, kernel[step_t, step_r], preferred_element_type=jnp.float32)  7.83 us
    ppermute x3, waiting for transfers between devices, strip_gather(): down = lax.ppermute(down, axis, down_pairs)  7.55 us
    ppermute x3, starting transfers between devices, strip_gather(): down = lax.ppermute(down, axis, down_pairs)  7.12 us
    ppermute x1, starting transfers between devices, shards(): lax.ppermute(to_next.astype(jnp.bfloat16), 'strip', [(i, i + 1) for i in...  3.46 us
    ppermute x1, waiting for transfers between devices, shards(): lax.ppermute(prior, 'tm', [(i, i + 1) for i in range(1, lax.axis_size('tm...  2.94 us
  transfers between devices with their start and end apart: 10, of which 8 were waited for; matrix products, arithmetic and copies ran while one was open for 20% of the time, Pallas kernels for 0%

profile of v12, /device:TPU:10, one launch (start us, length us, event | category | flops | bytes accessed | tf_op | source)
XLA Modules:
  0.0 84.2 jit_solution(17588976504539321610)
XLA Ops:
  0.0 3.6 %collective-permute-start = (bf16[480,384]{1,0:T(8,128)(2,1)}, bf16[480,384]{1,0:T(8,128)(2,1)S(1)}, u32[]{:S(2)}, u32[]{:S(2)}) collective-permute-start(bf16[480,384]{1,0:T(8,128)(2,1)} %bitcast.118), channel_id=1, source_target_pairs={{0,4},{4,8},{8,12},{1,5},{5,9},{9,13},{2,6},{6,10},{10,14},{3,7},{... | collective-permute-start | bytes 1105928 | tf_op jit(solution)/shard_map/ppermute | solution.py:28
  3.6 2.4 %collective-permute-start.3 = (bf16[480,384]{1,0:T(8,128)(2,1)}, bf16[480,384]{1,0:T(8,128)(2,1)S(1)}, u32[]{:S(2)}, u32[]{:S(2)}) collective-permute-start(bf16[480,384]{1,0:T(8,128)(2,1)} %bitcast.119), channel_id=1, source_target_pairs={{4,0},{8,4},{12,8},{5,1},{9,5},{13,9},{6,2},{10,6},{14,10},{7,3},{... | collective-permute-start | bytes 1105928 | tf_op jit(solution)/shard_map/ppermute | solution.py:29
  6.0 6.6 %collective-permute-done = bf16[480,384]{1,0:T(8,128)(2,1)S(1)} collective-permute-done((bf16[480,384]{1,0:T(8,128)(2,1)}, bf16[480,384]{1,0:T(8,128)(2,1)S(1)}, u32[]{:S(2)}, u32[]{:S(2)}) %collective-permute-start) | collective-permute-done | bytes 368672 | tf_op jit(solution)/shard_map/ppermute | solution.py:28
  12.6 3.5 %collective-permute-start.1 = (bf16[480,384]{1,0:T(8,128)(2,1)S(1)}, bf16[480,384]{1,0:T(8,128)(2,1)S(1)}, u32[]{:S(2)}, u32[]{:S(2)}) collective-permute-start(bf16[480,384]{1,0:T(8,128)(2,1)S(1)} %collective-permute-done), channel_id=1, source_target_pairs={{0,4},{4,8},{8,12},{1,5},{5,9},{9,13},{2,6},{6,10},{10,14},{3,7},{... | collective-permute-start | bytes 1105928 | tf_op jit(solution)/shard_map/ppermute | solution.py:28
  16.0 1.3 %reshape.73.cgain_ref = f32[1,384]{1,0:T(1,128)} reshape(f32[384]{0:T(512)} %param.16) | data formatting | bytes 3072 | tf_op jit(solution)/shard_map/reshape | solution.py:131
  17.3 1.3 %broadcast_in_dim.4.again_ref = f32[1,384]{1,0:T(1,128)} reshape(f32[384]{0:T(512)} %param.11) | data formatting | bytes 3072 | tf_op jit(solution)/shard_map/broadcast_in_dim | solution.py:39
  18.6 1.2 %multiply_reduce_fusion = f32[3,160]{1,0:T(4,128)S(1)} fusion(bf16[1,3,160,384]{3,2,1,0:T(8,128)(2,1)} %param.9), kind=kLoop, calls=%fused_computation.44 | loop fusion | flops 552480 | bytes 370560 | tf_op jit(solution)/shard_map/reduce_sum | solution.py:39
  19.9 2.4 %collective-permute-start.4 = (bf16[480,384]{1,0:T(8,128)(2,1)S(1)}, bf16[480,384]{1,0:T(8,128)(2,1)S(1)}, u32[]{:S(2)}, u32[]{:S(2)}) collective-permute-start(bf16[480,384]{1,0:T(8,128)(2,1)S(1)} %collective-permute-done.3), channel_id=1, source_target_pairs={{4,0},{8,4},{12,8},{5,1},{9,5},{13,9},{6,2},{10,6},{14,10},{7,3},{... | collective-permute-start | bytes 1105928 | tf_op jit(solution)/shard_map/ppermute | solution.py:29
  22.2 1.7 %collective-permute-done.1 = bf16[480,384]{1,0:T(8,128)(2,1)S(1)} collective-permute-done((bf16[480,384]{1,0:T(8,128)(2,1)S(1)}, bf16[480,384]{1,0:T(8,128)(2,1)S(1)}, u32[]{:S(2)}, u32[]{:S(2)}) %collective-permute-start.1) | collective-permute-done | bytes 368672 | tf_op jit(solution)/shard_map/ppermute | solution.py:28
  23.9 3.5 %collective-permute-start.2 = (bf16[480,384]{1,0:T(8,128)(2,1)S(1)}, bf16[480,384]{1,0:T(8,128)(2,1)S(1)}, u32[]{:S(2)}, u32[]{:S(2)}) collective-permute-start(bf16[480,384]{1,0:T(8,128)(2,1)S(1)} %collective-permute-done.1), channel_id=1, source_target_pairs={{0,4},{4,8},{8,12},{1,5},{5,9},{9,13},{2,6},{6,10},{10,14},{3,7},{... | collective-permute-start | bytes 1105928 | tf_op jit(solution)/shard_map/ppermute | solution.py:28
  27.6 2.2 %convolution_convert_fusion.query_ref = bf16[480,384]{1,0:T(8,128)(2,1)} fusion(bf16[384,384]{1,0:T(8,128)(2,1)S(1)} %copy-done, bf16[480,384]{1,0:T(8,128)(2,1)} %bitcast.120, f32[384]{0:T(512)} %param.11, f32[480]{0:T(512)S(1)} %rsqrt.12), kind=kOutput, calls=%fused_computation.10 | convolution fusion | flops 142479360 | bytes 1035648 | tf_op jit(solution)/shard_map/dot_general | solution.py:154
  29.7 1.2 %collective-permute-done.4 = bf16[480,384]{1,0:T(8,128)(2,1)S(1)} collective-permute-done((bf16[480,384]{1,0:T(8,128)(2,1)S(1)}, bf16[480,384]{1,0:T(8,128)(2,1)S(1)}, u32[]{:S(2)}, u32[]{:S(2)}) %collective-permute-start.4) | collective-permute-done | bytes 368672 | tf_op jit(solution)/shard_map/ppermute | solution.py:29
  30.9 2.4 %collective-permute-start.5 = (bf16[480,384]{1,0:T(8,128)(2,1)S(1)}, bf16[480,384]{1,0:T(8,128)(2,1)S(1)}, u32[]{:S(2)}, u32[]{:S(2)}) collective-permute-start(bf16[480,384]{1,0:T(8,128)(2,1)S(1)} %collective-permute-done.4), channel_id=1, source_target_pairs={{4,0},{8,4},{12,8},{5,1},{9,5},{13,9},{6,2},{10,6},{14,10},{7,3},{... | collective-permute-start | bytes 1105928 | tf_op jit(solution)/shard_map/ppermute | solution.py:29
  33.3 1.1 %collective-permute-done.2 = bf16[480,384]{1,0:T(8,128)(2,1)S(1)} collective-permute-done((bf16[480,384]{1,0:T(8,128)(2,1)S(1)}, bf16[480,384]{1,0:T(8,128)(2,1)S(1)}, u32[]{:S(2)}, u32[]{:S(2)}) %collective-permute-start.2) | collective-permute-done | bytes 368672 | tf_op jit(solution)/shard_map/ppermute | solution.py:28
  34.8 6.4 %collective-permute-done.5 = bf16[480,384]{1,0:T(8,128)(2,1)S(1)} collective-permute-done((bf16[480,384]{1,0:T(8,128)(2,1)S(1)}, bf16[480,384]{1,0:T(8,128)(2,1)S(1)}, u32[]{:S(2)}, u32[]{:S(2)}) %collective-permute-start.5) | collective-permute-done | bytes 368672 | tf_op jit(solution)/shard_map/ppermute | solution.py:29
  41.2 1.5 %copy-done.4 = bf16[3360,384]{1,0:T(8,128)(2,1)} copy-done((bf16[3360,384]{1,0:T(8,128)(2,1)}, bf16[3360,384]{1,0:T(8,128)(2,1)S(1)}, u32[]{:S(2)}) %copy-start.4) | copy-done | bytes 2580504
  42.7 10.8 %shard_map.91 = (bf16[480,384]{1,0:T(8,128)(2,1)}, bf16[480,384]{1,0:T(8,128)(2,1)}) custom-call(s32[1]{0:T(128)} %bitcast.start_ref, bf16[3360,384]{1,0:T(8,128)(2,1)} %copy-done.4, bf16[480,384]{1,0:T(8,128)(2,1)} %bitcast.121, bf16[480,384]{1,0:T(8,128)(2,1)} %convolution_convert_fusion.query_ref, f32[1,384]{1,0:T(1,128)} %broadcast_in_dim.4.again_ref, ...), custom_call_target="tpu_custom_call" | custom-call | flops 2689597440 | bytes 3833856 | tf_op jit(solution)/shard_map/pallas_call | solution.py:97
  53.5 2.2 %collective-permute-start.6 = (bf16[3,160,384]{2,1,0:T(8,128)(2,1)}, bf16[3,160,384]{2,1,0:T(8,128)(2,1)S(1)}, u32[]{:S(2)}, u32[]{:S(2)}) collective-permute-start(bf16[3,160,384]{2,1,0:T(8,128)(2,1)} %bitcast.126), channel_id=1, source_target_pairs={{0,1},{1,2},{2,3},{4,5},{5,6},{6,7},{8,9},{9,10},{10,11},{12,13},{... | collective-permute-start | bytes 1105928 | tf_op jit(solution)/shard_map/ppermute | solution.py:15
  55.7 1.5 %pad_slice_fusion.8 = (bf16[5,160,384]{2,1,0:T(8,128)(2,1)S(1)}, bf16[5,160,384]{2,1,0:T(8,128)(2,1)S(1)}, bf16[5,160,384]{2,1,0:T(8,128)(2,1)S(1)}) fusion(bf16[3,160,384]{2,1,0:T(8,128)(2,1)} %bitcast.127), kind=kLoop, calls=%fused_computation.39 | loop fusion | bytes 2211840 | tf_op jit(solution)/shard_map/slice | solution.py:171
  57.1 0.2 pad_maximum_fusion
  57.3 0.3 fusion.12
  57.6 0.4 fusion.5
  58.0 0.8 fusion.4
  58.8 0.8 convolution_add_fusion.5
  59.5 0.4 fusion.3
  59.9 0.8 convolution_add_fusion.4
  60.7 2.1 %collective-permute-done.6 = bf16[3,160,384]{2,1,0:T(8,128)(2,1)S(1)} collective-permute-done((bf16[3,160,384]{2,1,0:T(8,128)(2,1)}, bf16[3,160,384]{2,1,0:T(8,128)(2,1)S(1)}, u32[]{:S(2)}, u32[]{:S(2)}) %collective-permute-start.6) | collective-permute-done | bytes 368672 | tf_op jit(solution)/shard_map/ppermute | solution.py:15
  62.9 2.1 %collective-permute-start.7 = (bf16[3,160,384]{2,1,0:T(8,128)(2,1)S(1)}, bf16[3,160,384]{2,1,0:T(8,128)(2,1)S(1)}, u32[]{:S(2)}, u32[]{:S(2)}) collective-permute-start(bf16[3,160,384]{2,1,0:T(8,128)(2,1)S(1)} %bitcast_select_fusion.1), channel_id=1, source_target_pairs={{1,2},{2,3},{5,6},{6,7},{9,10},{10,11},{13,14},{14,15},{17,18},{18... | collective-permute-start | bytes 1105928 | tf_op jit(solution)/shard_map/ppermute | solution.py:163
  65.0 0.3 pad_slice_fusion.5
  65.2 0.2 pad_maximum_fusion.1
  65.4 0.3 fusion.13
  65.7 0.4 convolution_add_fusion.7
  66.1 0.8 fusion.6
  66.8 0.8 convolution_add_fusion.3
  67.6 0.4 convolution_add_fusion.9
  68.0 0.8 convolution_add_fusion.2
  68.8 2.9 %collective-permute-done.7 = bf16[3,160,384]{2,1,0:T(8,128)(2,1)S(1)} collective-permute-done((bf16[3,160,384]{2,1,0:T(8,128)(2,1)S(1)}, bf16[3,160,384]{2,1,0:T(8,128)(2,1)S(1)}, u32[]{:S(2)}, u32[]{:S(2)}) %collective-permute-start.7) | collective-permute-done | bytes 368672 | tf_op jit(solution)/shard_map/ppermute | solution.py:163
  71.8 0.3 pad_slice_fusion.2
  72.0 0.2 pad_maximum_fusion.2
  72.2 0.3 fusion.14
  72.5 0.4 fusion.2
  72.9 2.4 %collective-permute-start.9 = (bf16[160,384]{1,0:T(8,128)(2,1)S(1)}, bf16[160,384]{1,0:T(8,128)(2,1)S(1)}, u32[]{:S(2)}, u32[]{:S(2)}) collective-permute-start(bf16[160,384]{1,0:T(8,128)(2,1)S(1)} %fusion.2), channel_id=1, source_target_pairs={{4,0},{8,4},{12,8},{5,1},{9,5},{13,9},{6,2},{10,6},{14,10},{7,3},{... | collective-permute-start | bytes 368648 | tf_op jit(solution)/shard_map/ppermute | solution.py:190
  75.3 0.4 fusion.1
  75.6 3.5 %collective-permute-start.8 = (bf16[160,384]{1,0:T(8,128)(2,1)S(1)}, bf16[160,384]{1,0:T(8,128)(2,1)S(1)}, u32[]{:S(2)}, u32[]{:S(2)}) collective-permute-start(bf16[160,384]{1,0:T(8,128)(2,1)S(1)} %fusion.1), channel_id=1, source_target_pairs={{0,4},{4,8},{8,12},{1,5},{5,9},{9,13},{2,6},{6,10},{10,14},{3,7},{... | collective-permute-start | bytes 368648 | tf_op jit(solution)/shard_map/ppermute | solution.py:193
  79.1 0.8 fusion.7
  79.9 0.8 convolution_add_fusion.1
  80.7 1.7 %collective-permute-done.8 = bf16[160,384]{1,0:T(8,128)(2,1)S(1)} collective-permute-done((bf16[160,384]{1,0:T(8,128)(2,1)S(1)}, bf16[160,384]{1,0:T(8,128)(2,1)S(1)}, u32[]{:S(2)}, u32[]{:S(2)}) %collective-permute-start.8) | collective-permute-done | bytes 122912 | tf_op jit(solution)/shard_map/ppermute | solution.py:193
  82.6 1.6 %fusion.8 = bf16[480,384]{1,0:T(8,128)(2,1)} fusion(f32[3,160,384]{2,1,0:T(8,128)S(1)} %pad_maximum_fusion.3, f32[480,384]{1,0:T(8,128)S(1)} %convolution_add_fusion.1, bf16[480,1152]{1,0:T(8,128)(2,1)S(1)} %bitcast.95, bf16[3,3,1152,384]{3,2,1,0:T(8,128)(2,1)S(1)} %bitcast.117, f32[480,384]{1,0:T(8,128)S(1)} %convolution_add_fusion.2, ...), kind=kOutput, calls=%fused_computation.42 | convolution fusion | flops 425963520 | bytes 5677056 | tf_op jit(solution)/shard_map/dot_general | solution.py:178
  (31 shorter events, 0.9 us)
Async XLA Ops:
  0.0 27.6 %copy-start = (bf16[384,384]{1,0:T(8,128)(2,1)S(1)}, bf16[384,384]{1,0:T(8,128)(2,1)}, u32[]{:S(2)}) copy-start(bf16[384,384]{1,0:T(8,128)(2,1)} %param.12) | copy-start | bytes 884740
  0.0 12.6 %collective-permute-start = (bf16[480,384]{1,0:T(8,128)(2,1)}, bf16[480,384]{1,0:T(8,128)(2,1)S(1)}, u32[]{:S(2)}, u32[]{:S(2)}) collective-permute-start(bf16[480,384]{1,0:T(8,128)(2,1)} %bitcast.118), channel_id=1, source_target_pairs={{0,4},{4,8},{8,12},{1,5},{5,9},{9,13},{2,6},{6,10},{10,14},{3,7},{... | collective-permute-start | bytes 1105928 | tf_op jit(solution)/shard_map/ppermute | solution.py:28
  3.6 16.2 %collective-permute-start.3 = (bf16[480,384]{1,0:T(8,128)(2,1)}, bf16[480,384]{1,0:T(8,128)(2,1)S(1)}, u32[]{:S(2)}, u32[]{:S(2)}) collective-permute-start(bf16[480,384]{1,0:T(8,128)(2,1)} %bitcast.119), channel_id=1, source_target_pairs={{4,0},{8,4},{12,8},{5,1},{9,5},{13,9},{6,2},{10,6},{14,10},{7,3},{... | collective-permute-start | bytes 1105928 | tf_op jit(solution)/shard_map/ppermute | solution.py:29
  12.6 11.4 %collective-permute-start.1 = (bf16[480,384]{1,0:T(8,128)(2,1)S(1)}, bf16[480,384]{1,0:T(8,128)(2,1)S(1)}, u32[]{:S(2)}, u32[]{:S(2)}) collective-permute-start(bf16[480,384]{1,0:T(8,128)(2,1)S(1)} %collective-permute-done), channel_id=1, source_target_pairs={{0,4},{4,8},{8,12},{1,5},{5,9},{9,13},{2,6},{6,10},{10,14},{3,7},{... | collective-permute-start | bytes 1105928 | tf_op jit(solution)/shard_map/ppermute | solution.py:28
  18.6 16.0 %copy-start.2 = (bf16[1,3,160,384]{3,2,1,0:T(8,128)(2,1)S(1)}, bf16[1,3,160,384]{3,2,1,0:T(8,128)(2,1)}, u32[]{:S(2)}) copy-start(bf16[1,3,160,384]{3,2,1,0:T(8,128)(2,1)} %param.9) | copy-start | bytes 1105924
  19.9 11.1 %collective-permute-start.4 = (bf16[480,384]{1,0:T(8,128)(2,1)S(1)}, bf16[480,384]{1,0:T(8,128)(2,1)S(1)}, u32[]{:S(2)}, u32[]{:S(2)}) collective-permute-start(bf16[480,384]{1,0:T(8,128)(2,1)S(1)} %collective-permute-done.3), channel_id=1, source_target_pairs={{4,0},{8,4},{12,8},{5,1},{9,5},{13,9},{6,2},{10,6},{14,10},{7,3},{... | collective-permute-start | bytes 1105928 | tf_op jit(solution)/shard_map/ppermute | solution.py:29
  23.9 10.5 %collective-permute-start.2 = (bf16[480,384]{1,0:T(8,128)(2,1)S(1)}, bf16[480,384]{1,0:T(8,128)(2,1)S(1)}, u32[]{:S(2)}, u32[]{:S(2)}) collective-permute-start(bf16[480,384]{1,0:T(8,128)(2,1)S(1)} %collective-permute-done.1), channel_id=1, source_target_pairs={{0,4},{4,8},{8,12},{1,5},{5,9},{9,13},{2,6},{6,10},{10,14},{3,7},{... | collective-permute-start | bytes 1105928 | tf_op jit(solution)/shard_map/ppermute | solution.py:28
  30.9 10.2 %collective-permute-start.5 = (bf16[480,384]{1,0:T(8,128)(2,1)S(1)}, bf16[480,384]{1,0:T(8,128)(2,1)S(1)}, u32[]{:S(2)}, u32[]{:S(2)}) collective-permute-start(bf16[480,384]{1,0:T(8,128)(2,1)S(1)} %collective-permute-done.4), channel_id=1, source_target_pairs={{4,0},{8,4},{12,8},{5,1},{9,5},{13,9},{6,2},{10,6},{14,10},{7,3},{... | collective-permute-start | bytes 1105928 | tf_op jit(solution)/shard_map/ppermute | solution.py:29
  41.2 1.5 %copy-start.4 = (bf16[3360,384]{1,0:T(8,128)(2,1)}, bf16[3360,384]{1,0:T(8,128)(2,1)S(1)}, u32[]{:S(2)}) copy-start(bf16[3360,384]{1,0:T(8,128)(2,1)S(1)} %constant_dynamic-update-slice_fusion.stacked_ref) | copy-start | bytes 7741444
  42.7 14.9 %slice-start = ((s8[7962624]{0:T(1024)(128)(4,1)}), s8[3768320]{0:T(1024)(128)(4,1)S(1)}, s32[]{:S(2)}) async-start(s8[7962624]{0:T(1024)(128)(4,1)} %bitcast.101), calls=%async_computation | async-start | bytes 7536640
  53.5 4.1 %slice-start.1 = ((s8[7962624]{0:T(1024)(128)(4,1)}), s8[4194304]{0:T(1024)(128)(4,1)S(1)}, s32[]{:S(2)}) async-start(s8[7962624]{0:T(1024)(128)(4,1)} %bitcast.101), calls=%async_computation.1 | async-start | bytes 8388608
  53.5 9.3 %collective-permute-start.6 = (bf16[3,160,384]{2,1,0:T(8,128)(2,1)}, bf16[3,160,384]{2,1,0:T(8,128)(2,1)S(1)}, u32[]{:S(2)}, u32[]{:S(2)}) collective-permute-start(bf16[3,160,384]{2,1,0:T(8,128)(2,1)} %bitcast.126), channel_id=1, source_target_pairs={{0,1},{1,2},{2,3},{4,5},{5,6},{6,7},{8,9},{9,10},{10,11},{12,13},{... | collective-permute-start | bytes 1105928 | tf_op jit(solution)/shard_map/ppermute | solution.py:15
  59.9 2.9 %copy-start.1 = (bf16[2,3,160,384]{3,2,1,0:T(8,128)(2,1)S(1)}, bf16[2,3,160,384]{3,2,1,0:T(8,128)(2,1)}, u32[]{:S(2)}) copy-start(bf16[2,3,160,384]{3,2,1,0:T(8,128)(2,1)} %param.10) | copy-start | bytes 2211844
  62.9 8.8 %collective-permute-start.7 = (bf16[3,160,384]{2,1,0:T(8,128)(2,1)S(1)}, bf16[3,160,384]{2,1,0:T(8,128)(2,1)S(1)}, u32[]{:S(2)}, u32[]{:S(2)}) collective-permute-start(bf16[3,160,384]{2,1,0:T(8,128)(2,1)S(1)} %bitcast_select_fusion.1), channel_id=1, source_target_pairs={{1,2},{2,3},{5,6},{6,7},{9,10},{10,11},{13,14},{14,15},{17,18},{18... | collective-permute-start | bytes 1105928 | tf_op jit(solution)/shard_map/ppermute | solution.py:163
  72.9 7.8 %collective-permute-start.9 = (bf16[160,384]{1,0:T(8,128)(2,1)S(1)}, bf16[160,384]{1,0:T(8,128)(2,1)S(1)}, u32[]{:S(2)}, u32[]{:S(2)}) collective-permute-start(bf16[160,384]{1,0:T(8,128)(2,1)S(1)} %fusion.2), channel_id=1, source_target_pairs={{4,0},{8,4},{12,8},{5,1},{9,5},{13,9},{6,2},{10,6},{14,10},{7,3},{... | collective-permute-start | bytes 368648 | tf_op jit(solution)/shard_map/ppermute | solution.py:190
  75.6 6.8 %collective-permute-start.8 = (bf16[160,384]{1,0:T(8,128)(2,1)S(1)}, bf16[160,384]{1,0:T(8,128)(2,1)S(1)}, u32[]{:S(2)}, u32[]{:S(2)}) collective-permute-start(bf16[160,384]{1,0:T(8,128)(2,1)S(1)} %fusion.1), channel_id=1, source_target_pairs={{0,4},{4,8},{8,12},{1,5},{5,9},{9,13},{2,6},{6,10},{10,14},{3,7},{... | collective-permute-start | bytes 368648 | tf_op jit(solution)/shard_map/ppermute | solution.py:193
  80.7 1.9 %copy-start.3 = (bf16[480,384]{1,0:T(8,128)(2,1)S(1)}, bf16[480,384]{1,0:T(8,128)(2,1)}, u32[]{:S(2)}) copy-start(bf16[480,384]{1,0:T(8,128)(2,1)} %get-tuple-element.7) | copy-start | bytes 1105924

commit v13 on v11

--- a/solution.py
+++ b/solution.py
@@ -150,8 +150,12 @@
     frame_index = lax.axis_index("tm")
     prior = passed_along(act, "tm", 1)
     prior = jnp.where(frame_index == 0, cache_frames[1], prior)
-    older = passed_along(prior, "tm", 1)
+    nt = lax.axis_size("tm")
+    older_even = lax.ppermute(act, "tm", [(i, i + 2) for i in range(0, nt - 2, 2)])
+    older_odd = lax.ppermute(prior, "tm", [(i, i + 1) for i in range(2, nt - 1, 2)])
+    older = jnp.where(frame_index % 2 == 0, older_even, older_odd)
     older = jnp.where(frame_index == 0, cache_frames[0], older)
+    older = jnp.where(frame_index == 1, cache_frames[1], older)
     kernel = conv_weight.reshape(3, 3, 3 * width, width)
 
     def widen(frame):

time: 83.3 us -> 84.4 us (1.013)
    ppermute x0 -> x2, starting transfers between devices: none -> 3.04 us  [the longest x1 1.55 us: shards(): lax.ppermute(act, 'tm', [(i, i + 2) for i in range(0, nt - 2, 2)])]
    ppermute x2 -> x1, starting transfers between devices: 4.28 us -> 1.92 us  [passed_along(): return lax.ppermute(x, axis, pairs)]
    ppermute x2 -> x1, waiting for transfers between devices: 5 us -> 5.33 us  [passed_along(): return lax.ppermute(x, axis, pairs)]
  transfers between devices with their start and end apart: 10 -> 11, of which waited for: 8 -> 7; matrix products, arithmetic and copies ran while one was open for 21% -> 20% of each run, Pallas kernels for 0% -> 0%
where the time goes in v13:
time: 84.4 us; the launch traced here: 83.9 us
  starting transfers between devices  28.5 us (34%)
  waiting for transfers between devices  23.9 us (28%)
  matrix products  12.1 us (14%)
  Pallas kernels  9.71 us (12%)
  local copies, waits for them, and re-layouts  7.15 us (8%)
  other arithmetic  2.08 us (2%)
    ppermute x3, starting transfers between devices, strip_gather(): up = lax.ppermute(up, axis, up_pairs)  10.6 us
    pallas_call x1, Pallas kernels, attend(): pl.pallas_call(functools.partial(attention_kernel, scale), out_shape=(jax...  9.71 us
    ppermute x3, waiting for transfers between devices, strip_gather(): up = lax.ppermute(up, axis, up_pairs)  9.36 us
    dot_general x9, matrix products, frame_terms(): jnp.dot(window, kernel[step_t, step_r], preferred_element_type=jnp.float32)  7.77 us
    ppermute x3, waiting for transfers between devices, strip_gather(): down = lax.ppermute(down, axis, down_pairs)  7.52 us
    ppermute x3, starting transfers between devices, strip_gather(): down = lax.ppermute(down, axis, down_pairs)  7.12 us
    ppermute x1, waiting for transfers between devices, passed_along(): return lax.ppermute(x, axis, pairs)  5.33 us
    ppermute x1, starting transfers between devices, shards(): lax.ppermute(to_next.astype(jnp.bfloat16), 'strip', [(i, i + 1) for i in...  3.46 us
  transfers between devices with their start and end apart: 11, of which 7 were waited for; matrix products, arithmetic and copies ran while one was open for 20% of the time, Pallas kernels for 0%

profile of v13, /device:TPU:10, one launch (start us, length us, event | category | flops | bytes accessed | tf_op | source)
XLA Modules:
  0.0 83.9 jit_solution(11424281488398590620)
XLA Ops:
  0.0 3.6 %collective-permute-start = (bf16[480,384]{1,0:T(8,128)(2,1)}, bf16[480,384]{1,0:T(8,128)(2,1)S(1)}, u32[]{:S(2)}, u32[]{:S(2)}) collective-permute-start(bf16[480,384]{1,0:T(8,128)(2,1)} %bitcast.117), channel_id=1, source_target_pairs={{0,4},{4,8},{8,12},{1,5},{5,9},{9,13},{2,6},{6,10},{10,14},{3,7},{... | collective-permute-start | bytes 1105928 | tf_op jit(solution)/shard_map/ppermute | solution.py:28
  3.6 2.4 %collective-permute-start.3 = (bf16[480,384]{1,0:T(8,128)(2,1)}, bf16[480,384]{1,0:T(8,128)(2,1)S(1)}, u32[]{:S(2)}, u32[]{:S(2)}) collective-permute-start(bf16[480,384]{1,0:T(8,128)(2,1)} %bitcast.118), channel_id=1, source_target_pairs={{4,0},{8,4},{12,8},{5,1},{9,5},{13,9},{6,2},{10,6},{14,10},{7,3},{... | collective-permute-start | bytes 1105928 | tf_op jit(solution)/shard_map/ppermute | solution.py:29
  6.0 6.6 %collective-permute-done = bf16[480,384]{1,0:T(8,128)(2,1)S(1)} collective-permute-done((bf16[480,384]{1,0:T(8,128)(2,1)}, bf16[480,384]{1,0:T(8,128)(2,1)S(1)}, u32[]{:S(2)}, u32[]{:S(2)}) %collective-permute-start) | collective-permute-done | bytes 368672 | tf_op jit(solution)/shard_map/ppermute | solution.py:28
  12.6 3.5 %collective-permute-start.1 = (bf16[480,384]{1,0:T(8,128)(2,1)S(1)}, bf16[480,384]{1,0:T(8,128)(2,1)S(1)}, u32[]{:S(2)}, u32[]{:S(2)}) collective-permute-start(bf16[480,384]{1,0:T(8,128)(2,1)S(1)} %collective-permute-done), channel_id=1, source_target_pairs={{0,4},{4,8},{8,12},{1,5},{5,9},{9,13},{2,6},{6,10},{10,14},{3,7},{... | collective-permute-start | bytes 1105928 | tf_op jit(solution)/shard_map/ppermute | solution.py:28
  16.1 1.3 %reshape.69.cgain_ref = f32[1,384]{1,0:T(1,128)} reshape(f32[384]{0:T(512)} %param.16) | data formatting | bytes 3072 | tf_op jit(solution)/shard_map/reshape | solution.py:122
  17.3 1.3 %broadcast_in_dim.4.again_ref = f32[1,384]{1,0:T(1,128)} reshape(f32[384]{0:T(512)} %param.11) | data formatting | bytes 3072 | tf_op jit(solution)/shard_map/broadcast_in_dim | solution.py:39
  18.6 1.2 %multiply_reduce_fusion = f32[3,160]{1,0:T(4,128)S(1)} fusion(bf16[1,3,160,384]{3,2,1,0:T(8,128)(2,1)} %param.9), kind=kLoop, calls=%fused_computation.45 | loop fusion | flops 552480 | bytes 370560 | tf_op jit(solution)/shard_map/reduce_sum | solution.py:39
  19.8 2.4 %collective-permute-start.4 = (bf16[480,384]{1,0:T(8,128)(2,1)S(1)}, bf16[480,384]{1,0:T(8,128)(2,1)S(1)}, u32[]{:S(2)}, u32[]{:S(2)}) collective-permute-start(bf16[480,384]{1,0:T(8,128)(2,1)S(1)} %collective-permute-done.3), channel_id=1, source_target_pairs={{4,0},{8,4},{12,8},{5,1},{9,5},{13,9},{6,2},{10,6},{14,10},{7,3},{... | collective-permute-start | bytes 1105928 | tf_op jit(solution)/shard_map/ppermute | solution.py:29
  22.2 1.7 %collective-permute-done.1 = bf16[480,384]{1,0:T(8,128)(2,1)S(1)} collective-permute-done((bf16[480,384]{1,0:T(8,128)(2,1)S(1)}, bf16[480,384]{1,0:T(8,128)(2,1)S(1)}, u32[]{:S(2)}, u32[]{:S(2)}) %collective-permute-start.1) | collective-permute-done | bytes 368672 | tf_op jit(solution)/shard_map/ppermute | solution.py:28
  23.9 3.5 %collective-permute-start.2 = (bf16[480,384]{1,0:T(8,128)(2,1)S(1)}, bf16[480,384]{1,0:T(8,128)(2,1)S(1)}, u32[]{:S(2)}, u32[]{:S(2)}) collective-permute-start(bf16[480,384]{1,0:T(8,128)(2,1)S(1)} %collective-permute-done.1), channel_id=1, source_target_pairs={{0,4},{4,8},{8,12},{1,5},{5,9},{9,13},{2,6},{6,10},{10,14},{3,7},{... | collective-permute-start | bytes 1105928 | tf_op jit(solution)/shard_map/ppermute | solution.py:28
  27.6 2.2 %convolution_convert_fusion.query_ref = bf16[480,384]{1,0:T(8,128)(2,1)} fusion(bf16[384,384]{1,0:T(8,128)(2,1)S(1)} %copy-done, bf16[480,384]{1,0:T(8,128)(2,1)} %bitcast.119, f32[384]{0:T(512)} %param.11, f32[480]{0:T(512)S(1)} %rsqrt.12), kind=kOutput, calls=%fused_computation.11 | convolution fusion | flops 142479360 | bytes 1035648 | tf_op jit(solution)/shard_map/dot_general | solution.py:145
  29.7 1.2 %collective-permute-done.4 = bf16[480,384]{1,0:T(8,128)(2,1)S(1)} collective-permute-done((bf16[480,384]{1,0:T(8,128)(2,1)S(1)}, bf16[480,384]{1,0:T(8,128)(2,1)S(1)}, u32[]{:S(2)}, u32[]{:S(2)}) %collective-permute-start.4) | collective-permute-done | bytes 368672 | tf_op jit(solution)/shard_map/ppermute | solution.py:29
  30.9 2.4 %collective-permute-start.5 = (bf16[480,384]{1,0:T(8,128)(2,1)S(1)}, bf16[480,384]{1,0:T(8,128)(2,1)S(1)}, u32[]{:S(2)}, u32[]{:S(2)}) collective-permute-start(bf16[480,384]{1,0:T(8,128)(2,1)S(1)} %collective-permute-done.4), channel_id=1, source_target_pairs={{4,0},{8,4},{12,8},{5,1},{9,5},{13,9},{6,2},{10,6},{14,10},{7,3},{... | collective-permute-start | bytes 1105928 | tf_op jit(solution)/shard_map/ppermute | solution.py:29
  33.3 1.1 %collective-permute-done.2 = bf16[480,384]{1,0:T(8,128)(2,1)S(1)} collective-permute-done((bf16[480,384]{1,0:T(8,128)(2,1)S(1)}, bf16[480,384]{1,0:T(8,128)(2,1)S(1)}, u32[]{:S(2)}, u32[]{:S(2)}) %collective-permute-start.2) | collective-permute-done | bytes 368672 | tf_op jit(solution)/shard_map/ppermute | solution.py:28
  34.8 6.3 %collective-permute-done.5 = bf16[480,384]{1,0:T(8,128)(2,1)S(1)} collective-permute-done((bf16[480,384]{1,0:T(8,128)(2,1)S(1)}, bf16[480,384]{1,0:T(8,128)(2,1)S(1)}, u32[]{:S(2)}, u32[]{:S(2)}) %collective-permute-start.5) | collective-permute-done | bytes 368672 | tf_op jit(solution)/shard_map/ppermute | solution.py:29
  41.2 1.3 %constant_dynamic-slice_fusion.whole_ref = bf16[1920,384]{1,0:T(8,128)(2,1)} fusion(bf16[3360,384]{1,0:T(8,128)(2,1)S(1)} %constant_dynamic-update-slice_fusion, s32[]{:T(128)S(6)} %select_n.34), kind=kLoop, calls=%fused_computation.67 | loop fusion | bytes 2949124 | tf_op jit(solution)/shard_map/dynamic_slice | solution.py:34
  42.5 9.7 %shard_map.91 = (bf16[480,384]{1,0:T(8,128)(2,1)}, bf16[480,384]{1,0:T(8,128)(2,1)}) custom-call(bf16[1920,384]{1,0:T(8,128)(2,1)} %constant_dynamic-slice_fusion.whole_ref, bf16[480,384]{1,0:T(8,128)(2,1)} %bitcast.120, bf16[480,384]{1,0:T(8,128)(2,1)} %convolution_convert_fusion.query_ref, f32[1,384]{1,0:T(1,128)} %broadcast_in_dim.4.again_ref, ...), custom_call_target="tpu_custom_call" | custom-call | flops 2689597440 | bytes 3833856 | tf_op jit(solution)/shard_map/pallas_call | solution.py:92
  52.2 1.6 %collective-permute-start.7 = (bf16[3,160,384]{2,1,0:T(8,128)(2,1)}, bf16[3,160,384]{2,1,0:T(8,128)(2,1)S(1)}, u32[]{:S(2)}, u32[]{:S(2)}) collective-permute-start(bf16[3,160,384]{2,1,0:T(8,128)(2,1)} %bitcast.125), channel_id=1, source_target_pairs={{0,2},{4,6},{8,10},{12,14},{16,18},{20,22},{24,26},{28,30}} | collective-permute-start | bytes 1105928 | tf_op jit(solution)/shard_map/ppermute | solution.py:154
  53.8 1.9 %collective-permute-start.6 = (bf16[3,160,384]{2,1,0:T(8,128)(2,1)}, bf16[3,160,384]{2,1,0:T(8,128)(2,1)S(1)}, u32[]{:S(2)}, u32[]{:S(2)}) collective-permute-start(bf16[3,160,384]{2,1,0:T(8,128)(2,1)} %bitcast.126), channel_id=1, source_target_pairs={{0,1},{1,2},{2,3},{4,5},{5,6},{6,7},{8,9},{9,10},{10,11},{12,13},{... | collective-permute-start | bytes 1105928 | tf_op jit(solution)/shard_map/ppermute | solution.py:15
  55.7 1.5 %pad_slice_fusion.8 = (bf16[5,160,384]{2,1,0:T(8,128)(2,1)S(1)}, bf16[5,160,384]{2,1,0:T(8,128)(2,1)S(1)}, bf16[5,160,384]{2,1,0:T(8,128)(2,1)S(1)}) fusion(bf16[3,160,384]{2,1,0:T(8,128)(2,1)} %bitcast.127), kind=kLoop, calls=%fused_computation.40 | loop fusion | bytes 2211840 | tf_op jit(solution)/shard_map/slice | solution.py:164
  57.2 0.2 pad_maximum_fusion
  57.3 0.3 fusion.14
  57.6 0.4 fusion.6
  58.0 0.8 fusion.5
  58.8 0.8 convolution_add_fusion.5
  59.5 0.4 fusion.4
  59.9 0.8 convolution_add_fusion.4
  60.7 5.3 %collective-permute-done.6 = bf16[3,160,384]{2,1,0:T(8,128)(2,1)S(1)} collective-permute-done((bf16[3,160,384]{2,1,0:T(8,128)(2,1)}, bf16[3,160,384]{2,1,0:T(8,128)(2,1)S(1)}, u32[]{:S(2)}, u32[]{:S(2)}) %collective-permute-start.6) | collective-permute-done | bytes 368672 | tf_op jit(solution)/shard_map/ppermute | solution.py:15
  66.1 1.5 %collective-permute-start.8 = (bf16[3,160,384]{2,1,0:T(8,128)(2,1)S(1)}, bf16[3,160,384]{2,1,0:T(8,128)(2,1)S(1)}, u32[]{:S(2)}, u32[]{:S(2)}) collective-permute-start(bf16[3,160,384]{2,1,0:T(8,128)(2,1)S(1)} %bitcast_select_fusion.1), channel_id=1, source_target_pairs={{2,3},{6,7},{10,11},{14,15},{18,19},{22,23},{26,27},{30,31}} | collective-permute-start | bytes 1105928 | tf_op jit(solution)/shard_map/ppermute | solution.py:155
  67.6 0.3 pad_slice_fusion.5
  67.9 0.2 pad_maximum_fusion.1
  68.1 0.3 fusion.15
  68.3 0.4 convolution_add_fusion.7
  68.7 0.8 fusion.7
  69.5 0.8 convolution_add_fusion.3
  70.2 0.4 convolution_add_fusion.9
  70.6 0.8 fusion.1
  71.6 0.3 pad_slice_fusion.2
  71.8 0.2 pad_maximum_fusion.2
  72.0 0.3 fusion.13
  72.3 0.4 fusion.3
  72.6 2.4 %collective-permute-start.10 = (bf16[160,384]{1,0:T(8,128)(2,1)S(1)}, bf16[160,384]{1,0:T(8,128)(2,1)S(1)}, u32[]{:S(2)}, u32[]{:S(2)}) collective-permute-start(bf16[160,384]{1,0:T(8,128)(2,1)S(1)} %fusion.3), channel_id=1, source_target_pairs={{4,0},{8,4},{12,8},{5,1},{9,5},{13,9},{6,2},{10,6},{14,10},{7,3},{... | collective-permute-start | bytes 368648 | tf_op jit(solution)/shard_map/ppermute | solution.py:183
  75.0 0.4 fusion.2
  75.4 3.5 %collective-permute-start.9 = (bf16[160,384]{1,0:T(8,128)(2,1)S(1)}, bf16[160,384]{1,0:T(8,128)(2,1)S(1)}, u32[]{:S(2)}, u32[]{:S(2)}) collective-permute-start(bf16[160,384]{1,0:T(8,128)(2,1)S(1)} %fusion.2), channel_id=1, source_target_pairs={{0,4},{4,8},{8,12},{1,5},{5,9},{9,13},{2,6},{6,10},{10,14},{3,7},{... | collective-permute-start | bytes 368648 | tf_op jit(solution)/shard_map/ppermute | solution.py:186
  78.9 0.8 fusion.8
  79.6 0.8 convolution_add_fusion.1
  80.5 1.7 %collective-permute-done.9 = bf16[160,384]{1,0:T(8,128)(2,1)S(1)} collective-permute-done((bf16[160,384]{1,0:T(8,128)(2,1)S(1)}, bf16[160,384]{1,0:T(8,128)(2,1)S(1)}, u32[]{:S(2)}, u32[]{:S(2)}) %collective-permute-start.9) | collective-permute-done | bytes 122912 | tf_op jit(solution)/shard_map/ppermute | solution.py:186
  82.3 1.6 %fusion.9 = bf16[480,384]{1,0:T(8,128)(2,1)} fusion(f32[3,160,384]{2,1,0:T(8,128)S(1)} %pad_maximum_fusion.3, f32[480,384]{1,0:T(8,128)S(1)} %fusion.1, f32[480,384]{1,0:T(8,128)S(1)} %convolution_add_fusion.1, bf16[480,1152]{1,0:T(8,128)(2,1)S(1)} %bitcast.94, bf16[3,3,1152,384]{3,2,1,0:T(8,128)(2,1)S(1)} %bitcast.116), kind=kOutput, calls=%fused_computation.43 | convolution fusion | flops 425410560 | bytes 4571136 | tf_op jit(solution)/shard_map/dot_general | solution.py:171
  (32 shorter events, 0.9 us)
Async XLA Ops:
  0.0 27.6 %copy-start = (bf16[384,384]{1,0:T(8,128)(2,1)S(1)}, bf16[384,384]{1,0:T(8,128)(2,1)}, u32[]{:S(2)}) copy-start(bf16[384,384]{1,0:T(8,128)(2,1)} %param.12) | copy-start | bytes 884740
  0.0 12.6 %collective-permute-start = (bf16[480,384]{1,0:T(8,128)(2,1)}, bf16[480,384]{1,0:T(8,128)(2,1)S(1)}, u32[]{:S(2)}, u32[]{:S(2)}) collective-permute-start(bf16[480,384]{1,0:T(8,128)(2,1)} %bitcast.117), channel_id=1, source_target_pairs={{0,4},{4,8},{8,12},{1,5},{5,9},{9,13},{2,6},{6,10},{10,14},{3,7},{... | collective-permute-start | bytes 1105928 | tf_op jit(solution)/shard_map/ppermute | solution.py:28
  3.6 16.2 %collective-permute-start.3 = (bf16[480,384]{1,0:T(8,128)(2,1)}, bf16[480,384]{1,0:T(8,128)(2,1)S(1)}, u32[]{:S(2)}, u32[]{:S(2)}) collective-permute-start(bf16[480,384]{1,0:T(8,128)(2,1)} %bitcast.118), channel_id=1, source_target_pairs={{4,0},{8,4},{12,8},{5,1},{9,5},{13,9},{6,2},{10,6},{14,10},{7,3},{... | collective-permute-start | bytes 1105928 | tf_op jit(solution)/shard_map/ppermute | solution.py:29
  12.6 11.4 %collective-permute-start.1 = (bf16[480,384]{1,0:T(8,128)(2,1)S(1)}, bf16[480,384]{1,0:T(8,128)(2,1)S(1)}, u32[]{:S(2)}, u32[]{:S(2)}) collective-permute-start(bf16[480,384]{1,0:T(8,128)(2,1)S(1)} %collective-permute-done), channel_id=1, source_target_pairs={{0,4},{4,8},{8,12},{1,5},{5,9},{9,13},{2,6},{6,10},{10,14},{3,7},{... | collective-permute-start | bytes 1105928 | tf_op jit(solution)/shard_map/ppermute | solution.py:28
  18.6 16.0 %copy-start.2 = (bf16[1,3,160,384]{3,2,1,0:T(8,128)(2,1)S(1)}, bf16[1,3,160,384]{3,2,1,0:T(8,128)(2,1)}, u32[]{:S(2)}) copy-start(bf16[1,3,160,384]{3,2,1,0:T(8,128)(2,1)} %param.9) | copy-start | bytes 1105924
  19.8 11.1 %collective-permute-start.4 = (bf16[480,384]{1,0:T(8,128)(2,1)S(1)}, bf16[480,384]{1,0:T(8,128)(2,1)S(1)}, u32[]{:S(2)}, u32[]{:S(2)}) collective-permute-start(bf16[480,384]{1,0:T(8,128)(2,1)S(1)} %collective-permute-done.3), channel_id=1, source_target_pairs={{4,0},{8,4},{12,8},{5,1},{9,5},{13,9},{6,2},{10,6},{14,10},{7,3},{... | collective-permute-start | bytes 1105928 | tf_op jit(solution)/shard_map/ppermute | solution.py:29
  23.9 10.5 %collective-permute-start.2 = (bf16[480,384]{1,0:T(8,128)(2,1)S(1)}, bf16[480,384]{1,0:T(8,128)(2,1)S(1)}, u32[]{:S(2)}, u32[]{:S(2)}) collective-permute-start(bf16[480,384]{1,0:T(8,128)(2,1)S(1)} %collective-permute-done.1), channel_id=1, source_target_pairs={{0,4},{4,8},{8,12},{1,5},{5,9},{9,13},{2,6},{6,10},{10,14},{3,7},{... | collective-permute-start | bytes 1105928 | tf_op jit(solution)/shard_map/ppermute | solution.py:28
  30.9 10.2 %collective-permute-start.5 = (bf16[480,384]{1,0:T(8,128)(2,1)S(1)}, bf16[480,384]{1,0:T(8,128)(2,1)S(1)}, u32[]{:S(2)}, u32[]{:S(2)}) collective-permute-start(bf16[480,384]{1,0:T(8,128)(2,1)S(1)} %collective-permute-done.4), channel_id=1, source_target_pairs={{4,0},{8,4},{12,8},{5,1},{9,5},{13,9},{6,2},{10,6},{14,10},{7,3},{... | collective-permute-start | bytes 1105928 | tf_op jit(solution)/shard_map/ppermute | solution.py:29
  42.5 15.1 %slice-start = ((s8[7962624]{0:T(1024)(128)(4,1)}), s8[3768320]{0:T(1024)(128)(4,1)S(1)}, s32[]{:S(2)}) async-start(s8[7962624]{0:T(1024)(128)(4,1)} %bitcast.100), calls=%async_computation | async-start | bytes 7536640
  52.2 5.4 %slice-start.1 = ((s8[7962624]{0:T(1024)(128)(4,1)}), s8[4194304]{0:T(1024)(128)(4,1)S(1)}, s32[]{:S(2)}) async-start(s8[7962624]{0:T(1024)(128)(4,1)} %bitcast.100), calls=%async_computation.1 | async-start | bytes 8388608
  52.2 19.2 %collective-permute-start.7 = (bf16[3,160,384]{2,1,0:T(8,128)(2,1)}, bf16[3,160,384]{2,1,0:T(8,128)(2,1)S(1)}, u32[]{:S(2)}, u32[]{:S(2)}) collective-permute-start(bf16[3,160,384]{2,1,0:T(8,128)(2,1)} %bitcast.125), channel_id=1, source_target_pairs={{0,2},{4,6},{8,10},{12,14},{16,18},{20,22},{24,26},{28,30}} | collective-permute-start | bytes 1105928 | tf_op jit(solution)/shard_map/ppermute | solution.py:154
  53.8 12.3 %collective-permute-start.6 = (bf16[3,160,384]{2,1,0:T(8,128)(2,1)}, bf16[3,160,384]{2,1,0:T(8,128)(2,1)S(1)}, u32[]{:S(2)}, u32[]{:S(2)}) collective-permute-start(bf16[3,160,384]{2,1,0:T(8,128)(2,1)} %bitcast.126), channel_id=1, source_target_pairs={{0,1},{1,2},{2,3},{4,5},{5,6},{6,7},{8,9},{9,10},{10,11},{12,13},{... | collective-permute-start | bytes 1105928 | tf_op jit(solution)/shard_map/ppermute | solution.py:15
  59.9 6.1 %copy-start.1 = (bf16[2,3,160,384]{3,2,1,0:T(8,128)(2,1)S(1)}, bf16[2,3,160,384]{3,2,1,0:T(8,128)(2,1)}, u32[]{:S(2)}) copy-start(bf16[2,3,160,384]{3,2,1,0:T(8,128)(2,1)} %param.10) | copy-start | bytes 2211844
  66.1 5.3 %collective-permute-start.8 = (bf16[3,160,384]{2,1,0:T(8,128)(2,1)S(1)}, bf16[3,160,384]{2,1,0:T(8,128)(2,1)S(1)}, u32[]{:S(2)}, u32[]{:S(2)}) collective-permute-start(bf16[3,160,384]{2,1,0:T(8,128)(2,1)S(1)} %bitcast_select_fusion.1), channel_id=1, source_target_pairs={{2,3},{6,7},{10,11},{14,15},{18,19},{22,23},{26,27},{30,31}} | collective-permute-start | bytes 1105928 | tf_op jit(solution)/shard_map/ppermute | solution.py:155
  69.5 1.2 %copy-start.3 = (bf16[480,384]{1,0:T(8,128)(2,1)S(1)}, bf16[480,384]{1,0:T(8,128)(2,1)}, u32[]{:S(2)}) copy-start(bf16[480,384]{1,0:T(8,128)(2,1)} %get-tuple-element.7) | copy-start | bytes 1105924
  72.6 7.8 %collective-permute-start.10 = (bf16[160,384]{1,0:T(8,128)(2,1)S(1)}, bf16[160,384]{1,0:T(8,128)(2,1)S(1)}, u32[]{:S(2)}, u32[]{:S(2)}) collective-permute-start(bf16[160,384]{1,0:T(8,128)(2,1)S(1)} %fusion.3), channel_id=1, source_target_pairs={{4,0},{8,4},{12,8},{5,1},{9,5},{13,9},{6,2},{10,6},{14,10},{7,3},{... | collective-permute-start | bytes 368648 | tf_op jit(solution)/shard_map/ppermute | solution.py:183
  75.4 6.8 %collective-permute-start.9 = (bf16[160,384]{1,0:T(8,128)(2,1)S(1)}, bf16[160,384]{1,0:T(8,128)(2,1)S(1)}, u32[]{:S(2)}, u32[]{:S(2)}) collective-permute-start(bf16[160,384]{1,0:T(8,128)(2,1)S(1)} %fusion.2), channel_id=1, source_target_pairs={{0,4},{4,8},{8,12},{1,5},{5,9},{9,13},{2,6},{6,10},{10,14},{3,7},{... | collective-permute-start | bytes 368648 | tf_op jit(solution)/shard_map/ppermute | solution.py:186

commit v14 on v11

--- a/solution.py
+++ b/solution.py
@@ -84,7 +84,7 @@
 def attend(whole, flat, query, attn_gain, key_weight, value_weight, out_weight, conv_gain, scale):
     count, width = query.shape
     total_keys = whole.shape[0]
-    block = 160 if count % 160 == 0 else count
+    block = 160 if count % 160 == 0 and count * total_keys > 2 ** 21 else count
     full = lambda shape: pl.BlockSpec(shape, lambda i: (0, 0))
     rows_of = pl.BlockSpec((block, width), lambda i: (i, 0))
     flops = 4 * count * total_keys * width + 4 * total_keys * width * width

time: 83.3 us -> 81.6 us (0.980)
  Pallas kernels: 9.71 us -> 7.99 us
    pallas_call x1, Pallas kernels: 9.71 us -> 7.99 us  [attend(): pl.pallas_call(functools.partial(attention_kernel, scale), out_shape=(jax...]
where the time goes in v14:
time: 81.6 us; the launch traced here: 81.1 us
  starting transfers between devices  27.8 us (34%)
  waiting for transfers between devices  23.6 us (29%)
  matrix products  12.1 us (15%)
  Pallas kernels  7.99 us (10%)
  local copies, waits for them, and re-layouts  7.17 us (9%)
  other arithmetic  2.04 us (2%)
    ppermute x3, starting transfers between devices, strip_gather(): up = lax.ppermute(up, axis, up_pairs)  10.6 us
    ppermute x3, waiting for transfers between devices, strip_gather(): up = lax.ppermute(up, axis, up_pairs)  9.35 us
    pallas_call x1, Pallas kernels, attend(): pl.pallas_call(functools.partial(attention_kernel, scale), out_shape=(jax...  7.99 us
    dot_general x9, matrix products, frame_terms(): jnp.dot(window, kernel[step_t, step_r], preferred_element_type=jnp.float32)  7.76 us
    ppermute x3, waiting for transfers between devices, strip_gather(): down = lax.ppermute(down, axis, down_pairs)  7.53 us
    ppermute x3, starting transfers between devices, strip_gather(): down = lax.ppermute(down, axis, down_pairs)  7.12 us
    ppermute x2, waiting for transfers between devices, passed_along(): return lax.ppermute(x, axis, pairs)  5.01 us
    ppermute x2, starting transfers between devices, passed_along(): return lax.ppermute(x, axis, pairs)  4.27 us
  transfers between devices with their start and end apart: 10, of which 8 were waited for; matrix products, arithmetic and copies ran while one was open for 21% of the time, Pallas kernels for 0%

profile of v14, /device:TPU:10, one launch (start us, length us, event | category | flops | bytes accessed | tf_op | source)
XLA Modules:
  0.0 81.1 jit_solution(5272646307803079991)
XLA Ops:
  0.0 3.6 %collective-permute-start = (bf16[480,384]{1,0:T(8,128)(2,1)}, bf16[480,384]{1,0:T(8,128)(2,1)S(1)}, u32[]{:S(2)}, u32[]{:S(2)}) collective-permute-start(bf16[480,384]{1,0:T(8,128)(2,1)} %bitcast.114), channel_id=1, source_target_pairs={{0,4},{4,8},{8,12},{1,5},{5,9},{9,13},{2,6},{6,10},{10,14},{3,7},{... | collective-permute-start | bytes 1105928 | tf_op jit(solution)/shard_map/ppermute | solution.py:28
  3.6 2.4 %collective-permute-start.3 = (bf16[480,384]{1,0:T(8,128)(2,1)}, bf16[480,384]{1,0:T(8,128)(2,1)S(1)}, u32[]{:S(2)}, u32[]{:S(2)}) collective-permute-start(bf16[480,384]{1,0:T(8,128)(2,1)} %bitcast.115), channel_id=1, source_target_pairs={{4,0},{8,4},{12,8},{5,1},{9,5},{13,9},{6,2},{10,6},{14,10},{7,3},{... | collective-permute-start | bytes 1105928 | tf_op jit(solution)/shard_map/ppermute | solution.py:29
  6.0 6.6 %collective-permute-done = bf16[480,384]{1,0:T(8,128)(2,1)S(1)} collective-permute-done((bf16[480,384]{1,0:T(8,128)(2,1)}, bf16[480,384]{1,0:T(8,128)(2,1)S(1)}, u32[]{:S(2)}, u32[]{:S(2)}) %collective-permute-start) | collective-permute-done | bytes 368672 | tf_op jit(solution)/shard_map/ppermute | solution.py:28
  12.6 3.5 %collective-permute-start.1 = (bf16[480,384]{1,0:T(8,128)(2,1)S(1)}, bf16[480,384]{1,0:T(8,128)(2,1)S(1)}, u32[]{:S(2)}, u32[]{:S(2)}) collective-permute-start(bf16[480,384]{1,0:T(8,128)(2,1)S(1)} %collective-permute-done), channel_id=1, source_target_pairs={{0,4},{4,8},{8,12},{1,5},{5,9},{9,13},{2,6},{6,10},{10,14},{3,7},{... | collective-permute-start | bytes 1105928 | tf_op jit(solution)/shard_map/ppermute | solution.py:28
  16.0 1.3 %reshape.69.cgain_ref = f32[1,384]{1,0:T(1,128)} reshape(f32[384]{0:T(512)} %param.16) | data formatting | bytes 3072 | tf_op jit(solution)/shard_map/reshape | solution.py:122
  17.3 1.3 %broadcast_in_dim.4.again_ref = f32[1,384]{1,0:T(1,128)} reshape(f32[384]{0:T(512)} %param.11) | data formatting | bytes 3072 | tf_op jit(solution)/shard_map/broadcast_in_dim | solution.py:39
  18.6 1.2 %multiply_reduce_fusion = f32[3,160]{1,0:T(4,128)S(1)} fusion(bf16[1,3,160,384]{3,2,1,0:T(8,128)(2,1)} %param.9), kind=kLoop, calls=%fused_computation.45 | loop fusion | flops 552480 | bytes 370560 | tf_op jit(solution)/shard_map/reduce_sum | solution.py:39
  19.8 2.4 %collective-permute-start.4 = (bf16[480,384]{1,0:T(8,128)(2,1)S(1)}, bf16[480,384]{1,0:T(8,128)(2,1)S(1)}, u32[]{:S(2)}, u32[]{:S(2)}) collective-permute-start(bf16[480,384]{1,0:T(8,128)(2,1)S(1)} %collective-permute-done.3), channel_id=1, source_target_pairs={{4,0},{8,4},{12,8},{5,1},{9,5},{13,9},{6,2},{10,6},{14,10},{7,3},{... | collective-permute-start | bytes 1105928 | tf_op jit(solution)/shard_map/ppermute | solution.py:29
  22.2 1.7 %collective-permute-done.1 = bf16[480,384]{1,0:T(8,128)(2,1)S(1)} collective-permute-done((bf16[480,384]{1,0:T(8,128)(2,1)S(1)}, bf16[480,384]{1,0:T(8,128)(2,1)S(1)}, u32[]{:S(2)}, u32[]{:S(2)}) %collective-permute-start.1) | collective-permute-done | bytes 368672 | tf_op jit(solution)/shard_map/ppermute | solution.py:28
  23.9 3.5 %collective-permute-start.2 = (bf16[480,384]{1,0:T(8,128)(2,1)S(1)}, bf16[480,384]{1,0:T(8,128)(2,1)S(1)}, u32[]{:S(2)}, u32[]{:S(2)}) collective-permute-start(bf16[480,384]{1,0:T(8,128)(2,1)S(1)} %collective-permute-done.1), channel_id=1, source_target_pairs={{0,4},{4,8},{8,12},{1,5},{5,9},{9,13},{2,6},{6,10},{10,14},{3,7},{... | collective-permute-start | bytes 1105928 | tf_op jit(solution)/shard_map/ppermute | solution.py:28
  27.6 2.2 %convolution_convert_fusion.query_ref = bf16[480,384]{1,0:T(8,128)(2,1)} fusion(bf16[384,384]{1,0:T(8,128)(2,1)S(1)} %copy-done, bf16[480,384]{1,0:T(8,128)(2,1)} %bitcast.116, f32[384]{0:T(512)} %param.11, f32[480]{0:T(512)S(1)} %rsqrt.12), kind=kOutput, calls=%fused_computation.11 | convolution fusion | flops 142479360 | bytes 1035648 | tf_op jit(solution)/shard_map/dot_general | solution.py:145
  29.7 1.2 %collective-permute-done.4 = bf16[480,384]{1,0:T(8,128)(2,1)S(1)} collective-permute-done((bf16[480,384]{1,0:T(8,128)(2,1)S(1)}, bf16[480,384]{1,0:T(8,128)(2,1)S(1)}, u32[]{:S(2)}, u32[]{:S(2)}) %collective-permute-start.4) | collective-permute-done | bytes 368672 | tf_op jit(solution)/shard_map/ppermute | solution.py:29
  30.9 2.4 %collective-permute-start.5 = (bf16[480,384]{1,0:T(8,128)(2,1)S(1)}, bf16[480,384]{1,0:T(8,128)(2,1)S(1)}, u32[]{:S(2)}, u32[]{:S(2)}) collective-permute-start(bf16[480,384]{1,0:T(8,128)(2,1)S(1)} %collective-permute-done.4), channel_id=1, source_target_pairs={{4,0},{8,4},{12,8},{5,1},{9,5},{13,9},{6,2},{10,6},{14,10},{7,3},{... | collective-permute-start | bytes 1105928 | tf_op jit(solution)/shard_map/ppermute | solution.py:29
  33.3 1.1 %collective-permute-done.2 = bf16[480,384]{1,0:T(8,128)(2,1)S(1)} collective-permute-done((bf16[480,384]{1,0:T(8,128)(2,1)S(1)}, bf16[480,384]{1,0:T(8,128)(2,1)S(1)}, u32[]{:S(2)}, u32[]{:S(2)}) %collective-permute-start.2) | collective-permute-done | bytes 368672 | tf_op jit(solution)/shard_map/ppermute | solution.py:28
  34.8 6.3 %collective-permute-done.5 = bf16[480,384]{1,0:T(8,128)(2,1)S(1)} collective-permute-done((bf16[480,384]{1,0:T(8,128)(2,1)S(1)}, bf16[480,384]{1,0:T(8,128)(2,1)S(1)}, u32[]{:S(2)}, u32[]{:S(2)}) %collective-permute-start.5) | collective-permute-done | bytes 368672 | tf_op jit(solution)/shard_map/ppermute | solution.py:29
  41.2 1.3 %constant_dynamic-slice_fusion.whole_ref = bf16[1920,384]{1,0:T(8,128)(2,1)} fusion(bf16[3360,384]{1,0:T(8,128)(2,1)S(1)} %constant_dynamic-update-slice_fusion, s32[]{:T(128)S(6)} %select_n.15), kind=kLoop, calls=%fused_computation.66 | loop fusion | bytes 2949124 | tf_op jit(solution)/shard_map/dynamic_slice | solution.py:34
  42.5 8.0 %shard_map.91 = (bf16[480,384]{1,0:T(8,128)(2,1)}, bf16[480,384]{1,0:T(8,128)(2,1)}) custom-call(bf16[1920,384]{1,0:T(8,128)(2,1)} %constant_dynamic-slice_fusion.whole_ref, bf16[480,384]{1,0:T(8,128)(2,1)} %bitcast.117, bf16[480,384]{1,0:T(8,128)(2,1)} %convolution_convert_fusion.query_ref, f32[1,384]{1,0:T(1,128)} %broadcast_in_dim.4.again_ref, ...), custom_call_target="tpu_custom_call" | custom-call | flops 2689597440 | bytes 3833856 | tf_op jit(solution)/shard_map/pallas_call | solution.py:92
  50.5 2.2 %collective-permute-start.6 = (bf16[3,160,384]{2,1,0:T(8,128)(2,1)}, bf16[3,160,384]{2,1,0:T(8,128)(2,1)S(1)}, u32[]{:S(2)}, u32[]{:S(2)}) collective-permute-start(bf16[3,160,384]{2,1,0:T(8,128)(2,1)} %bitcast.122), channel_id=1, source_target_pairs={{0,1},{1,2},{2,3},{4,5},{5,6},{6,7},{8,9},{9,10},{10,11},{12,13},{... | collective-permute-start | bytes 1105928 | tf_op jit(solution)/shard_map/ppermute | solution.py:15
  52.7 1.5 %pad_slice_fusion.8 = (bf16[5,160,384]{2,1,0:T(8,128)(2,1)S(1)}, bf16[5,160,384]{2,1,0:T(8,128)(2,1)S(1)}, bf16[5,160,384]{2,1,0:T(8,128)(2,1)S(1)}) fusion(bf16[3,160,384]{2,1,0:T(8,128)(2,1)} %bitcast.123), kind=kLoop, calls=%fused_computation.40 | loop fusion | bytes 2211840 | tf_op jit(solution)/shard_map/slice | solution.py:160
  54.1 0.2 pad_maximum_fusion
  54.3 0.3 fusion.13
  54.6 0.4 fusion.6
  55.0 0.8 fusion.5
  55.8 0.8 convolution_add_fusion.5
  56.5 0.4 fusion.4
  56.9 0.8 convolution_add_fusion.4
  57.7 2.1 %collective-permute-done.6 = bf16[3,160,384]{2,1,0:T(8,128)(2,1)S(1)} collective-permute-done((bf16[3,160,384]{2,1,0:T(8,128)(2,1)}, bf16[3,160,384]{2,1,0:T(8,128)(2,1)S(1)}, u32[]{:S(2)}, u32[]{:S(2)}) %collective-permute-start.6) | collective-permute-done | bytes 368672 | tf_op jit(solution)/shard_map/ppermute | solution.py:15
  59.9 2.1 %collective-permute-start.7 = (bf16[3,160,384]{2,1,0:T(8,128)(2,1)S(1)}, bf16[3,160,384]{2,1,0:T(8,128)(2,1)S(1)}, u32[]{:S(2)}, u32[]{:S(2)}) collective-permute-start(bf16[3,160,384]{2,1,0:T(8,128)(2,1)S(1)} %bitcast_select_fusion.1), channel_id=1, source_target_pairs={{0,1},{1,2},{2,3},{4,5},{5,6},{6,7},{8,9},{9,10},{10,11},{12,13},{... | collective-permute-start | bytes 1105928 | tf_op jit(solution)/shard_map/ppermute | solution.py:15
  62.0 0.3 pad_slice_fusion.5
  62.2 0.2 pad_maximum_fusion.1
  62.4 0.3 fusion.14
  62.7 0.4 convolution_add_fusion.7
  63.0 0.8 fusion.7
  63.8 0.8 convolution_add_fusion.3
  64.6 0.4 convolution_add_fusion.9
  65.0 0.8 %fusion.1 = f32[480,384]{1,0:T(8,128)S(1)} fusion(f32[480,384]{1,0:T(8,128)S(1)} %convolution_add_fusion.3, bf16[480,1152]{1,0:T(8,128)(2,1)S(1)} %bitcast.93, bf16[3,3,1152,384]{3,2,1,0:T(8,128)(2,1)S(1)} %bitcast.108, f32[480,384]{1,0:T(8,128)S(1)} %convolution_add_fusion.4, bf16[480,384]{1,0:T(8,128)(2,1)S(1)} %copy-done.3), kind=kOutput, calls=%fused_computation.7 | convolution fusion | flops 425410560 | bytes 4571136 | tf_op jit(solution)/shard_map/dot_general | solution.py:167
  65.8 2.9 %collective-permute-done.7 = bf16[3,160,384]{2,1,0:T(8,128)(2,1)S(1)} collective-permute-done((bf16[3,160,384]{2,1,0:T(8,128)(2,1)S(1)}, bf16[3,160,384]{2,1,0:T(8,128)(2,1)S(1)}, u32[]{:S(2)}, u32[]{:S(2)}) %collective-permute-start.7) | collective-permute-done | bytes 368672 | tf_op jit(solution)/shard_map/ppermute | solution.py:15
  68.8 0.3 pad_slice_fusion.2
  69.0 0.2 pad_maximum_fusion.2
  69.2 0.3 fusion.12
  69.5 0.4 fusion.3
  69.8 2.4 %collective-permute-start.9 = (bf16[160,384]{1,0:T(8,128)(2,1)S(1)}, bf16[160,384]{1,0:T(8,128)(2,1)S(1)}, u32[]{:S(2)}, u32[]{:S(2)}) collective-permute-start(bf16[160,384]{1,0:T(8,128)(2,1)S(1)} %fusion.3), channel_id=1, source_target_pairs={{4,0},{8,4},{12,8},{5,1},{9,5},{13,9},{6,2},{10,6},{14,10},{7,3},{... | collective-permute-start | bytes 368648 | tf_op jit(solution)/shard_map/ppermute | solution.py:179
  72.2 0.4 fusion.2
  72.6 3.5 %collective-permute-start.8 = (bf16[160,384]{1,0:T(8,128)(2,1)S(1)}, bf16[160,384]{1,0:T(8,128)(2,1)S(1)}, u32[]{:S(2)}, u32[]{:S(2)}) collective-permute-start(bf16[160,384]{1,0:T(8,128)(2,1)S(1)} %fusion.2), channel_id=1, source_target_pairs={{0,4},{4,8},{8,12},{1,5},{5,9},{9,13},{2,6},{6,10},{10,14},{3,7},{... | collective-permute-start | bytes 368648 | tf_op jit(solution)/shard_map/ppermute | solution.py:182
  76.1 0.8 fusion.8
  76.8 0.8 convolution_add_fusion.1
  77.7 1.7 %collective-permute-done.8 = bf16[160,384]{1,0:T(8,128)(2,1)S(1)} collective-permute-done((bf16[160,384]{1,0:T(8,128)(2,1)S(1)}, bf16[160,384]{1,0:T(8,128)(2,1)S(1)}, u32[]{:S(2)}, u32[]{:S(2)}) %collective-permute-start.8) | collective-permute-done | bytes 122912 | tf_op jit(solution)/shard_map/ppermute | solution.py:182
  79.5 1.6 %fusion.9 = bf16[480,384]{1,0:T(8,128)(2,1)} fusion(f32[3,160,384]{2,1,0:T(8,128)S(1)} %pad_maximum_fusion.3, f32[480,384]{1,0:T(8,128)S(1)} %fusion.1, f32[480,384]{1,0:T(8,128)S(1)} %convolution_add_fusion.1, bf16[480,1152]{1,0:T(8,128)(2,1)S(1)} %bitcast.91, bf16[3,3,1152,384]{3,2,1,0:T(8,128)(2,1)S(1)} %bitcast.113), kind=kOutput, calls=%fused_computation.43 | convolution fusion | flops 425410560 | bytes 4571136 | tf_op jit(solution)/shard_map/dot_general | solution.py:167
  (30 shorter events, 0.9 us)
Async XLA Ops:
  0.0 27.6 %copy-start = (bf16[384,384]{1,0:T(8,128)(2,1)S(1)}, bf16[384,384]{1,0:T(8,128)(2,1)}, u32[]{:S(2)}) copy-start(bf16[384,384]{1,0:T(8,128)(2,1)} %param.12) | copy-start | bytes 884740
  0.0 12.6 %collective-permute-start = (bf16[480,384]{1,0:T(8,128)(2,1)}, bf16[480,384]{1,0:T(8,128)(2,1)S(1)}, u32[]{:S(2)}, u32[]{:S(2)}) collective-permute-start(bf16[480,384]{1,0:T(8,128)(2,1)} %bitcast.114), channel_id=1, source_target_pairs={{0,4},{4,8},{8,12},{1,5},{5,9},{9,13},{2,6},{6,10},{10,14},{3,7},{... | collective-permute-start | bytes 1105928 | tf_op jit(solution)/shard_map/ppermute | solution.py:28
  3.6 16.2 %collective-permute-start.3 = (bf16[480,384]{1,0:T(8,128)(2,1)}, bf16[480,384]{1,0:T(8,128)(2,1)S(1)}, u32[]{:S(2)}, u32[]{:S(2)}) collective-permute-start(bf16[480,384]{1,0:T(8,128)(2,1)} %bitcast.115), channel_id=1, source_target_pairs={{4,0},{8,4},{12,8},{5,1},{9,5},{13,9},{6,2},{10,6},{14,10},{7,3},{... | collective-permute-start | bytes 1105928 | tf_op jit(solution)/shard_map/ppermute | solution.py:29
  12.6 11.4 %collective-permute-start.1 = (bf16[480,384]{1,0:T(8,128)(2,1)S(1)}, bf16[480,384]{1,0:T(8,128)(2,1)S(1)}, u32[]{:S(2)}, u32[]{:S(2)}) collective-permute-start(bf16[480,384]{1,0:T(8,128)(2,1)S(1)} %collective-permute-done), channel_id=1, source_target_pairs={{0,4},{4,8},{8,12},{1,5},{5,9},{9,13},{2,6},{6,10},{10,14},{3,7},{... | collective-permute-start | bytes 1105928 | tf_op jit(solution)/shard_map/ppermute | solution.py:28
  18.6 16.0 %copy-start.1 = (bf16[1,3,160,384]{3,2,1,0:T(8,128)(2,1)S(1)}, bf16[1,3,160,384]{3,2,1,0:T(8,128)(2,1)}, u32[]{:S(2)}) copy-start(bf16[1,3,160,384]{3,2,1,0:T(8,128)(2,1)} %param.9) | copy-start | bytes 1105924
  19.8 11.1 %collective-permute-start.4 = (bf16[480,384]{1,0:T(8,128)(2,1)S(1)}, bf16[480,384]{1,0:T(8,128)(2,1)S(1)}, u32[]{:S(2)}, u32[]{:S(2)}) collective-permute-start(bf16[480,384]{1,0:T(8,128)(2,1)S(1)} %collective-permute-done.3), channel_id=1, source_target_pairs={{4,0},{8,4},{12,8},{5,1},{9,5},{13,9},{6,2},{10,6},{14,10},{7,3},{... | collective-permute-start | bytes 1105928 | tf_op jit(solution)/shard_map/ppermute | solution.py:29
  23.9 10.5 %collective-permute-start.2 = (bf16[480,384]{1,0:T(8,128)(2,1)S(1)}, bf16[480,384]{1,0:T(8,128)(2,1)S(1)}, u32[]{:S(2)}, u32[]{:S(2)}) collective-permute-start(bf16[480,384]{1,0:T(8,128)(2,1)S(1)} %collective-permute-done.1), channel_id=1, source_target_pairs={{0,4},{4,8},{8,12},{1,5},{5,9},{9,13},{2,6},{6,10},{10,14},{3,7},{... | collective-permute-start | bytes 1105928 | tf_op jit(solution)/shard_map/ppermute | solution.py:28
  30.9 10.2 %collective-permute-start.5 = (bf16[480,384]{1,0:T(8,128)(2,1)S(1)}, bf16[480,384]{1,0:T(8,128)(2,1)S(1)}, u32[]{:S(2)}, u32[]{:S(2)}) collective-permute-start(bf16[480,384]{1,0:T(8,128)(2,1)S(1)} %collective-permute-done.4), channel_id=1, source_target_pairs={{4,0},{8,4},{12,8},{5,1},{9,5},{13,9},{6,2},{10,6},{14,10},{7,3},{... | collective-permute-start | bytes 1105928 | tf_op jit(solution)/shard_map/ppermute | solution.py:29
  42.5 12.1 %slice-start = ((s8[7962624]{0:T(1024)(128)(4,1)}), s8[3768320]{0:T(1024)(128)(4,1)S(1)}, s32[]{:S(2)}) async-start(s8[7962624]{0:T(1024)(128)(4,1)} %bitcast.97), calls=%async_computation | async-start | bytes 7536640
  50.5 4.1 %slice-start.1 = ((s8[7962624]{0:T(1024)(128)(4,1)}), s8[4194304]{0:T(1024)(128)(4,1)S(1)}, s32[]{:S(2)}) async-start(s8[7962624]{0:T(1024)(128)(4,1)} %bitcast.97), calls=%async_computation.1 | async-start | bytes 8388608
  50.5 9.3 %collective-permute-start.6 = (bf16[3,160,384]{2,1,0:T(8,128)(2,1)}, bf16[3,160,384]{2,1,0:T(8,128)(2,1)S(1)}, u32[]{:S(2)}, u32[]{:S(2)}) collective-permute-start(bf16[3,160,384]{2,1,0:T(8,128)(2,1)} %bitcast.122), channel_id=1, source_target_pairs={{0,1},{1,2},{2,3},{4,5},{5,6},{6,7},{8,9},{9,10},{10,11},{12,13},{... | collective-permute-start | bytes 1105928 | tf_op jit(solution)/shard_map/ppermute | solution.py:15
  56.9 2.9 %copy-start.2 = (bf16[2,3,160,384]{3,2,1,0:T(8,128)(2,1)S(1)}, bf16[2,3,160,384]{3,2,1,0:T(8,128)(2,1)}, u32[]{:S(2)}) copy-start(bf16[2,3,160,384]{3,2,1,0:T(8,128)(2,1)} %param.10) | copy-start | bytes 2211844
  59.9 8.8 %collective-permute-start.7 = (bf16[3,160,384]{2,1,0:T(8,128)(2,1)S(1)}, bf16[3,160,384]{2,1,0:T(8,128)(2,1)S(1)}, u32[]{:S(2)}, u32[]{:S(2)}) collective-permute-start(bf16[3,160,384]{2,1,0:T(8,128)(2,1)S(1)} %bitcast_select_fusion.1), channel_id=1, source_target_pairs={{0,1},{1,2},{2,3},{4,5},{5,6},{6,7},{8,9},{9,10},{10,11},{12,13},{... | collective-permute-start | bytes 1105928 | tf_op jit(solution)/shard_map/ppermute | solution.py:15
  63.8 1.2 %copy-start.3 = (bf16[480,384]{1,0:T(8,128)(2,1)S(1)}, bf16[480,384]{1,0:T(8,128)(2,1)}, u32[]{:S(2)}) copy-start(bf16[480,384]{1,0:T(8,128)(2,1)} %get-tuple-element.7) | copy-start | bytes 1105924
  69.8 7.8 %collective-permute-start.9 = (bf16[160,384]{1,0:T(8,128)(2,1)S(1)}, bf16[160,384]{1,0:T(8,128)(2,1)S(1)}, u32[]{:S(2)}, u32[]{:S(2)}) collective-permute-start(bf16[160,384]{1,0:T(8,128)(2,1)S(1)} %fusion.3), channel_id=1, source_target_pairs={{4,0},{8,4},{12,8},{5,1},{9,5},{13,9},{6,2},{10,6},{14,10},{7,3},{... | collective-permute-start | bytes 368648 | tf_op jit(solution)/shard_map/ppermute | solution.py:179
  72.6 6.8 %collective-permute-start.8 = (bf16[160,384]{1,0:T(8,128)(2,1)S(1)}, bf16[160,384]{1,0:T(8,128)(2,1)S(1)}, u32[]{:S(2)}, u32[]{:S(2)}) collective-permute-start(bf16[160,384]{1,0:T(8,128)(2,1)S(1)} %fusion.2), channel_id=1, source_target_pairs={{0,4},{4,8},{8,12},{1,5},{5,9},{9,13},{2,6},{6,10},{10,14},{3,7},{... | collective-permute-start | bytes 368648 | tf_op jit(solution)/shard_map/ppermute | solution.py:182

commit v15 on v14

--- a/solution.py
+++ b/solution.py
@@ -20,13 +20,11 @@
     if n == 1:
         return x
     m = x.shape[0]
-    up_pairs = [(i, i + 1) for i in range(n - 1)]
-    down_pairs = [(i + 1, i) for i in range(n - 1)]
     ups, downs = [], []
     up, down = x, x
-    for _ in range(n - 1):
-        up = lax.ppermute(up, axis, up_pairs)
-        down = lax.ppermute(down, axis, down_pairs)
+    for step in range(1, n):
+        up = lax.ppermute(up, axis, [(i, i + 1) for i in range(step - 1, n - 1)])
+        down = lax.ppermute(down, axis, [(i + 1, i) for i in range(0, n - step)])
         ups.append(up)
         downs.append(down)
     stacked = jnp.concatenate(ups[::-1] + [x] + downs, axis=0)
@@ -45,18 +43,18 @@
 
 
 def attention_kernel(
-    scale, whole_ref, flat_ref, query_ref, again_ref, wk_ref, wv_ref, wo_ref, cgain_ref,
+    scale, whole_ref, flat_ref, query_ref, again_ref, wkv_ref, wo_ref, cgain_ref,
     resid_ref, act_ref, keys_ref, values_ref,
 ):
     @pl.when(pl.program_id(0) == 0)
     def _():
         normed_all = scaled(whole_ref[...], again_ref[...]).astype(jnp.bfloat16)
-        keys_ref[...] = jnp.dot(
-            normed_all, wk_ref[...], preferred_element_type=jnp.float32
+        both = jnp.dot(
+            normed_all, wkv_ref[...], preferred_element_type=jnp.float32
         ).astype(jnp.bfloat16)
-        values_ref[...] = jnp.dot(
-            normed_all, wv_ref[...], preferred_element_type=jnp.float32
-        ).astype(jnp.bfloat16)
+        width = keys_ref.shape[1]
+        keys_ref[...] = both[:, :width]
+        values_ref[...] = both[:, width:]
 
     scores = (
         lax.dot_general(
@@ -101,8 +99,7 @@
             rows_of,
             rows_of,
             full((1, width)),
-            full((width, width)),
-            full((width, width)),
+            full((width, 2 * width)),
             full((width, width)),
             full((1, width)),
         ],
@@ -118,7 +115,8 @@
             bytes_accessed=2 * width * (total_keys + 4 * count + 3 * width),
         ),
     )(
-        whole, flat, query, attn_gain.reshape(1, width), key_weight, value_weight, out_weight,
+        whole, flat, query, attn_gain.reshape(1, width),
+        jnp.concatenate([key_weight, value_weight], axis=1), out_weight,
         conv_gain.reshape(1, width),
     )
 

time: 81.6 us -> 81.6 us (level)
  starting transfers between devices: 27.8 us -> 24.9 us
  other arithmetic: 2.04 us -> 3.91 us
  waiting for transfers between devices: 23.6 us -> 24.7 us
    ppermute x6, starting transfers between devices: 17.7 us -> 14.3 us  [the longest x3 7.77 us: strip_gather(): up = lax.ppermute(up, axis, [(i, i + 1) for i in range(step - 1, n - 1)])]
    ppermute x1, starting transfers between devices: 2.38 us -> 4.39 us  [shards(): lax.ppermute(to_prev.astype(jnp.bfloat16), 'strip', [(i + 1, i) for i in...]
    concatenate x0 -> x1, other arithmetic: none -> 1.94 us  [attend(): jnp.concatenate([key_weight, value_weight], axis=1)]
    ppermute x1, starting transfers between devices: 3.47 us -> 1.92 us  [shards(): lax.ppermute(to_next.astype(jnp.bfloat16), 'strip', [(i, i + 1) for i in...]
    ppermute x1, waiting for transfers between devices: 1.7 us -> 3.25 us  [shards(): lax.ppermute(to_next.astype(jnp.bfloat16), 'strip', [(i, i + 1) for i in...]
  transfers between devices with their start and end apart: 10 -> 10, of which waited for: 8 -> 7; matrix products, arithmetic and copies ran while one was open for 21% -> 24% of each run, Pallas kernels for 0% -> 0%
where the time goes in v15:
time: 81.6 us; the launch traced here: 81.1 us
  starting transfers between devices  24.9 us (31%)
  waiting for transfers between devices  24.7 us (30%)
  matrix products  12.2 us (15%)
  Pallas kernels  7.78 us (10%)
  local copies, waits for them, and re-layouts  7.3 us (9%)
  other arithmetic  3.91 us (5%)
    ppermute x3, waiting for transfers between devices, strip_gather(): down = lax.ppermute(down, axis, [(i + 1, i) for i in range(0, n - step)])  8.85 us
    pallas_call x1, Pallas kernels, attend(): pl.pallas_call(functools.partial(attention_kernel, scale), out_shape=(jax...  7.78 us
    ppermute x3, starting transfers between devices, strip_gather(): up = lax.ppermute(up, axis, [(i, i + 1) for i in range(step - 1, n - 1)])  7.77 us
    dot_general x9, matrix products, frame_terms(): jnp.dot(window, kernel[step_t, step_r], preferred_element_type=jnp.float32)  7.77 us
    ppermute x3, waiting for transfers between devices, strip_gather(): up = lax.ppermute(up, axis, [(i, i + 1) for i in range(step - 1, n - 1)])  7.68 us
    ppermute x3, starting transfers between devices, strip_gather(): down = lax.ppermute(down, axis, [(i + 1, i) for i in range(0, n - step)])  6.5 us
    ppermute x2, waiting for transfers between devices, passed_along(): return lax.ppermute(x, axis, pairs)  4.89 us
    ppermute x1, starting transfers between devices, shards(): lax.ppermute(to_prev.astype(jnp.bfloat16), 'strip', [(i + 1, i) for i in...  4.39 us
  transfers between devices with their start and end apart: 10, of which 7 were waited for; matrix products, arithmetic and copies ran while one was open for 24% of the time, Pallas kernels for 0%

profile of v15, /device:TPU:10, one launch (start us, length us, event | category | flops | bytes accessed | tf_op | source)
XLA Modules:
  0.0 81.1 jit_solution(10747639312749221850)
XLA Ops:
  0.0 3.6 %collective-permute-start = (bf16[480,384]{1,0:T(8,128)(2,1)}, bf16[480,384]{1,0:T(8,128)(2,1)S(1)}, u32[]{:S(2)}, u32[]{:S(2)}) collective-permute-start(bf16[480,384]{1,0:T(8,128)(2,1)} %bitcast.114), channel_id=1, source_target_pairs={{0,4},{4,8},{8,12},{1,5},{5,9},{9,13},{2,6},{6,10},{10,14},{3,7},{... | collective-permute-start | bytes 1105928 | tf_op jit(solution)/shard_map/ppermute | solution.py:26
  3.6 2.4 %collective-permute-start.3 = (bf16[480,384]{1,0:T(8,128)(2,1)}, bf16[480,384]{1,0:T(8,128)(2,1)S(1)}, u32[]{:S(2)}, u32[]{:S(2)}) collective-permute-start(bf16[480,384]{1,0:T(8,128)(2,1)} %bitcast.115), channel_id=1, source_target_pairs={{4,0},{8,4},{12,8},{5,1},{9,5},{13,9},{6,2},{10,6},{14,10},{7,3},{... | collective-permute-start | bytes 1105928 | tf_op jit(solution)/shard_map/ppermute | solution.py:27
  6.0 6.6 %collective-permute-done = bf16[480,384]{1,0:T(8,128)(2,1)S(1)} collective-permute-done((bf16[480,384]{1,0:T(8,128)(2,1)}, bf16[480,384]{1,0:T(8,128)(2,1)S(1)}, u32[]{:S(2)}, u32[]{:S(2)}) %collective-permute-start) | collective-permute-done | bytes 368672 | tf_op jit(solution)/shard_map/ppermute | solution.py:26
  12.6 3.5 %collective-permute-start.1 = (bf16[480,384]{1,0:T(8,128)(2,1)S(1)}, bf16[480,384]{1,0:T(8,128)(2,1)S(1)}, u32[]{:S(2)}, u32[]{:S(2)}) collective-permute-start(bf16[480,384]{1,0:T(8,128)(2,1)S(1)} %collective-permute-done), channel_id=1, source_target_pairs={{4,8},{8,12},{5,9},{9,13},{6,10},{10,14},{7,11},{11,15},{20,24},{2... | collective-permute-start | bytes 1105928 | tf_op jit(solution)/shard_map/ppermute | solution.py:26
  16.1 1.3 %reshape.69.cgain_ref = f32[1,384]{1,0:T(1,128)} reshape(f32[384]{0:T(512)} %param.16) | data formatting | bytes 3072 | tf_op jit(solution)/shard_map/reshape | solution.py:120
  17.3 1.3 %broadcast_in_dim.4.again_ref = f32[1,384]{1,0:T(1,128)} reshape(f32[384]{0:T(512)} %param.11) | data formatting | bytes 3072 | tf_op jit(solution)/shard_map/broadcast_in_dim | solution.py:37
  18.6 1.2 %multiply_reduce_fusion = f32[3,160]{1,0:T(4,128)S(1)} fusion(bf16[1,3,160,384]{3,2,1,0:T(8,128)(2,1)} %param.9), kind=kLoop, calls=%fused_computation.45 | loop fusion | flops 552480 | bytes 370560 | tf_op jit(solution)/shard_map/reduce_sum | solution.py:37
  20.0 1.9 %collective-permute-start.4 = (bf16[480,384]{1,0:T(8,128)(2,1)S(1)}, bf16[480,384]{1,0:T(8,128)(2,1)S(1)}, u32[]{:S(2)}, u32[]{:S(2)}) collective-permute-start(bf16[480,384]{1,0:T(8,128)(2,1)S(1)} %collective-permute-done.3), channel_id=1, source_target_pairs={{4,0},{8,4},{5,1},{9,5},{6,2},{10,6},{7,3},{11,7},{20,16},{24,20},... | collective-permute-start | bytes 1105928 | tf_op jit(solution)/shard_map/ppermute | solution.py:27
  21.9 1.1 %collective-permute-done.1 = bf16[480,384]{1,0:T(8,128)(2,1)S(1)} collective-permute-done((bf16[480,384]{1,0:T(8,128)(2,1)S(1)}, bf16[480,384]{1,0:T(8,128)(2,1)S(1)}, u32[]{:S(2)}, u32[]{:S(2)}) %collective-permute-start.1) | collective-permute-done | bytes 368672 | tf_op jit(solution)/shard_map/ppermute | solution.py:26
  23.0 0.7 collective-permute-start.2
  23.7 1.9 %pad_maximum_fusion.4.wkv_ref = bf16[384,768]{1,0:T(8,128)(2,1)} fusion(bf16[384,384]{1,0:T(8,128)(2,1)} %param.14, bf16[384,384]{1,0:T(8,128)(2,1)} %param.13), kind=kLoop, calls=%fused_computation.46 | loop fusion | flops 1179648 | bytes 1179648 | tf_op jit(solution)/shard_map/concatenate | solution.py:119
  25.6 2.2 %convolution_convert_fusion.query_ref = bf16[480,384]{1,0:T(8,128)(2,1)} fusion(bf16[384,384]{1,0:T(8,128)(2,1)S(1)} %copy-done, bf16[480,384]{1,0:T(8,128)(2,1)} %bitcast.116, f32[384]{0:T(512)} %param.11, f32[480]{0:T(512)S(1)} %rsqrt.12), kind=kOutput, calls=%fused_computation.11 | convolution fusion | flops 142479360 | bytes 1035648 | tf_op jit(solution)/shard_map/dot_general | solution.py:143
  27.9 3.2 %collective-permute-done.4 = bf16[480,384]{1,0:T(8,128)(2,1)S(1)} collective-permute-done((bf16[480,384]{1,0:T(8,128)(2,1)S(1)}, bf16[480,384]{1,0:T(8,128)(2,1)S(1)}, u32[]{:S(2)}, u32[]{:S(2)}) %collective-permute-start.4) | collective-permute-done | bytes 368672 | tf_op jit(solution)/shard_map/ppermute | solution.py:27
  31.0 2.2 %collective-permute-start.5 = (bf16[480,384]{1,0:T(8,128)(2,1)S(1)}, bf16[480,384]{1,0:T(8,128)(2,1)S(1)}, u32[]{:S(2)}, u32[]{:S(2)}) collective-permute-start(bf16[480,384]{1,0:T(8,128)(2,1)S(1)} %collective-permute-done.4), channel_id=1, source_target_pairs={{4,0},{5,1},{6,2},{7,3},{20,16},{21,17},{22,18},{23,19}} | collective-permute-start | bytes 1105928 | tf_op jit(solution)/shard_map/ppermute | solution.py:27
  33.7 5.7 %collective-permute-done.5 = bf16[480,384]{1,0:T(8,128)(2,1)S(1)} collective-permute-done((bf16[480,384]{1,0:T(8,128)(2,1)S(1)}, bf16[480,384]{1,0:T(8,128)(2,1)S(1)}, u32[]{:S(2)}, u32[]{:S(2)}) %collective-permute-start.5) | collective-permute-done | bytes 368672 | tf_op jit(solution)/shard_map/ppermute | solution.py:27
  39.4 1.3 %constant_dynamic-slice_fusion.whole_ref = bf16[1920,384]{1,0:T(8,128)(2,1)} fusion(bf16[3360,384]{1,0:T(8,128)(2,1)S(1)} %constant_dynamic-update-slice_fusion, s32[]{:T(128)S(6)} %select_n.15), kind=kLoop, calls=%fused_computation.67 | loop fusion | bytes 2949124 | tf_op jit(solution)/shard_map/dynamic_slice | solution.py:32
  40.7 7.8 %shard_map.91 = (bf16[480,384]{1,0:T(8,128)(2,1)}, bf16[480,384]{1,0:T(8,128)(2,1)}) custom-call(bf16[1920,384]{1,0:T(8,128)(2,1)} %constant_dynamic-slice_fusion.whole_ref, bf16[480,384]{1,0:T(8,128)(2,1)} %bitcast.117, bf16[480,384]{1,0:T(8,128)(2,1)} %convolution_convert_fusion.query_ref, f32[1,384]{1,0:T(1,128)} %broadcast_in_dim.4.again_ref, ...), custom_call_target="tpu_custom_call" | custom-call | flops 2689597440 | bytes 3833856 | tf_op jit(solution)/shard_map/pallas_call | solution.py:90
  48.5 2.2 %collective-permute-start.6 = (bf16[3,160,384]{2,1,0:T(8,128)(2,1)}, bf16[3,160,384]{2,1,0:T(8,128)(2,1)S(1)}, u32[]{:S(2)}, u32[]{:S(2)}) collective-permute-start(bf16[3,160,384]{2,1,0:T(8,128)(2,1)} %bitcast.122), channel_id=1, source_target_pairs={{0,1},{1,2},{2,3},{4,5},{5,6},{6,7},{8,9},{9,10},{10,11},{12,13},{... | collective-permute-start | bytes 1105928 | tf_op jit(solution)/shard_map/ppermute | solution.py:15
  50.7 1.6 %pad_slice_fusion.8 = (bf16[5,160,384]{2,1,0:T(8,128)(2,1)S(1)}, bf16[5,160,384]{2,1,0:T(8,128)(2,1)S(1)}, bf16[5,160,384]{2,1,0:T(8,128)(2,1)S(1)}) fusion(bf16[3,160,384]{2,1,0:T(8,128)(2,1)} %bitcast.123), kind=kLoop, calls=%fused_computation.40 | loop fusion | bytes 2211840 | tf_op jit(solution)/shard_map/slice | solution.py:158
  52.3 0.2 pad_maximum_fusion
  52.4 0.3 fusion.13
  52.7 0.4 fusion.6
  53.1 0.8 fusion.5
  53.9 0.8 convolution_add_fusion.5
  54.6 0.4 fusion.4
  55.0 0.8 convolution_add_fusion.4
  55.8 2.0 %collective-permute-done.6 = bf16[3,160,384]{2,1,0:T(8,128)(2,1)S(1)} collective-permute-done((bf16[3,160,384]{2,1,0:T(8,128)(2,1)}, bf16[3,160,384]{2,1,0:T(8,128)(2,1)S(1)}, u32[]{:S(2)}, u32[]{:S(2)}) %collective-permute-start.6) | collective-permute-done | bytes 368672 | tf_op jit(solution)/shard_map/ppermute | solution.py:15
  57.9 2.1 %collective-permute-start.7 = (bf16[3,160,384]{2,1,0:T(8,128)(2,1)S(1)}, bf16[3,160,384]{2,1,0:T(8,128)(2,1)S(1)}, u32[]{:S(2)}, u32[]{:S(2)}) collective-permute-start(bf16[3,160,384]{2,1,0:T(8,128)(2,1)S(1)} %bitcast_select_fusion.1), channel_id=1, source_target_pairs={{0,1},{1,2},{2,3},{4,5},{5,6},{6,7},{8,9},{9,10},{10,11},{12,13},{... | collective-permute-start | bytes 1105928 | tf_op jit(solution)/shard_map/ppermute | solution.py:15
  60.0 0.3 pad_slice_fusion.5
  60.2 0.2 pad_maximum_fusion.1
  60.4 0.3 fusion.14
  60.7 0.4 convolution_add_fusion.7
  61.0 0.8 fusion.7
  61.8 0.8 convolution_add_fusion.3
  62.6 0.4 convolution_add_fusion.9
  63.0 0.8 %fusion.1 = f32[480,384]{1,0:T(8,128)S(1)} fusion(f32[480,384]{1,0:T(8,128)S(1)} %convolution_add_fusion.3, bf16[480,1152]{1,0:T(8,128)(2,1)S(1)} %bitcast.93, bf16[3,3,1152,384]{3,2,1,0:T(8,128)(2,1)S(1)} %bitcast.108, f32[480,384]{1,0:T(8,128)S(1)} %convolution_add_fusion.4, bf16[480,384]{1,0:T(8,128)(2,1)S(1)} %copy-done.3), kind=kOutput, calls=%fused_computation.7 | convolution fusion | flops 425410560 | bytes 4571136 | tf_op jit(solution)/shard_map/dot_general | solution.py:165
  63.8 2.9 %collective-permute-done.7 = bf16[3,160,384]{2,1,0:T(8,128)(2,1)S(1)} collective-permute-done((bf16[3,160,384]{2,1,0:T(8,128)(2,1)S(1)}, bf16[3,160,384]{2,1,0:T(8,128)(2,1)S(1)}, u32[]{:S(2)}, u32[]{:S(2)}) %collective-permute-start.7) | collective-permute-done | bytes 368672 | tf_op jit(solution)/shard_map/ppermute | solution.py:15
  66.8 0.3 pad_slice_fusion.2
  67.0 0.2 pad_maximum_fusion.2
  67.2 0.3 fusion.12
  67.5 0.4 fusion.3
  67.8 4.4 %collective-permute-start.9 = (bf16[160,384]{1,0:T(8,128)(2,1)S(1)}, bf16[160,384]{1,0:T(8,128)(2,1)S(1)}, u32[]{:S(2)}, u32[]{:S(2)}) collective-permute-start(bf16[160,384]{1,0:T(8,128)(2,1)S(1)} %fusion.3), channel_id=1, source_target_pairs={{4,0},{8,4},{12,8},{5,1},{9,5},{13,9},{6,2},{10,6},{14,10},{7,3},{... | collective-permute-start | bytes 368648 | tf_op jit(solution)/shard_map/ppermute | solution.py:177
  72.2 0.4 fusion.2
  72.6 1.9 %collective-permute-start.8 = (bf16[160,384]{1,0:T(8,128)(2,1)S(1)}, bf16[160,384]{1,0:T(8,128)(2,1)S(1)}, u32[]{:S(2)}, u32[]{:S(2)}) collective-permute-start(bf16[160,384]{1,0:T(8,128)(2,1)S(1)} %fusion.2), channel_id=1, source_target_pairs={{0,4},{4,8},{8,12},{1,5},{5,9},{9,13},{2,6},{6,10},{10,14},{3,7},{... | collective-permute-start | bytes 368648 | tf_op jit(solution)/shard_map/ppermute | solution.py:180
  74.5 0.8 fusion.8
  75.3 0.8 convolution_add_fusion.1
  76.1 3.2 %collective-permute-done.8 = bf16[160,384]{1,0:T(8,128)(2,1)S(1)} collective-permute-done((bf16[160,384]{1,0:T(8,128)(2,1)S(1)}, bf16[160,384]{1,0:T(8,128)(2,1)S(1)}, u32[]{:S(2)}, u32[]{:S(2)}) %collective-permute-start.8) | collective-permute-done | bytes 122912 | tf_op jit(solution)/shard_map/ppermute | solution.py:180
  79.5 1.6 %fusion.9 = bf16[480,384]{1,0:T(8,128)(2,1)} fusion(f32[3,160,384]{2,1,0:T(8,128)S(1)} %pad_maximum_fusion.3, f32[480,384]{1,0:T(8,128)S(1)} %fusion.1, f32[480,384]{1,0:T(8,128)S(1)} %convolution_add_fusion.1, bf16[480,1152]{1,0:T(8,128)(2,1)S(1)} %bitcast.91, bf16[3,3,1152,384]{3,2,1,0:T(8,128)(2,1)S(1)} %bitcast.113), kind=kOutput, calls=%fused_computation.43 | convolution fusion | flops 425410560 | bytes 4571136 | tf_op jit(solution)/shard_map/dot_general | solution.py:165
  (31 shorter events, 0.9 us)
Async XLA Ops:
  0.0 25.6 %copy-start = (bf16[384,384]{1,0:T(8,128)(2,1)S(1)}, bf16[384,384]{1,0:T(8,128)(2,1)}, u32[]{:S(2)}) copy-start(bf16[384,384]{1,0:T(8,128)(2,1)} %param.12) | copy-start | bytes 884740
  0.0 12.6 %collective-permute-start = (bf16[480,384]{1,0:T(8,128)(2,1)}, bf16[480,384]{1,0:T(8,128)(2,1)S(1)}, u32[]{:S(2)}, u32[]{:S(2)}) collective-permute-start(bf16[480,384]{1,0:T(8,128)(2,1)} %bitcast.114), channel_id=1, source_target_pairs={{0,4},{4,8},{8,12},{1,5},{5,9},{9,13},{2,6},{6,10},{10,14},{3,7},{... | collective-permute-start | bytes 1105928 | tf_op jit(solution)/shard_map/ppermute | solution.py:26
  3.6 16.3 %collective-permute-start.3 = (bf16[480,384]{1,0:T(8,128)(2,1)}, bf16[480,384]{1,0:T(8,128)(2,1)S(1)}, u32[]{:S(2)}, u32[]{:S(2)}) collective-permute-start(bf16[480,384]{1,0:T(8,128)(2,1)} %bitcast.115), channel_id=1, source_target_pairs={{4,0},{8,4},{12,8},{5,1},{9,5},{13,9},{6,2},{10,6},{14,10},{7,3},{... | collective-permute-start | bytes 1105928 | tf_op jit(solution)/shard_map/ppermute | solution.py:27
  12.6 10.5 %collective-permute-start.1 = (bf16[480,384]{1,0:T(8,128)(2,1)S(1)}, bf16[480,384]{1,0:T(8,128)(2,1)S(1)}, u32[]{:S(2)}, u32[]{:S(2)}) collective-permute-start(bf16[480,384]{1,0:T(8,128)(2,1)S(1)} %collective-permute-done), channel_id=1, source_target_pairs={{4,8},{8,12},{5,9},{9,13},{6,10},{10,14},{7,11},{11,15},{20,24},{2... | collective-permute-start | bytes 1105928 | tf_op jit(solution)/shard_map/ppermute | solution.py:26
  20.0 11.1 %collective-permute-start.4 = (bf16[480,384]{1,0:T(8,128)(2,1)S(1)}, bf16[480,384]{1,0:T(8,128)(2,1)S(1)}, u32[]{:S(2)}, u32[]{:S(2)}) collective-permute-start(bf16[480,384]{1,0:T(8,128)(2,1)S(1)} %collective-permute-done.3), channel_id=1, source_target_pairs={{4,0},{8,4},{5,1},{9,5},{6,2},{10,6},{7,3},{11,7},{20,16},{24,20},... | collective-permute-start | bytes 1105928 | tf_op jit(solution)/shard_map/ppermute | solution.py:27
  23.0 10.3 %collective-permute-start.2 = (bf16[480,384]{1,0:T(8,128)(2,1)S(1)}, bf16[480,384]{1,0:T(8,128)(2,1)S(1)}, u32[]{:S(2)}, u32[]{:S(2)}) collective-permute-start(bf16[480,384]{1,0:T(8,128)(2,1)S(1)} %collective-permute-done.1), channel_id=1, source_target_pairs={{8,12},{9,13},{10,14},{11,15},{24,28},{25,29},{26,30},{27,31}} | collective-permute-start | bytes 1105928 | tf_op jit(solution)/shard_map/ppermute | solution.py:26
  25.6 7.8 %copy-start.1 = (bf16[1,3,160,384]{3,2,1,0:T(8,128)(2,1)S(1)}, bf16[1,3,160,384]{3,2,1,0:T(8,128)(2,1)}, u32[]{:S(2)}) copy-start(bf16[1,3,160,384]{3,2,1,0:T(8,128)(2,1)} %param.9) | copy-start | bytes 1105924
  31.0 8.3 %collective-permute-start.5 = (bf16[480,384]{1,0:T(8,128)(2,1)S(1)}, bf16[480,384]{1,0:T(8,128)(2,1)S(1)}, u32[]{:S(2)}, u32[]{:S(2)}) collective-permute-start(bf16[480,384]{1,0:T(8,128)(2,1)S(1)} %collective-permute-done.4), channel_id=1, source_target_pairs={{4,0},{5,1},{6,2},{7,3},{20,16},{21,17},{22,18},{23,19}} | collective-permute-start | bytes 1105928 | tf_op jit(solution)/shard_map/ppermute | solution.py:27
  40.7 12.0 %slice-start = ((s8[7962624]{0:T(1024)(128)(4,1)}), s8[3768320]{0:T(1024)(128)(4,1)S(1)}, s32[]{:S(2)}) async-start(s8[7962624]{0:T(1024)(128)(4,1)} %bitcast.97), calls=%async_computation | async-start | bytes 7536640
  48.5 4.2 %slice-start.1 = ((s8[7962624]{0:T(1024)(128)(4,1)}), s8[4194304]{0:T(1024)(128)(4,1)S(1)}, s32[]{:S(2)}) async-start(s8[7962624]{0:T(1024)(128)(4,1)} %bitcast.97), calls=%async_computation.1 | async-start | bytes 8388608
  48.5 9.3 %collective-permute-start.6 = (bf16[3,160,384]{2,1,0:T(8,128)(2,1)}, bf16[3,160,384]{2,1,0:T(8,128)(2,1)S(1)}, u32[]{:S(2)}, u32[]{:S(2)}) collective-permute-start(bf16[3,160,384]{2,1,0:T(8,128)(2,1)} %bitcast.122), channel_id=1, source_target_pairs={{0,1},{1,2},{2,3},{4,5},{5,6},{6,7},{8,9},{9,10},{10,11},{12,13},{... | collective-permute-start | bytes 1105928 | tf_op jit(solution)/shard_map/ppermute | solution.py:15
  55.0 2.8 %copy-start.2 = (bf16[2,3,160,384]{3,2,1,0:T(8,128)(2,1)S(1)}, bf16[2,3,160,384]{3,2,1,0:T(8,128)(2,1)}, u32[]{:S(2)}) copy-start(bf16[2,3,160,384]{3,2,1,0:T(8,128)(2,1)} %param.10) | copy-start | bytes 2211844
  57.9 8.8 %collective-permute-start.7 = (bf16[3,160,384]{2,1,0:T(8,128)(2,1)S(1)}, bf16[3,160,384]{2,1,0:T(8,128)(2,1)S(1)}, u32[]{:S(2)}, u32[]{:S(2)}) collective-permute-start(bf16[3,160,384]{2,1,0:T(8,128)(2,1)S(1)} %bitcast_select_fusion.1), channel_id=1, source_target_pairs={{0,1},{1,2},{2,3},{4,5},{5,6},{6,7},{8,9},{9,10},{10,11},{12,13},{... | collective-permute-start | bytes 1105928 | tf_op jit(solution)/shard_map/ppermute | solution.py:15
  61.8 1.2 %copy-start.3 = (bf16[480,384]{1,0:T(8,128)(2,1)S(1)}, bf16[480,384]{1,0:T(8,128)(2,1)}, u32[]{:S(2)}) copy-start(bf16[480,384]{1,0:T(8,128)(2,1)} %get-tuple-element.7) | copy-start | bytes 1105924
  67.8 8.3 %collective-permute-start.9 = (bf16[160,384]{1,0:T(8,128)(2,1)S(1)}, bf16[160,384]{1,0:T(8,128)(2,1)S(1)}, u32[]{:S(2)}, u32[]{:S(2)}) collective-permute-start(bf16[160,384]{1,0:T(8,128)(2,1)S(1)} %fusion.3), channel_id=1, source_target_pairs={{4,0},{8,4},{12,8},{5,1},{9,5},{13,9},{6,2},{10,6},{14,10},{7,3},{... | collective-permute-start | bytes 368648 | tf_op jit(solution)/shard_map/ppermute | solution.py:177
  72.6 6.8 %collective-permute-start.8 = (bf16[160,384]{1,0:T(8,128)(2,1)S(1)}, bf16[160,384]{1,0:T(8,128)(2,1)S(1)}, u32[]{:S(2)}, u32[]{:S(2)}) collective-permute-start(bf16[160,384]{1,0:T(8,128)(2,1)S(1)} %fusion.2), channel_id=1, source_target_pairs={{0,4},{4,8},{8,12},{1,5},{5,9},{9,13},{2,6},{6,10},{10,14},{3,7},{... | collective-permute-start | bytes 368648 | tf_op jit(solution)/shard_map/ppermute | solution.py:180

commit v16 on v15

--- a/solution.py
+++ b/solution.py
@@ -13,6 +13,18 @@
     size = lax.axis_size(axis)
     pairs = [(i, i + by) for i in range(size) if 0 <= i + by < size]
     return lax.ppermute(x, axis, pairs)
+
+
+def relay(x, axis):
+    n = lax.axis_size(axis)
+    ups, downs = [], []
+    up, down = x, x
+    for step in range(1, n):
+        up = lax.ppermute(up, axis, [(i, i + 1) for i in range(step - 1, n - 1)])
+        down = lax.ppermute(down, axis, [(i + 1, i) for i in range(0, n - step)])
+        ups.append(up)
+        downs.append(down)
+    return ups, downs
 
 
 def strip_gather(x, axis):
@@ -121,6 +133,109 @@
     )
 
 
+def split_kernels_a(scale, blocks_ref, query_ref, again_ref, wkv_ref, bias_ref, m_ref, l_ref, o_ref):
+    width = query_ref.shape[1]
+    normed = scaled(blocks_ref[...], again_ref[...]).astype(jnp.bfloat16)
+    both = jnp.dot(normed, wkv_ref[...], preferred_element_type=jnp.float32).astype(jnp.bfloat16)
+    scores = (
+        lax.dot_general(
+            query_ref[...], both[:, :width], (((1,), (1,)), ((), ())),
+            preferred_element_type=jnp.float32,
+        )
+        * scale
+        + bias_ref[...]
+    )
+    peak = jnp.max(scores, axis=1, keepdims=True)
+    weights = jnp.exp(scores - peak)
+    m_ref[...] = peak
+    l_ref[...] = jnp.sum(weights, axis=1, keepdims=True)
+    o_ref[...] = jnp.dot(
+        weights.astype(jnp.bfloat16), both[:, width:], preferred_element_type=jnp.float32
+    )
+
+
+def split_kernels_b(
+    scale, blocks_ref, query_ref, again_ref, wkv_ref, bias_ref, m_ref, l_ref, o_ref, flat_ref,
+    wo_ref, cgain_ref, resid_ref, act_ref,
+):
+    width = query_ref.shape[1]
+    normed = scaled(blocks_ref[...], again_ref[...]).astype(jnp.bfloat16)
+    both = jnp.dot(normed, wkv_ref[...], preferred_element_type=jnp.float32).astype(jnp.bfloat16)
+    scores = (
+        lax.dot_general(
+            query_ref[...], both[:, :width], (((1,), (1,)), ((), ())),
+            preferred_element_type=jnp.float32,
+        )
+        * scale
+        + bias_ref[...]
+    )
+    earlier = m_ref[...]
+    peak = jnp.maximum(jnp.max(scores, axis=1, keepdims=True), earlier)
+    alpha = jnp.exp(earlier - peak)
+    weights = jnp.exp(scores - peak)
+    total = l_ref[...] * alpha + jnp.sum(weights, axis=1, keepdims=True)
+    summed = o_ref[...] * alpha + jnp.dot(
+        weights.astype(jnp.bfloat16), both[:, width:], preferred_element_type=jnp.float32
+    )
+    attended = (summed / total).astype(jnp.bfloat16)
+    resid = (
+        flat_ref[...].astype(jnp.float32)
+        + jnp.dot(attended, wo_ref[...], preferred_element_type=jnp.float32)
+    ).astype(jnp.bfloat16)
+    resid_ref[...] = resid
+    shown = scaled(resid, cgain_ref[...])
+    act_ref[...] = (shown / (1.0 + jnp.exp(-shown))).astype(jnp.bfloat16)
+
+
+def whole_call(kernel, inputs, outputs, flops, transcendentals):
+    return pl.pallas_call(
+        kernel,
+        out_shape=outputs,
+        grid=(1,),
+        in_specs=[pl.BlockSpec(x.shape, lambda i: (0, 0)) for x in inputs],
+        out_specs=tuple(pl.BlockSpec(o.shape, lambda i: (0, 0)) for o in outputs),
+        compiler_params=pltpu.CompilerParams(vmem_limit_bytes=60 * 1024 * 1024),
+        cost_estimate=pl.CostEstimate(
+            flops=flops,
+            transcendentals=transcendentals,
+            bytes_accessed=sum(x.size * x.dtype.itemsize for x in inputs),
+        ),
+    )(*inputs)
+
+
+def split_attend(
+    blocks_a, bias_a, blocks_b, bias_b, flat, query, attn_gain, key_weight, value_weight,
+    out_weight, conv_gain, scale,
+):
+    count, width = query.shape
+    wkv = jnp.concatenate([key_weight, value_weight], axis=1)
+    again = attn_gain.reshape(1, width)
+    f32 = jnp.float32
+    keys_a, keys_b = blocks_a.shape[0], blocks_b.shape[0]
+    m_a, l_a, o_a = whole_call(
+        functools.partial(split_kernels_a, scale),
+        [blocks_a, query, again, wkv, bias_a],
+        (
+            jax.ShapeDtypeStruct((count, 1), f32),
+            jax.ShapeDtypeStruct((count, 1), f32),
+            jax.ShapeDtypeStruct((count, width), f32),
+        ),
+        4 * keys_a * width * width + 4 * count * keys_a * width,
+        count * keys_a,
+    )
+    return whole_call(
+        functools.partial(split_kernels_b, scale),
+        [blocks_b, query, again, wkv, bias_b, m_a, l_a, o_a, flat, out_weight,
+         conv_gain.reshape(1, width)],
+        (
+            jax.ShapeDtypeStruct((count, width), jnp.bfloat16),
+            jax.ShapeDtypeStruct((count, width), jnp.bfloat16),
+        ),
+        4 * keys_b * width * width + 4 * count * keys_b * width + 2 * count * width * width,
+        count * keys_b + count * width,
+    )
+
+
 def shards(
     frames,
     cache_frames,
@@ -138,12 +253,34 @@
     flat = frames.reshape(-1, width)
     count = flat.shape[0]
     scale = float(np.float32(1.0) / np.sqrt(np.float32(width)))
-    whole = strip_gather(flat, "strip")
+    n = lax.axis_size("strip")
+    split_path = 3 <= n <= 4
+    if not split_path:
+        whole = strip_gather(flat, "strip")
     normed = rms_scale(flat, attn_gain).astype(jnp.bfloat16)
     query = jnp.dot(normed, query_weight, preferred_element_type=jnp.float32).astype(jnp.bfloat16)
-    resid, act = attend(
-        whole, flat, query, attn_gain, key_weight, value_weight, out_weight, conv_gain, scale
-    )
+    if split_path:
+        me = lax.axis_index("strip")
+        ups, downs = relay(flat, "strip")
+        early = range(1, n - 1)
+        blocks_a = [ups[k - 1] for k in early[::-1]] + [flat] + [downs[k - 1] for k in early]
+        valid_a = [me >= k for k in early[::-1]] + [me >= 0] + [me <= n - 1 - k for k in early]
+        blocks_b = [ups[n - 2], downs[n - 2]]
+        valid_b = [me >= n - 1, me <= 0]
+
+        def bias(valid):
+            rows_of = [jnp.broadcast_to(jnp.where(v, 0.0, -1e30), (count,)) for v in valid]
+            return jnp.concatenate(rows_of).astype(jnp.float32).reshape(1, -1)
+
+        resid, act = split_attend(
+            jnp.concatenate(blocks_a, axis=0), bias(valid_a), jnp.concatenate(blocks_b, axis=0),
+            bias(valid_b), flat, query, attn_gain, key_weight, value_weight, out_weight,
+            conv_gain, scale,
+        )
+    else:
+        resid, act = attend(
+            whole, flat, query, attn_gain, key_weight, value_weight, out_weight, conv_gain, scale
+        )
     act = act.reshape(rows, cols, width)
     frame_index = lax.axis_index("tm")
     prior = passed_along(act, "tm", 1)

time: 81.6 us -> 81.1 us (level)
  waiting for transfers between devices: 24.7 us -> 14 us
  Pallas kernels: 7.78 us -> 14.3 us
  local copies, waits for them, and re-layouts: 7.3 us -> 12.3 us
  other arithmetic: 3.91 us -> 2.92 us
    ppermute x6, waiting for transfers between devices: 16.5 us -> 9.52 us  [the longest x3 6.33 us: relay(): up = lax.ppermute(up, axis, [(i, i + 1) for i in range(step - 1, n - 1)])]
    pallas_call x1 -> x2, Pallas kernels: 7.78 us -> 14.3 us  [whole_call(): pl.pallas_call(kernel, out_shape=outputs, grid=(1,), in_specs=[pl.BlockSp...]
    unnamed x18 -> x25, local copies, waits for them, and re-layouts: 0.37 us -> 6.05 us
    ppermute x1, starting transfers between devices: 4.39 us -> 1.92 us  [shards(): lax.ppermute(to_prev.astype(jnp.bfloat16), 'strip', [(i + 1, i) for i in...]
    ppermute x1, waiting for transfers between devices: 3.25 us -> 1.24 us  [shards(): lax.ppermute(to_next.astype(jnp.bfloat16), 'strip', [(i, i + 1) for i in...]
    ppermute x1, starting transfers between devices: 1.92 us -> 3.93 us  [shards(): lax.ppermute(to_next.astype(jnp.bfloat16), 'strip', [(i, i + 1) for i in...]
    ppermute x2, waiting for transfers between devices: 4.89 us -> 3.27 us  [passed_along(): return lax.ppermute(x, axis, pairs)]
    concatenate x1 -> x4, local copies, waits for them, and re-layouts: 0.06 us -> 1.51 us  [the longest x1 0.78 us: shards(): jnp.concatenate(blocks_a, axis=0)]
  transfers between devices with their start and end apart: 10 -> 10, of which waited for: 7 -> 5; matrix products, arithmetic and copies ran while one was open for 24% -> 27% of each run, Pallas kernels for 0% -> 10%
where the time goes in v16:
time: 81.1 us; the launch traced here: 80.1 us
  starting transfers between devices  24.1 us (30%)
  Pallas kernels  14.3 us (18%)
  waiting for transfers between devices  14 us (17%)
  local copies, waits for them, and re-layouts  12.3 us (15%)
  matrix products  12.1 us (15%)
  other arithmetic  2.92 us (4%)
    pallas_call x2, Pallas kernels, whole_call(): pl.pallas_call(kernel, out_shape=outputs, grid=(1,), in_specs=[pl.BlockSp...  14.3 us
    dot_general x9, matrix products, frame_terms(): jnp.dot(window, kernel[step_t, step_r], preferred_element_type=jnp.float32)  7.77 us
    ppermute x3, starting transfers between devices, relay(): up = lax.ppermute(up, axis, [(i, i + 1) for i in range(step - 1, n - 1)])  7.65 us
    ppermute x3, starting transfers between devices, relay(): down = lax.ppermute(down, axis, [(i + 1, i) for i in range(0, n - step)])  6.61 us
    ppermute x3, waiting for transfers between devices, relay(): up = lax.ppermute(up, axis, [(i, i + 1) for i in range(step - 1, n - 1)])  6.33 us
    unnamed x25, local copies, waits for them, and re-layouts  6.05 us
    ppermute x2, starting transfers between devices, passed_along(): return lax.ppermute(x, axis, pairs)  4.01 us
    ppermute x1, starting transfers between devices, shards(): lax.ppermute(to_next.astype(jnp.bfloat16), 'strip', [(i, i + 1) for i in...  3.93 us
  transfers between devices with their start and end apart: 10, of which 5 were waited for; matrix products, arithmetic and copies ran while one was open for 27% of the time, Pallas kernels for 10%

profile of v16, /device:TPU:10, one launch (start us, length us, event | category | flops | bytes accessed | tf_op | source)
XLA Modules:
  0.0 80.1 jit_solution(5101728771685451440)
XLA Ops:
  0.0 2.5 %collective-permute-start.3 = (bf16[480,384]{1,0:T(8,128)(2,1)}, bf16[480,384]{1,0:T(8,128)(2,1)S(1)}, u32[]{:S(2)}, u32[]{:S(2)}) collective-permute-start(bf16[480,384]{1,0:T(8,128)(2,1)} %bitcast.115), channel_id=1, source_target_pairs={{4,0},{8,4},{12,8},{5,1},{9,5},{13,9},{6,2},{10,6},{14,10},{7,3},{... | collective-permute-start | bytes 1105928 | tf_op jit(solution)/shard_map/ppermute | solution.py:24
  2.5 3.5 %collective-permute-start = (bf16[480,384]{1,0:T(8,128)(2,1)}, bf16[480,384]{1,0:T(8,128)(2,1)S(1)}, u32[]{:S(2)}, u32[]{:S(2)}) collective-permute-start(bf16[480,384]{1,0:T(8,128)(2,1)} %bitcast.116), channel_id=1, source_target_pairs={{0,4},{4,8},{8,12},{1,5},{5,9},{9,13},{2,6},{6,10},{10,14},{3,7},{... | collective-permute-start | bytes 1105928 | tf_op jit(solution)/shard_map/ppermute | solution.py:23
  6.0 1.2 %multiply_reduce_fusion = f32[3,160]{1,0:T(4,128)S(1)} fusion(bf16[1,3,160,384]{3,2,1,0:T(8,128)(2,1)} %param.9), kind=kLoop, calls=%fused_computation.46 | loop fusion | flops 552480 | bytes 370560 | tf_op jit(solution)/shard_map/reduce_sum | solution.py:49
  7.3 1.0 %constant_dynamic-update-slice_fusion.1 = bf16[384,768]{1,0:T(8,128)(2,1)S(1)} fusion(bf16[384,384]{1,0:T(8,128)(2,1)} %param.13), kind=kLoop, calls=%fused_computation.60 | loop fusion | bytes 589824
  8.3 6.3 %collective-permute-done = bf16[480,384]{1,0:T(8,128)(2,1)S(1)} collective-permute-done((bf16[480,384]{1,0:T(8,128)(2,1)}, bf16[480,384]{1,0:T(8,128)(2,1)S(1)}, u32[]{:S(2)}, u32[]{:S(2)}) %collective-permute-start) | collective-permute-done | bytes 368672 | tf_op jit(solution)/shard_map/ppermute | solution.py:23
  14.7 3.5 %collective-permute-start.1 = (bf16[480,384]{1,0:T(8,128)(2,1)S(1)}, bf16[480,384]{1,0:T(8,128)(2,1)S(1)}, u32[]{:S(2)}, u32[]{:S(2)}) collective-permute-start(bf16[480,384]{1,0:T(8,128)(2,1)S(1)} %collective-permute-done), channel_id=1, source_target_pairs={{4,8},{8,12},{5,9},{9,13},{6,10},{10,14},{7,11},{11,15},{20,24},{2... | collective-permute-start | bytes 1105928 | tf_op jit(solution)/shard_map/ppermute | solution.py:23
  18.2 2.2 %convolution_convert_fusion.query_ref = bf16[480,384]{1,0:T(8,128)(2,1)} fusion(bf16[384,384]{1,0:T(8,128)(2,1)S(1)} %copy-done, bf16[480,384]{1,0:T(8,128)(2,1)} %bitcast.117, f32[384]{0:T(512)} %param.11, f32[480]{0:T(512)S(1)} %rsqrt.12), kind=kOutput, calls=%fused_computation.11 | convolution fusion | flops 142479360 | bytes 1035648 | tf_op jit(solution)/shard_map/dot_general | solution.py:261
  20.4 1.9 %collective-permute-start.4 = (bf16[480,384]{1,0:T(8,128)(2,1)S(1)}, bf16[480,384]{1,0:T(8,128)(2,1)S(1)}, u32[]{:S(2)}, u32[]{:S(2)}) collective-permute-start(bf16[480,384]{1,0:T(8,128)(2,1)S(1)} %collective-permute-done.3), channel_id=1, source_target_pairs={{4,0},{8,4},{5,1},{9,5},{6,2},{10,6},{7,3},{11,7},{20,16},{24,20},... | collective-permute-start | bytes 1105928 | tf_op jit(solution)/shard_map/ppermute | solution.py:24
  22.4 0.6 broadcast_in_dim.28.again_ref
  23.0 0.5 reshape.77.cgain_ref
  23.7 0.6 reshape.76.bias_ref
  24.4 0.6 concatenate.29
  25.0 0.7 collective-permute-start.2
  25.6 0.8 constant_dynamic-update-slice_fusion.6
  26.4 0.8 constant_dynamic-update-slice_fusion.5
  27.2 0.8 constant_dynamic-update-slice_fusion.4
  28.0 3.2 %collective-permute-done.4 = bf16[480,384]{1,0:T(8,128)(2,1)S(1)} collective-permute-done((bf16[480,384]{1,0:T(8,128)(2,1)S(1)}, bf16[480,384]{1,0:T(8,128)(2,1)S(1)}, u32[]{:S(2)}, u32[]{:S(2)}) %collective-permute-start.4) | collective-permute-done | bytes 368672 | tf_op jit(solution)/shard_map/ppermute | solution.py:24
  31.2 2.2 %collective-permute-start.5 = (bf16[480,384]{1,0:T(8,128)(2,1)S(1)}, bf16[480,384]{1,0:T(8,128)(2,1)S(1)}, u32[]{:S(2)}, u32[]{:S(2)}) collective-permute-start(bf16[480,384]{1,0:T(8,128)(2,1)S(1)} %collective-permute-done.4), channel_id=1, source_target_pairs={{4,0},{5,1},{6,2},{7,3},{20,16},{21,17},{22,18},{23,19}} | collective-permute-start | bytes 1105928 | tf_op jit(solution)/shard_map/ppermute | solution.py:24
  33.4 0.8 constant_dynamic-update-slice_fusion.3
  34.1 0.8 constant_dynamic-update-slice_fusion.2.blocks_ref
  34.9 8.2 %shard_map.91 = (f32[480,1]{1,0:T(8,128)}, f32[480,1]{1,0:T(8,128)}, f32[480,384]{1,0:T(8,128)}) custom-call(bf16[2400,384]{1,0:T(8,128)(2,1)} %constant_dynamic-update-slice_fusion.2.blocks_ref, bf16[480,384]{1,0:T(8,128)(2,1)} %convolution_convert_fusion.query_ref, f32[1,384]{1,0:T(1,128)} %broadcast_in_dim.28.again_ref, bf16[384,768]{1,0:T(8,128)(2,1)} %copy-done.5, ...), custom_call_target="tpu_custom_call" | custom-call | flops 3185049600 | bytes 2812800 | tf_op jit(solution)/shard_map/pallas_call | solution.py:191
  43.1 0.9 %pad_maximum_fusion.3.blocks_ref = bf16[960,384]{1,0:T(8,128)(2,1)} fusion(bf16[480,384]{1,0:T(8,128)(2,1)S(1)} %collective-permute-done.5, bf16[480,384]{1,0:T(8,128)(2,1)S(1)} %collective-permute-done.2), kind=kLoop, calls=%fused_computation.41 | loop fusion | flops 1474560 | bytes 1474560 | tf_op jit(solution)/shard_map/concatenate | solution.py:276
  44.1 6.1 %shard_map.92 = (bf16[480,384]{1,0:T(8,128)(2,1)}, bf16[480,384]{1,0:T(8,128)(2,1)}) custom-call(bf16[960,384]{1,0:T(8,128)(2,1)} %pad_maximum_fusion.3.blocks_ref, bf16[480,384]{1,0:T(8,128)(2,1)} %convolution_convert_fusion.query_ref, f32[1,384]{1,0:T(1,128)} %broadcast_in_dim.28.again_ref, bf16[384,768]{1,0:T(8,128)(2,1)} %copy-done.5, ...), custom_call_target="tpu_custom_call" | custom-call | flops 1415577600 | bytes 3107328 | tf_op jit(solution)/shard_map/pallas_call | solution.py:191
  50.1 2.1 %collective-permute-start.6 = (bf16[3,160,384]{2,1,0:T(8,128)(2,1)}, bf16[3,160,384]{2,1,0:T(8,128)(2,1)S(1)}, u32[]{:S(2)}, u32[]{:S(2)}) collective-permute-start(bf16[3,160,384]{2,1,0:T(8,128)(2,1)} %bitcast.123), channel_id=1, source_target_pairs={{0,1},{1,2},{2,3},{4,5},{5,6},{6,7},{8,9},{9,10},{10,11},{12,13},{... | collective-permute-start | bytes 1105928 | tf_op jit(solution)/shard_map/ppermute | solution.py:15
  52.2 1.5 %pad_slice_fusion.8 = (bf16[5,160,384]{2,1,0:T(8,128)(2,1)S(1)}, bf16[5,160,384]{2,1,0:T(8,128)(2,1)S(1)}, bf16[5,160,384]{2,1,0:T(8,128)(2,1)S(1)}) fusion(bf16[3,160,384]{2,1,0:T(8,128)(2,1)} %bitcast.124), kind=kLoop, calls=%fused_computation.40 | loop fusion | bytes 2211840 | tf_op jit(solution)/shard_map/slice | solution.py:295
  53.9 0.3 fusion.13
  54.2 1.7 %slice-done.1 = s8[4194304]{0:T(1024)(128)(4,1)S(1)} async-done(((s8[7962624]{0:T(1024)(128)(4,1)}), s8[4194304]{0:T(1024)(128)(4,1)S(1)}, s32[]{:S(2)}) %slice-start.1) | async-done | bytes 4194328
  55.9 0.4 fusion.6
  56.3 0.8 fusion.5
  57.0 0.8 convolution_add_fusion.5
  57.8 0.4 fusion.4
  58.2 0.8 convolution_add_fusion.4
  59.4 1.9 %collective-permute-start.7 = (bf16[3,160,384]{2,1,0:T(8,128)(2,1)S(1)}, bf16[3,160,384]{2,1,0:T(8,128)(2,1)S(1)}, u32[]{:S(2)}, u32[]{:S(2)}) collective-permute-start(bf16[3,160,384]{2,1,0:T(8,128)(2,1)S(1)} %bitcast_select_fusion.1), channel_id=1, source_target_pairs={{0,1},{1,2},{2,3},{4,5},{5,6},{6,7},{8,9},{9,10},{10,11},{12,13},{... | collective-permute-start | bytes 1105928 | tf_op jit(solution)/shard_map/ppermute | solution.py:15
  62.0 0.4 convolution_add_fusion.7
  62.4 0.8 fusion.7
  63.2 0.8 convolution_add_fusion.3
  63.9 0.4 convolution_add_fusion.9
  64.3 0.8 %fusion.1 = f32[480,384]{1,0:T(8,128)S(1)} fusion(f32[480,384]{1,0:T(8,128)S(1)} %convolution_add_fusion.3, bf16[480,1152]{1,0:T(8,128)(2,1)S(1)} %bitcast.94, bf16[3,3,1152,384]{3,2,1,0:T(8,128)(2,1)S(1)} %bitcast.109, f32[480,384]{1,0:T(8,128)S(1)} %convolution_add_fusion.4, bf16[480,384]{1,0:T(8,128)(2,1)S(1)} %copy-done.3), kind=kOutput, calls=%fused_computation.7 | convolution fusion | flops 425410560 | bytes 4571136 | tf_op jit(solution)/shard_map/dot_general | solution.py:302
  65.1 3.1 %collective-permute-done.7 = bf16[3,160,384]{2,1,0:T(8,128)(2,1)S(1)} collective-permute-done((bf16[3,160,384]{2,1,0:T(8,128)(2,1)S(1)}, bf16[3,160,384]{2,1,0:T(8,128)(2,1)S(1)}, u32[]{:S(2)}, u32[]{:S(2)}) %collective-permute-start.7) | collective-permute-done | bytes 368672 | tf_op jit(solution)/shard_map/ppermute | solution.py:15
  68.7 0.3 fusion.12
  69.0 0.4 fusion.3
  69.3 1.9 %collective-permute-start.9 = (bf16[160,384]{1,0:T(8,128)(2,1)S(1)}, bf16[160,384]{1,0:T(8,128)(2,1)S(1)}, u32[]{:S(2)}, u32[]{:S(2)}) collective-permute-start(bf16[160,384]{1,0:T(8,128)(2,1)S(1)} %fusion.3), channel_id=1, source_target_pairs={{4,0},{8,4},{12,8},{5,1},{9,5},{13,9},{6,2},{10,6},{14,10},{7,3},{... | collective-permute-start | bytes 368648 | tf_op jit(solution)/shard_map/ppermute | solution.py:314
  71.3 0.4 fusion.2
  71.6 3.9 %collective-permute-start.8 = (bf16[160,384]{1,0:T(8,128)(2,1)S(1)}, bf16[160,384]{1,0:T(8,128)(2,1)S(1)}, u32[]{:S(2)}, u32[]{:S(2)}) collective-permute-start(bf16[160,384]{1,0:T(8,128)(2,1)S(1)} %fusion.2), channel_id=1, source_target_pairs={{0,4},{4,8},{8,12},{1,5},{5,9},{9,13},{2,6},{6,10},{10,14},{3,7},{... | collective-permute-start | bytes 368648 | tf_op jit(solution)/shard_map/ppermute | solution.py:317
  75.6 0.8 fusion.8
  76.4 0.8 convolution_add_fusion.1
  77.2 1.2 %collective-permute-done.8 = bf16[160,384]{1,0:T(8,128)(2,1)S(1)} collective-permute-done((bf16[160,384]{1,0:T(8,128)(2,1)S(1)}, bf16[160,384]{1,0:T(8,128)(2,1)S(1)}, u32[]{:S(2)}, u32[]{:S(2)}) %collective-permute-start.8) | collective-permute-done | bytes 122912 | tf_op jit(solution)/shard_map/ppermute | solution.py:317
  78.6 1.6 %fusion.9 = bf16[480,384]{1,0:T(8,128)(2,1)} fusion(f32[3,160,384]{2,1,0:T(8,128)S(1)} %pad_maximum_fusion.4, f32[480,384]{1,0:T(8,128)S(1)} %fusion.1, f32[480,384]{1,0:T(8,128)S(1)} %convolution_add_fusion.1, bf16[480,1152]{1,0:T(8,128)(2,1)S(1)} %bitcast.92, bf16[3,3,1152,384]{3,2,1,0:T(8,128)(2,1)S(1)} %bitcast.114), kind=kOutput, calls=%fused_computation.44 | convolution fusion | flops 425410560 | bytes 4571136 | tf_op jit(solution)/shard_map/dot_general | solution.py:302
  (48 shorter events, 2.2 us)
Async XLA Ops:
  0.0 18.2 %copy-start = (bf16[384,384]{1,0:T(8,128)(2,1)S(1)}, bf16[384,384]{1,0:T(8,128)(2,1)}, u32[]{:S(2)}) copy-start(bf16[384,384]{1,0:T(8,128)(2,1)} %param.12) | copy-start | bytes 884740
  0.0 22.4 %copy-start.6 = (f32[384]{0:T(512)S(1)}, f32[384]{0:T(512)}, u32[]{:S(2)}) copy-start(f32[384]{0:T(512)} %param.11) | copy-start | bytes 4612
  0.0 22.3 %copy-start.4 = (bf16[384,384]{1,0:T(8,128)(2,1)S(1)}, bf16[384,384]{1,0:T(8,128)(2,1)}, u32[]{:S(2)}) copy-start(bf16[384,384]{1,0:T(8,128)(2,1)} %param.14) | copy-start | bytes 884740
  0.0 23.0 %copy-start.7 = (f32[384]{0:T(512)S(1)}, f32[384]{0:T(512)}, u32[]{:S(2)}) copy-start(f32[384]{0:T(512)} %param.16) | copy-start | bytes 4612
  0.0 20.3 %collective-permute-start.3 = (bf16[480,384]{1,0:T(8,128)(2,1)}, bf16[480,384]{1,0:T(8,128)(2,1)S(1)}, u32[]{:S(2)}, u32[]{:S(2)}) collective-permute-start(bf16[480,384]{1,0:T(8,128)(2,1)} %bitcast.115), channel_id=1, source_target_pairs={{4,0},{8,4},{12,8},{5,1},{9,5},{13,9},{6,2},{10,6},{14,10},{7,3},{... | collective-permute-start | bytes 1105928 | tf_op jit(solution)/shard_map/ppermute | solution.py:24
  2.5 12.2 %collective-permute-start = (bf16[480,384]{1,0:T(8,128)(2,1)}, bf16[480,384]{1,0:T(8,128)(2,1)S(1)}, u32[]{:S(2)}, u32[]{:S(2)}) collective-permute-start(bf16[480,384]{1,0:T(8,128)(2,1)} %bitcast.116), channel_id=1, source_target_pairs={{0,4},{4,8},{8,12},{1,5},{5,9},{9,13},{2,6},{6,10},{10,14},{3,7},{... | collective-permute-start | bytes 1105928 | tf_op jit(solution)/shard_map/ppermute | solution.py:23
  7.3 19.9 %copy-start.1 = (bf16[1,3,160,384]{3,2,1,0:T(8,128)(2,1)S(1)}, bf16[1,3,160,384]{3,2,1,0:T(8,128)(2,1)}, u32[]{:S(2)}) copy-start(bf16[1,3,160,384]{3,2,1,0:T(8,128)(2,1)} %param.9) | copy-start | bytes 1105924
  14.7 10.3 %collective-permute-start.1 = (bf16[480,384]{1,0:T(8,128)(2,1)S(1)}, bf16[480,384]{1,0:T(8,128)(2,1)S(1)}, u32[]{:S(2)}, u32[]{:S(2)}) collective-permute-start(bf16[480,384]{1,0:T(8,128)(2,1)S(1)} %collective-permute-done), channel_id=1, source_target_pairs={{4,8},{8,12},{5,9},{9,13},{6,10},{10,14},{7,11},{11,15},{20,24},{2... | collective-permute-start | bytes 1105928 | tf_op jit(solution)/shard_map/ppermute | solution.py:23
  20.4 10.8 %collective-permute-start.4 = (bf16[480,384]{1,0:T(8,128)(2,1)S(1)}, bf16[480,384]{1,0:T(8,128)(2,1)S(1)}, u32[]{:S(2)}, u32[]{:S(2)}) collective-permute-start(bf16[480,384]{1,0:T(8,128)(2,1)S(1)} %collective-permute-done.3), channel_id=1, source_target_pairs={{4,0},{8,4},{5,1},{9,5},{6,2},{10,6},{7,3},{11,7},{20,16},{24,20},... | collective-permute-start | bytes 1105928 | tf_op jit(solution)/shard_map/ppermute | solution.py:24
  22.3 12.6 %copy-start.5 = (bf16[384,768]{1,0:T(8,128)(2,1)}, bf16[384,768]{1,0:T(8,128)(2,1)S(1)}, u32[]{:S(2)}) copy-start(bf16[384,768]{1,0:T(8,128)(2,1)S(1)} %constant_dynamic-update-slice_fusion.wkv_ref) | copy-start | bytes 1769476
  25.0 18.2 %collective-permute-start.2 = (bf16[480,384]{1,0:T(8,128)(2,1)S(1)}, bf16[480,384]{1,0:T(8,128)(2,1)S(1)}, u32[]{:S(2)}, u32[]{:S(2)}) collective-permute-start(bf16[480,384]{1,0:T(8,128)(2,1)S(1)} %collective-permute-done.1), channel_id=1, source_target_pairs={{8,12},{9,13},{10,14},{11,15},{24,28},{25,29},{26,30},{27,31}} | collective-permute-start | bytes 1105928 | tf_op jit(solution)/shard_map/ppermute | solution.py:23
  31.2 12.0 %collective-permute-start.5 = (bf16[480,384]{1,0:T(8,128)(2,1)S(1)}, bf16[480,384]{1,0:T(8,128)(2,1)S(1)}, u32[]{:S(2)}, u32[]{:S(2)}) collective-permute-start(bf16[480,384]{1,0:T(8,128)(2,1)S(1)} %collective-permute-done.4), channel_id=1, source_target_pairs={{4,0},{5,1},{6,2},{7,3},{20,16},{21,17},{22,18},{23,19}} | collective-permute-start | bytes 1105928 | tf_op jit(solution)/shard_map/ppermute | solution.py:24
  44.1 10.1 %slice-start = ((s8[7962624]{0:T(1024)(128)(4,1)}), s8[3768320]{0:T(1024)(128)(4,1)S(1)}, s32[]{:S(2)}) async-start(s8[7962624]{0:T(1024)(128)(4,1)} %bitcast.98), calls=%async_computation | async-start | bytes 7536640
  50.1 9.0 %collective-permute-start.6 = (bf16[3,160,384]{2,1,0:T(8,128)(2,1)}, bf16[3,160,384]{2,1,0:T(8,128)(2,1)S(1)}, u32[]{:S(2)}, u32[]{:S(2)}) collective-permute-start(bf16[3,160,384]{2,1,0:T(8,128)(2,1)} %bitcast.123), channel_id=1, source_target_pairs={{0,1},{1,2},{2,3},{4,5},{5,6},{6,7},{8,9},{9,10},{10,11},{12,13},{... | collective-permute-start | bytes 1105928 | tf_op jit(solution)/shard_map/ppermute | solution.py:15
  53.7 2.2 %slice-start.1 = ((s8[7962624]{0:T(1024)(128)(4,1)}), s8[4194304]{0:T(1024)(128)(4,1)S(1)}, s32[]{:S(2)}) async-start(s8[7962624]{0:T(1024)(128)(4,1)} %bitcast.98), calls=%async_computation.1 | async-start | bytes 8388608
  58.2 1.1 %copy-start.2 = (bf16[2,3,160,384]{3,2,1,0:T(8,128)(2,1)S(1)}, bf16[2,3,160,384]{3,2,1,0:T(8,128)(2,1)}, u32[]{:S(2)}) copy-start(bf16[2,3,160,384]{3,2,1,0:T(8,128)(2,1)} %param.10) | copy-start | bytes 2211844
  59.4 8.8 %collective-permute-start.7 = (bf16[3,160,384]{2,1,0:T(8,128)(2,1)S(1)}, bf16[3,160,384]{2,1,0:T(8,128)(2,1)S(1)}, u32[]{:S(2)}, u32[]{:S(2)}) collective-permute-start(bf16[3,160,384]{2,1,0:T(8,128)(2,1)S(1)} %bitcast_select_fusion.1), channel_id=1, source_target_pairs={{0,1},{1,2},{2,3},{4,5},{5,6},{6,7},{8,9},{9,10},{10,11},{12,13},{... | collective-permute-start | bytes 1105928 | tf_op jit(solution)/shard_map/ppermute | solution.py:15
  63.1 1.2 %copy-start.3 = (bf16[480,384]{1,0:T(8,128)(2,1)S(1)}, bf16[480,384]{1,0:T(8,128)(2,1)}, u32[]{:S(2)}) copy-start(bf16[480,384]{1,0:T(8,128)(2,1)} %get-tuple-element.13) | copy-start | bytes 1105924
  69.3 7.8 %collective-permute-start.9 = (bf16[160,384]{1,0:T(8,128)(2,1)S(1)}, bf16[160,384]{1,0:T(8,128)(2,1)S(1)}, u32[]{:S(2)}, u32[]{:S(2)}) collective-permute-start(bf16[160,384]{1,0:T(8,128)(2,1)S(1)} %fusion.3), channel_id=1, source_target_pairs={{4,0},{8,4},{12,8},{5,1},{9,5},{13,9},{6,2},{10,6},{14,10},{7,3},{... | collective-permute-start | bytes 368648 | tf_op jit(solution)/shard_map/ppermute | solution.py:314
  71.6 6.8 %collective-permute-start.8 = (bf16[160,384]{1,0:T(8,128)(2,1)S(1)}, bf16[160,384]{1,0:T(8,128)(2,1)S(1)}, u32[]{:S(2)}, u32[]{:S(2)}) collective-permute-start(bf16[160,384]{1,0:T(8,128)(2,1)S(1)} %fusion.2), channel_id=1, source_target_pairs={{0,4},{4,8},{8,12},{1,5},{5,9},{9,13},{2,6},{6,10},{10,14},{3,7},{... | collective-permute-start | bytes 368648 | tf_op jit(solution)/shard_map/ppermute | solution.py:317

commit v17 on v16

--- a/solution.py
+++ b/solution.py
@@ -133,10 +133,17 @@
     )
 
 
-def split_kernels_a(scale, blocks_ref, query_ref, again_ref, wkv_ref, bias_ref, m_ref, l_ref, o_ref):
+def split_kernels_a(scale, count, *refs):
+    blocks = refs[:count]
+    query_ref, again_ref, wkv_ref, bias_ref, m_ref, l_ref, o_ref, kv_ref = refs[count:]
     width = query_ref.shape[1]
-    normed = scaled(blocks_ref[...], again_ref[...]).astype(jnp.bfloat16)
-    both = jnp.dot(normed, wkv_ref[...], preferred_element_type=jnp.float32).astype(jnp.bfloat16)
+    rows = blocks[0].shape[0]
+    for index, block_ref in enumerate(blocks):
+        normed = scaled(block_ref[...], again_ref[...]).astype(jnp.bfloat16)
+        kv_ref[index * rows : (index + 1) * rows, :] = jnp.dot(
+            normed, wkv_ref[...], preferred_element_type=jnp.float32
+        ).astype(jnp.bfloat16)
+    both = kv_ref[...]
     scores = (
         lax.dot_general(
             query_ref[...], both[:, :width], (((1,), (1,)), ((), ())),
@@ -187,13 +194,14 @@
     act_ref[...] = (shown / (1.0 + jnp.exp(-shown))).astype(jnp.bfloat16)
 
 
-def whole_call(kernel, inputs, outputs, flops, transcendentals):
+def whole_call(kernel, inputs, outputs, flops, transcendentals, scratch=()):
     return pl.pallas_call(
         kernel,
         out_shape=outputs,
         grid=(1,),
         in_specs=[pl.BlockSpec(x.shape, lambda i: (0, 0)) for x in inputs],
         out_specs=tuple(pl.BlockSpec(o.shape, lambda i: (0, 0)) for o in outputs),
+        scratch_shapes=list(scratch),
         compiler_params=pltpu.CompilerParams(vmem_limit_bytes=60 * 1024 * 1024),
         cost_estimate=pl.CostEstimate(
             flops=flops,
@@ -211,10 +219,10 @@
     wkv = jnp.concatenate([key_weight, value_weight], axis=1)
     again = attn_gain.reshape(1, width)
     f32 = jnp.float32
-    keys_a, keys_b = blocks_a.shape[0], blocks_b.shape[0]
+    keys_a, keys_b = count * len(blocks_a), blocks_b.shape[0]
     m_a, l_a, o_a = whole_call(
-        functools.partial(split_kernels_a, scale),
-        [blocks_a, query, again, wkv, bias_a],
+        functools.partial(split_kernels_a, scale, len(blocks_a)),
+        list(blocks_a) + [query, again, wkv, bias_a],
         (
             jax.ShapeDtypeStruct((count, 1), f32),
             jax.ShapeDtypeStruct((count, 1), f32),
@@ -222,6 +230,7 @@
         ),
         4 * keys_a * width * width + 4 * count * keys_a * width,
         count * keys_a,
+        [pltpu.VMEM((keys_a, 2 * width), jnp.bfloat16)],
     )
     return whole_call(
         functools.partial(split_kernels_b, scale),
@@ -254,7 +263,7 @@
     count = flat.shape[0]
     scale = float(np.float32(1.0) / np.sqrt(np.float32(width)))
     n = lax.axis_size("strip")
-    split_path = 3 <= n <= 4
+    split_path = n == 4
     if not split_path:
         whole = strip_gather(flat, "strip")
     normed = rms_scale(flat, attn_gain).astype(jnp.bfloat16)
@@ -262,18 +271,18 @@
     if split_path:
         me = lax.axis_index("strip")
         ups, downs = relay(flat, "strip")
-        early = range(1, n - 1)
-        blocks_a = [ups[k - 1] for k in early[::-1]] + [flat] + [downs[k - 1] for k in early]
-        valid_a = [me >= k for k in early[::-1]] + [me >= 0] + [me <= n - 1 - k for k in early]
-        blocks_b = [ups[n - 2], downs[n - 2]]
-        valid_b = [me >= n - 1, me <= 0]
+        far = jnp.where(me <= 1, downs[1], ups[1])
+        blocks_a = [flat, ups[0], downs[0], far]
+        valid_a = [me >= 0, me >= 1, me <= n - 2, me >= 0]
+        blocks_b = jnp.where(me == n - 1, ups[n - 2], downs[n - 2])
+        valid_b = [(me == 0) | (me == n - 1)]
 
         def bias(valid):
             rows_of = [jnp.broadcast_to(jnp.where(v, 0.0, -1e30), (count,)) for v in valid]
             return jnp.concatenate(rows_of).astype(jnp.float32).reshape(1, -1)
 
         resid, act = split_attend(
-            jnp.concatenate(blocks_a, axis=0), bias(valid_a), jnp.concatenate(blocks_b, axis=0),
+            blocks_a, bias(valid_a), blocks_b,
             bias(valid_b), flat, query, attn_gain, key_weight, value_weight, out_weight,
             conv_gain, scale,
         )

time: 81.1 us -> 74.7 us (0.921)
  the two profiles are of different devices: /device:TPU:10 before, /device:TPU:26 now
where the time goes in v17:
time: 74.7 us; the launch traced here: 74 us
  waiting for transfers between devices  18.5 us (25%)
  starting transfers between devices  16.4 us (22%)
  matrix products  12.4 us (17%)
  Pallas kernels  12.2 us (16%)
  local copies, waits for them, and re-layouts  10.5 us (14%)
  other arithmetic  3.55 us (5%)
    pallas_call x2, Pallas kernels, whole_call(): pl.pallas_call(kernel, out_shape=outputs, grid=(1,), in_specs=[pl.BlockSp...  12.2 us
    ppermute x3, waiting for transfers between devices, relay(): up = lax.ppermute(up, axis, [(i, i + 1) for i in range(step - 1, n - 1)])  10.2 us
    dot_general x9, matrix products, frame_terms(): jnp.dot(window, kernel[step_t, step_r], preferred_element_type=jnp.float32)  7.83 us
    ppermute x2, starting transfers between devices, passed_along(): return lax.ppermute(x, axis, pairs)  4.01 us
    ppermute x1, waiting for transfers between devices, shards(): lax.ppermute(to_next.astype(jnp.bfloat16), 'strip', [(i, i + 1) for i in...  3.87 us
    ppermute x3, starting transfers between devices, relay(): up = lax.ppermute(up, axis, [(i, i + 1) for i in range(step - 1, n - 1)])  3.85 us
    ppermute x3, starting transfers between devices, relay(): down = lax.ppermute(down, axis, [(i + 1, i) for i in range(0, n - step)])  3.84 us
    ppermute x1, starting transfers between devices, shards(): lax.ppermute(to_prev.astype(jnp.bfloat16), 'strip', [(i + 1, i) for i in...  3.42 us
  transfers between devices with their start and end apart: 10, of which 7 were waited for; matrix products, arithmetic and copies ran while one was open for 28% of the time, Pallas kernels for 9%

profile of v17, /device:TPU:26, one launch (start us, length us, event | category | flops | bytes accessed | tf_op | source)
XLA Modules:
  0.0 74.0 jit_solution(10213212392746721248)
XLA Ops:
  0.0 2.5 %collective-permute-start.3 = (bf16[480,384]{1,0:T(8,128)(2,1)}, bf16[480,384]{1,0:T(8,128)(2,1)S(1)}, u32[]{:S(2)}, u32[]{:S(2)}) collective-permute-start(bf16[480,384]{1,0:T(8,128)(2,1)} %bitcast.114), channel_id=1, source_target_pairs={{4,0},{8,4},{12,8},{5,1},{9,5},{13,9},{6,2},{10,6},{14,10},{7,3},{... | collective-permute-start | bytes 1105928 | tf_op jit(solution)/shard_map/ppermute | solution.py:24
  2.5 1.3 %collective-permute-start = (bf16[480,384]{1,0:T(8,128)(2,1)}, bf16[480,384]{1,0:T(8,128)(2,1)S(1)}, u32[]{:S(2)}, u32[]{:S(2)}) collective-permute-start(bf16[480,384]{1,0:T(8,128)(2,1)} %bitcast.115), channel_id=1, source_target_pairs={{0,4},{4,8},{8,12},{1,5},{5,9},{9,13},{2,6},{6,10},{10,14},{3,7},{... | collective-permute-start | bytes 1105928 | tf_op jit(solution)/shard_map/ppermute | solution.py:23
  3.8 1.2 %multiply_reduce_fusion = f32[3,160]{1,0:T(4,128)S(1)} fusion(bf16[1,3,160,384]{3,2,1,0:T(8,128)(2,1)} %param.9), kind=kLoop, calls=%fused_computation.44 | loop fusion | flops 552480 | bytes 370560 | tf_op jit(solution)/shard_map/reduce_sum | solution.py:49
  5.0 1.2 %broadcast_in_dim.20.refs_5_.again_ref = f32[1,384]{1,0:T(1,128)} reshape(f32[384]{0:T(512)} %param.11) | data formatting | bytes 3072 | tf_op jit(solution)/shard_map/broadcast_in_dim | solution.py:49
  6.3 1.3 %reshape.77.cgain_ref = f32[1,384]{1,0:T(1,128)} reshape(f32[384]{0:T(512)} %param.16) | data formatting | bytes 3072 | tf_op jit(solution)/shard_map/reshape | solution.py:238
  7.6 0.6 reshape.76.refs_7_
  8.4 1.0 %constant_dynamic-update-slice_fusion.1 = bf16[384,768]{1,0:T(8,128)(2,1)S(1)} fusion(bf16[384,384]{1,0:T(8,128)(2,1)} %param.13), kind=kLoop, calls=%fused_computation.60 | loop fusion | bytes 589824
  9.4 1.2 %collective-permute-done.3.refs_2_ = bf16[480,384]{1,0:T(8,128)(2,1)S(1)} collective-permute-done((bf16[480,384]{1,0:T(8,128)(2,1)}, bf16[480,384]{1,0:T(8,128)(2,1)S(1)}, u32[]{:S(2)}, u32[]{:S(2)}) %collective-permute-start.3) | collective-permute-done | bytes 368672 | tf_op jit(solution)/shard_map/ppermute | solution.py:24
  10.6 0.7 collective-permute-start.4
  11.3 3.4 %collective-permute-done.refs_1_ = bf16[480,384]{1,0:T(8,128)(2,1)S(1)} collective-permute-done((bf16[480,384]{1,0:T(8,128)(2,1)}, bf16[480,384]{1,0:T(8,128)(2,1)S(1)}, u32[]{:S(2)}, u32[]{:S(2)}) %collective-permute-start) | collective-permute-done | bytes 368672 | tf_op jit(solution)/shard_map/ppermute | solution.py:23
  14.7 1.3 %collective-permute-start.1 = (bf16[480,384]{1,0:T(8,128)(2,1)S(1)}, bf16[480,384]{1,0:T(8,128)(2,1)S(1)}, u32[]{:S(2)}, u32[]{:S(2)}) collective-permute-start(bf16[480,384]{1,0:T(8,128)(2,1)S(1)} %collective-permute-done.refs_1_), channel_id=1, source_target_pairs={{4,8},{8,12},{5,9},{9,13},{6,10},{10,14},{7,11},{11,15},{20,24},{2... | collective-permute-start | bytes 1105928 | tf_op jit(solution)/shard_map/ppermute | solution.py:23
  16.0 1.0 %constant_dynamic-update-slice_fusion.refs_6_.wkv_ref = bf16[384,768]{1,0:T(8,128)(2,1)S(1)} fusion(bf16[384,768]{1,0:T(8,128)(2,1)S(1)} %constant_dynamic-update-slice_fusion.1, bf16[384,384]{1,0:T(8,128)(2,1)} %param.14), kind=kLoop, calls=%fused_computation.59 | loop fusion | bytes 589824 | tf_op jit(solution)/shard_map/concatenate | solution.py:219
  17.0 2.4 %convolution_convert_fusion.refs_4_.query_ref = bf16[480,384]{1,0:T(8,128)(2,1)} fusion(bf16[384,384]{1,0:T(8,128)(2,1)S(1)} %copy-done, bf16[480,384]{1,0:T(8,128)(2,1)} %bitcast.116, f32[384]{0:T(512)} %param.11, f32[480]{0:T(512)S(1)} %rsqrt.12), kind=kOutput, calls=%fused_computation.10 | convolution fusion | flops 142479360 | bytes 1035648 | tf_op jit(solution)/shard_map/dot_general | solution.py:270
  19.4 0.7 collective-permute-start.5
  20.1 5.7 %collective-permute-done.1 = bf16[480,384]{1,0:T(8,128)(2,1)S(1)} collective-permute-done((bf16[480,384]{1,0:T(8,128)(2,1)S(1)}, bf16[480,384]{1,0:T(8,128)(2,1)S(1)}, u32[]{:S(2)}, u32[]{:S(2)}) %collective-permute-start.1) | collective-permute-done | bytes 368672 | tf_op jit(solution)/shard_map/ppermute | solution.py:23
  25.7 1.3 %collective-permute-start.2 = (bf16[480,384]{1,0:T(8,128)(2,1)S(1)}, bf16[480,384]{1,0:T(8,128)(2,1)S(1)}, u32[]{:S(2)}, u32[]{:S(2)}) collective-permute-start(bf16[480,384]{1,0:T(8,128)(2,1)S(1)} %collective-permute-done.1), channel_id=1, source_target_pairs={{8,12},{9,13},{10,14},{11,15},{24,28},{25,29},{26,30},{27,31}} | collective-permute-start | bytes 1105928 | tf_op jit(solution)/shard_map/ppermute | solution.py:23
  27.0 0.8 %broadcast_select_fusion.refs_3_ = bf16[480,384]{1,0:T(8,128)(2,1)} fusion(bf16[480,384]{1,0:T(8,128)(2,1)S(1)} %collective-permute-done.4, bf16[480,384]{1,0:T(8,128)(2,1)S(1)} %collective-permute-done.1, pred[]{:T(512)S(6)} %le.6), kind=kLoop, calls=%fused_computation.55 | loop fusion | flops 184320 | bytes 1105921 | tf_op jit(solution)/shard_map/jit(_where)/select_n | solution.py:274
  27.8 7.0 %shard_map.91 = (f32[480,1]{1,0:T(8,128)}, f32[480,1]{1,0:T(8,128)}, f32[480,384]{1,0:T(8,128)}) custom-call(bf16[480,384]{1,0:T(8,128)(2,1)} %bitcast.117, bf16[480,384]{1,0:T(8,128)(2,1)} %copy-done.5, bf16[480,384]{1,0:T(8,128)(2,1)} %copy-done.4, bf16[480,384]{1,0:T(8,128)(2,1)} %broadcast_select_fusion.refs_3_, ...), custom_call_target="tpu_custom_call" | custom-call | flops 2548039680 | bytes 2442240 | tf_op jit(solution)/shard_map/pallas_call | solution.py:198
  34.8 1.2 %collective-permute-done.2 = bf16[480,384]{1,0:T(8,128)(2,1)S(1)} collective-permute-done((bf16[480,384]{1,0:T(8,128)(2,1)S(1)}, bf16[480,384]{1,0:T(8,128)(2,1)S(1)}, u32[]{:S(2)}, u32[]{:S(2)}) %collective-permute-start.2) | collective-permute-done | bytes 368672 | tf_op jit(solution)/shard_map/ppermute | solution.py:23
  36.0 0.8 %broadcast_select_fusion.1.blocks_ref = bf16[480,384]{1,0:T(8,128)(2,1)} fusion(bf16[480,384]{1,0:T(8,128)(2,1)S(1)} %collective-permute-done.2, bf16[480,384]{1,0:T(8,128)(2,1)S(1)} %collective-permute-done.5, pred[]{:T(512)S(6)} %eq.11), kind=kLoop, calls=%fused_computation.56 | loop fusion | flops 184320 | bytes 1105921 | tf_op jit(solution)/shard_map/jit(_where)/select_n | solution.py:277
  36.8 0.5 reshape.75.bias_ref
  37.3 5.3 %shard_map.92 = (bf16[480,384]{1,0:T(8,128)(2,1)}, bf16[480,384]{1,0:T(8,128)(2,1)}) custom-call(bf16[480,384]{1,0:T(8,128)(2,1)} %broadcast_select_fusion.1.blocks_ref, bf16[480,384]{1,0:T(8,128)(2,1)} %convolution_convert_fusion.refs_4_.query_ref, f32[1,384]{1,0:T(1,128)} %broadcast_in_dim.20.refs_5_.again_ref, bf16[384,768]{1,0:T(8,128)(2,1)} %copy-done.1, ...), custom_call_target="tpu_custom_call" | custom-call | flops 778567680 | bytes 2736768 | tf_op jit(solution)/shard_map/pallas_call | solution.py:198
  42.6 1.9 %collective-permute-start.6 = (bf16[3,160,384]{2,1,0:T(8,128)(2,1)}, bf16[3,160,384]{2,1,0:T(8,128)(2,1)S(1)}, u32[]{:S(2)}, u32[]{:S(2)}) collective-permute-start(bf16[3,160,384]{2,1,0:T(8,128)(2,1)} %bitcast.122), channel_id=1, source_target_pairs={{0,1},{1,2},{2,3},{4,5},{5,6},{6,7},{8,9},{9,10},{10,11},{12,13},{... | collective-permute-start | bytes 1105928 | tf_op jit(solution)/shard_map/ppermute | solution.py:15
  44.5 1.5 %pad_slice_fusion.8 = (bf16[5,160,384]{2,1,0:T(8,128)(2,1)S(1)}, bf16[5,160,384]{2,1,0:T(8,128)(2,1)S(1)}, bf16[5,160,384]{2,1,0:T(8,128)(2,1)S(1)}) fusion(bf16[3,160,384]{2,1,0:T(8,128)(2,1)} %bitcast.123), kind=kLoop, calls=%fused_computation.39 | loop fusion | bytes 2211840 | tf_op jit(solution)/shard_map/slice | solution.py:304
  46.2 0.3 fusion.11
  46.5 1.7 %slice-done.1 = s8[4194304]{0:T(1024)(128)(4,1)S(1)} async-done(((s8[7962624]{0:T(1024)(128)(4,1)}), s8[4194304]{0:T(1024)(128)(4,1)S(1)}, s32[]{:S(2)}) %slice-start.1) | async-done | bytes 4194328
  48.2 0.4 fusion.5
  48.6 0.8 %fusion.4 = f32[480,384]{1,0:T(8,128)S(1)} fusion(bf16[480,1152]{1,0:T(8,128)(2,1)S(1)} %bitcast.121, bf16[3,3,1152,384]{3,2,1,0:T(8,128)(2,1)S(1)} %bitcast.100), kind=kOutput, calls=%fused_computation.27 | convolution fusion | flops 424673280 | bytes 2727936 | tf_op jit(solution)/shard_map/dot_general | solution.py:311
  49.4 0.8 %convolution_add_fusion.5 = f32[480,384]{1,0:T(8,128)S(1)} fusion(f32[480,384]{1,0:T(8,128)S(1)} %fusion.4, bf16[480,1152]{1,0:T(8,128)(2,1)S(1)} %bitcast.96, bf16[3,3,1152,384]{3,2,1,0:T(8,128)(2,1)S(1)} %bitcast.101), kind=kOutput, calls=%fused_computation.9 | convolution fusion | flops 424857600 | bytes 3465216 | tf_op jit(solution)/shard_map/dot_general | solution.py:311
  50.1 0.4 fusion.3
  50.5 0.8 %convolution_add_fusion.4 = f32[480,384]{1,0:T(8,128)S(1)} fusion(f32[480,384]{1,0:T(8,128)S(1)} %convolution_add_fusion.5, bf16[480,1152]{1,0:T(8,128)(2,1)S(1)} %bitcast.94, bf16[3,3,1152,384]{3,2,1,0:T(8,128)(2,1)S(1)} %bitcast.103), kind=kOutput, calls=%fused_computation.8 | convolution fusion | flops 424857600 | bytes 3465216 | tf_op jit(solution)/shard_map/dot_general | solution.py:311
  51.3 0.3 collective-permute-done.6
  51.7 2.1 %collective-permute-start.7 = (bf16[3,160,384]{2,1,0:T(8,128)(2,1)S(1)}, bf16[3,160,384]{2,1,0:T(8,128)(2,1)S(1)}, u32[]{:S(2)}, u32[]{:S(2)}) collective-permute-start(bf16[3,160,384]{2,1,0:T(8,128)(2,1)S(1)} %bitcast_select_fusion.1), channel_id=1, source_target_pairs={{0,1},{1,2},{2,3},{4,5},{5,6},{6,7},{8,9},{9,10},{10,11},{12,13},{... | collective-permute-start | bytes 1105928 | tf_op jit(solution)/shard_map/ppermute | solution.py:15
  54.5 0.4 convolution_add_fusion.7
  54.9 0.8 %fusion.6 = f32[480,384]{1,0:T(8,128)S(1)} fusion(bf16[480,1152]{1,0:T(8,128)(2,1)S(1)} %bitcast.120, bf16[3,3,1152,384]{3,2,1,0:T(8,128)(2,1)S(1)} %bitcast.105), kind=kOutput, calls=%fused_computation.29 | convolution fusion | flops 424673280 | bytes 2727936 | tf_op jit(solution)/shard_map/dot_general | solution.py:311
  55.6 0.8 %convolution_add_fusion.3 = f32[480,384]{1,0:T(8,128)S(1)} fusion(f32[480,384]{1,0:T(8,128)S(1)} %fusion.6, bf16[480,1152]{1,0:T(8,128)(2,1)S(1)} %bitcast.95, bf16[3,3,1152,384]{3,2,1,0:T(8,128)(2,1)S(1)} %bitcast.106), kind=kOutput, calls=%fused_computation.7 | convolution fusion | flops 424857600 | bytes 3465216 | tf_op jit(solution)/shard_map/dot_general | solution.py:311
  56.4 0.4 convolution_add_fusion.9
  56.8 0.8 %convolution_add_fusion.2 = f32[480,384]{1,0:T(8,128)S(1)} fusion(f32[480,384]{1,0:T(8,128)S(1)} %convolution_add_fusion.3, bf16[480,1152]{1,0:T(8,128)(2,1)S(1)} %bitcast.93, bf16[3,3,1152,384]{3,2,1,0:T(8,128)(2,1)S(1)} %bitcast.108), kind=kOutput, calls=%fused_computation.6 | convolution fusion | flops 424857600 | bytes 3465216 | tf_op jit(solution)/shard_map/dot_general | solution.py:311
  57.6 2.9 %collective-permute-done.7 = bf16[3,160,384]{2,1,0:T(8,128)(2,1)S(1)} collective-permute-done((bf16[3,160,384]{2,1,0:T(8,128)(2,1)S(1)}, bf16[3,160,384]{2,1,0:T(8,128)(2,1)S(1)}, u32[]{:S(2)}, u32[]{:S(2)}) %collective-permute-start.7) | collective-permute-done | bytes 368672 | tf_op jit(solution)/shard_map/ppermute | solution.py:15
  61.0 0.3 fusion.13
  61.3 0.4 fusion.2
  61.7 3.4 %collective-permute-start.9 = (bf16[160,384]{1,0:T(8,128)(2,1)S(1)}, bf16[160,384]{1,0:T(8,128)(2,1)S(1)}, u32[]{:S(2)}, u32[]{:S(2)}) collective-permute-start(bf16[160,384]{1,0:T(8,128)(2,1)S(1)} %fusion.2), channel_id=1, source_target_pairs={{4,0},{8,4},{12,8},{5,1},{9,5},{13,9},{6,2},{10,6},{14,10},{7,3},{... | collective-permute-start | bytes 368648 | tf_op jit(solution)/shard_map/ppermute | solution.py:323
  65.1 0.4 fusion.1
  65.5 1.3 %collective-permute-start.8 = (bf16[160,384]{1,0:T(8,128)(2,1)S(1)}, bf16[160,384]{1,0:T(8,128)(2,1)S(1)}, u32[]{:S(2)}, u32[]{:S(2)}) collective-permute-start(bf16[160,384]{1,0:T(8,128)(2,1)S(1)} %fusion.1), channel_id=1, source_target_pairs={{0,4},{4,8},{8,12},{1,5},{5,9},{9,13},{2,6},{6,10},{10,14},{3,7},{... | collective-permute-start | bytes 368648 | tf_op jit(solution)/shard_map/ppermute | solution.py:326
  66.8 0.8 %fusion.7 = f32[480,384]{1,0:T(8,128)S(1)} fusion(bf16[480,1152]{1,0:T(8,128)(2,1)S(1)} %bitcast.119, bf16[3,3,1152,384]{3,2,1,0:T(8,128)(2,1)S(1)} %bitcast.111), kind=kOutput, calls=%fused_computation.30 | convolution fusion | flops 424673280 | bytes 2727936 | tf_op jit(solution)/shard_map/dot_general | solution.py:311
  67.5 0.8 %convolution_add_fusion.1 = f32[480,384]{1,0:T(8,128)S(1)} fusion(f32[480,384]{1,0:T(8,128)S(1)} %fusion.7, bf16[480,1152]{1,0:T(8,128)(2,1)S(1)} %bitcast.92, bf16[3,3,1152,384]{3,2,1,0:T(8,128)(2,1)S(1)} %bitcast.112), kind=kOutput, calls=%fused_computation.5 | convolution fusion | flops 424857600 | bytes 3465216 | tf_op jit(solution)/shard_map/dot_general | solution.py:311
  68.4 3.9 %collective-permute-done.8 = bf16[160,384]{1,0:T(8,128)(2,1)S(1)} collective-permute-done((bf16[160,384]{1,0:T(8,128)(2,1)S(1)}, bf16[160,384]{1,0:T(8,128)(2,1)S(1)}, u32[]{:S(2)}, u32[]{:S(2)}) %collective-permute-start.8) | collective-permute-done | bytes 122912 | tf_op jit(solution)/shard_map/ppermute | solution.py:326
  72.4 1.6 %fusion.8 = bf16[480,384]{1,0:T(8,128)(2,1)} fusion(f32[3,160,384]{2,1,0:T(8,128)S(1)} %pad_maximum_fusion.3, f32[480,384]{1,0:T(8,128)S(1)} %convolution_add_fusion.1, bf16[480,1152]{1,0:T(8,128)(2,1)S(1)} %bitcast.91, bf16[3,3,1152,384]{3,2,1,0:T(8,128)(2,1)S(1)} %bitcast.113, f32[480,384]{1,0:T(8,128)S(1)} %convolution_add_fusion.2, ...), kind=kOutput, calls=%fused_computation.42 | convolution fusion | flops 425963520 | bytes 5677056 | tf_op jit(solution)/shard_map/dot_general | solution.py:311
  (37 shorter events, 1.9 us)
Async XLA Ops:
  0.0 17.0 %copy-start = (bf16[384,384]{1,0:T(8,128)(2,1)S(1)}, bf16[384,384]{1,0:T(8,128)(2,1)}, u32[]{:S(2)}) copy-start(bf16[384,384]{1,0:T(8,128)(2,1)} %param.12) | copy-start | bytes 884740
  0.0 10.6 %collective-permute-start.3 = (bf16[480,384]{1,0:T(8,128)(2,1)}, bf16[480,384]{1,0:T(8,128)(2,1)S(1)}, u32[]{:S(2)}, u32[]{:S(2)}) collective-permute-start(bf16[480,384]{1,0:T(8,128)(2,1)} %bitcast.114), channel_id=1, source_target_pairs={{4,0},{8,4},{12,8},{5,1},{9,5},{13,9},{6,2},{10,6},{14,10},{7,3},{... | collective-permute-start | bytes 1105928 | tf_op jit(solution)/shard_map/ppermute | solution.py:24
  2.5 12.2 %collective-permute-start = (bf16[480,384]{1,0:T(8,128)(2,1)}, bf16[480,384]{1,0:T(8,128)(2,1)S(1)}, u32[]{:S(2)}, u32[]{:S(2)}) collective-permute-start(bf16[480,384]{1,0:T(8,128)(2,1)} %bitcast.115), channel_id=1, source_target_pairs={{0,4},{4,8},{8,12},{1,5},{5,9},{9,13},{2,6},{6,10},{10,14},{3,7},{... | collective-permute-start | bytes 1105928 | tf_op jit(solution)/shard_map/ppermute | solution.py:23
  10.6 17.2 %copy-start.4 = (bf16[480,384]{1,0:T(8,128)(2,1)}, bf16[480,384]{1,0:T(8,128)(2,1)S(1)}, u32[]{:S(2)}) copy-start(bf16[480,384]{1,0:T(8,128)(2,1)S(1)} %collective-permute-done.3.refs_2_) | copy-start | bytes 1105924
  10.6 8.8 %collective-permute-start.4 = (bf16[480,384]{1,0:T(8,128)(2,1)S(1)}, bf16[480,384]{1,0:T(8,128)(2,1)S(1)}, u32[]{:S(2)}, u32[]{:S(2)}) collective-permute-start(bf16[480,384]{1,0:T(8,128)(2,1)S(1)} %collective-permute-done.3.refs_2_), channel_id=1, source_target_pairs={{4,0},{8,4},{5,1},{9,5},{6,2},{10,6},{7,3},{11,7},{20,16},{24,20},... | collective-permute-start | bytes 1105928 | tf_op jit(solution)/shard_map/ppermute | solution.py:24
  14.7 13.2 %copy-start.5 = (bf16[480,384]{1,0:T(8,128)(2,1)}, bf16[480,384]{1,0:T(8,128)(2,1)S(1)}, u32[]{:S(2)}) copy-start(bf16[480,384]{1,0:T(8,128)(2,1)S(1)} %collective-permute-done.refs_1_) | copy-start | bytes 1105924
  14.7 11.1 %collective-permute-start.1 = (bf16[480,384]{1,0:T(8,128)(2,1)S(1)}, bf16[480,384]{1,0:T(8,128)(2,1)S(1)}, u32[]{:S(2)}, u32[]{:S(2)}) collective-permute-start(bf16[480,384]{1,0:T(8,128)(2,1)S(1)} %collective-permute-done.refs_1_), channel_id=1, source_target_pairs={{4,8},{8,12},{5,9},{9,13},{6,10},{10,14},{7,11},{11,15},{20,24},{2... | collective-permute-start | bytes 1105928 | tf_op jit(solution)/shard_map/ppermute | solution.py:23
  17.0 10.9 %copy-start.1 = (bf16[384,768]{1,0:T(8,128)(2,1)}, bf16[384,768]{1,0:T(8,128)(2,1)S(1)}, u32[]{:S(2)}) copy-start(bf16[384,768]{1,0:T(8,128)(2,1)S(1)} %constant_dynamic-update-slice_fusion.refs_6_.wkv_ref) | copy-start | bytes 1769476
  19.4 15.4 %collective-permute-start.5 = (bf16[480,384]{1,0:T(8,128)(2,1)S(1)}, bf16[480,384]{1,0:T(8,128)(2,1)S(1)}, u32[]{:S(2)}, u32[]{:S(2)}) collective-permute-start(bf16[480,384]{1,0:T(8,128)(2,1)S(1)} %collective-permute-done.4), channel_id=1, source_target_pairs={{4,0},{5,1},{6,2},{7,3},{20,16},{21,17},{22,18},{23,19}} | collective-permute-start | bytes 1105928 | tf_op jit(solution)/shard_map/ppermute | solution.py:24
  25.7 10.2 %collective-permute-start.2 = (bf16[480,384]{1,0:T(8,128)(2,1)S(1)}, bf16[480,384]{1,0:T(8,128)(2,1)S(1)}, u32[]{:S(2)}, u32[]{:S(2)}) collective-permute-start(bf16[480,384]{1,0:T(8,128)(2,1)S(1)} %collective-permute-done.1), channel_id=1, source_target_pairs={{8,12},{9,13},{10,14},{11,15},{24,28},{25,29},{26,30},{27,31}} | collective-permute-start | bytes 1105928 | tf_op jit(solution)/shard_map/ppermute | solution.py:23
  37.3 9.2 %slice-start = ((s8[7962624]{0:T(1024)(128)(4,1)}), s8[3768320]{0:T(1024)(128)(4,1)S(1)}, s32[]{:S(2)}) async-start(s8[7962624]{0:T(1024)(128)(4,1)} %bitcast.97), calls=%async_computation | async-start | bytes 7536640
  42.6 9.0 %collective-permute-start.6 = (bf16[3,160,384]{2,1,0:T(8,128)(2,1)}, bf16[3,160,384]{2,1,0:T(8,128)(2,1)S(1)}, u32[]{:S(2)}, u32[]{:S(2)}) collective-permute-start(bf16[3,160,384]{2,1,0:T(8,128)(2,1)} %bitcast.122), channel_id=1, source_target_pairs={{0,1},{1,2},{2,3},{4,5},{5,6},{6,7},{8,9},{9,10},{10,11},{12,13},{... | collective-permute-start | bytes 1105928 | tf_op jit(solution)/shard_map/ppermute | solution.py:15
  46.0 2.2 %slice-start.1 = ((s8[7962624]{0:T(1024)(128)(4,1)}), s8[4194304]{0:T(1024)(128)(4,1)S(1)}, s32[]{:S(2)}) async-start(s8[7962624]{0:T(1024)(128)(4,1)} %bitcast.97), calls=%async_computation.1 | async-start | bytes 8388608
  50.5 1.1 %copy-start.2 = (bf16[2,3,160,384]{3,2,1,0:T(8,128)(2,1)S(1)}, bf16[2,3,160,384]{3,2,1,0:T(8,128)(2,1)}, u32[]{:S(2)}) copy-start(bf16[2,3,160,384]{3,2,1,0:T(8,128)(2,1)} %param.10) | copy-start | bytes 2211844
  51.7 8.8 %collective-permute-start.7 = (bf16[3,160,384]{2,1,0:T(8,128)(2,1)S(1)}, bf16[3,160,384]{2,1,0:T(8,128)(2,1)S(1)}, u32[]{:S(2)}, u32[]{:S(2)}) collective-permute-start(bf16[3,160,384]{2,1,0:T(8,128)(2,1)S(1)} %bitcast_select_fusion.1), channel_id=1, source_target_pairs={{0,1},{1,2},{2,3},{4,5},{5,6},{6,7},{8,9},{9,10},{10,11},{12,13},{... | collective-permute-start | bytes 1105928 | tf_op jit(solution)/shard_map/ppermute | solution.py:15
  61.7 6.7 %collective-permute-start.9 = (bf16[160,384]{1,0:T(8,128)(2,1)S(1)}, bf16[160,384]{1,0:T(8,128)(2,1)S(1)}, u32[]{:S(2)}, u32[]{:S(2)}) collective-permute-start(bf16[160,384]{1,0:T(8,128)(2,1)S(1)} %fusion.2), channel_id=1, source_target_pairs={{4,0},{8,4},{12,8},{5,1},{9,5},{13,9},{6,2},{10,6},{14,10},{7,3},{... | collective-permute-start | bytes 368648 | tf_op jit(solution)/shard_map/ppermute | solution.py:323
  65.5 6.8 %collective-permute-start.8 = (bf16[160,384]{1,0:T(8,128)(2,1)S(1)}, bf16[160,384]{1,0:T(8,128)(2,1)S(1)}, u32[]{:S(2)}, u32[]{:S(2)}) collective-permute-start(bf16[160,384]{1,0:T(8,128)(2,1)S(1)} %fusion.1), channel_id=1, source_target_pairs={{0,4},{4,8},{8,12},{1,5},{5,9},{9,13},{2,6},{6,10},{10,14},{3,7},{... | collective-permute-start | bytes 368648 | tf_op jit(solution)/shard_map/ppermute | solution.py:326
  68.3 4.1 %copy-start.3 = (bf16[480,384]{1,0:T(8,128)(2,1)S(1)}, bf16[480,384]{1,0:T(8,128)(2,1)}, u32[]{:S(2)}) copy-start(bf16[480,384]{1,0:T(8,128)(2,1)} %get-tuple-element.13) | copy-start | bytes 1105924

commit v18 on v17

--- a/solution.py
+++ b/solution.py
@@ -133,9 +133,9 @@
     )
 
 
-def split_kernels_a(scale, count, *refs):
+def split_kernels_a(scale, count, parts, me_ref, *refs):
     blocks = refs[:count]
-    query_ref, again_ref, wkv_ref, bias_ref, m_ref, l_ref, o_ref, kv_ref = refs[count:]
+    query_ref, again_ref, wkv_ref, m_ref, l_ref, o_ref, kv_ref = refs[count:]
     width = query_ref.shape[1]
     rows = blocks[0].shape[0]
     for index, block_ref in enumerate(blocks):
@@ -150,8 +150,13 @@
             preferred_element_type=jnp.float32,
         )
         * scale
-        + bias_ref[...]
-    )
+    )
+    me = me_ref[0]
+    column = lax.broadcasted_iota(jnp.int32, scores.shape, 1)
+    second = (column >= rows) & (column < 2 * rows)
+    third = (column >= 2 * rows) & (column < 3 * rows)
+    hidden = (second & (me < 1)) | (third & (me > parts - 2))
+    scores = jnp.where(hidden, -1e30, scores)
     peak = jnp.max(scores, axis=1, keepdims=True)
     weights = jnp.exp(scores - peak)
     m_ref[...] = peak
@@ -162,11 +167,13 @@
 
 
 def split_kernels_b(
-    scale, blocks_ref, query_ref, again_ref, wkv_ref, bias_ref, m_ref, l_ref, o_ref, flat_ref,
-    wo_ref, cgain_ref, resid_ref, act_ref,
+    scale, parts, me_ref, up_ref, down_ref, query_ref, again_ref, wkv_ref, m_ref, l_ref, o_ref,
+    flat_ref, wo_ref, cgain_ref, resid_ref, act_ref,
 ):
     width = query_ref.shape[1]
-    normed = scaled(blocks_ref[...], again_ref[...]).astype(jnp.bfloat16)
+    me = me_ref[0]
+    block = jnp.where(me == parts - 1, up_ref[...], down_ref[...])
+    normed = scaled(block, again_ref[...]).astype(jnp.bfloat16)
     both = jnp.dot(normed, wkv_ref[...], preferred_element_type=jnp.float32).astype(jnp.bfloat16)
     scores = (
         lax.dot_general(
@@ -174,8 +181,8 @@
             preferred_element_type=jnp.float32,
         )
         * scale
-        + bias_ref[...]
-    )
+    )
+    scores = jnp.where((me == 0) | (me == parts - 1), scores, -1e30)
     earlier = m_ref[...]
     peak = jnp.maximum(jnp.max(scores, axis=1, keepdims=True), earlier)
     alpha = jnp.exp(earlier - peak)
@@ -194,35 +201,39 @@
     act_ref[...] = (shown / (1.0 + jnp.exp(-shown))).astype(jnp.bfloat16)
 
 
-def whole_call(kernel, inputs, outputs, flops, transcendentals, scratch=()):
+def whole_call(kernel, me, inputs, outputs, flops, transcendentals, scratch=()):
     return pl.pallas_call(
         kernel,
         out_shape=outputs,
-        grid=(1,),
-        in_specs=[pl.BlockSpec(x.shape, lambda i: (0, 0)) for x in inputs],
-        out_specs=tuple(pl.BlockSpec(o.shape, lambda i: (0, 0)) for o in outputs),
-        scratch_shapes=list(scratch),
+        grid_spec=pltpu.PrefetchScalarGridSpec(
+            num_scalar_prefetch=1,
+            grid=(1,),
+            in_specs=[pl.BlockSpec(x.shape, lambda i, me: (0, 0)) for x in inputs],
+            out_specs=tuple(pl.BlockSpec(o.shape, lambda i, me: (0, 0)) for o in outputs),
+            scratch_shapes=list(scratch),
+        ),
         compiler_params=pltpu.CompilerParams(vmem_limit_bytes=60 * 1024 * 1024),
         cost_estimate=pl.CostEstimate(
             flops=flops,
             transcendentals=transcendentals,
             bytes_accessed=sum(x.size * x.dtype.itemsize for x in inputs),
         ),
-    )(*inputs)
+    )(me, *inputs)
 
 
 def split_attend(
-    blocks_a, bias_a, blocks_b, bias_b, flat, query, attn_gain, key_weight, value_weight,
+    me, parts, blocks_a, up_b, down_b, flat, query, attn_gain, key_weight, value_weight,
     out_weight, conv_gain, scale,
 ):
     count, width = query.shape
     wkv = jnp.concatenate([key_weight, value_weight], axis=1)
     again = attn_gain.reshape(1, width)
     f32 = jnp.float32
-    keys_a, keys_b = count * len(blocks_a), blocks_b.shape[0]
+    keys_a, keys_b = count * len(blocks_a), count
     m_a, l_a, o_a = whole_call(
-        functools.partial(split_kernels_a, scale, len(blocks_a)),
-        list(blocks_a) + [query, again, wkv, bias_a],
+        functools.partial(split_kernels_a, scale, len(blocks_a), parts),
+        me,
+        list(blocks_a) + [query, again, wkv],
         (
             jax.ShapeDtypeStruct((count, 1), f32),
             jax.ShapeDtypeStruct((count, 1), f32),
@@ -233,8 +244,9 @@
         [pltpu.VMEM((keys_a, 2 * width), jnp.bfloat16)],
     )
     return whole_call(
-        functools.partial(split_kernels_b, scale),
-        [blocks_b, query, again, wkv, bias_b, m_a, l_a, o_a, flat, out_weight,
+        functools.partial(split_kernels_b, scale, parts),
+        me,
+        [up_b, down_b, query, again, wkv, m_a, l_a, o_a, flat, out_weight,
          conv_gain.reshape(1, width)],
         (
             jax.ShapeDtypeStruct((count, width), jnp.bfloat16),
@@ -272,18 +284,9 @@
         me = lax.axis_index("strip")
         ups, downs = relay(flat, "strip")
         far = jnp.where(me <= 1, downs[1], ups[1])
-        blocks_a = [flat, ups[0], downs[0], far]
-        valid_a = [me >= 0, me >= 1, me <= n - 2, me >= 0]
-        blocks_b = jnp.where(me == n - 1, ups[n - 2], downs[n - 2])
-        valid_b = [(me == 0) | (me == n - 1)]
-
-        def bias(valid):
-            rows_of = [jnp.broadcast_to(jnp.where(v, 0.0, -1e30), (count,)) for v in valid]
-            return jnp.concatenate(rows_of).astype(jnp.float32).reshape(1, -1)
-
         resid, act = split_attend(
-            blocks_a, bias(valid_a), blocks_b,
-            bias(valid_b), flat, query, attn_gain, key_weight, value_weight, out_weight,
+            me.astype(jnp.int32).reshape(1), n, [flat, ups[0], downs[0], far], ups[n - 2],
+            downs[n - 2], flat, query, attn_gain, key_weight, value_weight, out_weight,
             conv_gain, scale,
         )
     else:

time: 74.7 us -> 73.7 us (0.987)
  the two profiles are of different devices: /device:TPU:26 before, /device:TPU:10 now
where the time goes in v18:
time: 73.7 us; the launch traced here: 72.5 us
  starting transfers between devices  26.5 us (36%)
  Pallas kernels  12.5 us (17%)
  matrix products  11.5 us (16%)
  local copies, waits for them, and re-layouts  10.9 us (15%)
  waiting for transfers between devices  7.04 us (10%)
  other arithmetic  3.64 us (5%)
    pallas_call x2, Pallas kernels, whole_call(): pl.pallas_call(kernel, out_shape=outputs, grid_spec=pltpu.PrefetchScalarG...  12.5 us
    ppermute x3, starting transfers between devices, relay(): up = lax.ppermute(up, axis, [(i, i + 1) for i in range(step - 1, n - 1)])  7.69 us
    ppermute x3, starting transfers between devices, relay(): down = lax.ppermute(down, axis, [(i + 1, i) for i in range(0, n - step)])  7.19 us
    dot_general x9, matrix products, frame_terms(): jnp.dot(window, kernel[step_t, step_r], preferred_element_type=jnp.float32)  6.94 us
    ppermute x1, starting transfers between devices, shards(): lax.ppermute(to_next.astype(jnp.bfloat16), 'strip', [(i, i + 1) for i in...  5.72 us
    unnamed x21, local copies, waits for them, and re-layouts  4.37 us
    ppermute x2, starting transfers between devices, passed_along(): return lax.ppermute(x, axis, pairs)  4.01 us
    ppermute x3, waiting for transfers between devices, relay(): down = lax.ppermute(down, axis, [(i + 1, i) for i in range(0, n - step)])  3.77 us
  transfers between devices with their start and end apart: 10, of which 5 were waited for; matrix products, arithmetic and copies ran while one was open for 28% of the time, Pallas kernels for 10%

profile of v18, /device:TPU:10, one launch (start us, length us, event | category | flops | bytes accessed | tf_op | source)
XLA Modules:
  0.0 72.5 jit_solution(5544453351497703393)
XLA Ops:
  0.0 2.5 %collective-permute-start.3 = (bf16[480,384]{1,0:T(8,128)(2,1)}, bf16[480,384]{1,0:T(8,128)(2,1)S(1)}, u32[]{:S(2)}, u32[]{:S(2)}) collective-permute-start(bf16[480,384]{1,0:T(8,128)(2,1)} %bitcast.113), channel_id=1, source_target_pairs={{4,0},{8,4},{12,8},{5,1},{9,5},{13,9},{6,2},{10,6},{14,10},{7,3},{... | collective-permute-start | bytes 1105928 | tf_op jit(solution)/shard_map/ppermute | solution.py:24
  2.5 3.5 %collective-permute-start = (bf16[480,384]{1,0:T(8,128)(2,1)}, bf16[480,384]{1,0:T(8,128)(2,1)S(1)}, u32[]{:S(2)}, u32[]{:S(2)}) collective-permute-start(bf16[480,384]{1,0:T(8,128)(2,1)} %bitcast.114), channel_id=1, source_target_pairs={{0,4},{4,8},{8,12},{1,5},{5,9},{9,13},{2,6},{6,10},{10,14},{3,7},{... | collective-permute-start | bytes 1105928 | tf_op jit(solution)/shard_map/ppermute | solution.py:23
  6.0 1.2 %multiply_reduce_fusion = f32[3,160]{1,0:T(4,128)S(1)} fusion(bf16[1,3,160,384]{3,2,1,0:T(8,128)(2,1)} %param.9), kind=kLoop, calls=%fused_computation.43 | loop fusion | flops 552480 | bytes 370560 | tf_op jit(solution)/shard_map/reduce_sum | solution.py:49
  7.2 1.2 %broadcast_in_dim.4.refs_5_.again_ref = f32[1,384]{1,0:T(1,128)} reshape(f32[384]{0:T(512)} %param.11) | data formatting | bytes 3072 | tf_op jit(solution)/shard_map/broadcast_in_dim | solution.py:49
  8.4 1.3 %reshape.73.cgain_ref = f32[1,384]{1,0:T(1,128)} reshape(f32[384]{0:T(512)} %param.16) | data formatting | bytes 3072 | tf_op jit(solution)/shard_map/reshape | solution.py:250
  9.8 1.0 %constant_dynamic-update-slice_fusion.1 = bf16[384,768]{1,0:T(8,128)(2,1)S(1)} fusion(bf16[384,384]{1,0:T(8,128)(2,1)} %param.13), kind=kLoop, calls=%fused_computation.58 | loop fusion | bytes 589824
  10.8 1.7 %collective-permute-done.3.refs_2_ = bf16[480,384]{1,0:T(8,128)(2,1)S(1)} collective-permute-done((bf16[480,384]{1,0:T(8,128)(2,1)}, bf16[480,384]{1,0:T(8,128)(2,1)S(1)}, u32[]{:S(2)}, u32[]{:S(2)}) %collective-permute-start.3) | collective-permute-done | bytes 368672 | tf_op jit(solution)/shard_map/ppermute | solution.py:24
  12.6 2.3 %collective-permute-start.4 = (bf16[480,384]{1,0:T(8,128)(2,1)S(1)}, bf16[480,384]{1,0:T(8,128)(2,1)S(1)}, u32[]{:S(2)}, u32[]{:S(2)}) collective-permute-start(bf16[480,384]{1,0:T(8,128)(2,1)S(1)} %collective-permute-done.3.refs_2_), channel_id=1, source_target_pairs={{4,0},{8,4},{5,1},{9,5},{6,2},{10,6},{7,3},{11,7},{20,16},{24,20},... | collective-permute-start | bytes 1105928 | tf_op jit(solution)/shard_map/ppermute | solution.py:24
  14.9 3.5 %collective-permute-start.1 = (bf16[480,384]{1,0:T(8,128)(2,1)S(1)}, bf16[480,384]{1,0:T(8,128)(2,1)S(1)}, u32[]{:S(2)}, u32[]{:S(2)}) collective-permute-start(bf16[480,384]{1,0:T(8,128)(2,1)S(1)} %collective-permute-done.refs_1_), channel_id=1, source_target_pairs={{4,8},{8,12},{5,9},{9,13},{6,10},{10,14},{7,11},{11,15},{20,24},{2... | collective-permute-start | bytes 1105928 | tf_op jit(solution)/shard_map/ppermute | solution.py:23
  18.5 1.0 %constant_dynamic-update-slice_fusion.refs_6_.wkv_ref = bf16[384,768]{1,0:T(8,128)(2,1)S(1)} fusion(bf16[384,768]{1,0:T(8,128)(2,1)S(1)} %constant_dynamic-update-slice_fusion.1, bf16[384,384]{1,0:T(8,128)(2,1)} %param.14), kind=kLoop, calls=%fused_computation.57 | loop fusion | bytes 589824 | tf_op jit(solution)/shard_map/concatenate | solution.py:229
  19.5 2.4 %convolution_convert_fusion.refs_4_.query_ref = bf16[480,384]{1,0:T(8,128)(2,1)} fusion(bf16[384,384]{1,0:T(8,128)(2,1)S(1)} %copy-done, bf16[480,384]{1,0:T(8,128)(2,1)} %bitcast.115, f32[384]{0:T(512)} %param.11, f32[480]{0:T(512)S(1)} %rsqrt.12), kind=kOutput, calls=%fused_computation.9 | convolution fusion | flops 142479360 | bytes 1035648 | tf_op jit(solution)/shard_map/dot_general | solution.py:282
  21.9 2.0 %collective-permute-done.4 = bf16[480,384]{1,0:T(8,128)(2,1)S(1)} collective-permute-done((bf16[480,384]{1,0:T(8,128)(2,1)S(1)}, bf16[480,384]{1,0:T(8,128)(2,1)S(1)}, u32[]{:S(2)}, u32[]{:S(2)}) %collective-permute-start.4) | collective-permute-done | bytes 368672 | tf_op jit(solution)/shard_map/ppermute | solution.py:24
  23.9 2.4 %collective-permute-start.5 = (bf16[480,384]{1,0:T(8,128)(2,1)S(1)}, bf16[480,384]{1,0:T(8,128)(2,1)S(1)}, u32[]{:S(2)}, u32[]{:S(2)}) collective-permute-start(bf16[480,384]{1,0:T(8,128)(2,1)S(1)} %collective-permute-done.4), channel_id=1, source_target_pairs={{4,0},{5,1},{6,2},{7,3},{20,16},{21,17},{22,18},{23,19}} | collective-permute-start | bytes 1105928 | tf_op jit(solution)/shard_map/ppermute | solution.py:24
  26.3 0.7 collective-permute-start.2
  27.0 0.8 %broadcast_select_fusion.refs_3_ = bf16[480,384]{1,0:T(8,128)(2,1)} fusion(bf16[480,384]{1,0:T(8,128)(2,1)S(1)} %collective-permute-done.4, bf16[480,384]{1,0:T(8,128)(2,1)S(1)} %collective-permute-done.1, pred[]{:T(512)S(6)} %le.3), kind=kLoop, calls=%fused_computation.54 | loop fusion | flops 184320 | bytes 1105921 | tf_op jit(solution)/shard_map/jit(_where)/select_n | solution.py:286
  27.8 7.0 %shard_map.91 = (f32[480,1]{1,0:T(8,128)}, f32[480,1]{1,0:T(8,128)}, f32[480,384]{1,0:T(8,128)}) custom-call(s32[1]{0:T(128)} %bitcast.me_ref, bf16[480,384]{1,0:T(8,128)(2,1)} %bitcast.116, bf16[480,384]{1,0:T(8,128)(2,1)} %copy-done.7, bf16[480,384]{1,0:T(8,128)(2,1)} %copy-done.6, bf16[480,384]{1,0:T(8,128)(2,1)} %broadcast_select_fusion.refs_3_, ...), custom_call_target="tpu_custom_call" | custom-call | flops 2548039680 | bytes 2434560 | tf_op jit(solution)/shard_map/pallas_call | solution.py:205
  34.9 0.7 copy-done.4
  35.7 5.4 %shard_map.92 = (bf16[480,384]{1,0:T(8,128)(2,1)}, bf16[480,384]{1,0:T(8,128)(2,1)}) custom-call(s32[1]{0:T(128)} %bitcast.me_ref, bf16[480,384]{1,0:T(8,128)(2,1)} %copy-done.5, bf16[480,384]{1,0:T(8,128)(2,1)} %copy-done.4, bf16[480,384]{1,0:T(8,128)(2,1)} %convolution_convert_fusion.refs_4_.query_ref, f32[1,384]{1,0:T(1,128)} %broadcast_in_dim.4.refs_5_.again_ref, ...), custom_call_target="tpu_custom_call" | custom-call | flops 778567680 | bytes 3103488 | tf_op jit(solution)/shard_map/pallas_call | solution.py:205
  41.1 1.9 %collective-permute-start.6 = (bf16[3,160,384]{2,1,0:T(8,128)(2,1)}, bf16[3,160,384]{2,1,0:T(8,128)(2,1)S(1)}, u32[]{:S(2)}, u32[]{:S(2)}) collective-permute-start(bf16[3,160,384]{2,1,0:T(8,128)(2,1)} %bitcast.121), channel_id=1, source_target_pairs={{0,1},{1,2},{2,3},{4,5},{5,6},{6,7},{8,9},{9,10},{10,11},{12,13},{... | collective-permute-start | bytes 1105928 | tf_op jit(solution)/shard_map/ppermute | solution.py:15
  43.1 1.5 %pad_slice_fusion.8 = (bf16[5,160,384]{2,1,0:T(8,128)(2,1)S(1)}, bf16[5,160,384]{2,1,0:T(8,128)(2,1)S(1)}, bf16[5,160,384]{2,1,0:T(8,128)(2,1)S(1)}) fusion(bf16[3,160,384]{2,1,0:T(8,128)(2,1)} %bitcast.122), kind=kLoop, calls=%fused_computation.38 | loop fusion | bytes 2211840 | tf_op jit(solution)/shard_map/slice | solution.py:307
  44.8 0.3 fusion.10
  45.0 1.7 %slice-done.1 = s8[4194304]{0:T(1024)(128)(4,1)S(1)} async-done(((s8[7962624]{0:T(1024)(128)(4,1)}), s8[4194304]{0:T(1024)(128)(4,1)S(1)}, s32[]{:S(2)}) %slice-start.1) | async-done | bytes 4194328
  46.8 0.4 fusion.4
  47.1 0.8 %fusion.3 = f32[480,384]{1,0:T(8,128)S(1)} fusion(bf16[480,1152]{1,0:T(8,128)(2,1)S(1)} %bitcast.120, bf16[3,3,1152,384]{3,2,1,0:T(8,128)(2,1)S(1)} %bitcast.99), kind=kOutput, calls=%fused_computation.26 | convolution fusion | flops 424673280 | bytes 2727936 | tf_op jit(solution)/shard_map/dot_general | solution.py:314
  47.9 0.8 %convolution_add_fusion.5 = f32[480,384]{1,0:T(8,128)S(1)} fusion(f32[480,384]{1,0:T(8,128)S(1)} %fusion.3, bf16[480,1152]{1,0:T(8,128)(2,1)S(1)} %bitcast.95, bf16[3,3,1152,384]{3,2,1,0:T(8,128)(2,1)S(1)} %bitcast.100), kind=kOutput, calls=%fused_computation.8 | convolution fusion | flops 424857600 | bytes 3465216 | tf_op jit(solution)/shard_map/dot_general | solution.py:314
  48.7 0.4 fusion.2
  49.1 0.8 %convolution_add_fusion.4 = f32[480,384]{1,0:T(8,128)S(1)} fusion(f32[480,384]{1,0:T(8,128)S(1)} %convolution_add_fusion.5, bf16[480,1152]{1,0:T(8,128)(2,1)S(1)} %bitcast.93, bf16[3,3,1152,384]{3,2,1,0:T(8,128)(2,1)S(1)} %bitcast.102), kind=kOutput, calls=%fused_computation.7 | convolution fusion | flops 424857600 | bytes 3465216 | tf_op jit(solution)/shard_map/dot_general | solution.py:314
  49.9 0.3 collective-permute-done.6
  50.2 2.1 %collective-permute-start.7 = (bf16[3,160,384]{2,1,0:T(8,128)(2,1)S(1)}, bf16[3,160,384]{2,1,0:T(8,128)(2,1)S(1)}, u32[]{:S(2)}, u32[]{:S(2)}) collective-permute-start(bf16[3,160,384]{2,1,0:T(8,128)(2,1)S(1)} %bitcast_select_fusion.1), channel_id=1, source_target_pairs={{0,1},{1,2},{2,3},{4,5},{5,6},{6,7},{8,9},{9,10},{10,11},{12,13},{... | collective-permute-start | bytes 1105928 | tf_op jit(solution)/shard_map/ppermute | solution.py:15
  52.4 0.3 pad_slice_fusion.5
  52.8 0.3 fusion.11
  53.1 0.4 convolution_add_fusion.7
  53.5 0.8 %fusion.5 = f32[480,384]{1,0:T(8,128)S(1)} fusion(bf16[480,1152]{1,0:T(8,128)(2,1)S(1)} %bitcast.119, bf16[3,3,1152,384]{3,2,1,0:T(8,128)(2,1)S(1)} %bitcast.104), kind=kOutput, calls=%fused_computation.28 | convolution fusion | flops 424673280 | bytes 2727936 | tf_op jit(solution)/shard_map/dot_general | solution.py:314
  54.2 0.8 %convolution_add_fusion.3 = f32[480,384]{1,0:T(8,128)S(1)} fusion(f32[480,384]{1,0:T(8,128)S(1)} %fusion.5, bf16[480,1152]{1,0:T(8,128)(2,1)S(1)} %bitcast.94, bf16[3,3,1152,384]{3,2,1,0:T(8,128)(2,1)S(1)} %bitcast.105), kind=kOutput, calls=%fused_computation.6 | convolution fusion | flops 424857600 | bytes 3465216 | tf_op jit(solution)/shard_map/dot_general | solution.py:314
  55.0 0.4 convolution_add_fusion.9
  55.4 0.8 %convolution_add_fusion.2 = f32[480,384]{1,0:T(8,128)S(1)} fusion(f32[480,384]{1,0:T(8,128)S(1)} %convolution_add_fusion.3, bf16[480,1152]{1,0:T(8,128)(2,1)S(1)} %bitcast.92, bf16[3,3,1152,384]{3,2,1,0:T(8,128)(2,1)S(1)} %bitcast.107), kind=kOutput, calls=%fused_computation.5 | convolution fusion | flops 424857600 | bytes 3465216 | tf_op jit(solution)/shard_map/dot_general | solution.py:314
  56.2 2.9 %collective-permute-done.7 = bf16[3,160,384]{2,1,0:T(8,128)(2,1)S(1)} collective-permute-done((bf16[3,160,384]{2,1,0:T(8,128)(2,1)S(1)}, bf16[3,160,384]{2,1,0:T(8,128)(2,1)S(1)}, u32[]{:S(2)}, u32[]{:S(2)}) %collective-permute-start.7) | collective-permute-done | bytes 368672 | tf_op jit(solution)/shard_map/ppermute | solution.py:15
  59.1 0.3 pad_slice_fusion.2
  59.6 0.3 fusion.12
  59.9 0.4 fusion.1
  60.2 1.9 %collective-permute-start.9 = (bf16[160,384]{1,0:T(8,128)(2,1)S(1)}, bf16[160,384]{1,0:T(8,128)(2,1)S(1)}, u32[]{:S(2)}, u32[]{:S(2)}) collective-permute-start(bf16[160,384]{1,0:T(8,128)(2,1)S(1)} %fusion.1), channel_id=1, source_target_pairs={{4,0},{8,4},{12,8},{5,1},{9,5},{13,9},{6,2},{10,6},{14,10},{7,3},{... | collective-permute-start | bytes 368648 | tf_op jit(solution)/shard_map/ppermute | solution.py:326
  62.2 0.4 fusion
  62.5 5.7 %collective-permute-start.8 = (bf16[160,384]{1,0:T(8,128)(2,1)S(1)}, bf16[160,384]{1,0:T(8,128)(2,1)S(1)}, u32[]{:S(2)}, u32[]{:S(2)}) collective-permute-start(bf16[160,384]{1,0:T(8,128)(2,1)S(1)} %fusion), channel_id=1, source_target_pairs={{0,4},{4,8},{8,12},{1,5},{5,9},{9,13},{2,6},{6,10},{10,14},{3,7},{... | collective-permute-start | bytes 368648 | tf_op jit(solution)/shard_map/ppermute | solution.py:329
  68.3 0.8 %fusion.6 = f32[480,384]{1,0:T(8,128)S(1)} fusion(bf16[480,1152]{1,0:T(8,128)(2,1)S(1)} %bitcast.118, bf16[3,3,1152,384]{3,2,1,0:T(8,128)(2,1)S(1)} %bitcast.110), kind=kOutput, calls=%fused_computation.29 | convolution fusion | flops 424673280 | bytes 2727936 | tf_op jit(solution)/shard_map/dot_general | solution.py:314
  69.0 0.8 %convolution_add_fusion.1 = f32[480,384]{1,0:T(8,128)S(1)} fusion(f32[480,384]{1,0:T(8,128)S(1)} %fusion.6, bf16[480,1152]{1,0:T(8,128)(2,1)S(1)} %bitcast.91, bf16[3,3,1152,384]{3,2,1,0:T(8,128)(2,1)S(1)} %bitcast.111), kind=kOutput, calls=%fused_computation.4 | convolution fusion | flops 424857600 | bytes 3465216 | tf_op jit(solution)/shard_map/dot_general | solution.py:314
  69.8 0.8 %convolution_add_fusion = f32[480,384]{1,0:T(8,128)S(1)} fusion(f32[480,384]{1,0:T(8,128)S(1)} %convolution_add_fusion.1, bf16[480,1152]{1,0:T(8,128)(2,1)S(1)} %bitcast.90, bf16[3,3,1152,384]{3,2,1,0:T(8,128)(2,1)S(1)} %bitcast.112), kind=kOutput, calls=%fused_computation.3 | convolution fusion | flops 424857600 | bytes 3465216 | tf_op jit(solution)/shard_map/dot_general | solution.py:314
  70.8 0.7 %copy-done.3 = bf16[480,384]{1,0:T(8,128)(2,1)S(1)} copy-done((bf16[480,384]{1,0:T(8,128)(2,1)S(1)}, bf16[480,384]{1,0:T(8,128)(2,1)}, u32[]{:S(2)}) %copy-start.3) | copy-done | bytes 368664
  71.6 0.9 %fusion.7 = bf16[480,384]{1,0:T(8,128)(2,1)} fusion(f32[3,160,384]{2,1,0:T(8,128)S(1)} %pad_maximum_fusion.3, f32[480,384]{1,0:T(8,128)S(1)} %convolution_add_fusion, f32[480,384]{1,0:T(8,128)S(1)} %convolution_add_fusion.2, f32[480,384]{1,0:T(8,128)S(1)} %convolution_add_fusion.4, bf16[480,384]{1,0:T(8,128)(2,1)S(1)} %copy-done.3), kind=kLoop, calls=%fused_computation.41 | loop fusion | flops 1105920 | bytes 3686400 | tf_op jit(solution)/shard_map/convert_element_type | solution.py:342
  (35 shorter events, 1.2 us)
Async XLA Ops:
  0.0 19.5 %copy-start = (bf16[384,384]{1,0:T(8,128)(2,1)S(1)}, bf16[384,384]{1,0:T(8,128)(2,1)}, u32[]{:S(2)}) copy-start(bf16[384,384]{1,0:T(8,128)(2,1)} %param.12) | copy-start | bytes 884740
  0.0 12.6 %collective-permute-start.3 = (bf16[480,384]{1,0:T(8,128)(2,1)}, bf16[480,384]{1,0:T(8,128)(2,1)S(1)}, u32[]{:S(2)}, u32[]{:S(2)}) collective-permute-start(bf16[480,384]{1,0:T(8,128)(2,1)} %bitcast.113), channel_id=1, source_target_pairs={{4,0},{8,4},{12,8},{5,1},{9,5},{13,9},{6,2},{10,6},{14,10},{7,3},{... | collective-permute-start | bytes 1105928 | tf_op jit(solution)/shard_map/ppermute | solution.py:24
  2.5 12.4 %collective-permute-start = (bf16[480,384]{1,0:T(8,128)(2,1)}, bf16[480,384]{1,0:T(8,128)(2,1)S(1)}, u32[]{:S(2)}, u32[]{:S(2)}) collective-permute-start(bf16[480,384]{1,0:T(8,128)(2,1)} %bitcast.114), channel_id=1, source_target_pairs={{0,4},{4,8},{8,12},{1,5},{5,9},{9,13},{2,6},{6,10},{10,14},{3,7},{... | collective-permute-start | bytes 1105928 | tf_op jit(solution)/shard_map/ppermute | solution.py:23
  12.6 15.2 %copy-start.6 = (bf16[480,384]{1,0:T(8,128)(2,1)}, bf16[480,384]{1,0:T(8,128)(2,1)S(1)}, u32[]{:S(2)}) copy-start(bf16[480,384]{1,0:T(8,128)(2,1)S(1)} %collective-permute-done.3.refs_2_) | copy-start | bytes 1105924
  12.6 11.4 %collective-permute-start.4 = (bf16[480,384]{1,0:T(8,128)(2,1)S(1)}, bf16[480,384]{1,0:T(8,128)(2,1)S(1)}, u32[]{:S(2)}, u32[]{:S(2)}) collective-permute-start(bf16[480,384]{1,0:T(8,128)(2,1)S(1)} %collective-permute-done.3.refs_2_), channel_id=1, source_target_pairs={{4,0},{8,4},{5,1},{9,5},{6,2},{10,6},{7,3},{11,7},{20,16},{24,20},... | collective-permute-start | bytes 1105928 | tf_op jit(solution)/shard_map/ppermute | solution.py:24
  14.9 12.9 %copy-start.7 = (bf16[480,384]{1,0:T(8,128)(2,1)}, bf16[480,384]{1,0:T(8,128)(2,1)S(1)}, u32[]{:S(2)}) copy-start(bf16[480,384]{1,0:T(8,128)(2,1)S(1)} %collective-permute-done.refs_1_) | copy-start | bytes 1105924
  14.9 11.4 %collective-permute-start.1 = (bf16[480,384]{1,0:T(8,128)(2,1)S(1)}, bf16[480,384]{1,0:T(8,128)(2,1)S(1)}, u32[]{:S(2)}, u32[]{:S(2)}) collective-permute-start(bf16[480,384]{1,0:T(8,128)(2,1)S(1)} %collective-permute-done.refs_1_), channel_id=1, source_target_pairs={{4,8},{8,12},{5,9},{9,13},{6,10},{10,14},{7,11},{11,15},{20,24},{2... | collective-permute-start | bytes 1105928 | tf_op jit(solution)/shard_map/ppermute | solution.py:23
  19.5 8.3 %copy-start.1 = (bf16[384,768]{1,0:T(8,128)(2,1)}, bf16[384,768]{1,0:T(8,128)(2,1)S(1)}, u32[]{:S(2)}) copy-start(bf16[384,768]{1,0:T(8,128)(2,1)S(1)} %constant_dynamic-update-slice_fusion.refs_6_.wkv_ref) | copy-start | bytes 1769476
  23.9 10.9 %collective-permute-start.5 = (bf16[480,384]{1,0:T(8,128)(2,1)S(1)}, bf16[480,384]{1,0:T(8,128)(2,1)S(1)}, u32[]{:S(2)}, u32[]{:S(2)}) collective-permute-start(bf16[480,384]{1,0:T(8,128)(2,1)S(1)} %collective-permute-done.4), channel_id=1, source_target_pairs={{4,0},{5,1},{6,2},{7,3},{20,16},{21,17},{22,18},{23,19}} | collective-permute-start | bytes 1105928 | tf_op jit(solution)/shard_map/ppermute | solution.py:24
  26.3 8.6 %collective-permute-start.2 = (bf16[480,384]{1,0:T(8,128)(2,1)S(1)}, bf16[480,384]{1,0:T(8,128)(2,1)S(1)}, u32[]{:S(2)}, u32[]{:S(2)}) collective-permute-start(bf16[480,384]{1,0:T(8,128)(2,1)S(1)} %collective-permute-done.1), channel_id=1, source_target_pairs={{8,12},{9,13},{10,14},{11,15},{24,28},{25,29},{26,30},{27,31}} | collective-permute-start | bytes 1105928 | tf_op jit(solution)/shard_map/ppermute | solution.py:23
  34.8 0.7 %copy-start.4 = (bf16[480,384]{1,0:T(8,128)(2,1)}, bf16[480,384]{1,0:T(8,128)(2,1)S(1)}, u32[]{:S(2)}) copy-start(bf16[480,384]{1,0:T(8,128)(2,1)S(1)} %collective-permute-done.5.down_ref) | copy-start | bytes 1105924
  34.9 0.9 %copy-start.5 = (bf16[480,384]{1,0:T(8,128)(2,1)}, bf16[480,384]{1,0:T(8,128)(2,1)S(1)}, u32[]{:S(2)}) copy-start(bf16[480,384]{1,0:T(8,128)(2,1)S(1)} %collective-permute-done.2.up_ref) | copy-start | bytes 1105924
  35.7 9.3 %slice-start = ((s8[7962624]{0:T(1024)(128)(4,1)}), s8[3768320]{0:T(1024)(128)(4,1)S(1)}, s32[]{:S(2)}) async-start(s8[7962624]{0:T(1024)(128)(4,1)} %bitcast.96), calls=%async_computation | async-start | bytes 7536640
  41.1 9.0 %collective-permute-start.6 = (bf16[3,160,384]{2,1,0:T(8,128)(2,1)}, bf16[3,160,384]{2,1,0:T(8,128)(2,1)S(1)}, u32[]{:S(2)}, u32[]{:S(2)}) collective-permute-start(bf16[3,160,384]{2,1,0:T(8,128)(2,1)} %bitcast.121), channel_id=1, source_target_pairs={{0,1},{1,2},{2,3},{4,5},{5,6},{6,7},{8,9},{9,10},{10,11},{12,13},{... | collective-permute-start | bytes 1105928 | tf_op jit(solution)/shard_map/ppermute | solution.py:15
  44.6 2.2 %slice-start.1 = ((s8[7962624]{0:T(1024)(128)(4,1)}), s8[4194304]{0:T(1024)(128)(4,1)S(1)}, s32[]{:S(2)}) async-start(s8[7962624]{0:T(1024)(128)(4,1)} %bitcast.96), calls=%async_computation.1 | async-start | bytes 8388608
  49.1 1.1 %copy-start.2 = (bf16[2,3,160,384]{3,2,1,0:T(8,128)(2,1)S(1)}, bf16[2,3,160,384]{3,2,1,0:T(8,128)(2,1)}, u32[]{:S(2)}) copy-start(bf16[2,3,160,384]{3,2,1,0:T(8,128)(2,1)} %param.10) | copy-start | bytes 2211844
  50.2 8.8 %collective-permute-start.7 = (bf16[3,160,384]{2,1,0:T(8,128)(2,1)S(1)}, bf16[3,160,384]{2,1,0:T(8,128)(2,1)S(1)}, u32[]{:S(2)}, u32[]{:S(2)}) collective-permute-start(bf16[3,160,384]{2,1,0:T(8,128)(2,1)S(1)} %bitcast_select_fusion.1), channel_id=1, source_target_pairs={{0,1},{1,2},{2,3},{4,5},{5,6},{6,7},{8,9},{9,10},{10,11},{12,13},{... | collective-permute-start | bytes 1105928 | tf_op jit(solution)/shard_map/ppermute | solution.py:15
  60.2 10.4 %collective-permute-start.9 = (bf16[160,384]{1,0:T(8,128)(2,1)S(1)}, bf16[160,384]{1,0:T(8,128)(2,1)S(1)}, u32[]{:S(2)}, u32[]{:S(2)}) collective-permute-start(bf16[160,384]{1,0:T(8,128)(2,1)S(1)} %fusion.1), channel_id=1, source_target_pairs={{4,0},{8,4},{12,8},{5,1},{9,5},{13,9},{6,2},{10,6},{14,10},{7,3},{... | collective-permute-start | bytes 368648 | tf_op jit(solution)/shard_map/ppermute | solution.py:326
  62.5 8.2 %collective-permute-start.8 = (bf16[160,384]{1,0:T(8,128)(2,1)S(1)}, bf16[160,384]{1,0:T(8,128)(2,1)S(1)}, u32[]{:S(2)}, u32[]{:S(2)}) collective-permute-start(bf16[160,384]{1,0:T(8,128)(2,1)S(1)} %fusion), channel_id=1, source_target_pairs={{0,4},{4,8},{8,12},{1,5},{5,9},{9,13},{2,6},{6,10},{10,14},{3,7},{... | collective-permute-start | bytes 368648 | tf_op jit(solution)/shard_map/ppermute | solution.py:329
  70.6 1.0 %copy-start.3 = (bf16[480,384]{1,0:T(8,128)(2,1)S(1)}, bf16[480,384]{1,0:T(8,128)(2,1)}, u32[]{:S(2)}) copy-start(bf16[480,384]{1,0:T(8,128)(2,1)} %get-tuple-element.13) | copy-start | bytes 1105924

commit v19 on v18

--- a/solution.py
+++ b/solution.py
@@ -212,7 +212,7 @@
             out_specs=tuple(pl.BlockSpec(o.shape, lambda i, me: (0, 0)) for o in outputs),
             scratch_shapes=list(scratch),
         ),
-        compiler_params=pltpu.CompilerParams(vmem_limit_bytes=60 * 1024 * 1024),
+        compiler_params=pltpu.CompilerParams(vmem_limit_bytes=24 * 1024 * 1024),
         cost_estimate=pl.CostEstimate(
             flops=flops,
             transcendentals=transcendentals,

time: 73.7 us -> 67.6 us (0.917)
  Pallas kernels: 12.5 us -> 7.11 us
  waiting for transfers between devices: 7.04 us -> 11.6 us
  local copies, waits for them, and re-layouts: 10.9 us -> 6.94 us
  matrix products: 11.5 us -> 10.5 us
    pallas_call x2, Pallas kernels: 12.5 us -> 7.11 us  [whole_call(): pl.pallas_call(kernel, out_shape=outputs, grid_spec=pltpu.PrefetchScalarG...]
    ppermute x3, waiting for transfers between devices: 3.77 us -> 6.52 us  [relay(): down = lax.ppermute(down, axis, [(i + 1, i) for i in range(0, n - step)])]
    ppermute x1, starting transfers between devices: 1.92 us -> 4.39 us  [shards(): lax.ppermute(to_prev.astype(jnp.bfloat16), 'strip', [(i + 1, i) for i in...]
    ppermute x1, starting transfers between devices: 5.72 us -> 3.68 us  [shards(): lax.ppermute(to_next.astype(jnp.bfloat16), 'strip', [(i, i + 1) for i in...]
    unnamed x21 -> x13, local copies, waits for them, and re-layouts: 4.37 us -> 2.77 us
    slice x3, local copies, waits for them, and re-layouts: 2.04 us -> 0.77 us  [widen(): padded[:, 0:cols]]
    ppermute x2, waiting for transfers between devices: 3.21 us -> 4.33 us  [passed_along(): return lax.ppermute(x, axis, pairs)]
    dot_general x1, matrix products: 2.38 us -> 1.43 us  [shards(): jnp.dot(normed, query_weight, preferred_element_type=jnp.float32)]
  transfers between devices with their start and end apart: 10 -> 10, of which waited for: 5 -> 6; matrix products, arithmetic and copies ran while one was open for 28% -> 25% of each run, Pallas kernels for 10% -> 7%
where the time goes in v19:
time: 67.6 us; the launch traced here: 66.4 us
  starting transfers between devices  27 us (40%)
  waiting for transfers between devices  11.6 us (17%)
  matrix products  10.5 us (16%)
  Pallas kernels  7.11 us (11%)
  local copies, waits for them, and re-layouts  6.94 us (10%)
  other arithmetic  2.92 us (4%)
    ppermute x3, starting transfers between devices, relay(): up = lax.ppermute(up, axis, [(i, i + 1) for i in range(step - 1, n - 1)])  7.69 us
    ppermute x3, starting transfers between devices, relay(): down = lax.ppermute(down, axis, [(i + 1, i) for i in range(0, n - step)])  7.19 us
    pallas_call x2, Pallas kernels, whole_call(): pl.pallas_call(kernel, out_shape=outputs, grid_spec=pltpu.PrefetchScalarG...  7.11 us
    dot_general x9, matrix products, frame_terms(): jnp.dot(window, kernel[step_t, step_r], preferred_element_type=jnp.float32)  6.88 us
    ppermute x3, waiting for transfers between devices, relay(): down = lax.ppermute(down, axis, [(i + 1, i) for i in range(0, n - step)])  6.52 us
    ppermute x1, starting transfers between devices, shards(): lax.ppermute(to_prev.astype(jnp.bfloat16), 'strip', [(i + 1, i) for i in...  4.39 us
    ppermute x2, waiting for transfers between devices, passed_along(): return lax.ppermute(x, axis, pairs)  4.33 us
    ppermute x2, starting transfers between devices, passed_along(): return lax.ppermute(x, axis, pairs)  4.02 us
  transfers between devices with their start and end apart: 10, of which 6 were waited for; matrix products, arithmetic and copies ran while one was open for 25% of the time, Pallas kernels for 7%

profile of v19, /device:TPU:10, one launch (start us, length us, event | category | flops | bytes accessed | tf_op | source)
XLA Modules:
  0.0 66.4 jit_solution(8479090031742929242)
XLA Ops:
  0.0 2.5 %collective-permute-start.3 = (bf16[480,384]{1,0:T(8,128)(2,1)}, bf16[480,384]{1,0:T(8,128)(2,1)S(1)}, u32[]{:S(2)}, u32[]{:S(2)}) collective-permute-start(bf16[480,384]{1,0:T(8,128)(2,1)} %bitcast.90), channel_id=1, source_target_pairs={{4,0},{8,4},{12,8},{5,1},{9,5},{13,9},{6,2},{10,6},{14,10},{7,3},{... | collective-permute-start | bytes 1105928 | tf_op jit(solution)/shard_map/ppermute | solution.py:24
  2.5 3.5 %collective-permute-start = (bf16[480,384]{1,0:T(8,128)(2,1)}, bf16[480,384]{1,0:T(8,128)(2,1)S(1)}, u32[]{:S(2)}, u32[]{:S(2)}) collective-permute-start(bf16[480,384]{1,0:T(8,128)(2,1)} %bitcast.91), channel_id=1, source_target_pairs={{0,4},{4,8},{8,12},{1,5},{5,9},{9,13},{2,6},{6,10},{10,14},{3,7},{... | collective-permute-start | bytes 1105928 | tf_op jit(solution)/shard_map/ppermute | solution.py:23
  6.0 1.2 %multiply_reduce_fusion = f32[3,160]{1,0:T(4,128)S(1)} fusion(bf16[1,3,160,384]{3,2,1,0:T(8,128)(2,1)} %param.9), kind=kLoop, calls=%fused_computation.43 | loop fusion | flops 552480 | bytes 370560 | tf_op jit(solution)/shard_map/reduce_sum | solution.py:49
  7.2 0.7 %broadcast_in_dim.4.refs_5_.again_ref = f32[1,384]{1,0:T(1,128)S(1)} reshape(f32[384]{0:T(512)} %param.11) | data formatting | bytes 3072 | tf_op jit(solution)/shard_map/broadcast_in_dim | solution.py:49
  7.9 0.7 %reshape.73.cgain_ref = f32[1,384]{1,0:T(1,128)S(1)} reshape(f32[384]{0:T(512)} %param.16) | data formatting | bytes 3072 | tf_op jit(solution)/shard_map/reshape | solution.py:250
  8.8 1.0 %constant_dynamic-update-slice_fusion.1 = bf16[384,768]{1,0:T(8,128)(2,1)S(1)} fusion(bf16[384,384]{1,0:T(8,128)(2,1)} %param.13), kind=kLoop, calls=%fused_computation.58 | loop fusion | bytes 589824
  9.8 2.8 %collective-permute-done.3.refs_2_ = bf16[480,384]{1,0:T(8,128)(2,1)S(1)} collective-permute-done((bf16[480,384]{1,0:T(8,128)(2,1)}, bf16[480,384]{1,0:T(8,128)(2,1)S(1)}, u32[]{:S(2)}, u32[]{:S(2)}) %collective-permute-start.3) | collective-permute-done | bytes 368672 | tf_op jit(solution)/shard_map/ppermute | solution.py:24
  12.6 2.3 %collective-permute-start.4 = (bf16[480,384]{1,0:T(8,128)(2,1)S(1)}, bf16[480,384]{1,0:T(8,128)(2,1)S(1)}, u32[]{:S(2)}, u32[]{:S(2)}) collective-permute-start(bf16[480,384]{1,0:T(8,128)(2,1)S(1)} %collective-permute-done.3.refs_2_), channel_id=1, source_target_pairs={{4,0},{8,4},{5,1},{9,5},{6,2},{10,6},{7,3},{11,7},{20,16},{24,20},... | collective-permute-start | bytes 1105928 | tf_op jit(solution)/shard_map/ppermute | solution.py:24
  14.9 3.5 %collective-permute-start.1 = (bf16[480,384]{1,0:T(8,128)(2,1)S(1)}, bf16[480,384]{1,0:T(8,128)(2,1)S(1)}, u32[]{:S(2)}, u32[]{:S(2)}) collective-permute-start(bf16[480,384]{1,0:T(8,128)(2,1)S(1)} %collective-permute-done.refs_1_), channel_id=1, source_target_pairs={{4,8},{8,12},{5,9},{9,13},{6,10},{10,14},{7,11},{11,15},{20,24},{2... | collective-permute-start | bytes 1105928 | tf_op jit(solution)/shard_map/ppermute | solution.py:23
  18.5 1.0 %constant_dynamic-update-slice_fusion.refs_6_.wkv_ref = bf16[384,768]{1,0:T(8,128)(2,1)S(1)} fusion(bf16[384,768]{1,0:T(8,128)(2,1)S(1)} %constant_dynamic-update-slice_fusion.1, bf16[384,384]{1,0:T(8,128)(2,1)} %param.14), kind=kLoop, calls=%fused_computation.57 | loop fusion | bytes 589824 | tf_op jit(solution)/shard_map/concatenate | solution.py:229
  19.5 1.4 %convolution_convert_fusion.refs_4_.query_ref = bf16[480,384]{1,0:T(8,128)(2,1)S(1)} fusion(bf16[384,384]{1,0:T(8,128)(2,1)S(1)} %copy-done, bf16[480,384]{1,0:T(8,128)(2,1)} %bitcast.92, f32[384]{0:T(512)} %param.11, f32[480]{0:T(512)S(1)} %rsqrt.12), kind=kOutput, calls=%fused_computation.9 | convolution fusion | flops 142479360 | bytes 1035648 | tf_op jit(solution)/shard_map/dot_general | solution.py:282
  20.9 3.0 %collective-permute-done.4 = bf16[480,384]{1,0:T(8,128)(2,1)S(1)} collective-permute-done((bf16[480,384]{1,0:T(8,128)(2,1)S(1)}, bf16[480,384]{1,0:T(8,128)(2,1)S(1)}, u32[]{:S(2)}, u32[]{:S(2)}) %collective-permute-start.4) | collective-permute-done | bytes 368672 | tf_op jit(solution)/shard_map/ppermute | solution.py:24
  23.9 2.4 %collective-permute-start.5 = (bf16[480,384]{1,0:T(8,128)(2,1)S(1)}, bf16[480,384]{1,0:T(8,128)(2,1)S(1)}, u32[]{:S(2)}, u32[]{:S(2)}) collective-permute-start(bf16[480,384]{1,0:T(8,128)(2,1)S(1)} %collective-permute-done.4), channel_id=1, source_target_pairs={{4,0},{5,1},{6,2},{7,3},{20,16},{21,17},{22,18},{23,19}} | collective-permute-start | bytes 1105928 | tf_op jit(solution)/shard_map/ppermute | solution.py:24
  26.3 0.7 %collective-permute-start.2 = (bf16[480,384]{1,0:T(8,128)(2,1)S(1)}, bf16[480,384]{1,0:T(8,128)(2,1)S(1)}, u32[]{:S(2)}, u32[]{:S(2)}) collective-permute-start(bf16[480,384]{1,0:T(8,128)(2,1)S(1)} %collective-permute-done.1), channel_id=1, source_target_pairs={{8,12},{9,13},{10,14},{11,15},{24,28},{25,29},{26,30},{27,31}} | collective-permute-start | bytes 1105928 | tf_op jit(solution)/shard_map/ppermute | solution.py:23
  27.1 4.6 %shard_map.91 = (f32[480,1]{1,0:T(8,128)S(1)}, f32[480,1]{1,0:T(8,128)S(1)}, f32[480,384]{1,0:T(8,128)S(1)}) custom-call(s32[1]{0:T(128)} %bitcast.me_ref, bf16[480,384]{1,0:T(8,128)(2,1)S(1)} %bitcast.93, bf16[480,384]{1,0:T(8,128)(2,1)S(1)} %collective-permute-done.refs_1_, bf16[480,384]{1,0:T(8,128)(2,1)S(1)} %collective-permute-done.3.refs_2_, ...), custom_call_target="tpu_custom_call" | custom-call | flops 2548039680 | bytes 2434560 | tf_op jit(solution)/shard_map/pallas_call | solution.py:205
  31.6 0.7 %collective-permute-done.5.down_ref = bf16[480,384]{1,0:T(8,128)(2,1)S(1)} collective-permute-done((bf16[480,384]{1,0:T(8,128)(2,1)S(1)}, bf16[480,384]{1,0:T(8,128)(2,1)S(1)}, u32[]{:S(2)}, u32[]{:S(2)}) %collective-permute-start.5) | collective-permute-done | bytes 368672 | tf_op jit(solution)/shard_map/ppermute | solution.py:24
  32.4 2.5 %shard_map.92 = (bf16[480,384]{1,0:T(8,128)(2,1)S(1)}, bf16[480,384]{1,0:T(8,128)(2,1)S(1)}) custom-call(s32[1]{0:T(128)} %bitcast.me_ref, bf16[480,384]{1,0:T(8,128)(2,1)S(1)} %collective-permute-done.2.up_ref, bf16[480,384]{1,0:T(8,128)(2,1)S(1)} %collective-permute-done.5.down_ref, bf16[480,384]{1,0:T(8,128)(2,1)S(1)} %convolution_convert_fusion.refs_4_.query_ref, ...), custom_call_target="tpu_custom_call" | custom-call | flops 778567680 | bytes 3103488 | tf_op jit(solution)/shard_map/pallas_call | solution.py:205
  34.9 1.9 %collective-permute-start.6 = (bf16[3,160,384]{2,1,0:T(8,128)(2,1)S(1)}, bf16[3,160,384]{2,1,0:T(8,128)(2,1)S(1)}, u32[]{:S(2)}, u32[]{:S(2)}) collective-permute-start(bf16[3,160,384]{2,1,0:T(8,128)(2,1)S(1)} %bitcast.95), channel_id=1, source_target_pairs={{0,1},{1,2},{2,3},{4,5},{5,6},{6,7},{8,9},{9,10},{10,11},{12,13},{... | collective-permute-start | bytes 1105928 | tf_op jit(solution)/shard_map/ppermute | solution.py:15
  36.9 0.3 pad_slice_fusion.8
  37.3 0.3 fusion.10
  37.6 1.7 %slice-done.1 = s8[4194304]{0:T(1024)(128)(4,1)S(1)} async-done(((s8[7962624]{0:T(1024)(128)(4,1)}), s8[4194304]{0:T(1024)(128)(4,1)S(1)}, s32[]{:S(2)}) %slice-start.1) | async-done | bytes 4194328
  39.3 0.4 fusion.4
  39.7 0.8 %fusion.3 = f32[480,384]{1,0:T(8,128)S(1)} fusion(bf16[480,1152]{1,0:T(8,128)(2,1)S(1)} %bitcast.122, bf16[3,3,1152,384]{3,2,1,0:T(8,128)(2,1)S(1)} %bitcast.106), kind=kOutput, calls=%fused_computation.26 | convolution fusion | flops 424673280 | bytes 2727936 | tf_op jit(solution)/shard_map/dot_general | solution.py:314
  40.5 0.8 %convolution_add_fusion.5 = f32[480,384]{1,0:T(8,128)S(1)} fusion(f32[480,384]{1,0:T(8,128)S(1)} %fusion.3, bf16[480,1152]{1,0:T(8,128)(2,1)S(1)} %bitcast.102, bf16[3,3,1152,384]{3,2,1,0:T(8,128)(2,1)S(1)} %bitcast.107), kind=kOutput, calls=%fused_computation.8 | convolution fusion | flops 424857600 | bytes 3465216 | tf_op jit(solution)/shard_map/dot_general | solution.py:314
  41.2 0.4 fusion.2
  41.6 0.8 %convolution_add_fusion.4 = f32[480,384]{1,0:T(8,128)S(1)} fusion(f32[480,384]{1,0:T(8,128)S(1)} %convolution_add_fusion.5, bf16[480,1152]{1,0:T(8,128)(2,1)S(1)} %bitcast.100, bf16[3,3,1152,384]{3,2,1,0:T(8,128)(2,1)S(1)} %bitcast.109), kind=kOutput, calls=%fused_computation.7 | convolution fusion | flops 424857600 | bytes 3465216 | tf_op jit(solution)/shard_map/dot_general | solution.py:314
  42.4 1.4 %collective-permute-done.6 = bf16[3,160,384]{2,1,0:T(8,128)(2,1)S(1)} collective-permute-done((bf16[3,160,384]{2,1,0:T(8,128)(2,1)S(1)}, bf16[3,160,384]{2,1,0:T(8,128)(2,1)S(1)}, u32[]{:S(2)}, u32[]{:S(2)}) %collective-permute-start.6) | collective-permute-done | bytes 368672 | tf_op jit(solution)/shard_map/ppermute | solution.py:15
  43.8 2.1 %collective-permute-start.7 = (bf16[3,160,384]{2,1,0:T(8,128)(2,1)S(1)}, bf16[3,160,384]{2,1,0:T(8,128)(2,1)S(1)}, u32[]{:S(2)}, u32[]{:S(2)}) collective-permute-start(bf16[3,160,384]{2,1,0:T(8,128)(2,1)S(1)} %bitcast_select_fusion.1), channel_id=1, source_target_pairs={{0,1},{1,2},{2,3},{4,5},{5,6},{6,7},{8,9},{9,10},{10,11},{12,13},{... | collective-permute-start | bytes 1105928 | tf_op jit(solution)/shard_map/ppermute | solution.py:15
  45.9 0.3 pad_slice_fusion.5
  46.2 0.2 pad_maximum_fusion.1
  46.4 0.3 fusion.11
  46.7 0.4 convolution_add_fusion.7
  47.0 0.8 %fusion.5 = f32[480,384]{1,0:T(8,128)S(1)} fusion(bf16[480,1152]{1,0:T(8,128)(2,1)S(1)} %bitcast.121, bf16[3,3,1152,384]{3,2,1,0:T(8,128)(2,1)S(1)} %bitcast.111), kind=kOutput, calls=%fused_computation.28 | convolution fusion | flops 424673280 | bytes 2727936 | tf_op jit(solution)/shard_map/dot_general | solution.py:314
  47.8 0.8 %convolution_add_fusion.3 = f32[480,384]{1,0:T(8,128)S(1)} fusion(f32[480,384]{1,0:T(8,128)S(1)} %fusion.5, bf16[480,1152]{1,0:T(8,128)(2,1)S(1)} %bitcast.101, bf16[3,3,1152,384]{3,2,1,0:T(8,128)(2,1)S(1)} %bitcast.112), kind=kOutput, calls=%fused_computation.6 | convolution fusion | flops 424857600 | bytes 3465216 | tf_op jit(solution)/shard_map/dot_general | solution.py:314
  48.6 0.4 convolution_add_fusion.9
  48.9 0.8 %convolution_add_fusion.2 = f32[480,384]{1,0:T(8,128)S(1)} fusion(f32[480,384]{1,0:T(8,128)S(1)} %convolution_add_fusion.3, bf16[480,1152]{1,0:T(8,128)(2,1)S(1)} %bitcast.99, bf16[3,3,1152,384]{3,2,1,0:T(8,128)(2,1)S(1)} %bitcast.114), kind=kOutput, calls=%fused_computation.5 | convolution fusion | flops 424857600 | bytes 3465216 | tf_op jit(solution)/shard_map/dot_general | solution.py:314
  49.7 2.9 %collective-permute-done.7 = bf16[3,160,384]{2,1,0:T(8,128)(2,1)S(1)} collective-permute-done((bf16[3,160,384]{2,1,0:T(8,128)(2,1)S(1)}, bf16[3,160,384]{2,1,0:T(8,128)(2,1)S(1)}, u32[]{:S(2)}, u32[]{:S(2)}) %collective-permute-start.7) | collective-permute-done | bytes 368672 | tf_op jit(solution)/shard_map/ppermute | solution.py:15
  52.7 0.3 pad_slice_fusion.2
  53.1 0.3 fusion.12
  53.4 0.4 fusion.1
  53.8 4.4 %collective-permute-start.9 = (bf16[160,384]{1,0:T(8,128)(2,1)S(1)}, bf16[160,384]{1,0:T(8,128)(2,1)S(1)}, u32[]{:S(2)}, u32[]{:S(2)}) collective-permute-start(bf16[160,384]{1,0:T(8,128)(2,1)S(1)} %fusion.1), channel_id=1, source_target_pairs={{4,0},{8,4},{12,8},{5,1},{9,5},{13,9},{6,2},{10,6},{14,10},{7,3},{... | collective-permute-start | bytes 368648 | tf_op jit(solution)/shard_map/ppermute | solution.py:326
  58.2 0.4 fusion
  58.6 3.7 %collective-permute-start.8 = (bf16[160,384]{1,0:T(8,128)(2,1)S(1)}, bf16[160,384]{1,0:T(8,128)(2,1)S(1)}, u32[]{:S(2)}, u32[]{:S(2)}) collective-permute-start(bf16[160,384]{1,0:T(8,128)(2,1)S(1)} %fusion), channel_id=1, source_target_pairs={{0,4},{4,8},{8,12},{1,5},{5,9},{9,13},{2,6},{6,10},{10,14},{3,7},{... | collective-permute-start | bytes 368648 | tf_op jit(solution)/shard_map/ppermute | solution.py:329
  62.3 0.8 %fusion.6 = f32[480,384]{1,0:T(8,128)S(1)} fusion(bf16[480,1152]{1,0:T(8,128)(2,1)S(1)} %bitcast.120, bf16[3,3,1152,384]{3,2,1,0:T(8,128)(2,1)S(1)} %bitcast.117), kind=kOutput, calls=%fused_computation.29 | convolution fusion | flops 424673280 | bytes 2727936 | tf_op jit(solution)/shard_map/dot_general | solution.py:314
  63.0 0.8 %convolution_add_fusion.1 = f32[480,384]{1,0:T(8,128)S(1)} fusion(f32[480,384]{1,0:T(8,128)S(1)} %fusion.6, bf16[480,1152]{1,0:T(8,128)(2,1)S(1)} %bitcast.98, bf16[3,3,1152,384]{3,2,1,0:T(8,128)(2,1)S(1)} %bitcast.118), kind=kOutput, calls=%fused_computation.4 | convolution fusion | flops 424857600 | bytes 3465216 | tf_op jit(solution)/shard_map/dot_general | solution.py:314
  63.8 0.8 %convolution_add_fusion = f32[480,384]{1,0:T(8,128)S(1)} fusion(f32[480,384]{1,0:T(8,128)S(1)} %convolution_add_fusion.1, bf16[480,1152]{1,0:T(8,128)(2,1)S(1)} %bitcast.97, bf16[3,3,1152,384]{3,2,1,0:T(8,128)(2,1)S(1)} %bitcast.119), kind=kOutput, calls=%fused_computation.3 | convolution fusion | flops 424857600 | bytes 3465216 | tf_op jit(solution)/shard_map/dot_general | solution.py:314
  64.6 0.7 %collective-permute-done.8 = bf16[160,384]{1,0:T(8,128)(2,1)S(1)} collective-permute-done((bf16[160,384]{1,0:T(8,128)(2,1)S(1)}, bf16[160,384]{1,0:T(8,128)(2,1)S(1)}, u32[]{:S(2)}, u32[]{:S(2)}) %collective-permute-start.8) | collective-permute-done | bytes 122912 | tf_op jit(solution)/shard_map/ppermute | solution.py:329
  65.5 0.9 %fusion.7 = bf16[480,384]{1,0:T(8,128)(2,1)} fusion(f32[3,160,384]{2,1,0:T(8,128)S(1)} %pad_maximum_fusion.3, f32[480,384]{1,0:T(8,128)S(1)} %convolution_add_fusion, f32[480,384]{1,0:T(8,128)S(1)} %convolution_add_fusion.2, f32[480,384]{1,0:T(8,128)S(1)} %convolution_add_fusion.4, bf16[480,384]{1,0:T(8,128)(2,1)S(1)} %get-tuple-element.13), kind=kLoop, calls=%fused_computation.41 | loop fusion | flops 1105920 | bytes 3686400 | tf_op jit(solution)/shard_map/convert_element_type | solution.py:342
  (27 shorter events, 0.8 us)
Async XLA Ops:
  0.0 19.5 %copy-start = (bf16[384,384]{1,0:T(8,128)(2,1)S(1)}, bf16[384,384]{1,0:T(8,128)(2,1)}, u32[]{:S(2)}) copy-start(bf16[384,384]{1,0:T(8,128)(2,1)} %param.12) | copy-start | bytes 884740
  0.0 12.6 %collective-permute-start.3 = (bf16[480,384]{1,0:T(8,128)(2,1)}, bf16[480,384]{1,0:T(8,128)(2,1)S(1)}, u32[]{:S(2)}, u32[]{:S(2)}) collective-permute-start(bf16[480,384]{1,0:T(8,128)(2,1)} %bitcast.90), channel_id=1, source_target_pairs={{4,0},{8,4},{12,8},{5,1},{9,5},{13,9},{6,2},{10,6},{14,10},{7,3},{... | collective-permute-start | bytes 1105928 | tf_op jit(solution)/shard_map/ppermute | solution.py:24
  2.5 12.4 %collective-permute-start = (bf16[480,384]{1,0:T(8,128)(2,1)}, bf16[480,384]{1,0:T(8,128)(2,1)S(1)}, u32[]{:S(2)}, u32[]{:S(2)}) collective-permute-start(bf16[480,384]{1,0:T(8,128)(2,1)} %bitcast.91), channel_id=1, source_target_pairs={{0,4},{4,8},{8,12},{1,5},{5,9},{9,13},{2,6},{6,10},{10,14},{3,7},{... | collective-permute-start | bytes 1105928 | tf_op jit(solution)/shard_map/ppermute | solution.py:23
  7.2 19.9 %copy-start.1 = (bf16[1,3,160,384]{3,2,1,0:T(8,128)(2,1)S(1)}, bf16[1,3,160,384]{3,2,1,0:T(8,128)(2,1)}, u32[]{:S(2)}) copy-start(bf16[1,3,160,384]{3,2,1,0:T(8,128)(2,1)} %param.9) | copy-start | bytes 1105924
  12.6 11.4 %collective-permute-start.4 = (bf16[480,384]{1,0:T(8,128)(2,1)S(1)}, bf16[480,384]{1,0:T(8,128)(2,1)S(1)}, u32[]{:S(2)}, u32[]{:S(2)}) collective-permute-start(bf16[480,384]{1,0:T(8,128)(2,1)S(1)} %collective-permute-done.3.refs_2_), channel_id=1, source_target_pairs={{4,0},{8,4},{5,1},{9,5},{6,2},{10,6},{7,3},{11,7},{20,16},{24,20},... | collective-permute-start | bytes 1105928 | tf_op jit(solution)/shard_map/ppermute | solution.py:24
  14.9 11.4 %collective-permute-start.1 = (bf16[480,384]{1,0:T(8,128)(2,1)S(1)}, bf16[480,384]{1,0:T(8,128)(2,1)S(1)}, u32[]{:S(2)}, u32[]{:S(2)}) collective-permute-start(bf16[480,384]{1,0:T(8,128)(2,1)S(1)} %collective-permute-done.refs_1_), channel_id=1, source_target_pairs={{4,8},{8,12},{5,9},{9,13},{6,10},{10,14},{7,11},{11,15},{20,24},{2... | collective-permute-start | bytes 1105928 | tf_op jit(solution)/shard_map/ppermute | solution.py:23
  23.9 8.5 %collective-permute-start.5 = (bf16[480,384]{1,0:T(8,128)(2,1)S(1)}, bf16[480,384]{1,0:T(8,128)(2,1)S(1)}, u32[]{:S(2)}, u32[]{:S(2)}) collective-permute-start(bf16[480,384]{1,0:T(8,128)(2,1)S(1)} %collective-permute-done.4), channel_id=1, source_target_pairs={{4,0},{5,1},{6,2},{7,3},{20,16},{21,17},{22,18},{23,19}} | collective-permute-start | bytes 1105928 | tf_op jit(solution)/shard_map/ppermute | solution.py:24
  26.3 6.1 %collective-permute-start.2 = (bf16[480,384]{1,0:T(8,128)(2,1)S(1)}, bf16[480,384]{1,0:T(8,128)(2,1)S(1)}, u32[]{:S(2)}, u32[]{:S(2)}) collective-permute-start(bf16[480,384]{1,0:T(8,128)(2,1)S(1)} %collective-permute-done.1), channel_id=1, source_target_pairs={{8,12},{9,13},{10,14},{11,15},{24,28},{25,29},{26,30},{27,31}} | collective-permute-start | bytes 1105928 | tf_op jit(solution)/shard_map/ppermute | solution.py:23
  27.1 5.3 %copy-start.2 = (bf16[384,384]{1,0:T(8,128)(2,1)S(1)}, bf16[384,384]{1,0:T(8,128)(2,1)}, u32[]{:S(2)}) copy-start(bf16[384,384]{1,0:T(8,128)(2,1)} %wo_ref.1) | copy-start | bytes 884740
  32.4 5.2 %slice-start = ((s8[7962624]{0:T(1024)(128)(4,1)}), s8[3768320]{0:T(1024)(128)(4,1)S(1)}, s32[]{:S(2)}) async-start(s8[7962624]{0:T(1024)(128)(4,1)} %bitcast.103), calls=%async_computation | async-start | bytes 7536640
  34.9 8.8 %collective-permute-start.6 = (bf16[3,160,384]{2,1,0:T(8,128)(2,1)S(1)}, bf16[3,160,384]{2,1,0:T(8,128)(2,1)S(1)}, u32[]{:S(2)}, u32[]{:S(2)}) collective-permute-start(bf16[3,160,384]{2,1,0:T(8,128)(2,1)S(1)} %bitcast.95), channel_id=1, source_target_pairs={{0,1},{1,2},{2,3},{4,5},{5,6},{6,7},{8,9},{9,10},{10,11},{12,13},{... | collective-permute-start | bytes 1105928 | tf_op jit(solution)/shard_map/ppermute | solution.py:15
  37.1 2.2 %slice-start.1 = ((s8[7962624]{0:T(1024)(128)(4,1)}), s8[4194304]{0:T(1024)(128)(4,1)S(1)}, s32[]{:S(2)}) async-start(s8[7962624]{0:T(1024)(128)(4,1)} %bitcast.103), calls=%async_computation.1 | async-start | bytes 8388608
  41.6 2.2 %copy-start.3 = (bf16[2,3,160,384]{3,2,1,0:T(8,128)(2,1)S(1)}, bf16[2,3,160,384]{3,2,1,0:T(8,128)(2,1)}, u32[]{:S(2)}) copy-start(bf16[2,3,160,384]{3,2,1,0:T(8,128)(2,1)} %param.10) | copy-start | bytes 2211844
  43.8 8.8 %collective-permute-start.7 = (bf16[3,160,384]{2,1,0:T(8,128)(2,1)S(1)}, bf16[3,160,384]{2,1,0:T(8,128)(2,1)S(1)}, u32[]{:S(2)}, u32[]{:S(2)}) collective-permute-start(bf16[3,160,384]{2,1,0:T(8,128)(2,1)S(1)} %bitcast_select_fusion.1), channel_id=1, source_target_pairs={{0,1},{1,2},{2,3},{4,5},{5,6},{6,7},{8,9},{9,10},{10,11},{12,13},{... | collective-permute-start | bytes 1105928 | tf_op jit(solution)/shard_map/ppermute | solution.py:15
  53.8 10.8 %collective-permute-start.9 = (bf16[160,384]{1,0:T(8,128)(2,1)S(1)}, bf16[160,384]{1,0:T(8,128)(2,1)S(1)}, u32[]{:S(2)}, u32[]{:S(2)}) collective-permute-start(bf16[160,384]{1,0:T(8,128)(2,1)S(1)} %fusion.1), channel_id=1, source_target_pairs={{4,0},{8,4},{12,8},{5,1},{9,5},{13,9},{6,2},{10,6},{14,10},{7,3},{... | collective-permute-start | bytes 368648 | tf_op jit(solution)/shard_map/ppermute | solution.py:326
  58.6 6.8 %collective-permute-start.8 = (bf16[160,384]{1,0:T(8,128)(2,1)S(1)}, bf16[160,384]{1,0:T(8,128)(2,1)S(1)}, u32[]{:S(2)}, u32[]{:S(2)}) collective-permute-start(bf16[160,384]{1,0:T(8,128)(2,1)S(1)} %fusion), channel_id=1, source_target_pairs={{0,4},{4,8},{8,12},{1,5},{5,9},{9,13},{2,6},{6,10},{10,14},{3,7},{... | collective-permute-start | bytes 368648 | tf_op jit(solution)/shard_map/ppermute | solution.py:329

commit v20 on v19

--- a/solution.py
+++ b/solution.py
@@ -212,7 +212,7 @@
             out_specs=tuple(pl.BlockSpec(o.shape, lambda i, me: (0, 0)) for o in outputs),
             scratch_shapes=list(scratch),
         ),
-        compiler_params=pltpu.CompilerParams(vmem_limit_bytes=24 * 1024 * 1024),
+        compiler_params=pltpu.CompilerParams(vmem_limit_bytes=16 * 1024 * 1024),
         cost_estimate=pl.CostEstimate(
             flops=flops,
             transcendentals=transcendentals,

time: 67.6 us -> 67.6 us (level)
  no operation moved by 1% of the time
where the time goes in v20:
time: 67.6 us; the launch traced here: 66.4 us
  starting transfers between devices  27 us (40%)
  waiting for transfers between devices  11.7 us (17%)
  matrix products  10.4 us (15%)
  Pallas kernels  7.11 us (11%)
  local copies, waits for them, and re-layouts  6.81 us (10%)
  other arithmetic  2.93 us (4%)
    ppermute x3, starting transfers between devices, relay(): up = lax.ppermute(up, axis, [(i, i + 1) for i in range(step - 1, n - 1)])  7.69 us
    ppermute x3, starting transfers between devices, relay(): down = lax.ppermute(down, axis, [(i + 1, i) for i in range(0, n - step)])  7.19 us
    pallas_call x2, Pallas kernels, whole_call(): pl.pallas_call(kernel, out_shape=outputs, grid_spec=pltpu.PrefetchScalarG...  7.11 us
    dot_general x9, matrix products, frame_terms(): jnp.dot(window, kernel[step_t, step_r], preferred_element_type=jnp.float32)  6.85 us
    ppermute x3, waiting for transfers between devices, relay(): down = lax.ppermute(down, axis, [(i + 1, i) for i in range(0, n - step)])  6.52 us
    ppermute x2, waiting for transfers between devices, passed_along(): return lax.ppermute(x, axis, pairs)  4.46 us
    ppermute x1, starting transfers between devices, shards(): lax.ppermute(to_prev.astype(jnp.bfloat16), 'strip', [(i + 1, i) for i in...  4.39 us
    ppermute x2, starting transfers between devices, passed_along(): return lax.ppermute(x, axis, pairs)  4.02 us
  transfers between devices with their start and end apart: 10, of which 6 were waited for; matrix products, arithmetic and copies ran while one was open for 25% of the time, Pallas kernels for 7%

profile of v20, /device:TPU:10, one launch (start us, length us, event | category | flops | bytes accessed | tf_op | source)
XLA Modules:
  0.0 66.4 jit_solution(16137334829997885336)
XLA Ops:
  0.0 2.5 %collective-permute-start.3 = (bf16[480,384]{1,0:T(8,128)(2,1)}, bf16[480,384]{1,0:T(8,128)(2,1)S(1)}, u32[]{:S(2)}, u32[]{:S(2)}) collective-permute-start(bf16[480,384]{1,0:T(8,128)(2,1)} %bitcast.90), channel_id=1, source_target_pairs={{4,0},{8,4},{12,8},{5,1},{9,5},{13,9},{6,2},{10,6},{14,10},{7,3},{... | collective-permute-start | bytes 1105928 | tf_op jit(solution)/shard_map/ppermute | solution.py:24
  2.5 3.5 %collective-permute-start = (bf16[480,384]{1,0:T(8,128)(2,1)}, bf16[480,384]{1,0:T(8,128)(2,1)S(1)}, u32[]{:S(2)}, u32[]{:S(2)}) collective-permute-start(bf16[480,384]{1,0:T(8,128)(2,1)} %bitcast.91), channel_id=1, source_target_pairs={{0,4},{4,8},{8,12},{1,5},{5,9},{9,13},{2,6},{6,10},{10,14},{3,7},{... | collective-permute-start | bytes 1105928 | tf_op jit(solution)/shard_map/ppermute | solution.py:23
  6.0 1.2 %multiply_reduce_fusion = f32[3,160]{1,0:T(4,128)S(1)} fusion(bf16[1,3,160,384]{3,2,1,0:T(8,128)(2,1)} %param.9), kind=kLoop, calls=%fused_computation.43 | loop fusion | flops 552480 | bytes 370560 | tf_op jit(solution)/shard_map/reduce_sum | solution.py:49
  7.2 0.7 %broadcast_in_dim.4.refs_5_.again_ref = f32[1,384]{1,0:T(1,128)S(1)} reshape(f32[384]{0:T(512)} %param.11) | data formatting | bytes 3072 | tf_op jit(solution)/shard_map/broadcast_in_dim | solution.py:49
  7.9 0.7 %reshape.73.cgain_ref = f32[1,384]{1,0:T(1,128)S(1)} reshape(f32[384]{0:T(512)} %param.16) | data formatting | bytes 3072 | tf_op jit(solution)/shard_map/reshape | solution.py:250
  8.8 1.0 %constant_dynamic-update-slice_fusion.1 = bf16[384,768]{1,0:T(8,128)(2,1)S(1)} fusion(bf16[384,384]{1,0:T(8,128)(2,1)} %param.13), kind=kLoop, calls=%fused_computation.58 | loop fusion | bytes 589824
  9.8 2.8 %collective-permute-done.3.refs_2_ = bf16[480,384]{1,0:T(8,128)(2,1)S(1)} collective-permute-done((bf16[480,384]{1,0:T(8,128)(2,1)}, bf16[480,384]{1,0:T(8,128)(2,1)S(1)}, u32[]{:S(2)}, u32[]{:S(2)}) %collective-permute-start.3) | collective-permute-done | bytes 368672 | tf_op jit(solution)/shard_map/ppermute | solution.py:24
  12.6 2.3 %collective-permute-start.4 = (bf16[480,384]{1,0:T(8,128)(2,1)S(1)}, bf16[480,384]{1,0:T(8,128)(2,1)S(1)}, u32[]{:S(2)}, u32[]{:S(2)}) collective-permute-start(bf16[480,384]{1,0:T(8,128)(2,1)S(1)} %collective-permute-done.3.refs_2_), channel_id=1, source_target_pairs={{4,0},{8,4},{5,1},{9,5},{6,2},{10,6},{7,3},{11,7},{20,16},{24,20},... | collective-permute-start | bytes 1105928 | tf_op jit(solution)/shard_map/ppermute | solution.py:24
  14.9 3.5 %collective-permute-start.1 = (bf16[480,384]{1,0:T(8,128)(2,1)S(1)}, bf16[480,384]{1,0:T(8,128)(2,1)S(1)}, u32[]{:S(2)}, u32[]{:S(2)}) collective-permute-start(bf16[480,384]{1,0:T(8,128)(2,1)S(1)} %collective-permute-done.refs_1_), channel_id=1, source_target_pairs={{4,8},{8,12},{5,9},{9,13},{6,10},{10,14},{7,11},{11,15},{20,24},{2... | collective-permute-start | bytes 1105928 | tf_op jit(solution)/shard_map/ppermute | solution.py:23
  18.5 1.0 %constant_dynamic-update-slice_fusion.refs_6_.wkv_ref = bf16[384,768]{1,0:T(8,128)(2,1)S(1)} fusion(bf16[384,768]{1,0:T(8,128)(2,1)S(1)} %constant_dynamic-update-slice_fusion.1, bf16[384,384]{1,0:T(8,128)(2,1)} %param.14), kind=kLoop, calls=%fused_computation.57 | loop fusion | bytes 589824 | tf_op jit(solution)/shard_map/concatenate | solution.py:229
  19.5 1.4 %convolution_convert_fusion.refs_4_.query_ref = bf16[480,384]{1,0:T(8,128)(2,1)S(1)} fusion(bf16[384,384]{1,0:T(8,128)(2,1)S(1)} %copy-done, bf16[480,384]{1,0:T(8,128)(2,1)} %bitcast.92, f32[384]{0:T(512)} %param.11, f32[480]{0:T(512)S(1)} %rsqrt.12), kind=kOutput, calls=%fused_computation.9 | convolution fusion | flops 142479360 | bytes 1035648 | tf_op jit(solution)/shard_map/dot_general | solution.py:282
  20.9 3.0 %collective-permute-done.4 = bf16[480,384]{1,0:T(8,128)(2,1)S(1)} collective-permute-done((bf16[480,384]{1,0:T(8,128)(2,1)S(1)}, bf16[480,384]{1,0:T(8,128)(2,1)S(1)}, u32[]{:S(2)}, u32[]{:S(2)}) %collective-permute-start.4) | collective-permute-done | bytes 368672 | tf_op jit(solution)/shard_map/ppermute | solution.py:24
  23.9 2.4 %collective-permute-start.5 = (bf16[480,384]{1,0:T(8,128)(2,1)S(1)}, bf16[480,384]{1,0:T(8,128)(2,1)S(1)}, u32[]{:S(2)}, u32[]{:S(2)}) collective-permute-start(bf16[480,384]{1,0:T(8,128)(2,1)S(1)} %collective-permute-done.4), channel_id=1, source_target_pairs={{4,0},{5,1},{6,2},{7,3},{20,16},{21,17},{22,18},{23,19}} | collective-permute-start | bytes 1105928 | tf_op jit(solution)/shard_map/ppermute | solution.py:24
  26.3 0.7 %collective-permute-start.2 = (bf16[480,384]{1,0:T(8,128)(2,1)S(1)}, bf16[480,384]{1,0:T(8,128)(2,1)S(1)}, u32[]{:S(2)}, u32[]{:S(2)}) collective-permute-start(bf16[480,384]{1,0:T(8,128)(2,1)S(1)} %collective-permute-done.1), channel_id=1, source_target_pairs={{8,12},{9,13},{10,14},{11,15},{24,28},{25,29},{26,30},{27,31}} | collective-permute-start | bytes 1105928 | tf_op jit(solution)/shard_map/ppermute | solution.py:23
  27.1 4.6 %shard_map.91 = (f32[480,1]{1,0:T(8,128)S(1)}, f32[480,1]{1,0:T(8,128)S(1)}, f32[480,384]{1,0:T(8,128)S(1)}) custom-call(s32[1]{0:T(128)} %bitcast.me_ref, bf16[480,384]{1,0:T(8,128)(2,1)S(1)} %bitcast.93, bf16[480,384]{1,0:T(8,128)(2,1)S(1)} %collective-permute-done.refs_1_, bf16[480,384]{1,0:T(8,128)(2,1)S(1)} %collective-permute-done.3.refs_2_, ...), custom_call_target="tpu_custom_call" | custom-call | flops 2548039680 | bytes 2434560 | tf_op jit(solution)/shard_map/pallas_call | solution.py:205
  31.6 0.7 %collective-permute-done.5.down_ref = bf16[480,384]{1,0:T(8,128)(2,1)S(1)} collective-permute-done((bf16[480,384]{1,0:T(8,128)(2,1)S(1)}, bf16[480,384]{1,0:T(8,128)(2,1)S(1)}, u32[]{:S(2)}, u32[]{:S(2)}) %collective-permute-start.5) | collective-permute-done | bytes 368672 | tf_op jit(solution)/shard_map/ppermute | solution.py:24
  32.4 2.5 %shard_map.92 = (bf16[480,384]{1,0:T(8,128)(2,1)S(1)}, bf16[480,384]{1,0:T(8,128)(2,1)S(1)}) custom-call(s32[1]{0:T(128)} %bitcast.me_ref, bf16[480,384]{1,0:T(8,128)(2,1)S(1)} %collective-permute-done.2.up_ref, bf16[480,384]{1,0:T(8,128)(2,1)S(1)} %collective-permute-done.5.down_ref, bf16[480,384]{1,0:T(8,128)(2,1)S(1)} %convolution_convert_fusion.refs_4_.query_ref, ...), custom_call_target="tpu_custom_call" | custom-call | flops 778567680 | bytes 3103488 | tf_op jit(solution)/shard_map/pallas_call | solution.py:205
  34.9 1.9 %collective-permute-start.6 = (bf16[3,160,384]{2,1,0:T(8,128)(2,1)S(1)}, bf16[3,160,384]{2,1,0:T(8,128)(2,1)S(1)}, u32[]{:S(2)}, u32[]{:S(2)}) collective-permute-start(bf16[3,160,384]{2,1,0:T(8,128)(2,1)S(1)} %bitcast.95), channel_id=1, source_target_pairs={{0,1},{1,2},{2,3},{4,5},{5,6},{6,7},{8,9},{9,10},{10,11},{12,13},{... | collective-permute-start | bytes 1105928 | tf_op jit(solution)/shard_map/ppermute | solution.py:15
  36.9 0.3 pad_slice_fusion.8
  37.1 0.2 pad_maximum_fusion
  37.3 0.3 fusion.10
  37.6 1.6 %slice-done.1 = s8[3768320]{0:T(1024)(128)(4,1)S(1)} async-done(((s8[7962624]{0:T(1024)(128)(4,1)}), s8[3768320]{0:T(1024)(128)(4,1)S(1)}, s32[]{:S(2)}) %slice-start.1) | async-done | bytes 3768344
  39.2 0.4 fusion.4
  39.6 0.8 %fusion.3 = f32[480,384]{1,0:T(8,128)S(1)} fusion(bf16[480,1152]{1,0:T(8,128)(2,1)S(1)} %bitcast.122, bf16[3,3,1152,384]{3,2,1,0:T(8,128)(2,1)S(1)} %bitcast.106), kind=kOutput, calls=%fused_computation.26 | convolution fusion | flops 424673280 | bytes 2727936 | tf_op jit(solution)/shard_map/dot_general | solution.py:314
  40.3 0.8 %convolution_add_fusion.5 = f32[480,384]{1,0:T(8,128)S(1)} fusion(f32[480,384]{1,0:T(8,128)S(1)} %fusion.3, bf16[480,1152]{1,0:T(8,128)(2,1)S(1)} %bitcast.102, bf16[3,3,1152,384]{3,2,1,0:T(8,128)(2,1)S(1)} %bitcast.107), kind=kOutput, calls=%fused_computation.8 | convolution fusion | flops 424857600 | bytes 3465216 | tf_op jit(solution)/shard_map/dot_general | solution.py:314
  41.1 0.4 fusion.2
  41.5 0.8 %convolution_add_fusion.4 = f32[480,384]{1,0:T(8,128)S(1)} fusion(f32[480,384]{1,0:T(8,128)S(1)} %convolution_add_fusion.5, bf16[480,1152]{1,0:T(8,128)(2,1)S(1)} %bitcast.100, bf16[3,3,1152,384]{3,2,1,0:T(8,128)(2,1)S(1)} %bitcast.109), kind=kOutput, calls=%fused_computation.7 | convolution fusion | flops 424857600 | bytes 3465216 | tf_op jit(solution)/shard_map/dot_general | solution.py:314
  42.3 1.5 %collective-permute-done.6 = bf16[3,160,384]{2,1,0:T(8,128)(2,1)S(1)} collective-permute-done((bf16[3,160,384]{2,1,0:T(8,128)(2,1)S(1)}, bf16[3,160,384]{2,1,0:T(8,128)(2,1)S(1)}, u32[]{:S(2)}, u32[]{:S(2)}) %collective-permute-start.6) | collective-permute-done | bytes 368672 | tf_op jit(solution)/shard_map/ppermute | solution.py:15
  43.8 2.1 %collective-permute-start.7 = (bf16[3,160,384]{2,1,0:T(8,128)(2,1)S(1)}, bf16[3,160,384]{2,1,0:T(8,128)(2,1)S(1)}, u32[]{:S(2)}, u32[]{:S(2)}) collective-permute-start(bf16[3,160,384]{2,1,0:T(8,128)(2,1)S(1)} %bitcast_select_fusion.1), channel_id=1, source_target_pairs={{0,1},{1,2},{2,3},{4,5},{5,6},{6,7},{8,9},{9,10},{10,11},{12,13},{... | collective-permute-start | bytes 1105928 | tf_op jit(solution)/shard_map/ppermute | solution.py:15
  45.9 0.3 pad_slice_fusion.5
  46.4 0.3 fusion.11
  46.7 0.4 convolution_add_fusion.7
  47.0 0.8 %fusion.5 = f32[480,384]{1,0:T(8,128)S(1)} fusion(bf16[480,1152]{1,0:T(8,128)(2,1)S(1)} %bitcast.121, bf16[3,3,1152,384]{3,2,1,0:T(8,128)(2,1)S(1)} %bitcast.111), kind=kOutput, calls=%fused_computation.28 | convolution fusion | flops 424673280 | bytes 2727936 | tf_op jit(solution)/shard_map/dot_general | solution.py:314
  47.8 0.8 %convolution_add_fusion.3 = f32[480,384]{1,0:T(8,128)S(1)} fusion(f32[480,384]{1,0:T(8,128)S(1)} %fusion.5, bf16[480,1152]{1,0:T(8,128)(2,1)S(1)} %bitcast.101, bf16[3,3,1152,384]{3,2,1,0:T(8,128)(2,1)S(1)} %bitcast.112), kind=kOutput, calls=%fused_computation.6 | convolution fusion | flops 424857600 | bytes 3465216 | tf_op jit(solution)/shard_map/dot_general | solution.py:314
  48.6 0.4 convolution_add_fusion.9
  48.9 0.8 %convolution_add_fusion.2 = f32[480,384]{1,0:T(8,128)S(1)} fusion(f32[480,384]{1,0:T(8,128)S(1)} %convolution_add_fusion.3, bf16[480,1152]{1,0:T(8,128)(2,1)S(1)} %bitcast.99, bf16[3,3,1152,384]{3,2,1,0:T(8,128)(2,1)S(1)} %bitcast.114), kind=kOutput, calls=%fused_computation.5 | convolution fusion | flops 424857600 | bytes 3465216 | tf_op jit(solution)/shard_map/dot_general | solution.py:314
  49.7 3.0 %collective-permute-done.7 = bf16[3,160,384]{2,1,0:T(8,128)(2,1)S(1)} collective-permute-done((bf16[3,160,384]{2,1,0:T(8,128)(2,1)S(1)}, bf16[3,160,384]{2,1,0:T(8,128)(2,1)S(1)}, u32[]{:S(2)}, u32[]{:S(2)}) %collective-permute-start.7) | collective-permute-done | bytes 368672 | tf_op jit(solution)/shard_map/ppermute | solution.py:15
  52.7 0.3 pad_slice_fusion.2
  53.1 0.3 fusion.12
  53.4 0.4 fusion.1
  53.8 4.4 %collective-permute-start.9 = (bf16[160,384]{1,0:T(8,128)(2,1)S(1)}, bf16[160,384]{1,0:T(8,128)(2,1)S(1)}, u32[]{:S(2)}, u32[]{:S(2)}) collective-permute-start(bf16[160,384]{1,0:T(8,128)(2,1)S(1)} %fusion.1), channel_id=1, source_target_pairs={{4,0},{8,4},{12,8},{5,1},{9,5},{13,9},{6,2},{10,6},{14,10},{7,3},{... | collective-permute-start | bytes 368648 | tf_op jit(solution)/shard_map/ppermute | solution.py:326
  58.2 0.4 fusion
  58.6 3.7 %collective-permute-start.8 = (bf16[160,384]{1,0:T(8,128)(2,1)S(1)}, bf16[160,384]{1,0:T(8,128)(2,1)S(1)}, u32[]{:S(2)}, u32[]{:S(2)}) collective-permute-start(bf16[160,384]{1,0:T(8,128)(2,1)S(1)} %fusion), channel_id=1, source_target_pairs={{0,4},{4,8},{8,12},{1,5},{5,9},{9,13},{2,6},{6,10},{10,14},{3,7},{... | collective-permute-start | bytes 368648 | tf_op jit(solution)/shard_map/ppermute | solution.py:329
  62.3 0.8 %fusion.6 = f32[480,384]{1,0:T(8,128)S(1)} fusion(bf16[480,1152]{1,0:T(8,128)(2,1)S(1)} %bitcast.120, bf16[3,3,1152,384]{3,2,1,0:T(8,128)(2,1)S(1)} %bitcast.117), kind=kOutput, calls=%fused_computation.29 | convolution fusion | flops 424673280 | bytes 2727936 | tf_op jit(solution)/shard_map/dot_general | solution.py:314
  63.0 0.8 %convolution_add_fusion.1 = f32[480,384]{1,0:T(8,128)S(1)} fusion(f32[480,384]{1,0:T(8,128)S(1)} %fusion.6, bf16[480,1152]{1,0:T(8,128)(2,1)S(1)} %bitcast.98, bf16[3,3,1152,384]{3,2,1,0:T(8,128)(2,1)S(1)} %bitcast.118), kind=kOutput, calls=%fused_computation.4 | convolution fusion | flops 424857600 | bytes 3465216 | tf_op jit(solution)/shard_map/dot_general | solution.py:314
  63.8 0.8 %convolution_add_fusion = f32[480,384]{1,0:T(8,128)S(1)} fusion(f32[480,384]{1,0:T(8,128)S(1)} %convolution_add_fusion.1, bf16[480,1152]{1,0:T(8,128)(2,1)S(1)} %bitcast.97, bf16[3,3,1152,384]{3,2,1,0:T(8,128)(2,1)S(1)} %bitcast.119), kind=kOutput, calls=%fused_computation.3 | convolution fusion | flops 424857600 | bytes 3465216 | tf_op jit(solution)/shard_map/dot_general | solution.py:314
  64.6 0.8 %collective-permute-done.8 = bf16[160,384]{1,0:T(8,128)(2,1)S(1)} collective-permute-done((bf16[160,384]{1,0:T(8,128)(2,1)S(1)}, bf16[160,384]{1,0:T(8,128)(2,1)S(1)}, u32[]{:S(2)}, u32[]{:S(2)}) %collective-permute-start.8) | collective-permute-done | bytes 122912 | tf_op jit(solution)/shard_map/ppermute | solution.py:329
  65.5 0.9 %fusion.7 = bf16[480,384]{1,0:T(8,128)(2,1)} fusion(f32[3,160,384]{2,1,0:T(8,128)S(1)} %pad_maximum_fusion.3, f32[480,384]{1,0:T(8,128)S(1)} %convolution_add_fusion, f32[480,384]{1,0:T(8,128)S(1)} %convolution_add_fusion.2, f32[480,384]{1,0:T(8,128)S(1)} %convolution_add_fusion.4, bf16[480,384]{1,0:T(8,128)(2,1)S(1)} %get-tuple-element.13), kind=kLoop, calls=%fused_computation.41 | loop fusion | flops 1105920 | bytes 3686400 | tf_op jit(solution)/shard_map/convert_element_type | solution.py:342
  (27 shorter events, 0.9 us)
Async XLA Ops:
  0.0 19.5 %copy-start = (bf16[384,384]{1,0:T(8,128)(2,1)S(1)}, bf16[384,384]{1,0:T(8,128)(2,1)}, u32[]{:S(2)}) copy-start(bf16[384,384]{1,0:T(8,128)(2,1)} %param.12) | copy-start | bytes 884740
  0.0 12.6 %collective-permute-start.3 = (bf16[480,384]{1,0:T(8,128)(2,1)}, bf16[480,384]{1,0:T(8,128)(2,1)S(1)}, u32[]{:S(2)}, u32[]{:S(2)}) collective-permute-start(bf16[480,384]{1,0:T(8,128)(2,1)} %bitcast.90), channel_id=1, source_target_pairs={{4,0},{8,4},{12,8},{5,1},{9,5},{13,9},{6,2},{10,6},{14,10},{7,3},{... | collective-permute-start | bytes 1105928 | tf_op jit(solution)/shard_map/ppermute | solution.py:24
  2.5 12.4 %collective-permute-start = (bf16[480,384]{1,0:T(8,128)(2,1)}, bf16[480,384]{1,0:T(8,128)(2,1)S(1)}, u32[]{:S(2)}, u32[]{:S(2)}) collective-permute-start(bf16[480,384]{1,0:T(8,128)(2,1)} %bitcast.91), channel_id=1, source_target_pairs={{0,4},{4,8},{8,12},{1,5},{5,9},{9,13},{2,6},{6,10},{10,14},{3,7},{... | collective-permute-start | bytes 1105928 | tf_op jit(solution)/shard_map/ppermute | solution.py:23
  7.2 19.9 %copy-start.1 = (bf16[1,3,160,384]{3,2,1,0:T(8,128)(2,1)S(1)}, bf16[1,3,160,384]{3,2,1,0:T(8,128)(2,1)}, u32[]{:S(2)}) copy-start(bf16[1,3,160,384]{3,2,1,0:T(8,128)(2,1)} %param.9) | copy-start | bytes 1105924
  12.6 11.4 %collective-permute-start.4 = (bf16[480,384]{1,0:T(8,128)(2,1)S(1)}, bf16[480,384]{1,0:T(8,128)(2,1)S(1)}, u32[]{:S(2)}, u32[]{:S(2)}) collective-permute-start(bf16[480,384]{1,0:T(8,128)(2,1)S(1)} %collective-permute-done.3.refs_2_), channel_id=1, source_target_pairs={{4,0},{8,4},{5,1},{9,5},{6,2},{10,6},{7,3},{11,7},{20,16},{24,20},... | collective-permute-start | bytes 1105928 | tf_op jit(solution)/shard_map/ppermute | solution.py:24
  14.9 11.4 %collective-permute-start.1 = (bf16[480,384]{1,0:T(8,128)(2,1)S(1)}, bf16[480,384]{1,0:T(8,128)(2,1)S(1)}, u32[]{:S(2)}, u32[]{:S(2)}) collective-permute-start(bf16[480,384]{1,0:T(8,128)(2,1)S(1)} %collective-permute-done.refs_1_), channel_id=1, source_target_pairs={{4,8},{8,12},{5,9},{9,13},{6,10},{10,14},{7,11},{11,15},{20,24},{2... | collective-permute-start | bytes 1105928 | tf_op jit(solution)/shard_map/ppermute | solution.py:23
  23.9 8.5 %collective-permute-start.5 = (bf16[480,384]{1,0:T(8,128)(2,1)S(1)}, bf16[480,384]{1,0:T(8,128)(2,1)S(1)}, u32[]{:S(2)}, u32[]{:S(2)}) collective-permute-start(bf16[480,384]{1,0:T(8,128)(2,1)S(1)} %collective-permute-done.4), channel_id=1, source_target_pairs={{4,0},{5,1},{6,2},{7,3},{20,16},{21,17},{22,18},{23,19}} | collective-permute-start | bytes 1105928 | tf_op jit(solution)/shard_map/ppermute | solution.py:24
  26.3 6.1 %collective-permute-start.2 = (bf16[480,384]{1,0:T(8,128)(2,1)S(1)}, bf16[480,384]{1,0:T(8,128)(2,1)S(1)}, u32[]{:S(2)}, u32[]{:S(2)}) collective-permute-start(bf16[480,384]{1,0:T(8,128)(2,1)S(1)} %collective-permute-done.1), channel_id=1, source_target_pairs={{8,12},{9,13},{10,14},{11,15},{24,28},{25,29},{26,30},{27,31}} | collective-permute-start | bytes 1105928 | tf_op jit(solution)/shard_map/ppermute | solution.py:23
  27.1 5.3 %copy-start.2 = (bf16[384,384]{1,0:T(8,128)(2,1)S(1)}, bf16[384,384]{1,0:T(8,128)(2,1)}, u32[]{:S(2)}) copy-start(bf16[384,384]{1,0:T(8,128)(2,1)} %wo_ref.1) | copy-start | bytes 884740
  32.4 5.2 %slice-start = ((s8[7962624]{0:T(1024)(128)(4,1)}), s8[4194304]{0:T(1024)(128)(4,1)S(1)}, s32[]{:S(2)}) async-start(s8[7962624]{0:T(1024)(128)(4,1)} %bitcast.103), calls=%async_computation | async-start | bytes 8388608
  34.9 8.8 %collective-permute-start.6 = (bf16[3,160,384]{2,1,0:T(8,128)(2,1)S(1)}, bf16[3,160,384]{2,1,0:T(8,128)(2,1)S(1)}, u32[]{:S(2)}, u32[]{:S(2)}) collective-permute-start(bf16[3,160,384]{2,1,0:T(8,128)(2,1)S(1)} %bitcast.95), channel_id=1, source_target_pairs={{0,1},{1,2},{2,3},{4,5},{5,6},{6,7},{8,9},{9,10},{10,11},{12,13},{... | collective-permute-start | bytes 1105928 | tf_op jit(solution)/shard_map/ppermute | solution.py:15
  37.1 2.1 %slice-start.1 = ((s8[7962624]{0:T(1024)(128)(4,1)}), s8[3768320]{0:T(1024)(128)(4,1)S(1)}, s32[]{:S(2)}) async-start(s8[7962624]{0:T(1024)(128)(4,1)} %bitcast.103), calls=%async_computation.1 | async-start | bytes 7536640
  41.5 2.3 %copy-start.3 = (bf16[2,3,160,384]{3,2,1,0:T(8,128)(2,1)S(1)}, bf16[2,3,160,384]{3,2,1,0:T(8,128)(2,1)}, u32[]{:S(2)}) copy-start(bf16[2,3,160,384]{3,2,1,0:T(8,128)(2,1)} %param.10) | copy-start | bytes 2211844
  43.8 8.8 %collective-permute-start.7 = (bf16[3,160,384]{2,1,0:T(8,128)(2,1)S(1)}, bf16[3,160,384]{2,1,0:T(8,128)(2,1)S(1)}, u32[]{:S(2)}, u32[]{:S(2)}) collective-permute-start(bf16[3,160,384]{2,1,0:T(8,128)(2,1)S(1)} %bitcast_select_fusion.1), channel_id=1, source_target_pairs={{0,1},{1,2},{2,3},{4,5},{5,6},{6,7},{8,9},{9,10},{10,11},{12,13},{... | collective-permute-start | bytes 1105928 | tf_op jit(solution)/shard_map/ppermute | solution.py:15
  53.8 10.8 %collective-permute-start.9 = (bf16[160,384]{1,0:T(8,128)(2,1)S(1)}, bf16[160,384]{1,0:T(8,128)(2,1)S(1)}, u32[]{:S(2)}, u32[]{:S(2)}) collective-permute-start(bf16[160,384]{1,0:T(8,128)(2,1)S(1)} %fusion.1), channel_id=1, source_target_pairs={{4,0},{8,4},{12,8},{5,1},{9,5},{13,9},{6,2},{10,6},{14,10},{7,3},{... | collective-permute-start | bytes 368648 | tf_op jit(solution)/shard_map/ppermute | solution.py:326
  58.6 6.8 %collective-permute-start.8 = (bf16[160,384]{1,0:T(8,128)(2,1)S(1)}, bf16[160,384]{1,0:T(8,128)(2,1)S(1)}, u32[]{:S(2)}, u32[]{:S(2)}) collective-permute-start(bf16[160,384]{1,0:T(8,128)(2,1)S(1)} %fusion), channel_id=1, source_target_pairs={{0,4},{4,8},{8,12},{1,5},{5,9},{9,13},{2,6},{6,10},{10,14},{3,7},{... | collective-permute-start | bytes 368648 | tf_op jit(solution)/shard_map/ppermute | solution.py:329

commit v21 on v19

--- a/solution.py
+++ b/solution.py
@@ -299,7 +299,7 @@
     prior = jnp.where(frame_index == 0, cache_frames[1], prior)
     older = passed_along(prior, "tm", 1)
     older = jnp.where(frame_index == 0, cache_frames[0], older)
-    kernel = conv_weight.reshape(3, 3, 3 * width, width)
+    kernel = [conv_weight[t].reshape(3, 3 * width, width) for t in range(3)]
 
     def widen(frame):
         padded = jnp.pad(frame, ((1, 1), (1, 1), (0, 0)))
@@ -311,10 +311,10 @@
         main = None
         for step_r in range(3):
             window = wide[step_r : step_r + rows].reshape(-1, 3 * width)
-            part = jnp.dot(window, kernel[step_t, step_r], preferred_element_type=jnp.float32)
+            part = jnp.dot(window, kernel[step_t][step_r], preferred_element_type=jnp.float32)
             main = part if main is None else main + part
-        first = jnp.dot(wide[1], kernel[step_t, 2], preferred_element_type=jnp.float32)
-        last = jnp.dot(wide[rows], kernel[step_t, 0], preferred_element_type=jnp.float32)
+        first = jnp.dot(wide[1], kernel[step_t][2], preferred_element_type=jnp.float32)
+        last = jnp.dot(wide[rows], kernel[step_t][0], preferred_element_type=jnp.float32)
         return main, first, last
 
     own_main, own_first, own_last = frame_terms(widen(act), 2)

time: 67.6 us -> 70.5 us (1.043)
  the two profiles are of different devices: /device:TPU:10 before, /device:TPU:2 now
where the time goes in v21:
time: 70.5 us; the launch traced here: 70 us
  waiting for transfers between devices  24.4 us (35%)
  starting transfers between devices  15.6 us (22%)
  matrix products  10.5 us (15%)
  local copies, waits for them, and re-layouts  9.11 us (13%)
  Pallas kernels  7.08 us (10%)
  other arithmetic  2.96 us (4%)
    ppermute x3, waiting for transfers between devices, relay(): down = lax.ppermute(down, axis, [(i + 1, i) for i in range(0, n - step)])  13.3 us
    pallas_call x2, Pallas kernels, whole_call(): pl.pallas_call(kernel, out_shape=outputs, grid_spec=pltpu.PrefetchScalarG...  7.08 us
    dot_general x9, matrix products, frame_terms(): jnp.dot(window, kernel[step_t][step_r], preferred_element_type=jnp.float32)  6.88 us
    ppermute x2, waiting for transfers between devices, passed_along(): return lax.ppermute(x, axis, pairs)  6.57 us
    ppermute x3, starting transfers between devices, relay(): up = lax.ppermute(up, axis, [(i, i + 1) for i in range(step - 1, n - 1)])  4.98 us
    ppermute x2, starting transfers between devices, passed_along(): return lax.ppermute(x, axis, pairs)  4.02 us
    slice x1, local copies, waits for them, and re-layouts, frame_terms(): kernel[step_t][step_r]  3.94 us
    ppermute x1, waiting for transfers between devices, shards(): lax.ppermute(to_prev.astype(jnp.bfloat16), 'strip', [(i + 1, i) for i in...  3.89 us
  transfers between devices with their start and end apart: 10, of which 7 were waited for; matrix products, arithmetic and copies ran while one was open for 27% of the time, Pallas kernels for 6%

profile of v21, /device:TPU:2, one launch (start us, length us, event | category | flops | bytes accessed | tf_op | source)
XLA Modules:
  0.0 70.0 jit_solution(15293222979236230801)
XLA Ops:
  0.0 3.6 %collective-permute-start = (bf16[480,384]{1,0:T(8,128)(2,1)}, bf16[480,384]{1,0:T(8,128)(2,1)S(1)}, u32[]{:S(2)}, u32[]{:S(2)}) collective-permute-start(bf16[480,384]{1,0:T(8,128)(2,1)} %bitcast.80), channel_id=1, source_target_pairs={{0,4},{4,8},{8,12},{1,5},{5,9},{9,13},{2,6},{6,10},{10,14},{3,7},{... | collective-permute-start | bytes 1105928 | tf_op jit(solution)/shard_map/ppermute | solution.py:23
  3.6 1.3 %collective-permute-start.3 = (bf16[480,384]{1,0:T(8,128)(2,1)}, bf16[480,384]{1,0:T(8,128)(2,1)S(1)}, u32[]{:S(2)}, u32[]{:S(2)}) collective-permute-start(bf16[480,384]{1,0:T(8,128)(2,1)} %bitcast.81), channel_id=1, source_target_pairs={{4,0},{8,4},{12,8},{5,1},{9,5},{13,9},{6,2},{10,6},{14,10},{7,3},{... | collective-permute-start | bytes 1105928 | tf_op jit(solution)/shard_map/ppermute | solution.py:24
  4.9 1.2 %multiply_reduce_fusion = f32[3,160]{1,0:T(4,128)S(1)} fusion(bf16[1,3,160,384]{3,2,1,0:T(8,128)(2,1)} %param.9), kind=kLoop, calls=%fused_computation.29 | loop fusion | flops 552480 | bytes 370560 | tf_op jit(solution)/shard_map/reduce_sum | solution.py:49
  6.2 1.0 %constant_dynamic-update-slice_fusion.1 = bf16[384,768]{1,0:T(8,128)(2,1)S(1)} fusion(bf16[384,384]{1,0:T(8,128)(2,1)} %param.13), kind=kLoop, calls=%fused_computation.46 | loop fusion | bytes 589824
  7.2 0.7 broadcast_in_dim.4.refs_5_.again_ref
  7.9 0.7 reshape.88.cgain_ref
  8.7 1.0 %constant_dynamic-update-slice_fusion.refs_6_.wkv_ref = bf16[384,768]{1,0:T(8,128)(2,1)S(1)} fusion(bf16[384,768]{1,0:T(8,128)(2,1)S(1)} %constant_dynamic-update-slice_fusion.1, bf16[384,384]{1,0:T(8,128)(2,1)} %param.14), kind=kLoop, calls=%fused_computation.45 | loop fusion | bytes 589824 | tf_op jit(solution)/shard_map/concatenate | solution.py:229
  9.7 1.4 %convolution_convert_fusion.refs_4_.query_ref = bf16[480,384]{1,0:T(8,128)(2,1)S(1)} fusion(bf16[384,384]{1,0:T(8,128)(2,1)S(1)} %copy-done, bf16[480,384]{1,0:T(8,128)(2,1)} %bitcast.82, f32[384]{0:T(512)} %param.11, f32[480]{0:T(512)S(1)} %rsqrt.12), kind=kOutput, calls=%fused_computation.9 | convolution fusion | flops 142479360 | bytes 1035648 | tf_op jit(solution)/shard_map/dot_general | solution.py:282
  11.1 0.6 collective-permute-done.refs_1_
  11.8 0.7 collective-permute-start.1
  12.4 3.4 %collective-permute-done.3.refs_2_ = bf16[480,384]{1,0:T(8,128)(2,1)S(1)} collective-permute-done((bf16[480,384]{1,0:T(8,128)(2,1)}, bf16[480,384]{1,0:T(8,128)(2,1)S(1)}, u32[]{:S(2)}, u32[]{:S(2)}) %collective-permute-start.3) | collective-permute-done | bytes 368672 | tf_op jit(solution)/shard_map/ppermute | solution.py:24
  15.8 1.3 %collective-permute-start.4 = (bf16[480,384]{1,0:T(8,128)(2,1)S(1)}, bf16[480,384]{1,0:T(8,128)(2,1)S(1)}, u32[]{:S(2)}, u32[]{:S(2)}) collective-permute-start(bf16[480,384]{1,0:T(8,128)(2,1)S(1)} %collective-permute-done.3.refs_2_), channel_id=1, source_target_pairs={{4,0},{8,4},{5,1},{9,5},{6,2},{10,6},{7,3},{11,7},{20,16},{24,20},... | collective-permute-start | bytes 1105928 | tf_op jit(solution)/shard_map/ppermute | solution.py:24
  17.1 3.9 %fusion.7 = (bf16[1,1,3,384,384]{4,3,2,1,0:T(8,128)(2,1)S(1)}, bf16[1,1,3,384,384]{4,3,2,1,0:T(8,128)(2,1)S(1)}, bf16[1,1,3,384,384]{4,3,2,1,0:T(8,128)(2,1)S(1)...) fusion(bf16[3,3,3,384,384]{4,3,2,1,0:T(8,128)(2,1)} %param.17), kind=kLoop, calls=%fused_computation.48 | loop fusion | bytes 15925248 | tf_op jit(solution)/shard_map/slice | solution.py:314
  21.0 0.7 collective-permute-start.2
  21.7 5.4 %collective-permute-done.4 = bf16[480,384]{1,0:T(8,128)(2,1)S(1)} collective-permute-done((bf16[480,384]{1,0:T(8,128)(2,1)S(1)}, bf16[480,384]{1,0:T(8,128)(2,1)S(1)}, u32[]{:S(2)}, u32[]{:S(2)}) %collective-permute-start.4) | collective-permute-done | bytes 368672 | tf_op jit(solution)/shard_map/ppermute | solution.py:24
  27.1 1.3 %collective-permute-start.5 = (bf16[480,384]{1,0:T(8,128)(2,1)S(1)}, bf16[480,384]{1,0:T(8,128)(2,1)S(1)}, u32[]{:S(2)}, u32[]{:S(2)}) collective-permute-start(bf16[480,384]{1,0:T(8,128)(2,1)S(1)} %collective-permute-done.4), channel_id=1, source_target_pairs={{4,0},{5,1},{6,2},{7,3},{20,16},{21,17},{22,18},{23,19}} | collective-permute-start | bytes 1105928 | tf_op jit(solution)/shard_map/ppermute | solution.py:24
  28.5 4.5 %shard_map.91 = (f32[480,1]{1,0:T(8,128)S(1)}, f32[480,1]{1,0:T(8,128)S(1)}, f32[480,384]{1,0:T(8,128)S(1)}) custom-call(s32[1]{0:T(128)} %bitcast.me_ref, bf16[480,384]{1,0:T(8,128)(2,1)S(1)} %bitcast.83, bf16[480,384]{1,0:T(8,128)(2,1)S(1)} %collective-permute-done.refs_1_, bf16[480,384]{1,0:T(8,128)(2,1)S(1)} %collective-permute-done.3.refs_2_, ...), custom_call_target="tpu_custom_call" | custom-call | flops 2548039680 | bytes 2434560 | tf_op jit(solution)/shard_map/pallas_call | solution.py:205
  33.1 4.6 %collective-permute-done.5.down_ref = bf16[480,384]{1,0:T(8,128)(2,1)S(1)} collective-permute-done((bf16[480,384]{1,0:T(8,128)(2,1)S(1)}, bf16[480,384]{1,0:T(8,128)(2,1)S(1)}, u32[]{:S(2)}, u32[]{:S(2)}) %collective-permute-start.5) | collective-permute-done | bytes 368672 | tf_op jit(solution)/shard_map/ppermute | solution.py:24
  37.6 2.5 %shard_map.92 = (bf16[480,384]{1,0:T(8,128)(2,1)S(1)}, bf16[480,384]{1,0:T(8,128)(2,1)S(1)}) custom-call(s32[1]{0:T(128)} %bitcast.me_ref, bf16[480,384]{1,0:T(8,128)(2,1)S(1)} %collective-permute-done.2.up_ref, bf16[480,384]{1,0:T(8,128)(2,1)S(1)} %collective-permute-done.5.down_ref, bf16[480,384]{1,0:T(8,128)(2,1)S(1)} %convolution_convert_fusion.refs_4_.query_ref, ...), custom_call_target="tpu_custom_call" | custom-call | flops 778567680 | bytes 3103488 | tf_op jit(solution)/shard_map/pallas_call | solution.py:205
  40.2 0.3 pad_slice_fusion.8
  40.4 1.9 %collective-permute-start.6 = (bf16[3,160,384]{2,1,0:T(8,128)(2,1)S(1)}, bf16[3,160,384]{2,1,0:T(8,128)(2,1)S(1)}, u32[]{:S(2)}, u32[]{:S(2)}) collective-permute-start(bf16[3,160,384]{2,1,0:T(8,128)(2,1)S(1)} %bitcast.86), channel_id=1, source_target_pairs={{0,1},{1,2},{2,3},{4,5},{5,6},{6,7},{8,9},{9,10},{10,11},{12,13},{... | collective-permute-start | bytes 1105928 | tf_op jit(solution)/shard_map/ppermute | solution.py:15
  42.5 0.3 fusion.8
  42.8 0.4 fusion.4
  43.2 0.8 %fusion.11 = f32[480,384]{1,0:T(8,128)S(1)} fusion(bf16[480,1152]{1,0:T(8,128)(2,1)S(1)} %bitcast.108, bf16[1152,384]{1,0:T(8,128)(2,1)S(1)} %bitcast.104), kind=kOutput, calls=%fused_computation.52 | convolution fusion | flops 424673280 | bytes 2727936 | tf_op jit(solution)/shard_map/dot_general | solution.py:314
  44.0 0.8 %convolution_add_fusion.5 = f32[480,384]{1,0:T(8,128)S(1)} fusion(f32[480,384]{1,0:T(8,128)S(1)} %fusion.11, bf16[480,1152]{1,0:T(8,128)(2,1)S(1)} %bitcast.98, bf16[1152,384]{1,0:T(8,128)(2,1)S(1)} %bitcast.107), kind=kOutput, calls=%fused_computation.8 | convolution fusion | flops 424857600 | bytes 3465216 | tf_op jit(solution)/shard_map/dot_general | solution.py:314
  44.7 0.4 fusion.3
  45.1 0.8 %convolution_add_fusion.4 = f32[480,384]{1,0:T(8,128)S(1)} fusion(f32[480,384]{1,0:T(8,128)S(1)} %convolution_add_fusion.5, bf16[480,1152]{1,0:T(8,128)(2,1)S(1)} %bitcast.96, bf16[1152,384]{1,0:T(8,128)(2,1)S(1)} %bitcast.92), kind=kOutput, calls=%fused_computation.7 | convolution fusion | flops 424857600 | bytes 3465216 | tf_op jit(solution)/shard_map/dot_general | solution.py:314
  45.9 3.4 %collective-permute-done.6 = bf16[3,160,384]{2,1,0:T(8,128)(2,1)S(1)} collective-permute-done((bf16[3,160,384]{2,1,0:T(8,128)(2,1)S(1)}, bf16[3,160,384]{2,1,0:T(8,128)(2,1)S(1)}, u32[]{:S(2)}, u32[]{:S(2)}) %collective-permute-start.6) | collective-permute-done | bytes 368672 | tf_op jit(solution)/shard_map/ppermute | solution.py:15
  49.3 0.3 pad_slice_fusion.5
  49.6 2.1 %collective-permute-start.7 = (bf16[3,160,384]{2,1,0:T(8,128)(2,1)S(1)}, bf16[3,160,384]{2,1,0:T(8,128)(2,1)S(1)}, u32[]{:S(2)}, u32[]{:S(2)}) collective-permute-start(bf16[3,160,384]{2,1,0:T(8,128)(2,1)S(1)} %bitcast_select_fusion.1), channel_id=1, source_target_pairs={{0,1},{1,2},{2,3},{4,5},{5,6},{6,7},{8,9},{9,10},{10,11},{12,13},{... | collective-permute-start | bytes 1105928 | tf_op jit(solution)/shard_map/ppermute | solution.py:15
  51.9 0.3 fusion.9
  52.2 0.8 %fusion.12 = f32[480,384]{1,0:T(8,128)S(1)} fusion(bf16[480,1152]{1,0:T(8,128)(2,1)S(1)} %bitcast.109, bf16[1152,384]{1,0:T(8,128)(2,1)S(1)} %bitcast.101), kind=kOutput, calls=%fused_computation.53 | convolution fusion | flops 424673280 | bytes 2727936 | tf_op jit(solution)/shard_map/dot_general | solution.py:314
  52.9 0.4 convolution_add_fusion.9
  53.3 0.8 %convolution_add_fusion.3 = f32[480,384]{1,0:T(8,128)S(1)} fusion(f32[480,384]{1,0:T(8,128)S(1)} %fusion.12, bf16[480,1152]{1,0:T(8,128)(2,1)S(1)} %bitcast.97, bf16[1152,384]{1,0:T(8,128)(2,1)S(1)} %bitcast.106), kind=kOutput, calls=%fused_computation.6 | convolution fusion | flops 424857600 | bytes 3465216 | tf_op jit(solution)/shard_map/dot_general | solution.py:314
  54.1 0.4 convolution_add_fusion.7
  54.4 0.8 %convolution_add_fusion.2 = f32[480,384]{1,0:T(8,128)S(1)} fusion(f32[480,384]{1,0:T(8,128)S(1)} %convolution_add_fusion.3, bf16[480,1152]{1,0:T(8,128)(2,1)S(1)} %bitcast.95, bf16[1152,384]{1,0:T(8,128)(2,1)S(1)} %bitcast.90), kind=kOutput, calls=%fused_computation.5 | convolution fusion | flops 424857600 | bytes 3465216 | tf_op jit(solution)/shard_map/dot_general | solution.py:314
  55.2 3.2 %collective-permute-done.7 = bf16[3,160,384]{2,1,0:T(8,128)(2,1)S(1)} collective-permute-done((bf16[3,160,384]{2,1,0:T(8,128)(2,1)S(1)}, bf16[3,160,384]{2,1,0:T(8,128)(2,1)S(1)}, u32[]{:S(2)}, u32[]{:S(2)}) %collective-permute-start.7) | collective-permute-done | bytes 368672 | tf_op jit(solution)/shard_map/ppermute | solution.py:15
  58.5 0.3 pad_slice_fusion.2
  58.9 0.3 fusion.10
  59.2 0.8 %fusion.13 = f32[480,384]{1,0:T(8,128)S(1)} fusion(bf16[480,1152]{1,0:T(8,128)(2,1)S(1)} %bitcast.110, bf16[1152,384]{1,0:T(8,128)(2,1)S(1)} %bitcast.99), kind=kOutput, calls=%fused_computation.54 | convolution fusion | flops 424673280 | bytes 2727936 | tf_op jit(solution)/shard_map/dot_general | solution.py:314
  59.9 0.4 fusion
  60.3 1.5 %collective-permute-start.8 = (bf16[160,384]{1,0:T(8,128)(2,1)S(1)}, bf16[160,384]{1,0:T(8,128)(2,1)S(1)}, u32[]{:S(2)}, u32[]{:S(2)}) collective-permute-start(bf16[160,384]{1,0:T(8,128)(2,1)S(1)} %fusion), channel_id=1, source_target_pairs={{0,4},{4,8},{8,12},{1,5},{5,9},{9,13},{2,6},{6,10},{10,14},{3,7},{... | collective-permute-start | bytes 368648 | tf_op jit(solution)/shard_map/ppermute | solution.py:329
  61.8 0.4 fusion.1
  62.1 1.3 %collective-permute-start.9 = (bf16[160,384]{1,0:T(8,128)(2,1)S(1)}, bf16[160,384]{1,0:T(8,128)(2,1)S(1)}, u32[]{:S(2)}, u32[]{:S(2)}) collective-permute-start(bf16[160,384]{1,0:T(8,128)(2,1)S(1)} %fusion.1), channel_id=1, source_target_pairs={{4,0},{8,4},{12,8},{5,1},{9,5},{13,9},{6,2},{10,6},{14,10},{7,3},{... | collective-permute-start | bytes 368648 | tf_op jit(solution)/shard_map/ppermute | solution.py:326
  63.4 0.8 %convolution_add_fusion.1 = f32[480,384]{1,0:T(8,128)S(1)} fusion(f32[480,384]{1,0:T(8,128)S(1)} %fusion.13, bf16[480,1152]{1,0:T(8,128)(2,1)S(1)} %bitcast.94, bf16[1152,384]{1,0:T(8,128)(2,1)S(1)} %bitcast.105), kind=kOutput, calls=%fused_computation.4 | convolution fusion | flops 424857600 | bytes 3465216 | tf_op jit(solution)/shard_map/dot_general | solution.py:314
  64.2 0.8 %convolution_add_fusion = f32[480,384]{1,0:T(8,128)S(1)} fusion(f32[480,384]{1,0:T(8,128)S(1)} %convolution_add_fusion.1, bf16[480,1152]{1,0:T(8,128)(2,1)S(1)} %bitcast.93, bf16[1152,384]{1,0:T(8,128)(2,1)S(1)} %bitcast.88), kind=kOutput, calls=%fused_computation.3 | convolution fusion | flops 424857600 | bytes 3465216 | tf_op jit(solution)/shard_map/dot_general | solution.py:314
  65.0 3.9 %collective-permute-done.9 = bf16[160,384]{1,0:T(8,128)(2,1)S(1)} collective-permute-done((bf16[160,384]{1,0:T(8,128)(2,1)S(1)}, bf16[160,384]{1,0:T(8,128)(2,1)S(1)}, u32[]{:S(2)}, u32[]{:S(2)}) %collective-permute-start.9) | collective-permute-done | bytes 122912 | tf_op jit(solution)/shard_map/ppermute | solution.py:326
  69.1 1.0 %fusion.2 = bf16[480,384]{1,0:T(8,128)(2,1)} fusion(f32[3,160,384]{2,1,0:T(8,128)S(1)} %pad_maximum_fusion.3, f32[480,384]{1,0:T(8,128)S(1)} %convolution_add_fusion, f32[480,384]{1,0:T(8,128)S(1)} %convolution_add_fusion.2, f32[480,384]{1,0:T(8,128)S(1)} %convolution_add_fusion.4, bf16[480,384]{1,0:T(8,128)(2,1)S(1)} %get-tuple-element.13), kind=kLoop, calls=%fused_computation.27 | loop fusion | flops 1105920 | bytes 3686400 | tf_op jit(solution)/shard_map/convert_element_type | solution.py:342
  (23 shorter events, 1.0 us)
Async XLA Ops:
  0.0 9.7 %copy-start = (bf16[384,384]{1,0:T(8,128)(2,1)S(1)}, bf16[384,384]{1,0:T(8,128)(2,1)}, u32[]{:S(2)}) copy-start(bf16[384,384]{1,0:T(8,128)(2,1)} %param.12) | copy-start | bytes 884740
  0.0 11.8 %collective-permute-start = (bf16[480,384]{1,0:T(8,128)(2,1)}, bf16[480,384]{1,0:T(8,128)(2,1)S(1)}, u32[]{:S(2)}, u32[]{:S(2)}) collective-permute-start(bf16[480,384]{1,0:T(8,128)(2,1)} %bitcast.80), channel_id=1, source_target_pairs={{0,4},{4,8},{8,12},{1,5},{5,9},{9,13},{2,6},{6,10},{10,14},{3,7},{... | collective-permute-start | bytes 1105928 | tf_op jit(solution)/shard_map/ppermute | solution.py:23
  3.6 12.2 %collective-permute-start.3 = (bf16[480,384]{1,0:T(8,128)(2,1)}, bf16[480,384]{1,0:T(8,128)(2,1)S(1)}, u32[]{:S(2)}, u32[]{:S(2)}) collective-permute-start(bf16[480,384]{1,0:T(8,128)(2,1)} %bitcast.81), channel_id=1, source_target_pairs={{4,0},{8,4},{12,8},{5,1},{9,5},{13,9},{6,2},{10,6},{14,10},{7,3},{... | collective-permute-start | bytes 1105928 | tf_op jit(solution)/shard_map/ppermute | solution.py:24
  11.1 17.4 %copy-start.1 = (bf16[1,3,160,384]{3,2,1,0:T(8,128)(2,1)S(1)}, bf16[1,3,160,384]{3,2,1,0:T(8,128)(2,1)}, u32[]{:S(2)}) copy-start(bf16[1,3,160,384]{3,2,1,0:T(8,128)(2,1)} %param.9) | copy-start | bytes 1105924
  11.8 9.3 %collective-permute-start.1 = (bf16[480,384]{1,0:T(8,128)(2,1)S(1)}, bf16[480,384]{1,0:T(8,128)(2,1)S(1)}, u32[]{:S(2)}, u32[]{:S(2)}) collective-permute-start(bf16[480,384]{1,0:T(8,128)(2,1)S(1)} %collective-permute-done.refs_1_), channel_id=1, source_target_pairs={{4,8},{8,12},{5,9},{9,13},{6,10},{10,14},{7,11},{11,15},{20,24},{2... | collective-permute-start | bytes 1105928 | tf_op jit(solution)/shard_map/ppermute | solution.py:23
  15.8 11.3 %collective-permute-start.4 = (bf16[480,384]{1,0:T(8,128)(2,1)S(1)}, bf16[480,384]{1,0:T(8,128)(2,1)S(1)}, u32[]{:S(2)}, u32[]{:S(2)}) collective-permute-start(bf16[480,384]{1,0:T(8,128)(2,1)S(1)} %collective-permute-done.3.refs_2_), channel_id=1, source_target_pairs={{4,0},{8,4},{5,1},{9,5},{6,2},{10,6},{7,3},{11,7},{20,16},{24,20},... | collective-permute-start | bytes 1105928 | tf_op jit(solution)/shard_map/ppermute | solution.py:24
  21.0 12.0 %collective-permute-start.2 = (bf16[480,384]{1,0:T(8,128)(2,1)S(1)}, bf16[480,384]{1,0:T(8,128)(2,1)S(1)}, u32[]{:S(2)}, u32[]{:S(2)}) collective-permute-start(bf16[480,384]{1,0:T(8,128)(2,1)S(1)} %collective-permute-done.1), channel_id=1, source_target_pairs={{8,12},{9,13},{10,14},{11,15},{24,28},{25,29},{26,30},{27,31}} | collective-permute-start | bytes 1105928 | tf_op jit(solution)/shard_map/ppermute | solution.py:23
  27.1 10.5 %collective-permute-start.5 = (bf16[480,384]{1,0:T(8,128)(2,1)S(1)}, bf16[480,384]{1,0:T(8,128)(2,1)S(1)}, u32[]{:S(2)}, u32[]{:S(2)}) collective-permute-start(bf16[480,384]{1,0:T(8,128)(2,1)S(1)} %collective-permute-done.4), channel_id=1, source_target_pairs={{4,0},{5,1},{6,2},{7,3},{20,16},{21,17},{22,18},{23,19}} | collective-permute-start | bytes 1105928 | tf_op jit(solution)/shard_map/ppermute | solution.py:24
  28.5 9.1 %copy-start.2 = (bf16[384,384]{1,0:T(8,128)(2,1)S(1)}, bf16[384,384]{1,0:T(8,128)(2,1)}, u32[]{:S(2)}) copy-start(bf16[384,384]{1,0:T(8,128)(2,1)} %wo_ref.1) | copy-start | bytes 884740
  40.4 8.8 %collective-permute-start.6 = (bf16[3,160,384]{2,1,0:T(8,128)(2,1)S(1)}, bf16[3,160,384]{2,1,0:T(8,128)(2,1)S(1)}, u32[]{:S(2)}, u32[]{:S(2)}) collective-permute-start(bf16[3,160,384]{2,1,0:T(8,128)(2,1)S(1)} %bitcast.86), channel_id=1, source_target_pairs={{0,1},{1,2},{2,3},{4,5},{5,6},{6,7},{8,9},{9,10},{10,11},{12,13},{... | collective-permute-start | bytes 1105928 | tf_op jit(solution)/shard_map/ppermute | solution.py:15
  45.1 4.2 %copy-start.3 = (bf16[2,3,160,384]{3,2,1,0:T(8,128)(2,1)S(1)}, bf16[2,3,160,384]{3,2,1,0:T(8,128)(2,1)}, u32[]{:S(2)}) copy-start(bf16[2,3,160,384]{3,2,1,0:T(8,128)(2,1)} %param.10) | copy-start | bytes 2211844
  49.6 8.8 %collective-permute-start.7 = (bf16[3,160,384]{2,1,0:T(8,128)(2,1)S(1)}, bf16[3,160,384]{2,1,0:T(8,128)(2,1)S(1)}, u32[]{:S(2)}, u32[]{:S(2)}) collective-permute-start(bf16[3,160,384]{2,1,0:T(8,128)(2,1)S(1)} %bitcast_select_fusion.1), channel_id=1, source_target_pairs={{0,1},{1,2},{2,3},{4,5},{5,6},{6,7},{8,9},{9,10},{10,11},{12,13},{... | collective-permute-start | bytes 1105928 | tf_op jit(solution)/shard_map/ppermute | solution.py:15
  60.3 4.7 %collective-permute-start.8 = (bf16[160,384]{1,0:T(8,128)(2,1)S(1)}, bf16[160,384]{1,0:T(8,128)(2,1)S(1)}, u32[]{:S(2)}, u32[]{:S(2)}) collective-permute-start(bf16[160,384]{1,0:T(8,128)(2,1)S(1)} %fusion), channel_id=1, source_target_pairs={{0,4},{4,8},{8,12},{1,5},{5,9},{9,13},{2,6},{6,10},{10,14},{3,7},{... | collective-permute-start | bytes 368648 | tf_op jit(solution)/shard_map/ppermute | solution.py:329
  62.1 6.8 %collective-permute-start.9 = (bf16[160,384]{1,0:T(8,128)(2,1)S(1)}, bf16[160,384]{1,0:T(8,128)(2,1)S(1)}, u32[]{:S(2)}, u32[]{:S(2)}) collective-permute-start(bf16[160,384]{1,0:T(8,128)(2,1)S(1)} %fusion.1), channel_id=1, source_target_pairs={{4,0},{8,4},{12,8},{5,1},{9,5},{13,9},{6,2},{10,6},{14,10},{7,3},{... | collective-permute-start | bytes 368648 | tf_op jit(solution)/shard_map/ppermute | solution.py:326

commit v22 on v19

--- a/solution.py
+++ b/solution.py
@@ -330,15 +330,9 @@
         to_next.astype(jnp.bfloat16), "strip", [(i, i + 1) for i in range(n - 1)]
     )
     result = resid.astype(jnp.float32) + own_main + prior_main + older_main
-    edges = jnp.concatenate(
-        [
-            from_prev[None].astype(jnp.float32),
-            jnp.zeros((rows - 2, cols, width), jnp.float32),
-            from_next[None].astype(jnp.float32),
-        ],
-        axis=0,
-    )
-    result = result + edges.reshape(-1, width)
+    result = result.reshape(rows, cols, width)
+    result = result.at[0].add(from_prev.astype(jnp.float32))
+    result = result.at[rows - 1].add(from_next.astype(jnp.float32))
     return result.astype(jnp.bfloat16).reshape(1, rows, cols, width)
 
 

time: 67.6 us -> 67.4 us (level)
    convert_element_type x3 -> x0, other arithmetic: 0.96 us -> none  [the longest x1 0.93 us: shards(): return result.astype(jnp.bfloat16).reshape(1, rows, cols, width)]
    reshape x0 -> x1, other arithmetic: none -> 0.78 us  [shards(): return result.astype(jnp.bfloat16).reshape(1, rows, cols, width)]
    unnamed x13 -> x14, local copies, waits for them, and re-layouts: 2.77 us -> 2.82 us
where the time goes in v22:
time: 67.4 us; the launch traced here: 66.2 us
  starting transfers between devices  27 us (40%)
  waiting for transfers between devices  11.5 us (17%)
  matrix products  10.5 us (16%)
  Pallas kernels  7.11 us (11%)
  local copies, waits for them, and re-layouts  6.91 us (10%)
  other arithmetic  2.85 us (4%)
    ppermute x3, starting transfers between devices, relay(): up = lax.ppermute(up, axis, [(i, i + 1) for i in range(step - 1, n - 1)])  7.69 us
    ppermute x3, starting transfers between devices, relay(): down = lax.ppermute(down, axis, [(i + 1, i) for i in range(0, n - step)])  7.19 us
    pallas_call x2, Pallas kernels, whole_call(): pl.pallas_call(kernel, out_shape=outputs, grid_spec=pltpu.PrefetchScalarG...  7.11 us
    dot_general x9, matrix products, frame_terms(): jnp.dot(window, kernel[step_t, step_r], preferred_element_type=jnp.float32)  6.88 us
    ppermute x3, waiting for transfers between devices, relay(): down = lax.ppermute(down, axis, [(i + 1, i) for i in range(0, n - step)])  6.59 us
    ppermute x1, starting transfers between devices, shards(): lax.ppermute(to_prev.astype(jnp.bfloat16), 'strip', [(i + 1, i) for i in...  4.39 us
    ppermute x2, waiting for transfers between devices, passed_along(): return lax.ppermute(x, axis, pairs)  4.33 us
    ppermute x2, starting transfers between devices, passed_along(): return lax.ppermute(x, axis, pairs)  4.02 us
  transfers between devices with their start and end apart: 10, of which 6 were waited for; matrix products, arithmetic and copies ran while one was open for 25% of the time, Pallas kernels for 7%

profile of v22, /device:TPU:10, one launch (start us, length us, event | category | flops | bytes accessed | tf_op | source)
XLA Modules:
  0.0 66.2 jit_solution(13242428786848627976)
XLA Ops:
  0.0 2.5 %collective-permute-start.3 = (bf16[480,384]{1,0:T(8,128)(2,1)}, bf16[480,384]{1,0:T(8,128)(2,1)S(1)}, u32[]{:S(2)}, u32[]{:S(2)}) collective-permute-start(bf16[480,384]{1,0:T(8,128)(2,1)} %bitcast.88), channel_id=1, source_target_pairs={{4,0},{8,4},{12,8},{5,1},{9,5},{13,9},{6,2},{10,6},{14,10},{7,3},{... | collective-permute-start | bytes 1105928 | tf_op jit(solution)/shard_map/ppermute | solution.py:24
  2.5 3.5 %collective-permute-start = (bf16[480,384]{1,0:T(8,128)(2,1)}, bf16[480,384]{1,0:T(8,128)(2,1)S(1)}, u32[]{:S(2)}, u32[]{:S(2)}) collective-permute-start(bf16[480,384]{1,0:T(8,128)(2,1)} %bitcast.89), channel_id=1, source_target_pairs={{0,4},{4,8},{8,12},{1,5},{5,9},{9,13},{2,6},{6,10},{10,14},{3,7},{... | collective-permute-start | bytes 1105928 | tf_op jit(solution)/shard_map/ppermute | solution.py:23
  6.0 1.2 %multiply_reduce_fusion = f32[3,160]{1,0:T(4,128)S(1)} fusion(bf16[1,3,160,384]{3,2,1,0:T(8,128)(2,1)} %param.13), kind=kLoop, calls=%fused_computation.41 | loop fusion | flops 552480 | bytes 370560 | tf_op jit(solution)/shard_map/reduce_sum | solution.py:49
  7.2 0.7 %broadcast_in_dim.4.refs_5_.again_ref = f32[1,384]{1,0:T(1,128)S(1)} reshape(f32[384]{0:T(512)} %param.15) | data formatting | bytes 3072 | tf_op jit(solution)/shard_map/broadcast_in_dim | solution.py:49
  7.9 0.7 %reshape.132.cgain_ref = f32[1,384]{1,0:T(1,128)S(1)} reshape(f32[384]{0:T(512)} %param.20) | data formatting | bytes 3072 | tf_op jit(solution)/shard_map/reshape | solution.py:250
  8.7 1.0 %constant_dynamic-update-slice_fusion.1 = bf16[384,768]{1,0:T(8,128)(2,1)S(1)} fusion(bf16[384,384]{1,0:T(8,128)(2,1)} %param.17), kind=kLoop, calls=%fused_computation.60 | loop fusion | bytes 589824
  9.7 2.9 %collective-permute-done.3.refs_2_ = bf16[480,384]{1,0:T(8,128)(2,1)S(1)} collective-permute-done((bf16[480,384]{1,0:T(8,128)(2,1)}, bf16[480,384]{1,0:T(8,128)(2,1)S(1)}, u32[]{:S(2)}, u32[]{:S(2)}) %collective-permute-start.3) | collective-permute-done | bytes 368672 | tf_op jit(solution)/shard_map/ppermute | solution.py:24
  12.6 2.3 %collective-permute-start.4 = (bf16[480,384]{1,0:T(8,128)(2,1)S(1)}, bf16[480,384]{1,0:T(8,128)(2,1)S(1)}, u32[]{:S(2)}, u32[]{:S(2)}) collective-permute-start(bf16[480,384]{1,0:T(8,128)(2,1)S(1)} %collective-permute-done.3.refs_2_), channel_id=1, source_target_pairs={{4,0},{8,4},{5,1},{9,5},{6,2},{10,6},{7,3},{11,7},{20,16},{24,20},... | collective-permute-start | bytes 1105928 | tf_op jit(solution)/shard_map/ppermute | solution.py:24
  14.9 3.5 %collective-permute-start.1 = (bf16[480,384]{1,0:T(8,128)(2,1)S(1)}, bf16[480,384]{1,0:T(8,128)(2,1)S(1)}, u32[]{:S(2)}, u32[]{:S(2)}) collective-permute-start(bf16[480,384]{1,0:T(8,128)(2,1)S(1)} %collective-permute-done.refs_1_), channel_id=1, source_target_pairs={{4,8},{8,12},{5,9},{9,13},{6,10},{10,14},{7,11},{11,15},{20,24},{2... | collective-permute-start | bytes 1105928 | tf_op jit(solution)/shard_map/ppermute | solution.py:23
  18.5 1.0 %constant_dynamic-update-slice_fusion.refs_6_.wkv_ref = bf16[384,768]{1,0:T(8,128)(2,1)S(1)} fusion(bf16[384,768]{1,0:T(8,128)(2,1)S(1)} %constant_dynamic-update-slice_fusion.1, bf16[384,384]{1,0:T(8,128)(2,1)} %param.18), kind=kLoop, calls=%fused_computation.59 | loop fusion | bytes 589824 | tf_op jit(solution)/shard_map/concatenate | solution.py:229
  19.5 1.4 %convolution_convert_fusion.refs_4_.query_ref = bf16[480,384]{1,0:T(8,128)(2,1)S(1)} fusion(bf16[384,384]{1,0:T(8,128)(2,1)S(1)} %copy-done, bf16[480,384]{1,0:T(8,128)(2,1)} %bitcast.90, f32[384]{0:T(512)} %param.15, f32[480]{0:T(512)S(1)} %rsqrt.12), kind=kOutput, calls=%fused_computation.9 | convolution fusion | flops 142479360 | bytes 1035648 | tf_op jit(solution)/shard_map/dot_general | solution.py:282
  20.9 3.0 %collective-permute-done.4 = bf16[480,384]{1,0:T(8,128)(2,1)S(1)} collective-permute-done((bf16[480,384]{1,0:T(8,128)(2,1)S(1)}, bf16[480,384]{1,0:T(8,128)(2,1)S(1)}, u32[]{:S(2)}, u32[]{:S(2)}) %collective-permute-start.4) | collective-permute-done | bytes 368672 | tf_op jit(solution)/shard_map/ppermute | solution.py:24
  23.9 2.4 %collective-permute-start.5 = (bf16[480,384]{1,0:T(8,128)(2,1)S(1)}, bf16[480,384]{1,0:T(8,128)(2,1)S(1)}, u32[]{:S(2)}, u32[]{:S(2)}) collective-permute-start(bf16[480,384]{1,0:T(8,128)(2,1)S(1)} %collective-permute-done.4), channel_id=1, source_target_pairs={{4,0},{5,1},{6,2},{7,3},{20,16},{21,17},{22,18},{23,19}} | collective-permute-start | bytes 1105928 | tf_op jit(solution)/shard_map/ppermute | solution.py:24
  26.3 0.7 %collective-permute-start.2 = (bf16[480,384]{1,0:T(8,128)(2,1)S(1)}, bf16[480,384]{1,0:T(8,128)(2,1)S(1)}, u32[]{:S(2)}, u32[]{:S(2)}) collective-permute-start(bf16[480,384]{1,0:T(8,128)(2,1)S(1)} %collective-permute-done.1), channel_id=1, source_target_pairs={{8,12},{9,13},{10,14},{11,15},{24,28},{25,29},{26,30},{27,31}} | collective-permute-start | bytes 1105928 | tf_op jit(solution)/shard_map/ppermute | solution.py:23
  27.1 4.6 %shard_map.91 = (f32[480,1]{1,0:T(8,128)S(1)}, f32[480,1]{1,0:T(8,128)S(1)}, f32[480,384]{1,0:T(8,128)S(1)}) custom-call(s32[1]{0:T(128)} %bitcast.me_ref, bf16[480,384]{1,0:T(8,128)(2,1)S(1)} %bitcast.91, bf16[480,384]{1,0:T(8,128)(2,1)S(1)} %collective-permute-done.refs_1_, bf16[480,384]{1,0:T(8,128)(2,1)S(1)} %collective-permute-done.3.refs_2_, ...), custom_call_target="tpu_custom_call" | custom-call | flops 2548039680 | bytes 2434560 | tf_op jit(solution)/shard_map/pallas_call | solution.py:205
  31.6 0.7 %collective-permute-done.5.down_ref = bf16[480,384]{1,0:T(8,128)(2,1)S(1)} collective-permute-done((bf16[480,384]{1,0:T(8,128)(2,1)S(1)}, bf16[480,384]{1,0:T(8,128)(2,1)S(1)}, u32[]{:S(2)}, u32[]{:S(2)}) %collective-permute-start.5) | collective-permute-done | bytes 368672 | tf_op jit(solution)/shard_map/ppermute | solution.py:24
  32.4 2.5 %shard_map.92 = (bf16[480,384]{1,0:T(8,128)(2,1)S(1)}, bf16[480,384]{1,0:T(8,128)(2,1)S(1)}) custom-call(s32[1]{0:T(128)} %bitcast.me_ref, bf16[480,384]{1,0:T(8,128)(2,1)S(1)} %collective-permute-done.2.up_ref, bf16[480,384]{1,0:T(8,128)(2,1)S(1)} %collective-permute-done.5.down_ref, bf16[480,384]{1,0:T(8,128)(2,1)S(1)} %convolution_convert_fusion.refs_4_.query_ref, ...), custom_call_target="tpu_custom_call" | custom-call | flops 778567680 | bytes 3103488 | tf_op jit(solution)/shard_map/pallas_call | solution.py:205
  34.9 1.9 %collective-permute-start.6 = (bf16[3,160,384]{2,1,0:T(8,128)(2,1)S(1)}, bf16[3,160,384]{2,1,0:T(8,128)(2,1)S(1)}, u32[]{:S(2)}, u32[]{:S(2)}) collective-permute-start(bf16[3,160,384]{2,1,0:T(8,128)(2,1)S(1)} %bitcast.93), channel_id=1, source_target_pairs={{0,1},{1,2},{2,3},{4,5},{5,6},{6,7},{8,9},{9,10},{10,11},{12,13},{... | collective-permute-start | bytes 1105928 | tf_op jit(solution)/shard_map/ppermute | solution.py:15
  36.9 0.3 pad_slice_fusion.8
  37.3 0.3 fusion.12
  37.6 1.7 %slice-done.1 = s8[4194304]{0:T(1024)(128)(4,1)S(1)} async-done(((s8[7962624]{0:T(1024)(128)(4,1)}), s8[4194304]{0:T(1024)(128)(4,1)S(1)}, s32[]{:S(2)}) %slice-start.1) | async-done | bytes 4194328
  39.3 0.4 fusion.4
  39.7 0.8 %fusion.3 = f32[480,384]{1,0:T(8,128)S(1)} fusion(bf16[480,1152]{1,0:T(8,128)(2,1)S(1)} %bitcast.121, bf16[3,3,1152,384]{3,2,1,0:T(8,128)(2,1)S(1)} %bitcast.105), kind=kOutput, calls=%fused_computation.26 | convolution fusion | flops 424673280 | bytes 2727936 | tf_op jit(solution)/shard_map/dot_general | solution.py:314
  40.5 0.8 %convolution_add_fusion.5 = f32[480,384]{1,0:T(8,128)S(1)} fusion(f32[480,384]{1,0:T(8,128)S(1)} %fusion.3, bf16[480,1152]{1,0:T(8,128)(2,1)S(1)} %bitcast.100, bf16[3,3,1152,384]{3,2,1,0:T(8,128)(2,1)S(1)} %bitcast.106), kind=kOutput, calls=%fused_computation.8 | convolution fusion | flops 424857600 | bytes 3465216 | tf_op jit(solution)/shard_map/dot_general | solution.py:314
  41.2 0.4 fusion.2
  41.6 0.8 %convolution_add_fusion.4 = f32[480,384]{1,0:T(8,128)S(1)} fusion(f32[480,384]{1,0:T(8,128)S(1)} %convolution_add_fusion.5, bf16[480,1152]{1,0:T(8,128)(2,1)S(1)} %bitcast.98, bf16[3,3,1152,384]{3,2,1,0:T(8,128)(2,1)S(1)} %bitcast.108), kind=kOutput, calls=%fused_computation.7 | convolution fusion | flops 424857600 | bytes 3465216 | tf_op jit(solution)/shard_map/dot_general | solution.py:314
  42.4 1.4 %collective-permute-done.6 = bf16[3,160,384]{2,1,0:T(8,128)(2,1)S(1)} collective-permute-done((bf16[3,160,384]{2,1,0:T(8,128)(2,1)S(1)}, bf16[3,160,384]{2,1,0:T(8,128)(2,1)S(1)}, u32[]{:S(2)}, u32[]{:S(2)}) %collective-permute-start.6) | collective-permute-done | bytes 368672 | tf_op jit(solution)/shard_map/ppermute | solution.py:15
  43.8 2.1 %collective-permute-start.7 = (bf16[3,160,384]{2,1,0:T(8,128)(2,1)S(1)}, bf16[3,160,384]{2,1,0:T(8,128)(2,1)S(1)}, u32[]{:S(2)}, u32[]{:S(2)}) collective-permute-start(bf16[3,160,384]{2,1,0:T(8,128)(2,1)S(1)} %bitcast_select_fusion.1), channel_id=1, source_target_pairs={{0,1},{1,2},{2,3},{4,5},{5,6},{6,7},{8,9},{9,10},{10,11},{12,13},{... | collective-permute-start | bytes 1105928 | tf_op jit(solution)/shard_map/ppermute | solution.py:15
  45.9 0.3 pad_slice_fusion.5
  46.2 0.2 pad_maximum_fusion.1
  46.4 0.3 fusion.13
  46.7 0.4 convolution_add_fusion.7
  47.0 0.8 %fusion.5 = f32[480,384]{1,0:T(8,128)S(1)} fusion(bf16[480,1152]{1,0:T(8,128)(2,1)S(1)} %bitcast.120, bf16[3,3,1152,384]{3,2,1,0:T(8,128)(2,1)S(1)} %bitcast.110), kind=kOutput, calls=%fused_computation.28 | convolution fusion | flops 424673280 | bytes 2727936 | tf_op jit(solution)/shard_map/dot_general | solution.py:314
  47.8 0.8 %convolution_add_fusion.3 = f32[480,384]{1,0:T(8,128)S(1)} fusion(f32[480,384]{1,0:T(8,128)S(1)} %fusion.5, bf16[480,1152]{1,0:T(8,128)(2,1)S(1)} %bitcast.99, bf16[3,3,1152,384]{3,2,1,0:T(8,128)(2,1)S(1)} %bitcast.111), kind=kOutput, calls=%fused_computation.6 | convolution fusion | flops 424857600 | bytes 3465216 | tf_op jit(solution)/shard_map/dot_general | solution.py:314
  48.6 0.4 convolution_add_fusion.9
  48.9 0.8 %convolution_add_fusion.2 = f32[480,384]{1,0:T(8,128)S(1)} fusion(f32[480,384]{1,0:T(8,128)S(1)} %convolution_add_fusion.3, bf16[480,1152]{1,0:T(8,128)(2,1)S(1)} %bitcast.97, bf16[3,3,1152,384]{3,2,1,0:T(8,128)(2,1)S(1)} %bitcast.113), kind=kOutput, calls=%fused_computation.5 | convolution fusion | flops 424857600 | bytes 3465216 | tf_op jit(solution)/shard_map/dot_general | solution.py:314
  49.7 2.9 %collective-permute-done.7 = bf16[3,160,384]{2,1,0:T(8,128)(2,1)S(1)} collective-permute-done((bf16[3,160,384]{2,1,0:T(8,128)(2,1)S(1)}, bf16[3,160,384]{2,1,0:T(8,128)(2,1)S(1)}, u32[]{:S(2)}, u32[]{:S(2)}) %collective-permute-start.7) | collective-permute-done | bytes 368672 | tf_op jit(solution)/shard_map/ppermute | solution.py:15
  52.7 0.3 pad_slice_fusion.2
  53.1 0.3 fusion.14
  53.4 0.4 fusion.1
  53.8 4.4 %collective-permute-start.9 = (bf16[160,384]{1,0:T(8,128)(2,1)S(1)}, bf16[160,384]{1,0:T(8,128)(2,1)S(1)}, u32[]{:S(2)}, u32[]{:S(2)}) collective-permute-start(bf16[160,384]{1,0:T(8,128)(2,1)S(1)} %fusion.1), channel_id=1, source_target_pairs={{4,0},{8,4},{12,8},{5,1},{9,5},{13,9},{6,2},{10,6},{14,10},{7,3},{... | collective-permute-start | bytes 368648 | tf_op jit(solution)/shard_map/ppermute | solution.py:326
  58.2 0.4 fusion
  58.6 3.7 %collective-permute-start.8 = (bf16[160,384]{1,0:T(8,128)(2,1)S(1)}, bf16[160,384]{1,0:T(8,128)(2,1)S(1)}, u32[]{:S(2)}, u32[]{:S(2)}) collective-permute-start(bf16[160,384]{1,0:T(8,128)(2,1)S(1)} %fusion), channel_id=1, source_target_pairs={{0,4},{4,8},{8,12},{1,5},{5,9},{9,13},{2,6},{6,10},{10,14},{3,7},{... | collective-permute-start | bytes 368648 | tf_op jit(solution)/shard_map/ppermute | solution.py:329
  62.3 0.8 %fusion.6 = f32[480,384]{1,0:T(8,128)S(1)} fusion(bf16[480,1152]{1,0:T(8,128)(2,1)S(1)} %bitcast.119, bf16[3,3,1152,384]{3,2,1,0:T(8,128)(2,1)S(1)} %bitcast.116), kind=kOutput, calls=%fused_computation.29 | convolution fusion | flops 424673280 | bytes 2727936 | tf_op jit(solution)/shard_map/dot_general | solution.py:314
  63.0 0.8 %convolution_add_fusion.1 = f32[480,384]{1,0:T(8,128)S(1)} fusion(f32[480,384]{1,0:T(8,128)S(1)} %fusion.6, bf16[480,1152]{1,0:T(8,128)(2,1)S(1)} %bitcast.96, bf16[3,3,1152,384]{3,2,1,0:T(8,128)(2,1)S(1)} %bitcast.117), kind=kOutput, calls=%fused_computation.4 | convolution fusion | flops 424857600 | bytes 3465216 | tf_op jit(solution)/shard_map/dot_general | solution.py:314
  63.8 0.8 %convolution_add_fusion = f32[480,384]{1,0:T(8,128)S(1)} fusion(f32[480,384]{1,0:T(8,128)S(1)} %convolution_add_fusion.1, bf16[480,1152]{1,0:T(8,128)(2,1)S(1)} %bitcast.95, bf16[3,3,1152,384]{3,2,1,0:T(8,128)(2,1)S(1)} %bitcast.118), kind=kOutput, calls=%fused_computation.3 | convolution fusion | flops 424857600 | bytes 3465216 | tf_op jit(solution)/shard_map/dot_general | solution.py:314
  64.8 0.6 collective-permute-done.8
  65.4 0.8 %convert_bitcast_fusion = bf16[1,3,160,384]{3,2,1,0:T(8,128)(2,1)} fusion(f32[3,160,384]{2,1,0:T(8,128)S(1)} %fusion.9), kind=kLoop, calls=%fused_computation.50 | loop fusion | flops 184320 | bytes 1105920 | tf_op jit(solution)/shard_map/reshape | solution.py:336
  (27 shorter events, 0.9 us)
Async XLA Ops:
  0.0 19.5 %copy-start = (bf16[384,384]{1,0:T(8,128)(2,1)S(1)}, bf16[384,384]{1,0:T(8,128)(2,1)}, u32[]{:S(2)}) copy-start(bf16[384,384]{1,0:T(8,128)(2,1)} %param.16) | copy-start | bytes 884740
  0.0 12.6 %collective-permute-start.3 = (bf16[480,384]{1,0:T(8,128)(2,1)}, bf16[480,384]{1,0:T(8,128)(2,1)S(1)}, u32[]{:S(2)}, u32[]{:S(2)}) collective-permute-start(bf16[480,384]{1,0:T(8,128)(2,1)} %bitcast.88), channel_id=1, source_target_pairs={{4,0},{8,4},{12,8},{5,1},{9,5},{13,9},{6,2},{10,6},{14,10},{7,3},{... | collective-permute-start | bytes 1105928 | tf_op jit(solution)/shard_map/ppermute | solution.py:24
  2.5 12.4 %collective-permute-start = (bf16[480,384]{1,0:T(8,128)(2,1)}, bf16[480,384]{1,0:T(8,128)(2,1)S(1)}, u32[]{:S(2)}, u32[]{:S(2)}) collective-permute-start(bf16[480,384]{1,0:T(8,128)(2,1)} %bitcast.89), channel_id=1, source_target_pairs={{0,4},{4,8},{8,12},{1,5},{5,9},{9,13},{2,6},{6,10},{10,14},{3,7},{... | collective-permute-start | bytes 1105928 | tf_op jit(solution)/shard_map/ppermute | solution.py:23
  7.2 19.9 %copy-start.1 = (bf16[1,3,160,384]{3,2,1,0:T(8,128)(2,1)S(1)}, bf16[1,3,160,384]{3,2,1,0:T(8,128)(2,1)}, u32[]{:S(2)}) copy-start(bf16[1,3,160,384]{3,2,1,0:T(8,128)(2,1)} %param.13) | copy-start | bytes 1105924
  12.6 11.4 %collective-permute-start.4 = (bf16[480,384]{1,0:T(8,128)(2,1)S(1)}, bf16[480,384]{1,0:T(8,128)(2,1)S(1)}, u32[]{:S(2)}, u32[]{:S(2)}) collective-permute-start(bf16[480,384]{1,0:T(8,128)(2,1)S(1)} %collective-permute-done.3.refs_2_), channel_id=1, source_target_pairs={{4,0},{8,4},{5,1},{9,5},{6,2},{10,6},{7,3},{11,7},{20,16},{24,20},... | collective-permute-start | bytes 1105928 | tf_op jit(solution)/shard_map/ppermute | solution.py:24
  14.9 11.4 %collective-permute-start.1 = (bf16[480,384]{1,0:T(8,128)(2,1)S(1)}, bf16[480,384]{1,0:T(8,128)(2,1)S(1)}, u32[]{:S(2)}, u32[]{:S(2)}) collective-permute-start(bf16[480,384]{1,0:T(8,128)(2,1)S(1)} %collective-permute-done.refs_1_), channel_id=1, source_target_pairs={{4,8},{8,12},{5,9},{9,13},{6,10},{10,14},{7,11},{11,15},{20,24},{2... | collective-permute-start | bytes 1105928 | tf_op jit(solution)/shard_map/ppermute | solution.py:23
  23.9 8.5 %collective-permute-start.5 = (bf16[480,384]{1,0:T(8,128)(2,1)S(1)}, bf16[480,384]{1,0:T(8,128)(2,1)S(1)}, u32[]{:S(2)}, u32[]{:S(2)}) collective-permute-start(bf16[480,384]{1,0:T(8,128)(2,1)S(1)} %collective-permute-done.4), channel_id=1, source_target_pairs={{4,0},{5,1},{6,2},{7,3},{20,16},{21,17},{22,18},{23,19}} | collective-permute-start | bytes 1105928 | tf_op jit(solution)/shard_map/ppermute | solution.py:24
  26.3 6.1 %collective-permute-start.2 = (bf16[480,384]{1,0:T(8,128)(2,1)S(1)}, bf16[480,384]{1,0:T(8,128)(2,1)S(1)}, u32[]{:S(2)}, u32[]{:S(2)}) collective-permute-start(bf16[480,384]{1,0:T(8,128)(2,1)S(1)} %collective-permute-done.1), channel_id=1, source_target_pairs={{8,12},{9,13},{10,14},{11,15},{24,28},{25,29},{26,30},{27,31}} | collective-permute-start | bytes 1105928 | tf_op jit(solution)/shard_map/ppermute | solution.py:23
  27.1 5.3 %copy-start.2 = (bf16[384,384]{1,0:T(8,128)(2,1)S(1)}, bf16[384,384]{1,0:T(8,128)(2,1)}, u32[]{:S(2)}) copy-start(bf16[384,384]{1,0:T(8,128)(2,1)} %wo_ref.1) | copy-start | bytes 884740
  32.4 5.2 %slice-start = ((s8[7962624]{0:T(1024)(128)(4,1)}), s8[3768320]{0:T(1024)(128)(4,1)S(1)}, s32[]{:S(2)}) async-start(s8[7962624]{0:T(1024)(128)(4,1)} %bitcast.102), calls=%async_computation | async-start | bytes 7536640
  34.9 8.8 %collective-permute-start.6 = (bf16[3,160,384]{2,1,0:T(8,128)(2,1)S(1)}, bf16[3,160,384]{2,1,0:T(8,128)(2,1)S(1)}, u32[]{:S(2)}, u32[]{:S(2)}) collective-permute-start(bf16[3,160,384]{2,1,0:T(8,128)(2,1)S(1)} %bitcast.93), channel_id=1, source_target_pairs={{0,1},{1,2},{2,3},{4,5},{5,6},{6,7},{8,9},{9,10},{10,11},{12,13},{... | collective-permute-start | bytes 1105928 | tf_op jit(solution)/shard_map/ppermute | solution.py:15
  37.1 2.2 %slice-start.1 = ((s8[7962624]{0:T(1024)(128)(4,1)}), s8[4194304]{0:T(1024)(128)(4,1)S(1)}, s32[]{:S(2)}) async-start(s8[7962624]{0:T(1024)(128)(4,1)} %bitcast.102), calls=%async_computation.1 | async-start | bytes 8388608
  41.6 2.2 %copy-start.3 = (bf16[2,3,160,384]{3,2,1,0:T(8,128)(2,1)S(1)}, bf16[2,3,160,384]{3,2,1,0:T(8,128)(2,1)}, u32[]{:S(2)}) copy-start(bf16[2,3,160,384]{3,2,1,0:T(8,128)(2,1)} %param.14) | copy-start | bytes 2211844
  43.8 8.8 %collective-permute-start.7 = (bf16[3,160,384]{2,1,0:T(8,128)(2,1)S(1)}, bf16[3,160,384]{2,1,0:T(8,128)(2,1)S(1)}, u32[]{:S(2)}, u32[]{:S(2)}) collective-permute-start(bf16[3,160,384]{2,1,0:T(8,128)(2,1)S(1)} %bitcast_select_fusion.1), channel_id=1, source_target_pairs={{0,1},{1,2},{2,3},{4,5},{5,6},{6,7},{8,9},{9,10},{10,11},{12,13},{... | collective-permute-start | bytes 1105928 | tf_op jit(solution)/shard_map/ppermute | solution.py:15
  53.8 11.6 %collective-permute-start.9 = (bf16[160,384]{1,0:T(8,128)(2,1)S(1)}, bf16[160,384]{1,0:T(8,128)(2,1)S(1)}, u32[]{:S(2)}, u32[]{:S(2)}) collective-permute-start(bf16[160,384]{1,0:T(8,128)(2,1)S(1)} %fusion.1), channel_id=1, source_target_pairs={{4,0},{8,4},{12,8},{5,1},{9,5},{13,9},{6,2},{10,6},{14,10},{7,3},{... | collective-permute-start | bytes 368648 | tf_op jit(solution)/shard_map/ppermute | solution.py:326
  58.6 6.8 %collective-permute-start.8 = (bf16[160,384]{1,0:T(8,128)(2,1)S(1)}, bf16[160,384]{1,0:T(8,128)(2,1)S(1)}, u32[]{:S(2)}, u32[]{:S(2)}) collective-permute-start(bf16[160,384]{1,0:T(8,128)(2,1)S(1)} %fusion), channel_id=1, source_target_pairs={{0,4},{4,8},{8,12},{1,5},{5,9},{9,13},{2,6},{6,10},{10,14},{3,7},{... | collective-permute-start | bytes 368648 | tf_op jit(solution)/shard_map/ppermute | solution.py:329
